TPU v7x, 32 devices: a whole 2x2x4 slice. The times are simulated.
32 devices in a mesh: seq: 8 (over z, x), head: 4 (over y, core).
Axes of the slice: x: 2, y: 2, z: 4, core: 2. Of those that a mesh axis runs over, the one named last changes fastest.
Arguments:
- queries: bfloat16 [16384, 4096], P(('seq', 'head')), may hold values from -6 to 6, as said below
- keys: bfloat16 [16384, 1024], P(('seq', 'head')), may hold values from -6 to 6, as said below
- values: bfloat16 [16384, 1024], P(('seq', 'head')), may hold values from -6 to 6, as said below
- gate_logit: float32 [32], replicated, may hold values from -3 to 3
Outputs:
- attended: bfloat16 [16384, 4096], P(('seq', 'head'))
Inputs may be any that keep to these rules, and one draw needn't show every extreme that they name: queries are real-valued within the stated range. keys are real-valued within the stated range. values are real-valued within the stated range.
All inputs are finite; a program needn't handle non-finite values.
Results may differ from a plain program's by a relative error of at most 0.0034.
Values may be sent and summed in bfloat16 or wider, within the bound.
No kernel may reach another device: no remote copies, remote signals or barrier semaphores. Data moves between devices by JAX's collectives and lax.ppermute only.
A program may use at most 128 MiB of HBM per device.

v0:
```python
import math

import jax
import jax.numpy as jnp
from jax import lax
from jax.sharding import PartitionSpec as P

HQ = 32
KVH = 8
HD = 128
SEG = 2048


def shifted(value, axis, steps):
    count = lax.axis_size(axis)
    first, last = (max(0, -steps), min(count, count - steps))
    return lax.ppermute(value, axis, [(source, source + steps) for source in range(first, last)])


def feature(inputs):
    return jnp.where(inputs > 0, inputs + 1.0, jnp.exp(jnp.minimum(inputs, 0.0)))


def attend(query_rows, key_rows, value_rows, positions, memory, normalizer, gate_rows):
    highest = lax.Precision.HIGHEST
    score_scale = query_rows.shape[-1] ** (-0.5)
    scores = (
        jnp.einsum("rkgd,skd->kgrs", query_rows, key_rows, preferred_element_type=jnp.float32)
        * score_scale
    )
    allowed = jnp.arange(key_rows.shape[0], dtype=jnp.int32)[None, :] <= positions[:, None]
    scores = jnp.where(allowed, scores, -1e30)
    row_top = jnp.max(scores, axis=-1, keepdims=True)
    exp_scores = jnp.exp(scores - row_top)
    weights = (exp_scores / jnp.sum(exp_scores, axis=-1, keepdims=True)).astype(jnp.bfloat16)
    local_part = jnp.einsum(
        "kgrs,skd->rkgd", weights, value_rows, preferred_element_type=jnp.float32
    )
    query_feature = feature(query_rows.astype(jnp.float32))
    numerator = jnp.einsum("rkgd,kde->rkge", query_feature, memory, precision=highest)
    denominator = jnp.maximum(
        jnp.einsum("rkgd,kd->rkg", query_feature, normalizer, precision=highest), 1.0
    )
    retrieved = numerator / denominator[..., None]
    mixing = jax.nn.sigmoid(gate_rows)[None, :, :, None]
    return (mixing * retrieved + (1.0 - mixing) * local_part).astype(jnp.bfloat16)


def local_deltas(key_rows, value_rows):
    segment_count = key_rows.shape[0] // SEG
    head_count = key_rows.shape[1] // HD
    key_feature = feature(key_rows.astype(jnp.float32)).reshape(segment_count, SEG, head_count, HD)
    value_data = value_rows.astype(jnp.float32).reshape(segment_count, SEG, head_count, HD)
    memory_delta = jnp.einsum(
        "stgd,stge->sgde", key_feature, value_data, precision=lax.Precision.HIGHEST
    )
    normal_delta = jnp.sum(key_feature, axis=1)
    return (memory_delta, normal_delta)


def carried_chain(memory_total, normal_total):
    empty = (jnp.zeros_like(memory_total), jnp.zeros_like(normal_total))

    def one_hop(step_index, carry):
        return (
            shifted((carry[0] + memory_total).astype(jnp.bfloat16), "seq", 1).astype(jnp.float32),
            shifted((carry[1] + normal_total).astype(jnp.bfloat16), "seq", 1).astype(jnp.float32),
        )

    return lax.fori_loop(0, lax.axis_size("seq") - 1, one_hop, empty)


def before_states(key_rows, value_rows):
    memory_delta, normal_delta = local_deltas(key_rows, value_rows)
    incoming = carried_chain(jnp.sum(memory_delta, axis=0), jnp.sum(normal_delta, axis=0))
    memory_sums = jnp.cumsum(memory_delta, axis=0)
    normal_sums = jnp.cumsum(normal_delta, axis=0)
    memory_before = incoming[0][None] + jnp.concatenate(
        [jnp.zeros_like(memory_sums), memory_sums[:-1]], axis=0
    )
    normal_before = incoming[1][None] + jnp.concatenate(
        [jnp.zeros_like(normal_sums), normal_sums[:-1]], axis=0
    )
    return (memory_before, normal_before)


def body(queries, keys, values, gate_logit):
    head_place = lax.axis_index("head")
    group_size = HQ // KVH
    query_local, key_local, value_local = (
        lax.all_to_all(queries, "head", split_axis=1, concat_axis=0, tiled=True),
        lax.all_to_all(keys, "head", split_axis=1, concat_axis=0, tiled=True),
        lax.all_to_all(values, "head", split_axis=1, concat_axis=0, tiled=True),
    )
    memory_before, normal_before = before_states(key_local, value_local)
    kv_here = key_local.shape[1] // HD
    gate_rows = lax.dynamic_slice_in_dim(
        gate_logit, head_place * kv_here * group_size, kv_here * group_size
    ).reshape(kv_here, group_size)
    tokens_here = query_local.shape[0]
    segment_count = tokens_here // SEG
    block_rows = math.gcd(SEG, 512)
    block_count = SEG // block_rows
    query_view = query_local.reshape(
        segment_count, block_count, block_rows, kv_here, group_size, HD
    )
    key_view = key_local.reshape(segment_count, SEG, kv_here, HD)
    value_view = value_local.reshape(segment_count, SEG, kv_here, HD)

    def one_block(item_index):
        segment_at = item_index // block_count
        block_at = item_index % block_count
        positions = block_at * block_rows + jnp.arange(block_rows, dtype=jnp.int32)
        return attend(
            query_view[segment_at, block_at],
            key_view[segment_at],
            value_view[segment_at],
            positions,
            memory_before[segment_at],
            normal_before[segment_at],
            gate_rows,
        )

    blocks = lax.map(one_block, jnp.arange(segment_count * block_count, dtype=jnp.int32))
    attended = blocks.reshape(tokens_here, query_local.shape[1])
    return lax.all_to_all(attended, "head", split_axis=0, concat_axis=1, tiled=True)


def solution(mesh):
    in_specs = (P(("seq", "head"), None), P(("seq", "head"), None), P(("seq", "head"), None), P())
    out_specs = P(("seq", "head"), None)
    return jax.shard_map(body, mesh=mesh, in_specs=in_specs, out_specs=out_specs, check_vma=False)
```

profile of v0, /device:TPU:13, one launch (start us, length us, event | category | flops | bytes accessed | tf_op | source)
XLA Modules:
  0.0 343.7 jit_solution(5384518460228308360)
XLA Ops:
  0.0 2.4 copy.33
  2.4 4.3 %all-to-all-start.2 = ((bf16[512,4,256]{2,0,1:T(8,128)(2,1)}), bf16[512,4,256]{2,0,1:T(8,128)(2,1)S(1)}, u32[]{:S(2)}, u32[]{:S(2)}) async-start(bf16[512,4,256]{2,0,1:T(8,128)(2,1)} %bitcast.112), calls=%async_computation.2 | async-start | bytes 2097152 | tf_op jit(solution)/shard_map/all_to_all | solution.py:93
  7.7 11.5 %all-to-all-done.2 = bf16[512,4,256]{2,0,1:T(8,128)(2,1)S(1)} async-done(((bf16[512,4,256]{2,0,1:T(8,128)(2,1)}), bf16[512,4,256]{2,0,1:T(8,128)(2,1)S(1)}, u32[]{:S(2)}, u32[]{:S(2)}) %all-to-all-start.2) | async-done | bytes 1048608 | tf_op jit(solution)/shard_map/all_to_all | solution.py:93
  19.2 5.4 %all-to-all-start.1 = ((bf16[512,4,256]{2,0,1:T(8,128)(2,1)}), bf16[512,4,256]{2,0,1:T(8,128)(2,1)S(1)}, u32[]{:S(2)}, u32[]{:S(2)}) async-start(bf16[512,4,256]{2,0,1:T(8,128)(2,1)} %bitcast.113), calls=%async_computation.1 | async-start | bytes 2097152 | tf_op jit(solution)/shard_map/all_to_all | solution.py:92
  24.8 6.5 %copy.6 = bf16[512,4096]{0,1:T(8,128)(2,1)} copy(bf16[512,4096]{1,0:T(8,128)(2,1)} %param.8) | data formatting | bytes 8388608 | tf_op args[0]
  33.5 3.6 %all-to-all-done.1 = bf16[512,4,256]{2,0,1:T(8,128)(2,1)S(1)} async-done(((bf16[512,4,256]{2,0,1:T(8,128)(2,1)}), bf16[512,4,256]{2,0,1:T(8,128)(2,1)S(1)}, u32[]{:S(2)}, u32[]{:S(2)}) %all-to-all-start.1) | async-done | bytes 1048608 | tf_op jit(solution)/shard_map/all_to_all | solution.py:92
  37.2 6.7 %all-to-all-start = ((bf16[512,4,1024]{0,2,1:T(8,128)(2,1)}), bf16[512,4,1024]{0,2,1:T(8,128)(2,1)}, u32[]{:S(2)}, u32[]{:S(2)}) async-start(bf16[512,4,1024]{0,2,1:T(8,128)(2,1)} %bitcast.144), calls=%async_computation | async-start | bytes 8388608 | tf_op jit(solution)/shard_map/all_to_all | solution.py:91
  43.9 1.9 fusion.55
  45.8 2.3 select_n.61
  49.2 2.5 copy.12
  54.6 55.5 %while.27 = (s32[]{:T(128)}, f32[2,128,128]{2,1,0:T(8,128)S(1)}, f32[2,128]{1,0:T(2,128)S(1)}, f32[2,128,128]{2,1,0:T(8,128)S(1)}, f32[2,128]{1,0:T(2,128)S(1)}, /*index=5*/s32[]{:T(128)}, s32[]{:T(128)}) while((s32[]{:T(128)}, f32[2,128,128]{2,1,0:T(8,128)S(1)}, f32[2,128]{1,0:T(2,128)S(1)}, f32[2,128,128]{2,1,0:T(8,128)S(1)}, ...), condition=%wide.region_2.3_spmd.clone, body=%wide.region_1.2_spmd.clone.sunk | while | flops 132099 | bytes 792744 | solution.py:70
  54.7 3.1 collective-permute-start
  57.8 3.2 collective-permute-start.1
  61.0 2.0 collective-permute-done.1
  63.1 2.7 collective-permute-start
  65.8 3.6 %collective-permute-start.1 = (bf16[2,128]{1,0:T(2,128)(2,1)S(1)}, bf16[2,128]{1,0:T(2,128)(2,1)S(1)}, u32[]{:S(2)}, u32[]{:S(2)}) collective-permute-start(bf16[2,128]{1,0:T(2,128)(2,1)S(1)} %fusion.91), channel_id=1, source_target_pairs={{0,4},{4,8},{8,12},{12,16},{16,20},{20,24},{24,28},{1,5},{5,9},{9,... | collective-permute-start | bytes 1544 | tf_op jit(solution)/shard_map/while/body/eval_jaxpr/ppermute | solution.py:17
  71.3 2.8 collective-permute-start
  74.1 3.5 %collective-permute-start.1 = (bf16[2,128]{1,0:T(2,128)(2,1)S(1)}, bf16[2,128]{1,0:T(2,128)(2,1)S(1)}, u32[]{:S(2)}, u32[]{:S(2)}) collective-permute-start(bf16[2,128]{1,0:T(2,128)(2,1)S(1)} %fusion.91), channel_id=1, source_target_pairs={{0,4},{4,8},{8,12},{12,16},{16,20},{20,24},{24,28},{1,5},{5,9},{9,... | collective-permute-start | bytes 1544 | tf_op jit(solution)/shard_map/while/body/eval_jaxpr/ppermute | solution.py:17
  79.4 3.0 collective-permute-start
  82.4 3.3 collective-permute-start.1
  87.6 2.8 collective-permute-start
  90.5 2.4 collective-permute-start.1
  92.9 2.8 collective-permute-done.1
  95.7 1.9 collective-permute-start
  97.7 2.4 collective-permute-start.1
  100.1 2.8 collective-permute-done.1
  102.9 1.9 collective-permute-start
  104.9 2.4 collective-permute-start.1
  107.3 2.8 collective-permute-done.1
  110.1 166.7 %while.26 = (s32[]{:T(128)}, bf16[4,512,2,4,128]{1,4,3,2,0:T(8,128)(2,1)}, f32[1,2,4,1]{2,1,3,0:T(2,128)S(1)}, s32[4]{0:T(128)S(1)}, bf16[1,4,512,2,4,128]{2,5,4...) while((s32[]{:T(128)}, ...), condition=%wide.region_6.7_spmd, body=%wide.region_3.6_spmd.sunk | while | flops 5165816320 | bytes 96737288 | solution.py:124
  114.9 16.4 %fusion.86 = (f32[2,4,512]{2,1,0:T(4,128)S(1)}, f32[2,4,512,2048]{3,2,1,0:T(8,128)}) fusion(pred[512,2048]{1,0:T(8,128)(4,1)S(1)} %iota_compare_fusion.2, bf16[1,1,512,2,4,128]{2,5,4,3,1,0:T(8,128)(2,1)S(1)} %constant_dynamic-slice_fusion.2, bf16[1,2048,2,128]{3,1,2,0:T(8,128)(2,1)S(1)} %copy-done.3), kind=kOutput, calls=%fused_computation.67.clone.1 | convolution fusion | flops 2181040128 | bytes 36716544 | tf_op jit(solution)/shard_map/while/body/eval_jaxpr/sub | solution.py:34
  131.9 2.3 fusion.88
  134.8 2.4 fusion.87
  137.2 13.1 %fusion.89 = bf16[1,512,2,4,128]{4,1,3,2,0:T(8,128)(2,1)S(1)} fusion(f32[2,4,512,2048]{3,2,1,0:T(8,128)} %get-tuple-element.332, f32[2,4,512]{2,1,0:T(4,128)S(1)} %get-tuple-element.333, f32[2,512,4,128]{3,1,2,0:T(8,128)S(1)} %fusion.87, bf16[1,2048,2,128]{3,1,2,0:T(8,128)(2,1)S(1)} %copy-done.4, f32[2,4]{1,0:T(2,128)S(1)} %get-tuple-element.334, ...), kind=kOutput, calls=%fused_computation.25.clone.1 | convolution fusion | flops 2166882304 | bytes 37781568 | tf_op jit(solution)/shard_map/while/body/eval_jaxpr/kgrs,skd->rkgd/dot_general | solution.py:36
  156.5 16.4 %fusion.86 = (f32[2,4,512]{2,1,0:T(4,128)S(1)}, f32[2,4,512,2048]{3,2,1,0:T(8,128)}) fusion(pred[512,2048]{1,0:T(8,128)(4,1)S(1)} %iota_compare_fusion.2, bf16[1,1,512,2,4,128]{2,5,4,3,1,0:T(8,128)(2,1)S(1)} %constant_dynamic-slice_fusion.2, bf16[1,2048,2,128]{3,1,2,0:T(8,128)(2,1)S(1)} %copy-done.3), kind=kOutput, calls=%fused_computation.67.clone.1 | convolution fusion | flops 2181040128 | bytes 36716544 | tf_op jit(solution)/shard_map/while/body/eval_jaxpr/sub | solution.py:34
  173.5 2.3 fusion.88
  176.4 2.4 fusion.87
  178.8 13.1 %fusion.89 = bf16[1,512,2,4,128]{4,1,3,2,0:T(8,128)(2,1)S(1)} fusion(f32[2,4,512,2048]{3,2,1,0:T(8,128)} %get-tuple-element.332, f32[2,4,512]{2,1,0:T(4,128)S(1)} %get-tuple-element.333, f32[2,512,4,128]{3,1,2,0:T(8,128)S(1)} %fusion.87, bf16[1,2048,2,128]{3,1,2,0:T(8,128)(2,1)S(1)} %copy-done.4, f32[2,4]{1,0:T(2,128)S(1)} %get-tuple-element.334, ...), kind=kOutput, calls=%fused_computation.25.clone.1 | convolution fusion | flops 2166882304 | bytes 37781568 | tf_op jit(solution)/shard_map/while/body/eval_jaxpr/kgrs,skd->rkgd/dot_general | solution.py:36
  198.1 16.4 %fusion.86 = (f32[2,4,512]{2,1,0:T(4,128)S(1)}, f32[2,4,512,2048]{3,2,1,0:T(8,128)}) fusion(pred[512,2048]{1,0:T(8,128)(4,1)S(1)} %iota_compare_fusion.2, bf16[1,1,512,2,4,128]{2,5,4,3,1,0:T(8,128)(2,1)S(1)} %constant_dynamic-slice_fusion.2, bf16[1,2048,2,128]{3,1,2,0:T(8,128)(2,1)S(1)} %copy-done.3), kind=kOutput, calls=%fused_computation.67.clone.1 | convolution fusion | flops 2181040128 | bytes 36716544 | tf_op jit(solution)/shard_map/while/body/eval_jaxpr/sub | solution.py:34
  215.1 2.3 fusion.88
  218.0 2.4 fusion.87
  220.4 13.1 %fusion.89 = bf16[1,512,2,4,128]{4,1,3,2,0:T(8,128)(2,1)S(1)} fusion(f32[2,4,512,2048]{3,2,1,0:T(8,128)} %get-tuple-element.332, f32[2,4,512]{2,1,0:T(4,128)S(1)} %get-tuple-element.333, f32[2,512,4,128]{3,1,2,0:T(8,128)S(1)} %fusion.87, bf16[1,2048,2,128]{3,1,2,0:T(8,128)(2,1)S(1)} %copy-done.4, f32[2,4]{1,0:T(2,128)S(1)} %get-tuple-element.334, ...), kind=kOutput, calls=%fused_computation.25.clone.1 | convolution fusion | flops 2166882304 | bytes 37781568 | tf_op jit(solution)/shard_map/while/body/eval_jaxpr/kgrs,skd->rkgd/dot_general | solution.py:36
  239.7 16.4 %fusion.86 = (f32[2,4,512]{2,1,0:T(4,128)S(1)}, f32[2,4,512,2048]{3,2,1,0:T(8,128)}) fusion(pred[512,2048]{1,0:T(8,128)(4,1)S(1)} %iota_compare_fusion.2, bf16[1,1,512,2,4,128]{2,5,4,3,1,0:T(8,128)(2,1)S(1)} %constant_dynamic-slice_fusion.2, bf16[1,2048,2,128]{3,1,2,0:T(8,128)(2,1)S(1)} %copy-done.3), kind=kOutput, calls=%fused_computation.67.clone.1 | convolution fusion | flops 2181040128 | bytes 36716544 | tf_op jit(solution)/shard_map/while/body/eval_jaxpr/sub | solution.py:34
  256.7 2.3 fusion.88
  259.7 2.4 fusion.87
  262.1 13.1 %fusion.89 = bf16[1,512,2,4,128]{4,1,3,2,0:T(8,128)(2,1)S(1)} fusion(f32[2,4,512,2048]{3,2,1,0:T(8,128)} %get-tuple-element.332, f32[2,4,512]{2,1,0:T(4,128)S(1)} %get-tuple-element.333, f32[2,512,4,128]{3,1,2,0:T(8,128)S(1)} %fusion.87, bf16[1,2048,2,128]{3,1,2,0:T(8,128)(2,1)S(1)} %copy-done.4, f32[2,4]{1,0:T(2,128)S(1)} %get-tuple-element.334, ...), kind=kOutput, calls=%fused_computation.25.clone.1 | convolution fusion | flops 2166882304 | bytes 37781568 | tf_op jit(solution)/shard_map/while/body/eval_jaxpr/kgrs,skd->rkgd/dot_general | solution.py:36
  276.8 60.6 %all_to_all.67 = bf16[4,512,1024]{1,2,0:T(8,128)(2,1)} all-to-all(bf16[4,512,1024]{1,2,0:T(8,128)(2,1)} %bitcast.149), channel_id=1, replica_groups=mesh['seq'=8,'head'=4] {'head'}, dimensions={0} | all-to-all | bytes 8388608 | tf_op jit(solution)/shard_map/all_to_all | solution.py:126
  337.4 6.3 %copy.15 = bf16[512,4096]{1,0:T(8,128)(2,1)} copy(bf16[512,4096]{0,1:T(8,128)(2,1)} %bitcast.145) | data formatting | bytes 8388608 | tf_op jit(solution)/shard_map/all_to_all | solution.py:126
  (115 shorter events, 35.2 us)
Async XLA Ops:
  0.0 6.7 %copy-start.2 = (bf16[512,1024]{1,0:T(8,128)(2,1)S(1)}, bf16[512,1024]{1,0:T(8,128)(2,1)}, u32[]{:S(2)}) copy-start(bf16[512,1024]{1,0:T(8,128)(2,1)} %param.9) | copy-start | bytes 3145732
  2.4 16.9 %all-to-all-start.2 = ((bf16[512,4,256]{2,0,1:T(8,128)(2,1)}), bf16[512,4,256]{2,0,1:T(8,128)(2,1)S(1)}, u32[]{:S(2)}, u32[]{:S(2)}) async-start(bf16[512,4,256]{2,0,1:T(8,128)(2,1)} %bitcast.112), calls=%async_computation.2 | async-start | bytes 2097152 | tf_op jit(solution)/shard_map/all_to_all | solution.py:93
  6.7 18.0 %copy-start.5 = (f32[32]{0:T(128)S(1)}, f32[32]{0:T(128)}, u32[]{:S(2)}) copy-start(f32[32]{0:T(128)} %param.11) | copy-start | bytes 388
  19.2 18.0 %all-to-all-start.1 = ((bf16[512,4,256]{2,0,1:T(8,128)(2,1)}), bf16[512,4,256]{2,0,1:T(8,128)(2,1)S(1)}, u32[]{:S(2)}, u32[]{:S(2)}) async-start(bf16[512,4,256]{2,0,1:T(8,128)(2,1)} %bitcast.113), calls=%async_computation.1 | async-start | bytes 2097152 | tf_op jit(solution)/shard_map/all_to_all | solution.py:92
  37.2 72.9 %all-to-all-start = ((bf16[512,4,1024]{0,2,1:T(8,128)(2,1)}), bf16[512,4,1024]{0,2,1:T(8,128)(2,1)}, u32[]{:S(2)}, u32[]{:S(2)}) async-start(bf16[512,4,1024]{0,2,1:T(8,128)(2,1)} %bitcast.144), calls=%async_computation | async-start | bytes 8388608 | tf_op jit(solution)/shard_map/all_to_all | solution.py:91
  49.2 2.5 copy-start.1
  49.2 3.6 %copy-start = (bf16[2048,2,128]{2,1,0:T(2,128)(2,1)S(1)}, bf16[2048,2,128]{2,1,0:T(2,128)(2,1)}, u32[]{:S(2)}) copy-start(bf16[2048,2,128]{2,1,0:T(2,128)(2,1)} %reshape.101) | copy-start | bytes 3145732
  54.7 8.3 %collective-permute-start = (bf16[2,128,128]{2,1,0:T(8,128)(2,1)S(1)}, bf16[2,128,128]{2,1,0:T(8,128)(2,1)S(1)}, u32[]{:S(2)}, u32[]{:S(2)}) collective-permute-start(bf16[2,128,128]{2,1,0:T(8,128)(2,1)S(1)} %fusion.90), channel_id=1, source_target_pairs={{0,4},{4,8},{8,12},{12,16},{16,20},{20,24},{24,28},{1,5},{5,9},{9,... | collective-permute-start | bytes 196616 | tf_op jit(solution)/shard_map/while/body/eval_jaxpr/ppermute | solution.py:17
  57.8 5.2 %collective-permute-start.1 = (bf16[2,128]{1,0:T(2,128)(2,1)S(1)}, bf16[2,128]{1,0:T(2,128)(2,1)S(1)}, u32[]{:S(2)}, u32[]{:S(2)}) collective-permute-start(bf16[2,128]{1,0:T(2,128)(2,1)S(1)} %fusion.91), channel_id=1, source_target_pairs={{0,4},{4,8},{8,12},{12,16},{16,20},{20,24},{24,28},{1,5},{5,9},{9,... | collective-permute-start | bytes 1544 | tf_op jit(solution)/shard_map/while/body/eval_jaxpr/ppermute | solution.py:17
  63.1 8.2 %collective-permute-start = (bf16[2,128,128]{2,1,0:T(8,128)(2,1)S(1)}, bf16[2,128,128]{2,1,0:T(8,128)(2,1)S(1)}, u32[]{:S(2)}, u32[]{:S(2)}) collective-permute-start(bf16[2,128,128]{2,1,0:T(8,128)(2,1)S(1)} %fusion.90), channel_id=1, source_target_pairs={{0,4},{4,8},{8,12},{12,16},{16,20},{20,24},{24,28},{1,5},{5,9},{9,... | collective-permute-start | bytes 196616 | tf_op jit(solution)/shard_map/while/body/eval_jaxpr/ppermute | solution.py:17
  65.8 5.5 %collective-permute-start.1 = (bf16[2,128]{1,0:T(2,128)(2,1)S(1)}, bf16[2,128]{1,0:T(2,128)(2,1)S(1)}, u32[]{:S(2)}, u32[]{:S(2)}) collective-permute-start(bf16[2,128]{1,0:T(2,128)(2,1)S(1)} %fusion.91), channel_id=1, source_target_pairs={{0,4},{4,8},{8,12},{12,16},{16,20},{20,24},{24,28},{1,5},{5,9},{9,... | collective-permute-start | bytes 1544 | tf_op jit(solution)/shard_map/while/body/eval_jaxpr/ppermute | solution.py:17
  71.3 8.0 %collective-permute-start = (bf16[2,128,128]{2,1,0:T(8,128)(2,1)S(1)}, bf16[2,128,128]{2,1,0:T(8,128)(2,1)S(1)}, u32[]{:S(2)}, u32[]{:S(2)}) collective-permute-start(bf16[2,128,128]{2,1,0:T(8,128)(2,1)S(1)} %fusion.90), channel_id=1, source_target_pairs={{0,4},{4,8},{8,12},{12,16},{16,20},{20,24},{24,28},{1,5},{5,9},{9,... | collective-permute-start | bytes 196616 | tf_op jit(solution)/shard_map/while/body/eval_jaxpr/ppermute | solution.py:17
  74.1 5.2 %collective-permute-start.1 = (bf16[2,128]{1,0:T(2,128)(2,1)S(1)}, bf16[2,128]{1,0:T(2,128)(2,1)S(1)}, u32[]{:S(2)}, u32[]{:S(2)}) collective-permute-start(bf16[2,128]{1,0:T(2,128)(2,1)S(1)} %fusion.91), channel_id=1, source_target_pairs={{0,4},{4,8},{8,12},{12,16},{16,20},{20,24},{24,28},{1,5},{5,9},{9,... | collective-permute-start | bytes 1544 | tf_op jit(solution)/shard_map/while/body/eval_jaxpr/ppermute | solution.py:17
  79.4 8.2 %collective-permute-start = (bf16[2,128,128]{2,1,0:T(8,128)(2,1)S(1)}, bf16[2,128,128]{2,1,0:T(8,128)(2,1)S(1)}, u32[]{:S(2)}, u32[]{:S(2)}) collective-permute-start(bf16[2,128,128]{2,1,0:T(8,128)(2,1)S(1)} %fusion.90), channel_id=1, source_target_pairs={{0,4},{4,8},{8,12},{12,16},{16,20},{20,24},{24,28},{1,5},{5,9},{9,... | collective-permute-start | bytes 196616 | tf_op jit(solution)/shard_map/while/body/eval_jaxpr/ppermute | solution.py:17
  82.4 5.2 %collective-permute-start.1 = (bf16[2,128]{1,0:T(2,128)(2,1)S(1)}, bf16[2,128]{1,0:T(2,128)(2,1)S(1)}, u32[]{:S(2)}, u32[]{:S(2)}) collective-permute-start(bf16[2,128]{1,0:T(2,128)(2,1)S(1)} %fusion.91), channel_id=1, source_target_pairs={{0,4},{4,8},{8,12},{12,16},{16,20},{20,24},{24,28},{1,5},{5,9},{9,... | collective-permute-start | bytes 1544 | tf_op jit(solution)/shard_map/while/body/eval_jaxpr/ppermute | solution.py:17
  87.6 8.0 %collective-permute-start = (bf16[2,128,128]{2,1,0:T(8,128)(2,1)S(1)}, bf16[2,128,128]{2,1,0:T(8,128)(2,1)S(1)}, u32[]{:S(2)}, u32[]{:S(2)}) collective-permute-start(bf16[2,128,128]{2,1,0:T(8,128)(2,1)S(1)} %fusion.90), channel_id=1, source_target_pairs={{0,4},{4,8},{8,12},{12,16},{16,20},{20,24},{24,28},{1,5},{5,9},{9,... | collective-permute-start | bytes 196616 | tf_op jit(solution)/shard_map/while/body/eval_jaxpr/ppermute | solution.py:17
  90.5 5.2 %collective-permute-start.1 = (bf16[2,128]{1,0:T(2,128)(2,1)S(1)}, bf16[2,128]{1,0:T(2,128)(2,1)S(1)}, u32[]{:S(2)}, u32[]{:S(2)}) collective-permute-start(bf16[2,128]{1,0:T(2,128)(2,1)S(1)} %fusion.91), channel_id=1, source_target_pairs={{0,4},{4,8},{8,12},{12,16},{16,20},{20,24},{24,28},{1,5},{5,9},{9,... | collective-permute-start | bytes 1544 | tf_op jit(solution)/shard_map/while/body/eval_jaxpr/ppermute | solution.py:17
  95.7 7.1 %collective-permute-start = (bf16[2,128,128]{2,1,0:T(8,128)(2,1)S(1)}, bf16[2,128,128]{2,1,0:T(8,128)(2,1)S(1)}, u32[]{:S(2)}, u32[]{:S(2)}) collective-permute-start(bf16[2,128,128]{2,1,0:T(8,128)(2,1)S(1)} %fusion.90), channel_id=1, source_target_pairs={{0,4},{4,8},{8,12},{12,16},{16,20},{20,24},{24,28},{1,5},{5,9},{9,... | collective-permute-start | bytes 196616 | tf_op jit(solution)/shard_map/while/body/eval_jaxpr/ppermute | solution.py:17
  97.7 5.2 %collective-permute-start.1 = (bf16[2,128]{1,0:T(2,128)(2,1)S(1)}, bf16[2,128]{1,0:T(2,128)(2,1)S(1)}, u32[]{:S(2)}, u32[]{:S(2)}) collective-permute-start(bf16[2,128]{1,0:T(2,128)(2,1)S(1)} %fusion.91), channel_id=1, source_target_pairs={{0,4},{4,8},{8,12},{12,16},{16,20},{20,24},{24,28},{1,5},{5,9},{9,... | collective-permute-start | bytes 1544 | tf_op jit(solution)/shard_map/while/body/eval_jaxpr/ppermute | solution.py:17
  102.9 7.1 %collective-permute-start = (bf16[2,128,128]{2,1,0:T(8,128)(2,1)S(1)}, bf16[2,128,128]{2,1,0:T(8,128)(2,1)S(1)}, u32[]{:S(2)}, u32[]{:S(2)}) collective-permute-start(bf16[2,128,128]{2,1,0:T(8,128)(2,1)S(1)} %fusion.90), channel_id=1, source_target_pairs={{0,4},{4,8},{8,12},{12,16},{16,20},{20,24},{24,28},{1,5},{5,9},{9,... | collective-permute-start | bytes 196616 | tf_op jit(solution)/shard_map/while/body/eval_jaxpr/ppermute | solution.py:17
  104.9 5.2 %collective-permute-start.1 = (bf16[2,128]{1,0:T(2,128)(2,1)S(1)}, bf16[2,128]{1,0:T(2,128)(2,1)S(1)}, u32[]{:S(2)}, u32[]{:S(2)}) collective-permute-start(bf16[2,128]{1,0:T(2,128)(2,1)S(1)} %fusion.91), channel_id=1, source_target_pairs={{0,4},{4,8},{8,12},{12,16},{16,20},{20,24},{24,28},{1,5},{5,9},{9,... | collective-permute-start | bytes 1544 | tf_op jit(solution)/shard_map/while/body/eval_jaxpr/ppermute | solution.py:17
  110.3 4.6 %copy-start.3 = (bf16[1,2048,2,128]{3,1,2,0:T(8,128)(2,1)S(1)}, bf16[1,2048,2,128]{3,1,2,0:T(8,128)(2,1)}, u32[]{:S(2)}) copy-start(bf16[1,2048,2,128]{3,1,2,0:T(8,128)(2,1)} %get-tuple-element.397) | copy-start | bytes 3145732 | tf_op jit(solution)/shard_map/while
  134.8 2.4 copy-start.4
  151.9 4.5 %copy-start.3 = (bf16[1,2048,2,128]{3,1,2,0:T(8,128)(2,1)S(1)}, bf16[1,2048,2,128]{3,1,2,0:T(8,128)(2,1)}, u32[]{:S(2)}) copy-start(bf16[1,2048,2,128]{3,1,2,0:T(8,128)(2,1)} %get-tuple-element.397) | copy-start | bytes 3145732 | tf_op jit(solution)/shard_map/while
  176.4 2.4 copy-start.4
  193.5 4.5 %copy-start.3 = (bf16[1,2048,2,128]{3,1,2,0:T(8,128)(2,1)S(1)}, bf16[1,2048,2,128]{3,1,2,0:T(8,128)(2,1)}, u32[]{:S(2)}) copy-start(bf16[1,2048,2,128]{3,1,2,0:T(8,128)(2,1)} %get-tuple-element.397) | copy-start | bytes 3145732 | tf_op jit(solution)/shard_map/while
  218.0 2.4 copy-start.4
  235.2 4.5 %copy-start.3 = (bf16[1,2048,2,128]{3,1,2,0:T(8,128)(2,1)S(1)}, bf16[1,2048,2,128]{3,1,2,0:T(8,128)(2,1)}, u32[]{:S(2)}) copy-start(bf16[1,2048,2,128]{3,1,2,0:T(8,128)(2,1)} %get-tuple-element.397) | copy-start | bytes 3145732 | tf_op jit(solution)/shard_map/while
  259.6 2.4 copy-start.4
where the time goes:
time: 347 us; the launch traced here: 344 us
  matrix products  138 us (40%)
  blocking collectives  60.6 us (17%)
  starting transfers between devices  55.5 us (16%)
  local copies, waits for them, and re-layouts  44.9 us (13%)
  waiting for transfers between devices  30.9 us (9%)
  loops' own time  8.63 us (2%)
  other arithmetic  4.88 us (1%)
    sub x4, matrix products, attend(): exp_scores = jnp.exp(scores - row_top)  65.4 us
    all_to_all x1, blocking collectives, body(): lax.all_to_all(attended, 'head', split_axis=0, concat_axis=1, tiled=True)  60.6 us
    dot_general x4, matrix products, attend(): jnp.einsum('kgrs,skd->rkgd', weights, value_rows, preferred_element_type=...  52.3 us
    ppermute x14, starting transfers between devices, shifted(): lax.ppermute(value, axis, [(source, source + steps) for source in range(f...  39.1 us
    ppermute x14, waiting for transfers between devices, shifted(): lax.ppermute(value, axis, [(source, source + steps) for source in range(f...  15.7 us
    all_to_all x1, waiting for transfers between devices, body(): lax.all_to_all(values, 'head', split_axis=1, concat_axis=0, tiled=True)  11.5 us
    dot_general x4, matrix products, attend(): jnp.einsum('rkgd,kde->rkge', query_feature, memory, precision=highest)  9.51 us
    dot_general x4, matrix products, attend(): jnp.einsum('rkgd,kd->rkg', query_feature, normalizer, precision=highest)  9.15 us
  transfers between devices with their start and end apart: 17, of which 9 were waited for; matrix products, arithmetic and copies ran while one was open for 6% of the time, Pallas kernels for 0%

commit v1 on v0

v1 whole, which is shorter than its diff:
```python
import functools
import math

import jax
import jax.numpy as jnp
from jax import lax
from jax.experimental import pallas as pl
from jax.experimental.pallas import tpu as pltpu
from jax.sharding import PartitionSpec as P

HQ = 32
KVH = 8
HD = 128
SEG = 2048
BLOCK = 512


def feature(inputs):
    return jnp.where(inputs > 0, inputs + 1.0, jnp.exp(jnp.minimum(inputs, 0.0)))


def attention_kernel(
    gate_ref, q_ref, k_ref, v_ref, mem_ref, nrm_ref, o_ref, m_sc, l_sc, acc_sc, *, group_size
):
    head = pl.program_id(0)
    q_block = pl.program_id(1)
    k_block = pl.program_id(2)
    score_scale = HD ** (-0.5)

    @pl.when(k_block == 0)
    def _init():
        m_sc[...] = jnp.full(m_sc.shape, -jnp.inf, jnp.float32)
        l_sc[...] = jnp.zeros(l_sc.shape, jnp.float32)
        acc_sc[...] = jnp.zeros(acc_sc.shape, jnp.float32)

    def step(masked):
        scores = (
            lax.dot_general(
                q_ref[...], k_ref[...], (((1,), (1,)), ((), ())),
                preferred_element_type=jnp.float32,
            )
            * score_scale
        )
        if masked:
            rows = lax.broadcasted_iota(jnp.int32, scores.shape, 0)
            cols = lax.broadcasted_iota(jnp.int32, scores.shape, 1)
            scores = jnp.where(cols <= rows, scores, -1e30)
        m_prev = m_sc[...]
        m_new = jnp.maximum(m_prev, jnp.max(scores, axis=-1, keepdims=True))
        probs = jnp.exp(scores - m_new)
        alpha = jnp.exp(m_prev - m_new)
        l_sc[...] = alpha * l_sc[...] + jnp.sum(probs, axis=-1, keepdims=True)
        acc_sc[...] = alpha * acc_sc[...] + jnp.dot(
            probs.astype(jnp.bfloat16), v_ref[...], preferred_element_type=jnp.float32
        )
        m_sc[...] = m_new

    @pl.when(k_block < q_block)
    def _full():
        step(False)

    @pl.when(k_block == q_block)
    def _last():
        step(True)
        local_part = acc_sc[...] / l_sc[...]
        query_feature = feature(q_ref[...].astype(jnp.float32))
        numerator = jnp.dot(
            query_feature, mem_ref[0], precision=lax.Precision.HIGHEST,
            preferred_element_type=jnp.float32,
        )
        denominator = jnp.maximum(
            jnp.sum(query_feature * nrm_ref[0], axis=-1, keepdims=True), 1.0
        )
        mixing = gate_ref[head]
        o_ref[...] = (
            mixing * (numerator / denominator) + (1.0 - mixing) * local_part
        ).astype(o_ref.dtype)


def attention(query_local, key_local, value_local, memory, normalizer, mixing):
    tokens = query_local.shape[0]
    q_heads = query_local.shape[1] // HD
    kv_heads = key_local.shape[1] // HD
    group_size = q_heads // kv_heads
    blocks = tokens // BLOCK
    kernel = functools.partial(attention_kernel, group_size=group_size)
    return pl.pallas_call(
        kernel,
        grid=(q_heads, blocks, blocks),
        in_specs=[
            pl.BlockSpec(memory_space=pltpu.SMEM),
            pl.BlockSpec((BLOCK, HD), lambda h, i, j: (i, h)),
            pl.BlockSpec((BLOCK, HD), lambda h, i, j: (jnp.minimum(j, i), h // group_size)),
            pl.BlockSpec((BLOCK, HD), lambda h, i, j: (jnp.minimum(j, i), h // group_size)),
            pl.BlockSpec((1, HD, HD), lambda h, i, j: (h // group_size, 0, 0)),
            pl.BlockSpec((1, 1, HD), lambda h, i, j: (h // group_size, 0, 0)),
        ],
        out_specs=pl.BlockSpec((BLOCK, HD), lambda h, i, j: (i, h)),
        out_shape=jax.ShapeDtypeStruct(query_local.shape, jnp.bfloat16),
        scratch_shapes=[
            pltpu.VMEM((BLOCK, 1), jnp.float32),
            pltpu.VMEM((BLOCK, 1), jnp.float32),
            pltpu.VMEM((BLOCK, HD), jnp.float32),
        ],
        compiler_params=pltpu.CompilerParams(
            dimension_semantics=("arbitrary", "arbitrary", "arbitrary")
        ),
    )(mixing, query_local, key_local, value_local, memory, normalizer)


def before_states(key_local, value_local):
    kv_heads = key_local.shape[1] // HD
    key_feature = feature(key_local.astype(jnp.float32)).reshape(-1, kv_heads, HD)
    value_data = value_local.astype(jnp.float32).reshape(-1, kv_heads, HD)
    memory_delta = jnp.einsum(
        "tgd,tge->gde", key_feature, value_data, precision=lax.Precision.HIGHEST
    )
    normal_delta = jnp.sum(key_feature, axis=0)
    memory_all = lax.all_gather(memory_delta.astype(jnp.bfloat16), "seq").astype(jnp.float32)
    normal_all = lax.all_gather(normal_delta.astype(jnp.bfloat16), "seq").astype(jnp.float32)
    earlier = (
        jnp.arange(lax.axis_size("seq"), dtype=jnp.int32) < lax.axis_index("seq")
    ).astype(jnp.float32)
    memory = jnp.sum(memory_all * earlier[:, None, None, None], axis=0)
    normalizer = jnp.sum(normal_all * earlier[:, None, None], axis=0)
    return memory, normalizer[:, None, :]


def to_heads(rows, parts):
    tokens_here, cols = rows.shape
    split = rows.reshape(tokens_here, parts, cols // parts).transpose(1, 0, 2)
    gathered = lax.all_to_all(split, "head", split_axis=0, concat_axis=0, tiled=True)
    return gathered.reshape(parts * tokens_here, cols // parts)


def body(queries, keys, values, gate_logit):
    parts = lax.axis_size("head")
    head_place = lax.axis_index("head")
    key_local = to_heads(keys, parts)
    value_local = to_heads(values, parts)
    memory, normalizer = before_states(key_local, value_local)
    query_local = to_heads(queries, parts)
    q_heads = query_local.shape[1] // HD
    mixing = jax.nn.sigmoid(lax.dynamic_slice_in_dim(gate_logit, head_place * q_heads, q_heads))
    attended = attention(query_local, key_local, value_local, memory, normalizer, mixing)
    tokens_here = queries.shape[0]
    cols = attended.shape[1]
    split = attended.reshape(parts, tokens_here, cols)
    returned = lax.all_to_all(split, "head", split_axis=0, concat_axis=0, tiled=True)
    return returned.transpose(1, 0, 2).reshape(tokens_here, parts * cols)


def solution(mesh):
    in_specs = (P(("seq", "head"), None), P(("seq", "head"), None), P(("seq", "head"), None), P())
    out_specs = P(("seq", "head"), None)
    return jax.shard_map(body, mesh=mesh, in_specs=in_specs, out_specs=out_specs, check_vma=False)
```

time: 347 us -> 297 us (0.86)
  the two profiles are of different devices: /device:TPU:13 before, /device:TPU:0 now
where the time goes in v1:
time: 297 us; the launch traced here: 295 us
  Pallas kernels  133 us (45%)
  blocking collectives  105 us (35%)
  waiting for transfers between devices  23.1 us (8%)
  local copies, waits for them, and re-layouts  14.2 us (5%)
  starting transfers between devices  12.7 us (4%)
  other arithmetic  4 us (1%)
  matrix products  3.4 us (1%)
    pallas_call x1, Pallas kernels, attention(): pl.pallas_call(kernel, grid=(q_heads, blocks, blocks), in_specs=[pl.Block...  133 us
    all_to_all x1, blocking collectives, body(): lax.all_to_all(split, 'head', split_axis=0, concat_axis=0, tiled=True)  51.9 us
    all_gather x1, blocking collectives, before_states(): lax.all_gather(memory_delta.astype(jnp.bfloat16), 'seq').astype(jnp.float32)  31.5 us
    all_to_all x3, waiting for transfers between devices, to_heads(): lax.all_to_all(split, 'head', split_axis=0, concat_axis=0, tiled=True)  23.1 us
    all_gather x1, blocking collectives, before_states(): lax.all_gather(normal_delta.astype(jnp.bfloat16), 'seq').astype(jnp.float32)  21.4 us
    all_to_all x3, starting transfers between devices, to_heads(): lax.all_to_all(split, 'head', split_axis=0, concat_axis=0, tiled=True)  12.7 us
    reshape x3, local copies, waits for them, and re-layouts, to_heads(): split = rows.reshape(tokens_here, parts, cols // parts).transpose(1, 0, 2)  8.19 us
  transfers between devices with their start and end apart: 3, of which 2 were waited for; matrix products, arithmetic and copies ran while one was open for 6% of the time, Pallas kernels for 0%

profile of v1, /device:TPU:0, one launch (start us, length us, event | category | flops | bytes accessed | tf_op | source)
XLA Modules:
  0.0 295.4 jit_solution(4720709636544241964)
XLA Ops:
  0.0 0.0 copy-start.2
  0.0 2.4 copy.38
  2.4 4.2 %all-to-all-start.1 = ((bf16[4,512,256]{2,1,0:T(8,128)(2,1)}), bf16[4,512,256]{2,1,0:T(8,128)(2,1)S(1)}, u32[]{:S(2)}, u32[]{:S(2)}) async-start(bf16[4,512,256]{2,1,0:T(8,128)(2,1)} %bitcast.33), calls=%async_computation.1 | async-start | bytes 2097152 | tf_op jit(solution)/shard_map/all_to_all | solution.py:132
  6.6 0.0 copy-done.2
  6.6 1.0 copy.37
  7.6 13.4 %all-to-all-done.1 = bf16[4,512,256]{2,1,0:T(8,128)(2,1)S(1)} async-done(((bf16[4,512,256]{2,1,0:T(8,128)(2,1)}), bf16[4,512,256]{2,1,0:T(8,128)(2,1)S(1)}, u32[]{:S(2)}, u32[]{:S(2)}) %all-to-all-start.1) | async-done | bytes 1048608 | tf_op jit(solution)/shard_map/all_to_all | solution.py:132
  21.1 0.0 copy-start
  21.1 3.5 %all-to-all-start.2 = ((bf16[4,512,256]{2,1,0:T(8,128)(2,1)}), bf16[4,512,256]{2,1,0:T(8,128)(2,1)S(1)}, u32[]{:S(2)}, u32[]{:S(2)}) async-start(bf16[4,512,256]{2,1,0:T(8,128)(2,1)} %bitcast.31), calls=%async_computation.2 | async-start | bytes 2097152 | tf_op jit(solution)/shard_map/all_to_all | solution.py:132
  24.6 4.8 %copy.36 = bf16[64,4,8,1024]{3,2,0,1:T(8,128)(2,1)} copy(bf16[64,4,8,1024]{3,2,1,0:T(8,128)(2,1)} %bitcast.39) | data formatting | bytes 8388608 | tf_op jit(solution)/shard_map/reshape | solution.py:131
  29.4 9.6 %all-to-all-done.2 = bf16[4,512,256]{2,1,0:T(8,128)(2,1)S(1)} async-done(((bf16[4,512,256]{2,1,0:T(8,128)(2,1)}), bf16[4,512,256]{2,1,0:T(8,128)(2,1)S(1)}, u32[]{:S(2)}, u32[]{:S(2)}) %all-to-all-start.2) | async-done | bytes 1048608 | tf_op jit(solution)/shard_map/all_to_all | solution.py:132
  39.0 0.0 copy-start.1
  39.0 0.0 copy-start.3
  39.0 5.0 %all-to-all-start = ((bf16[4,512,1024]{2,1,0:T(8,128)(2,1)}), bf16[4,512,1024]{2,1,0:T(8,128)(2,1)}, u32[]{:S(2)}, u32[]{:S(2)}) async-start(bf16[4,512,1024]{2,1,0:T(8,128)(2,1)} %bitcast.34), calls=%async_computation | async-start | bytes 8388608 | tf_op jit(solution)/shard_map/all_to_all | solution.py:132
  44.0 0.0 copy-done.3
  44.0 0.6 add_divide_fusion.gate_ref
  44.7 0.0 copy-done
  44.7 1.9 fusion.9
  46.6 3.3 %reshape.73 = f32[2048,2,128]{2,1,0:T(2,128)} reshape(f32[4,512,256]{2,1,0:T(8,128)} %get-tuple-element.6) | data formatting | bytes 4194304 | tf_op jit(solution)/shard_map/jit(_where)/select_n | solution.py:19
  49.8 0.0 copy-done.1
  49.8 0.3 reshape.68
  50.1 21.4 %all_gather.12 = bf16[8,2,128]{2,1,0:T(2,128)(2,1)S(1)} all-gather(bf16[1,2,128]{2,1,0:T(2,128)(2,1)S(1)} %bitcast.44), channel_id=1, replica_groups=mesh['seq'=8,'head'=4] {'seq'}, dimensions={0}, use_global_device_ids=true | all-gather | bytes 4608 | tf_op jit(solution)/shard_map/all_gather | solution.py:120
  71.5 0.7 multiply_reduce_fusion
  72.2 3.4 %fusion.4 = bf16[2,128,128]{2,1,0:T(8,128)(2,1)S(1)} fusion(f32[2048,2,128]{2,1,0:T(2,128)} %reshape.73, bf16[2048,2,128]{2,1,0:T(2,128)(2,1)S(1)} %reshape.68), kind=kOutput, calls=%fused_computation.8 | convolution fusion | flops 805339136 | bytes 3211264 | tf_op jit(solution)/shard_map/tgd,tge->gde/dot_general | solution.py:115
  75.6 31.5 %all-gather = bf16[16,128,128]{2,1,0:T(8,128)(2,1)S(1)} all-gather(bf16[2,128,128]{2,1,0:T(8,128)(2,1)S(1)} %fusion.4), channel_id=2, replica_groups=mesh['seq'=8,'head'=4] {'seq'}, dimensions={0}, use_global_device_ids=true | all-gather | bytes 589824 | tf_op jit(solution)/shard_map/all_gather | solution.py:119
  107.0 0.8 fusion.7.mem_ref
  107.8 0.0 all-to-all-done
  107.9 133.2 %shard_map.46 = bf16[2048,1024]{1,0:T(8,128)(2,1)} custom-call(f32[8]{0:T(128)} %add_divide_fusion.gate_ref, bf16[2048,1024]{1,0:T(8,128)(2,1)} %bitcast.1.q_ref, bf16[2048,256]{1,0:T(8,128)(2,1)} %bitcast.37, bf16[2048,256]{1,0:T(8,128)(2,1)} %bitcast.38, f32[2,128,128]{2,1,0:T(8,128)} %fusion.7.mem_ref, f32[2,1,128]{2,1,0:T(1,128)} %bitcast.43), custom_call_target="tpu_custom_call" | custom-call | tf_op jit(solution)/shard_map/pallas_call | solution.py:87
  241.1 51.9 %all_to_all.20 = bf16[4,512,1024]{2,1,0:T(8,128)(2,1)S(1)} all-to-all(bf16[4,512,1024]{2,1,0:T(8,128)(2,1)} %bitcast.35), channel_id=1, replica_groups=mesh['seq'=8,'head'=4] {'head'}, dimensions={0} | all-to-all | bytes 8388608 | tf_op jit(solution)/shard_map/all_to_all | solution.py:149
  293.0 2.5 copy.26
  (1 shorter events, 0.0 us)
Async XLA Ops:
  0.0 6.6 %copy-start.2 = (bf16[512,1024]{1,0:T(8,128)(2,1)S(1)}, bf16[512,1024]{1,0:T(8,128)(2,1)}, u32[]{:S(2)}) copy-start(bf16[512,1024]{1,0:T(8,128)(2,1)} %param.6) | copy-start | bytes 3145732
  2.4 18.7 %all-to-all-start.1 = ((bf16[4,512,256]{2,1,0:T(8,128)(2,1)}), bf16[4,512,256]{2,1,0:T(8,128)(2,1)S(1)}, u32[]{:S(2)}, u32[]{:S(2)}) async-start(bf16[4,512,256]{2,1,0:T(8,128)(2,1)} %bitcast.33), calls=%async_computation.1 | async-start | bytes 2097152 | tf_op jit(solution)/shard_map/all_to_all | solution.py:132
  21.1 23.6 %copy-start = (bf16[4,512,256]{2,1,0:T(8,128)(2,1)}, bf16[4,512,256]{2,1,0:T(8,128)(2,1)S(1)}, u32[]{:S(2)}) copy-start(bf16[4,512,256]{2,1,0:T(8,128)(2,1)S(1)} %all-to-all-done.1) | copy-start | bytes 3145732
  21.1 18.0 %all-to-all-start.2 = ((bf16[4,512,256]{2,1,0:T(8,128)(2,1)}), bf16[4,512,256]{2,1,0:T(8,128)(2,1)S(1)}, u32[]{:S(2)}, u32[]{:S(2)}) async-start(bf16[4,512,256]{2,1,0:T(8,128)(2,1)} %bitcast.31), calls=%async_computation.2 | async-start | bytes 2097152 | tf_op jit(solution)/shard_map/all_to_all | solution.py:132
  39.0 10.8 %copy-start.1 = (bf16[4,512,256]{2,1,0:T(8,128)(2,1)}, bf16[4,512,256]{2,1,0:T(8,128)(2,1)S(1)}, u32[]{:S(2)}) copy-start(bf16[4,512,256]{2,1,0:T(8,128)(2,1)S(1)} %all-to-all-done.2) | copy-start | bytes 3145732
  39.0 5.0 %copy-start.3 = (f32[32]{0:T(128)S(1)}, f32[32]{0:T(128)}, u32[]{:S(2)}) copy-start(f32[32]{0:T(128)} %param.7) | copy-start | bytes 388
  39.0 68.8 %all-to-all-start = ((bf16[4,512,1024]{2,1,0:T(8,128)(2,1)}), bf16[4,512,1024]{2,1,0:T(8,128)(2,1)}, u32[]{:S(2)}, u32[]{:S(2)}) async-start(bf16[4,512,1024]{2,1,0:T(8,128)(2,1)} %bitcast.34), calls=%async_computation | async-start | bytes 8388608 | tf_op jit(solution)/shard_map/all_to_all | solution.py:132

commit v2 on v1

v2 whole, which is shorter than its diff:
```python
import functools

import jax
import jax.numpy as jnp
import numpy as np
from jax import lax
from jax.experimental import pallas as pl
from jax.experimental.pallas import tpu as pltpu
from jax.sharding import PartitionSpec as P

HQ = 32
KVH = 8
HD = 128
SEG = 2048
BLOCK = 512
LANES = 128


def feature(inputs):
    return jnp.where(inputs > 0, inputs + 1.0, jnp.exp(jnp.minimum(inputs, 0.0)))


def flash_kernel(qi_ref, kj_ref, q_ref, k_ref, v_ref, o_ref, m_sc, l_sc, acc_sc, *, group_size):
    step_at = pl.program_id(0)
    q_block = qi_ref[step_at]
    k_block = kj_ref[step_at]
    score_scale = HD ** (-0.5)

    @pl.when(k_block == 0)
    def _init():
        m_sc[...] = jnp.full(m_sc.shape, -jnp.inf, jnp.float32)
        l_sc[...] = jnp.zeros(l_sc.shape, jnp.float32)
        acc_sc[...] = jnp.zeros(acc_sc.shape, jnp.float32)

    def step(masked):
        key_rows = k_ref[...]
        value_rows = v_ref[...]
        if masked:
            rows = lax.broadcasted_iota(jnp.int32, (BLOCK, BLOCK), 0)
            cols = lax.broadcasted_iota(jnp.int32, (BLOCK, BLOCK), 1)
            allowed = cols <= rows
        for head in range(group_size):
            lanes = slice(head * HD, (head + 1) * HD)
            scores = (
                lax.dot_general(
                    q_ref[:, lanes], key_rows, (((1,), (1,)), ((), ())),
                    preferred_element_type=jnp.float32,
                )
                * score_scale
            )
            if masked:
                scores = jnp.where(allowed, scores, -1e30)
            m_prev = m_sc[head]
            m_new = jnp.maximum(m_prev, jnp.max(scores, axis=-1, keepdims=True))
            probs = jnp.exp(scores - m_new[:, :1])
            alpha = jnp.exp(m_prev - m_new)
            l_sc[head] = alpha * l_sc[head] + jnp.sum(probs, axis=-1, keepdims=True)
            acc_sc[:, lanes] = alpha * acc_sc[:, lanes] + jnp.dot(
                probs.astype(jnp.bfloat16), value_rows, preferred_element_type=jnp.float32
            )
            m_sc[head] = m_new

    @pl.when(k_block < q_block)
    def _full():
        step(False)

    @pl.when(k_block == q_block)
    def _last():
        step(True)
        for head in range(group_size):
            lanes = slice(head * HD, (head + 1) * HD)
            o_ref[:, lanes] = acc_sc[:, lanes] / l_sc[head]


def local_attention(query_rows, kv_rows, key_col, value_col):
    tokens, width = query_rows.shape
    group_size = width // HD
    blocks = tokens // BLOCK
    pairs = [(i, j) for i in range(blocks) for j in range(i + 1)]
    q_index = jnp.asarray(np.array([p[0] for p in pairs], np.int32))
    k_index = jnp.asarray(np.array([p[1] for p in pairs], np.int32))
    grid_spec = pltpu.PrefetchScalarGridSpec(
        num_scalar_prefetch=2,
        grid=(len(pairs),),
        in_specs=[
            pl.BlockSpec((BLOCK, width), lambda t, qi, kj: (qi[t], 0)),
            pl.BlockSpec((BLOCK, HD), lambda t, qi, kj: (kj[t], key_col)),
            pl.BlockSpec((BLOCK, HD), lambda t, qi, kj: (kj[t], value_col)),
        ],
        out_specs=pl.BlockSpec((BLOCK, width), lambda t, qi, kj: (qi[t], 0)),
        scratch_shapes=[
            pltpu.VMEM((group_size, BLOCK, LANES), jnp.float32),
            pltpu.VMEM((group_size, BLOCK, LANES), jnp.float32),
            pltpu.VMEM((BLOCK, width), jnp.float32),
        ],
    )
    return pl.pallas_call(
        functools.partial(flash_kernel, group_size=group_size),
        grid_spec=grid_spec,
        out_shape=jax.ShapeDtypeStruct((tokens, width), jnp.float32),
        compiler_params=pltpu.CompilerParams(dimension_semantics=("arbitrary",)),
    )(q_index, k_index, query_rows, kv_rows, kv_rows)


def mix(query_rows, local_part, state, mixing):
    tokens, width = query_rows.shape
    group_size = width // HD
    highest = lax.Precision.HIGHEST
    query_feature = feature(query_rows.astype(jnp.float32)).reshape(tokens, group_size, HD)
    numerator = jnp.einsum("tjd,de->tje", query_feature, state[:HD], precision=highest)
    denominator = jnp.maximum(
        jnp.einsum("tjd,d->tj", query_feature, state[HD], precision=highest), 1.0
    )
    retrieved = numerator / denominator[..., None]
    share = mixing[None, :, None]
    attended = share * retrieved + (1.0 - share) * local_part.reshape(tokens, group_size, HD)
    return attended.astype(jnp.bfloat16).reshape(tokens, width)


def before_states(key_local, value_local):
    kv_heads = key_local.shape[1] // HD
    key_feature = feature(key_local.astype(jnp.float32)).reshape(-1, kv_heads, HD)
    value_data = value_local.astype(jnp.float32).reshape(-1, kv_heads, HD)
    memory_delta = jnp.einsum(
        "tgd,tge->gde", key_feature, value_data, precision=lax.Precision.HIGHEST
    )
    normal_delta = jnp.sum(key_feature, axis=0)
    delta = jnp.concatenate([memory_delta, normal_delta[:, None, :]], axis=1)
    gathered = lax.all_gather(delta.astype(jnp.bfloat16), "seq").astype(jnp.float32)
    earlier = (
        jnp.arange(lax.axis_size("seq"), dtype=jnp.int32) < lax.axis_index("seq")
    ).astype(jnp.float32)
    return jnp.sum(gathered * earlier[:, None, None, None], axis=0)


def body(queries, keys, values, gate_logit):
    parts = lax.axis_size("head")
    head_place = lax.axis_index("head")
    tokens_here = queries.shape[0]
    kv_here = keys.shape[1] // (parts * HD)
    group_size = queries.shape[1] // (keys.shape[1])
    kv_split = jnp.stack(
        [keys.reshape(tokens_here, parts, kv_here * HD), values.reshape(tokens_here, parts, kv_here * HD)],
        axis=2,
    ).transpose(1, 0, 2, 3)
    kv_local = lax.all_to_all(kv_split, "head", split_axis=0, concat_axis=0, tiled=True)
    kv_local = kv_local.reshape(parts * tokens_here, 2 * kv_here * HD)
    state = before_states(kv_local[:, : kv_here * HD], kv_local[:, kv_here * HD :])
    mixing = jax.nn.sigmoid(
        lax.dynamic_slice_in_dim(gate_logit, head_place * kv_here * group_size, kv_here * group_size)
    ).reshape(kv_here, group_size)
    width = group_size * HD
    query_split = queries.reshape(tokens_here, parts, kv_here, width)
    returned = []
    for head in range(kv_here):
        query_rows = lax.all_to_all(
            query_split[:, :, head].transpose(1, 0, 2), "head", split_axis=0, concat_axis=0, tiled=True
        ).reshape(parts * tokens_here, width)
        local_part = local_attention(query_rows, kv_local, head, kv_here + head)
        attended = mix(query_rows, local_part, state[head], mixing[head])
        returned.append(
            lax.all_to_all(
                attended.reshape(parts, tokens_here, width), "head", split_axis=0, concat_axis=0, tiled=True
            )
        )
    stacked = jnp.stack(returned, axis=0).transpose(2, 1, 0, 3)
    return stacked.reshape(tokens_here, parts * kv_here * width)


def solution(mesh):
    in_specs = (P(("seq", "head"), None), P(("seq", "head"), None), P(("seq", "head"), None), P())
    out_specs = P(("seq", "head"), None)
    return jax.shard_map(body, mesh=mesh, in_specs=in_specs, out_specs=out_specs, check_vma=False)
```

time: 297 us -> 306 us (1.030)
  local copies, waits for them, and re-layouts: 14.2 us -> 107 us
  Pallas kernels: 133 us -> 64.5 us
  blocking collectives: 105 us -> 61.3 us
  matrix products: 3.4 us -> 28.5 us
  waiting for transfers between devices: 23.1 us -> 5.29 us
  other arithmetic: 4 us -> 20 us
  starting transfers between devices: 12.7 us -> 17.2 us
    pallas_call x1 -> x2, Pallas kernels: 133 us -> 64.5 us  [local_attention(): pl.pallas_call(functools.partial(flash_kernel, group_size=group_size), gr...]
    convert_element_type x0 -> x2, local copies, waits for them, and re-layouts: none -> 33.1 us  [mix(): return attended.astype(jnp.bfloat16).reshape(tokens, width)]
    dot_general x0 -> x4, matrix products: none -> 25.7 us  [the longest x2 13.1 us: mix(): jnp.einsum('tjd,d->tj', query_feature, state[HD], precision=highest)]
    all_to_all x1, blocking collectives: 51.9 us -> 28.7 us  [body(): lax.all_to_all(attended.reshape(parts, tokens_here, width), 'head', split...]
    all_gather x2 -> x1, blocking collectives: 52.9 us -> 32.6 us  [before_states(): lax.all_gather(delta.astype(jnp.bfloat16), 'seq').astype(jnp.float32)]
    all_to_all x3 -> x4, waiting for transfers between devices: 23.1 us -> 5.29 us  [the longest x1 5.28 us: body(): lax.all_to_all(kv_split, 'head', split_axis=0, concat_axis=0, tiled=True)]
    another operation x0 -> x6, local copies, waits for them, and re-layouts: none -> 13.8 us  [the longest x4 6.95 us: body(): jnp.stack([keys.reshape(tokens_here, parts, kv_here * HD), values.reshape...]
    slice x0 -> x2, local copies, waits for them, and re-layouts: none -> 10.2 us  [the longest x1 10.1 us: body(): query_split[:, :, head].transpose(1, 0, 2)]
  transfers between devices with their start and end apart: 3 -> 4, of which waited for: 2 -> 1; matrix products, arithmetic and copies ran while one was open for 6% -> 41% of each run, Pallas kernels for 0% -> 21%
where the time goes in v2:
time: 306 us; the launch traced here: 304 us
  local copies, waits for them, and re-layouts  107 us (35%)
  Pallas kernels  64.5 us (21%)
  blocking collectives  61.3 us (20%)
  matrix products  28.5 us (9%)
  other arithmetic  20 us (7%)
  starting transfers between devices  17.2 us (6%)
  waiting for transfers between devices  5.29 us (2%)
    pallas_call x2, Pallas kernels, local_attention(): pl.pallas_call(functools.partial(flash_kernel, group_size=group_size), gr...  64.5 us
    convert_element_type x2, local copies, waits for them, and re-layouts, mix(): return attended.astype(jnp.bfloat16).reshape(tokens, width)  33.1 us
    all_gather x1, blocking collectives, before_states(): lax.all_gather(delta.astype(jnp.bfloat16), 'seq').astype(jnp.float32)  32.6 us
    all_to_all x1, blocking collectives, body(): lax.all_to_all(attended.reshape(parts, tokens_here, width), 'head', split...  28.7 us
    dot_general x2, matrix products, mix(): jnp.einsum('tjd,d->tj', query_feature, state[HD], precision=highest)  13.1 us
    dot_general x2, matrix products, mix(): jnp.einsum('tjd,de->tje', query_feature, state[:HD], precision=highest)  12.6 us
    select_n x2, local copies, waits for them, and re-layouts, feature(): jnp.where(inputs > 0, inputs + 1.0, jnp.exp(jnp.minimum(inputs, 0.0)))  10.5 us
    slice x1, local copies, waits for them, and re-layouts, body(): query_split[:, :, head].transpose(1, 0, 2)  10.1 us
  transfers between devices with their start and end apart: 4, of which 1 were waited for; matrix products, arithmetic and copies ran while one was open for 41% of the time, Pallas kernels for 21%

profile of v2, /device:TPU:0, one launch (start us, length us, event | category | flops | bytes accessed | tf_op | source)
XLA Modules:
  0.0 304.2 jit_solution(7103364001868011930)
XLA Ops:
  0.0 1.9 stack_reshape.6
  1.9 1.6 copy.62
  3.5 1.9 stack_reshape.7
  5.4 1.6 copy.63
  7.0 5.6 %maximum_bitcast_fusion.1 = bf16[4,512,2,256]{3,2,1,0:T(2,128)(2,1)} fusion(bf16[512,4,1,256]{3,2,0,1:T(2,128)(2,1)S(1)} %copy.63, bf16[512,4,1,256]{3,2,0,1:T(2,128)(2,1)S(1)} %copy.62), kind=kLoop, calls=%fused_computation.30 | loop fusion | flops 4194304 | bytes 4194304 | tf_op jit(solution)/shard_map/transpose | solution.py:145
  12.6 4.2 %all-to-all-start.1 = ((bf16[4,512,2,256]{3,2,1,0:T(2,128)(2,1)}), bf16[4,512,2,256]{3,2,1,0:T(2,128)(2,1)S(1)}, u32[]{:S(2)}, u32[]{:S(2)}) async-start(bf16[4,512,2,256]{3,2,1,0:T(2,128)(2,1)} %maximum_bitcast_fusion.1), calls=%async_computation.1 | async-start | bytes 4194304 | tf_op jit(solution)/shard_map/all_to_all | solution.py:146
  16.8 7.8 %reshape.93 = bf16[512,4,2,512]{3,2,1,0:T(2,128)(2,1)} reshape(bf16[512,4096]{1,0:T(8,128)(2,1)} %param.8) | data formatting | bytes 8388608 | tf_op jit(solution)/shard_map/reshape | solution.py:153
  24.6 10.1 %fusion.26 = (bf16[512,4,1,512]{3,2,1,0:T(2,128)(2,1)S(1)}, bf16[512,4,1,512]{3,2,1,0:T(2,128)(2,1)}) fusion(bf16[512,4,2,512]{3,2,1,0:T(2,128)(2,1)} %reshape.93), kind=kLoop, calls=%fused_computation.50 | loop fusion | bytes 8388608 | tf_op jit(solution)/shard_map/slice | solution.py:157
  34.8 2.5 copy.111
  37.3 5.3 %all-to-all-done.1 = bf16[4,512,2,256]{3,2,1,0:T(2,128)(2,1)S(1)} async-done(((bf16[4,512,2,256]{3,2,1,0:T(2,128)(2,1)}), bf16[4,512,2,256]{3,2,1,0:T(2,128)(2,1)S(1)}, u32[]{:S(2)}, u32[]{:S(2)}) %all-to-all-start.1) | async-done | bytes 2097184 | tf_op jit(solution)/shard_map/all_to_all | solution.py:146
  42.5 4.9 %all-to-all-start = ((bf16[4,512,512]{2,1,0:T(8,128)(2,1)}), bf16[4,512,512]{2,1,0:T(8,128)(2,1)}, u32[]{:S(2)}, u32[]{:S(2)}) async-start(bf16[4,512,512]{2,1,0:T(8,128)(2,1)} %bitcast.77), calls=%async_computation | async-start | bytes 4194304 | tf_op jit(solution)/shard_map/all_to_all | solution.py:156
  47.4 0.0 copy-start.3
  47.4 4.7 %copy.110 = bf16[512,4,1,512]{3,0,1,2:T(8,128)(2,1)} copy(bf16[512,4,1,512]{3,2,1,0:T(2,128)(2,1)} %get-tuple-element.6) | data formatting | bytes 4194304
  52.2 0.1 add_divide_fusion
  52.2 0.1 fusion.28
  52.3 2.0 copy.89
  54.4 2.0 fusion.20
  56.4 2.9 copy.81
  59.3 2.7 fusion.22
  62.1 0.1 copy.67
  62.1 32.6 %all_gather.4 = bf16[8,2,129,128]{3,1,2,0:T(2,128)(2,1)S(1)} all-gather(bf16[1,2,129,128]{3,1,2,0:T(2,128)(2,1)S(1)} %copy.67), channel_id=1, replica_groups=mesh['seq'=8,'head'=4] {'seq'}, dimensions={0}, use_global_device_ids=true | all-gather | bytes 594432 | tf_op jit(solution)/shard_map/all_gather | solution.py:129
  94.7 0.0 all-to-all-done
  94.7 3.6 %all-to-all-start.3 = ((bf16[4,512,512]{2,1,0:T(8,128)(2,1)}), bf16[4,512,512]{2,1,0:T(8,128)(2,1)S(1)}, u32[]{:S(2)}, u32[]{:S(2)}) async-start(bf16[4,512,512]{2,1,0:T(8,128)(2,1)} %bitcast.86), calls=%async_computation.3 | async-start | bytes 4194304 | tf_op jit(solution)/shard_map/all_to_all | solution.py:156
  98.4 4.6 %fusion = f32[4,512,512]{2,1,0:T(8,128)} fusion(bf16[4,512,512]{2,1,0:T(8,128)(2,1)} %all-to-all-done), kind=kLoop, calls=%fused_computation.6 | loop fusion | flops 5242880 | bytes 6291456 | tf_op jit(solution)/shard_map/jit(_where)/select_n | solution.py:20
  102.9 5.2 %select_n.26 = f32[2048,4,128]{2,1,0:T(4,128)} reshape(f32[4,512,512]{2,1,0:T(8,128)} %fusion) | data formatting | bytes 8388608 | tf_op jit(solution)/shard_map/jit(_where)/select_n | solution.py:20
  108.2 0.7 multiply_reduce_fusion
  108.8 6.6 %fusion.12 = f32[1,2048,4]{0,1,2:T(8,128)} fusion(f32[2048,4,128]{2,1,0:T(4,128)} %select_n.26, f32[2,129,128]{2,0,1:T(2,128)S(1)} %multiply_reduce_fusion), kind=kOutput, calls=%fused_computation.21 | convolution fusion | flops 12582912 | bytes 4227584 | tf_op jit(solution)/shard_map/tjd,d->tj/dot_general | solution.py:112
  115.4 2.8 copy.79
  118.2 32.3 %shard_map.82 = f32[2048,512]{1,0:T(8,128)} custom-call(s32[10]{0:T(128)} %constant.7.clone.qi_ref, s32[10]{0:T(128)} %constant.8.clone.kj_ref, bf16[2048,512]{1,0:T(8,128)(2,1)} %bitcast.11.q_ref, bf16[2048,512]{1,0:T(8,128)(2,1)} %bitcast.80, bf16[2048,512]{1,0:T(8,128)(2,1)} %bitcast.81), custom_call_target="tpu_custom_call" | custom-call | tf_op jit(solution)/shard_map/pallas_call | solution.py:97
  150.5 0.1 fusion.27
  150.6 6.3 %fusion.7 = bf16[2048,4,128]{2,0,1:T(8,128)(2,1)S(1)} fusion(f32[128,128,1]{1,0,2:T(8,128)S(1)} %bitcast.91, f32[2048,4,128]{2,1,0:T(4,128)} %select_n.26, f32[4]{0:T(128)S(1)} %get-tuple-element.12, f32[2048,4]{0,1:T(4,128)S(1)} %bitcast_maximum_fusion.1, f32[4]{0:T(128)S(1)} %get-tuple-element.11, f32[2048,512]{1,0:T(8,128)} %shard_map.82), kind=kOutput, calls=%fused_computation.15 | convolution fusion | flops 1615855616 | bytes 10584096 | tf_op jit(solution)/shard_map/tjd,de->tje/dot_general | solution.py:110
  156.9 22.2 %copy.71 = bf16[2048,4,128]{2,1,0:T(4,128)(2,1)} copy(bf16[2048,4,128]{2,0,1:T(8,128)(2,1)S(1)} %fusion.7) | data formatting | bytes 4194304 | tf_op jit(solution)/shard_map/convert_element_type | solution.py:117
  179.1 4.2 %reshape_reshape.6 = bf16[4,512,512]{2,1,0:T(8,128)(2,1)} reshape(bf16[2048,4,128]{2,1,0:T(4,128)(2,1)} %copy.71) | data formatting | bytes 4194304 | tf_op jit(solution)/shard_map/reshape;reshape | solution.py:163
  183.3 0.0 all-to-all-done.3
  183.3 4.5 %all-to-all-start.2 = ((bf16[4,512,512]{2,1,0:T(8,128)(2,1)}), bf16[4,512,512]{2,1,0:T(8,128)(2,1)}, u32[]{:S(2)}, u32[]{:S(2)}) async-start(bf16[4,512,512]{2,1,0:T(8,128)(2,1)} %reshape_reshape.6), calls=%async_computation.2 | async-start | bytes 4194304 | tf_op jit(solution)/shard_map/all_to_all | solution.py:162
  187.8 3.0 fusion.2
  190.7 5.2 %select_n.29 = f32[2048,4,128]{2,1,0:T(4,128)} reshape(f32[4,512,512]{2,1,0:T(8,128)} %fusion.2) | data formatting | bytes 8388608 | tf_op jit(solution)/shard_map/jit(_where)/select_n | solution.py:20
  196.0 6.6 %fusion.8 = f32[1,2048,4]{0,1,2:T(8,128)} fusion(f32[2048,4,128]{2,1,0:T(4,128)} %select_n.29, f32[2,129,128]{2,0,1:T(2,128)S(1)} %multiply_reduce_fusion), kind=kOutput, calls=%fused_computation.17 | convolution fusion | flops 12582912 | bytes 4227584 | tf_op jit(solution)/shard_map/tjd,d->tj/dot_general | solution.py:112
  202.5 2.8 copy.80
  205.4 32.3 %shard_map.83 = f32[2048,512]{1,0:T(8,128)} custom-call(s32[10]{0:T(128)} %constant.7.clone.qi_ref, s32[10]{0:T(128)} %constant.8.clone.kj_ref, bf16[2048,512]{1,0:T(8,128)(2,1)} %bitcast.84, bf16[2048,512]{1,0:T(8,128)(2,1)} %bitcast.82, bf16[2048,512]{1,0:T(8,128)(2,1)} %bitcast.83), custom_call_target="tpu_custom_call" | custom-call | tf_op jit(solution)/shard_map/pallas_call | solution.py:97
  237.7 6.3 %fusion.5 = bf16[2048,4,128]{2,0,1:T(8,128)(2,1)S(1)} fusion(f32[128,128,1]{1,0,2:T(8,128)S(1)} %bitcast.90, f32[2048,4,128]{2,1,0:T(4,128)} %select_n.29, f32[4]{0:T(128)S(1)} %get-tuple-element.13, f32[2048,4]{0,1:T(4,128)S(1)} %bitcast_maximum_fusion, f32[4]{0:T(128)S(1)} %get-tuple-element.14, f32[2048,512]{1,0:T(8,128)} %shard_map.83), kind=kOutput, calls=%fused_computation.12 | convolution fusion | flops 1615855616 | bytes 10584096 | tf_op jit(solution)/shard_map/tjd,de->tje/dot_general | solution.py:110
  244.0 10.9 %copy.76 = bf16[2048,4,128]{2,1,0:T(4,128)(2,1)} copy(bf16[2048,4,128]{2,0,1:T(8,128)(2,1)S(1)} %fusion.5) | data formatting | bytes 4194304 | tf_op jit(solution)/shard_map/convert_element_type | solution.py:117
  254.9 2.7 reshape_reshape.7
  257.6 0.0 all-to-all-done.2
  257.6 28.7 %all_to_all.25 = bf16[4,512,512]{2,1,0:T(8,128)(2,1)S(1)} all-to-all(bf16[4,512,512]{2,1,0:T(8,128)(2,1)S(1)} %reshape_reshape.7), channel_id=1, replica_groups=mesh['seq'=8,'head'=4] {'head'}, dimensions={0} | all-to-all | bytes 4194304 | tf_op jit(solution)/shard_map/all_to_all | solution.py:162
  286.4 4.0 %maximum_bitcast_fusion = bf16[512,4,2,512]{3,0,1,2:T(8,128)(2,1)} fusion(bf16[1,4,512,512]{3,2,1,0:T(8,128)(2,1)S(1)} %bitcast.89, bf16[1,4,512,512]{3,2,1,0:T(8,128)(2,1)} %bitcast.12), kind=kLoop, calls=%fused_computation.16 | loop fusion | flops 2097152 | bytes 8388608 | tf_op jit(solution)/shard_map/transpose | solution.py:166
  290.4 7.3 %copy.77 = bf16[512,4,2,512]{0,3,2,1:T(8,128)(2,1)} copy(bf16[512,4,2,512]{3,0,1,2:T(8,128)(2,1)} %maximum_bitcast_fusion) | data formatting | bytes 8388608 | tf_op jit(solution)/shard_map/transpose | solution.py:166
  297.7 6.3 %copy.78 = bf16[512,4096]{1,0:T(8,128)(2,1)} copy(bf16[512,4096]{0,1:T(8,128)(2,1)} %bitcast.85) | data formatting | bytes 8388608 | tf_op jit(solution)/shard_map/reshape | solution.py:167
  (12 shorter events, 0.0 us)
Async XLA Ops:
  12.6 29.9 %all-to-all-start.1 = ((bf16[4,512,2,256]{3,2,1,0:T(2,128)(2,1)}), bf16[4,512,2,256]{3,2,1,0:T(2,128)(2,1)S(1)}, u32[]{:S(2)}, u32[]{:S(2)}) async-start(bf16[4,512,2,256]{3,2,1,0:T(2,128)(2,1)} %maximum_bitcast_fusion.1), calls=%async_computation.1 | async-start | bytes 4194304 | tf_op jit(solution)/shard_map/all_to_all | solution.py:146
  42.5 9.6 %copy-start.2 = (bf16[4,512,2,256]{3,2,1,0:T(2,128)(2,1)}, bf16[4,512,2,256]{3,2,1,0:T(2,128)(2,1)S(1)}, u32[]{:S(2)}) copy-start(bf16[4,512,2,256]{3,2,1,0:T(2,128)(2,1)S(1)} %all-to-all-done.1) | copy-start | bytes 6291460
  42.5 52.2 %all-to-all-start = ((bf16[4,512,512]{2,1,0:T(8,128)(2,1)}), bf16[4,512,512]{2,1,0:T(8,128)(2,1)}, u32[]{:S(2)}, u32[]{:S(2)}) async-start(bf16[4,512,512]{2,1,0:T(8,128)(2,1)} %bitcast.77), calls=%async_computation | async-start | bytes 4194304 | tf_op jit(solution)/shard_map/all_to_all | solution.py:156
  47.4 4.7 %copy-start.3 = (f32[32]{0:T(128)S(1)}, f32[32]{0:T(128)}, u32[]{:S(2)}) copy-start(f32[32]{0:T(128)} %param.11) | copy-start | bytes 388
  54.4 7.7 %copy-start = (bf16[256,8,2,256]{3,1,2,0:T(8,128)(2,1)}, bf16[256,8,2,256]{3,1,2,0:T(8,128)(2,1)S(1)}, u32[]{:S(2)}) copy-start(bf16[256,8,2,256]{3,1,2,0:T(8,128)(2,1)S(1)} %copy.89) | copy-start | bytes 6291460
  94.7 88.5 %all-to-all-start.3 = ((bf16[4,512,512]{2,1,0:T(8,128)(2,1)}), bf16[4,512,512]{2,1,0:T(8,128)(2,1)S(1)}, u32[]{:S(2)}, u32[]{:S(2)}) async-start(bf16[4,512,512]{2,1,0:T(8,128)(2,1)} %bitcast.86), calls=%async_computation.3 | async-start | bytes 4194304 | tf_op jit(solution)/shard_map/all_to_all | solution.py:156
  183.3 7.4 %copy-start.1 = (bf16[4,512,512]{2,1,0:T(8,128)(2,1)}, bf16[4,512,512]{2,1,0:T(8,128)(2,1)S(1)}, u32[]{:S(2)}) copy-start(bf16[4,512,512]{2,1,0:T(8,128)(2,1)S(1)} %all-to-all-done.3) | copy-start | bytes 6291460
  183.3 74.3 %all-to-all-start.2 = ((bf16[4,512,512]{2,1,0:T(8,128)(2,1)}), bf16[4,512,512]{2,1,0:T(8,128)(2,1)}, u32[]{:S(2)}, u32[]{:S(2)}) async-start(bf16[4,512,512]{2,1,0:T(8,128)(2,1)} %reshape_reshape.6), calls=%async_computation.2 | async-start | bytes 4194304 | tf_op jit(solution)/shard_map/all_to_all | solution.py:162

commit v3 on v2

v3 whole, which is shorter than its diff:
```python
import functools

import jax
import jax.numpy as jnp
import numpy as np
from jax import lax
from jax.experimental import pallas as pl
from jax.experimental.pallas import tpu as pltpu
from jax.sharding import PartitionSpec as P

HQ = 32
KVH = 8
HD = 128
SEG = 2048
LANES = 128
STATE_ROWS = HD + 8


def feature(inputs):
    return jnp.where(inputs > 0, inputs + 1.0, jnp.exp(jnp.minimum(inputs, 0.0)))


def shifted(value, axis, steps):
    count = lax.axis_size(axis)
    return lax.ppermute(value, axis, [(source, source + steps) for source in range(count - steps)])


def split_kernel(q_ref, *out_refs):
    width = out_refs[0].shape[-1]
    for head, out_ref in enumerate(out_refs):
        out_ref[...] = q_ref[:, head * width : (head + 1) * width]


def split_queries(queries, parts, kv_here):
    tokens_here, cols = queries.shape
    group_cols = cols // parts
    width = group_cols // kv_here
    shape = jax.ShapeDtypeStruct((parts, tokens_here, width), queries.dtype)
    return pl.pallas_call(
        split_kernel,
        grid=(parts,),
        in_specs=[pl.BlockSpec((tokens_here, group_cols), lambda p: (0, p))],
        out_specs=[pl.BlockSpec((None, tokens_here, width), lambda p: (p, 0, 0))] * kv_here,
        out_shape=[shape] * kv_here,
    )(queries)


def pair_kernel(k_ref, v_ref, o_ref):
    width = k_ref.shape[-1]
    o_ref[:, :width] = k_ref[...]
    o_ref[:, width:] = v_ref[...]


def split_keys_values(keys, values, parts):
    tokens_here, cols = keys.shape
    group_cols = cols // parts
    return pl.pallas_call(
        pair_kernel,
        grid=(parts,),
        in_specs=[pl.BlockSpec((tokens_here, group_cols), lambda p: (0, p))] * 2,
        out_specs=pl.BlockSpec((None, tokens_here, 2 * group_cols), lambda p: (p, 0, 0)),
        out_shape=jax.ShapeDtypeStruct((parts, tokens_here, 2 * group_cols), keys.dtype),
    )(keys, values)


def delta_kernel(k_ref, v_ref, o_ref):
    @pl.when(pl.program_id(1) == 0)
    def _init():
        o_ref[...] = jnp.zeros(o_ref.shape, jnp.float32)

    key_feature = feature(k_ref[...].astype(jnp.float32))
    value_data = v_ref[...].astype(jnp.float32)
    o_ref[:HD, :] += jnp.dot(
        key_feature.T, value_data, precision=lax.Precision.HIGHEST,
        preferred_element_type=jnp.float32,
    )
    o_ref[HD : HD + 1, :] += jnp.sum(key_feature, axis=0, keepdims=True)


def segment_deltas(kv_local, kv_here):
    parts, tokens_here, _ = kv_local.shape
    return pl.pallas_call(
        delta_kernel,
        grid=(kv_here, parts),
        in_specs=[
            pl.BlockSpec((None, tokens_here, HD), lambda g, t: (t, 0, g)),
            pl.BlockSpec((None, tokens_here, HD), lambda g, t: (t, 0, kv_here + g)),
        ],
        out_specs=pl.BlockSpec((None, STATE_ROWS, HD), lambda g, t: (g, 0, 0)),
        out_shape=jax.ShapeDtypeStruct((kv_here, STATE_ROWS, HD), jnp.float32),
        compiler_params=pltpu.CompilerParams(dimension_semantics=("arbitrary", "arbitrary")),
    )(kv_local, kv_local)


def earlier_sum(delta):
    count = lax.axis_size("seq")
    total = delta
    steps = 1
    while steps < count:
        total = total + shifted(total, "seq", steps)
        steps *= 2
    return total - delta


def flash_kernel(
    qi_ref, kj_ref, gate_ref, q_ref, k_ref, v_ref, s_ref, o_ref, m_sc, l_sc, acc_sc, *, group_size
):
    step_at = pl.program_id(0)
    q_block = qi_ref[step_at]
    k_block = kj_ref[step_at]
    block = q_ref.shape[0]
    score_scale = HD ** (-0.5)

    @pl.when(k_block == 0)
    def _init():
        m_sc[...] = jnp.full(m_sc.shape, -jnp.inf, jnp.float32)
        l_sc[...] = jnp.zeros(l_sc.shape, jnp.float32)
        acc_sc[...] = jnp.zeros(acc_sc.shape, jnp.float32)

    def step(masked):
        key_rows = k_ref[...]
        value_rows = v_ref[...]
        if masked:
            rows = lax.broadcasted_iota(jnp.int32, (block, block), 0)
            cols = lax.broadcasted_iota(jnp.int32, (block, block), 1)
            allowed = cols <= rows
        for head in range(group_size):
            lanes = slice(head * HD, (head + 1) * HD)
            scores = (
                lax.dot_general(
                    q_ref[:, lanes], key_rows, (((1,), (1,)), ((), ())),
                    preferred_element_type=jnp.float32,
                )
                * score_scale
            )
            if masked:
                scores = jnp.where(allowed, scores, -1e30)
            m_prev = m_sc[head]
            m_new = jnp.maximum(m_prev, jnp.max(scores, axis=-1, keepdims=True))
            probs = jnp.exp(scores - m_new[:, :1])
            alpha = jnp.exp(m_prev - m_new)
            l_sc[head] = alpha * l_sc[head] + jnp.sum(probs, axis=-1, keepdims=True)
            acc_sc[:, lanes] = alpha * acc_sc[:, lanes] + jnp.dot(
                probs.astype(jnp.bfloat16), value_rows, preferred_element_type=jnp.float32
            )
            m_sc[head] = m_new

    @pl.when(k_block < q_block)
    def _full():
        step(False)

    @pl.when(k_block == q_block)
    def _last():
        step(True)
        memory = s_ref[:HD, :]
        normalizer = s_ref[HD : HD + 1, :]
        for head in range(group_size):
            lanes = slice(head * HD, (head + 1) * HD)
            local_part = acc_sc[:, lanes] / l_sc[head]
            query_feature = feature(q_ref[:, lanes].astype(jnp.float32))
            numerator = jnp.dot(
                query_feature, memory, precision=lax.Precision.HIGHEST,
                preferred_element_type=jnp.float32,
            )
            denominator = jnp.maximum(
                jnp.sum(query_feature * normalizer, axis=-1, keepdims=True), 1.0
            )
            mixing = gate_ref[head]
            o_ref[:, lanes] = (
                mixing * (numerator / denominator) + (1.0 - mixing) * local_part
            ).astype(o_ref.dtype)


def attend(query_rows, kv_local, state, mixing, head, kv_here):
    parts, block, width = query_rows.shape
    group_size = width // HD
    pairs = [(i, j) for i in range(parts) for j in range(i + 1)]
    q_index = jnp.asarray(np.array([p[0] for p in pairs], np.int32))
    k_index = jnp.asarray(np.array([p[1] for p in pairs], np.int32))
    grid_spec = pltpu.PrefetchScalarGridSpec(
        num_scalar_prefetch=2,
        grid=(len(pairs),),
        in_specs=[
            pl.BlockSpec(memory_space=pltpu.SMEM),
            pl.BlockSpec((None, block, width), lambda t, qi, kj: (qi[t], 0, 0)),
            pl.BlockSpec((None, block, HD), lambda t, qi, kj: (kj[t], 0, head)),
            pl.BlockSpec((None, block, HD), lambda t, qi, kj: (kj[t], 0, kv_here + head)),
            pl.BlockSpec((None, STATE_ROWS, HD), lambda t, qi, kj: (head, 0, 0)),
        ],
        out_specs=pl.BlockSpec((None, block, width), lambda t, qi, kj: (qi[t], 0, 0)),
        scratch_shapes=[
            pltpu.VMEM((group_size, block, LANES), jnp.float32),
            pltpu.VMEM((group_size, block, LANES), jnp.float32),
            pltpu.VMEM((block, width), jnp.float32),
        ],
    )
    return pl.pallas_call(
        functools.partial(flash_kernel, group_size=group_size),
        grid_spec=grid_spec,
        out_shape=jax.ShapeDtypeStruct(query_rows.shape, jnp.bfloat16),
        compiler_params=pltpu.CompilerParams(dimension_semantics=("arbitrary",)),
    )(q_index, k_index, mixing, query_rows, kv_local, kv_local, state)


def merge_kernel(*refs):
    in_refs, out_ref = refs[:-1], refs[-1]
    width = in_refs[0].shape[-1]
    for head, in_ref in enumerate(in_refs):
        out_ref[:, head * width : (head + 1) * width] = in_ref[...]


def merge_heads(returned):
    parts, tokens_here, width = returned[0].shape
    kv_here = len(returned)
    return pl.pallas_call(
        merge_kernel,
        grid=(parts,),
        in_specs=[pl.BlockSpec((None, tokens_here, width), lambda p: (p, 0, 0))] * kv_here,
        out_specs=pl.BlockSpec((tokens_here, kv_here * width), lambda p: (0, p)),
        out_shape=jax.ShapeDtypeStruct((tokens_here, parts * kv_here * width), returned[0].dtype),
    )(*returned)


def body(queries, keys, values, gate_logit):
    parts = lax.axis_size("head")
    head_place = lax.axis_index("head")
    kv_here = keys.shape[1] // (parts * HD)
    group_size = queries.shape[1] // keys.shape[1]

    def exchange(blocks):
        return lax.all_to_all(blocks, "head", split_axis=0, concat_axis=0, tiled=True)

    kv_local = exchange(split_keys_values(keys, values, parts))
    state = earlier_sum(segment_deltas(kv_local, kv_here))
    query_parts = split_queries(queries, parts, kv_here)
    gate_here = lax.dynamic_slice_in_dim(
        gate_logit, head_place * kv_here * group_size, kv_here * group_size
    )
    mixing = jax.nn.sigmoid(gate_here).reshape(kv_here, group_size)
    returned = []
    for head in range(kv_here):
        query_rows = exchange(query_parts[head])
        attended = attend(query_rows, kv_local, state, mixing[head], head, kv_here)
        returned.append(exchange(attended))
    return merge_heads(returned)


def solution(mesh):
    in_specs = (P(("seq", "head"), None), P(("seq", "head"), None), P(("seq", "head"), None), P())
    out_specs = P(("seq", "head"), None)
    return jax.shard_map(body, mesh=mesh, in_specs=in_specs, out_specs=out_specs, check_vma=False)
```

time: 306 us -> 219 us (0.72)
  the two profiles are of different devices: /device:TPU:0 before, /device:TPU:13 now
where the time goes in v3:
time: 219 us; the launch traced here: 216 us
  Pallas kernels  93.5 us (43%)
  blocking collectives  58.6 us (27%)
  waiting for transfers between devices  32 us (15%)
  starting transfers between devices  27 us (12%)
  other arithmetic  2.62 us (1%)
    pallas_call x2, Pallas kernels, attend(): pl.pallas_call(functools.partial(flash_kernel, group_size=group_size), gr...  73.4 us
    all_to_all x2, blocking collectives, exchange(): lax.all_to_all(blocks, 'head', split_axis=0, concat_axis=0, tiled=True)  58.6 us
    all_to_all x3, waiting for transfers between devices, exchange(): lax.all_to_all(blocks, 'head', split_axis=0, concat_axis=0, tiled=True)  20 us
    all_to_all x3, starting transfers between devices, exchange(): lax.all_to_all(blocks, 'head', split_axis=0, concat_axis=0, tiled=True)  16.5 us
    ppermute x3, waiting for transfers between devices, shifted(): lax.ppermute(value, axis, [(source, source + steps) for source in range(c...  12 us
    ppermute x3, starting transfers between devices, shifted(): lax.ppermute(value, axis, [(source, source + steps) for source in range(c...  10.6 us
    pallas_call x1, Pallas kernels, segment_deltas(): pl.pallas_call(delta_kernel, grid=(kv_here, parts), in_specs=[pl.BlockSpe...  6.89 us
    pallas_call x1, Pallas kernels, split_queries(): pl.pallas_call(split_kernel, grid=(parts,), in_specs=[pl.BlockSpec((token...  4.72 us
  transfers between devices with their start and end apart: 6, of which 4 were waited for; matrix products, arithmetic and copies ran while one was open for 1% of the time, Pallas kernels for 39%

profile of v3, /device:TPU:13, one launch (start us, length us, event | category | flops | bytes accessed | tf_op | source)
XLA Modules:
  0.0 215.7 jit_solution(737679832307266183)
XLA Ops:
  0.0 4.7 %shard_map.82 = (bf16[4,512,512]{2,1,0:T(8,128)(2,1)}, bf16[4,512,512]{2,1,0:T(8,128)(2,1)}) custom-call(bf16[512,4096]{1,0:T(8,128)(2,1)} %q_ref.1), custom_call_target="tpu_custom_call" | custom-call | tf_op jit(solution)/shard_map/pallas_call | solution.py:39
  4.7 4.4 %all-to-all-start = ((bf16[4,512,512]{2,1,0:T(8,128)(2,1)}), bf16[4,512,512]{2,1,0:T(8,128)(2,1)S(1)}, u32[]{:S(2)}, u32[]{:S(2)}) async-start(bf16[4,512,512]{2,1,0:T(8,128)(2,1)} %get-tuple-element.7), calls=%async_computation | async-start | bytes 4194304 | tf_op jit(solution)/shard_map/all_to_all | solution.py:231
  9.1 3.8 %shard_map.83 = bf16[4,512,512]{2,1,0:T(8,128)(2,1)} custom-call(bf16[512,1024]{1,0:T(8,128)(2,1)} %k_ref.1, bf16[512,1024]{1,0:T(8,128)(2,1)} %v_ref.1), custom_call_target="tpu_custom_call" | custom-call | tf_op jit(solution)/shard_map/pallas_call | solution.py:57
  12.9 20.0 %all-to-all-done.q_ref = bf16[4,512,512]{2,1,0:T(8,128)(2,1)S(1)} async-done(((bf16[4,512,512]{2,1,0:T(8,128)(2,1)}), bf16[4,512,512]{2,1,0:T(8,128)(2,1)S(1)}, u32[]{:S(2)}, u32[]{:S(2)}) %all-to-all-start) | async-done | bytes 2097184 | tf_op jit(solution)/shard_map/all_to_all | solution.py:231
  32.9 0.0 copy-start.1
  32.9 30.1 %all_to_all.25.k_ref.v_ref = bf16[4,512,512]{2,1,0:T(8,128)(2,1)} all-to-all(bf16[4,512,512]{2,1,0:T(8,128)(2,1)} %shard_map.83), channel_id=1, replica_groups=mesh['seq'=8,'head'=4] {'head'}, dimensions={0} | all-to-all | bytes 4194304 | tf_op jit(solution)/shard_map/all_to_all | solution.py:231
  63.0 0.0 copy-done.1
  63.1 5.5 %all-to-all-start.3 = ((bf16[4,512,512]{2,1,0:T(8,128)(2,1)}), bf16[4,512,512]{2,1,0:T(8,128)(2,1)S(1)}, u32[]{:S(2)}, u32[]{:S(2)}) async-start(bf16[4,512,512]{2,1,0:T(8,128)(2,1)} %get-tuple-element.8), calls=%async_computation.3 | async-start | bytes 4194304 | tf_op jit(solution)/shard_map/all_to_all | solution.py:231
  68.5 0.0 copy-start.2
  68.6 6.9 %shard_map.84 = f32[2,136,128]{2,1,0:T(8,128)} custom-call(bf16[4,512,512]{2,1,0:T(8,128)(2,1)} %all_to_all.25.k_ref.v_ref, bf16[4,512,512]{2,1,0:T(8,128)(2,1)} %all_to_all.25.k_ref.v_ref), custom_call_target="tpu_custom_call" | custom-call | tf_op jit(solution)/shard_map/pallas_call | solution.py:82
  75.4 3.1 %collective-permute-start = (f32[2,136,128]{2,1,0:T(8,128)}, f32[2,136,128]{2,1,0:T(8,128)S(1)}, u32[]{:S(2)}, u32[]{:S(2)}) collective-permute-start(f32[2,136,128]{2,1,0:T(8,128)} %shard_map.84), channel_id=1, source_target_pairs={{0,4},{4,8},{8,12},{12,16},{16,20},{20,24},{24,28},{1,5},{5,9},{9,... | collective-permute-start | bytes 417800 | tf_op jit(solution)/shard_map/ppermute | solution.py:25
  78.6 4.8 %collective-permute-done = f32[2,136,128]{2,1,0:T(8,128)S(1)} collective-permute-done((f32[2,136,128]{2,1,0:T(8,128)}, f32[2,136,128]{2,1,0:T(8,128)S(1)}, u32[]{:S(2)}, u32[]{:S(2)}) %collective-permute-start) | collective-permute-done | bytes 139296 | tf_op jit(solution)/shard_map/ppermute | solution.py:25
  83.3 0.9 add.17
  84.2 3.2 %collective-permute-start.1 = (f32[2,136,128]{2,1,0:T(8,128)S(1)}, f32[2,136,128]{2,1,0:T(8,128)S(1)}, u32[]{:S(2)}, u32[]{:S(2)}) collective-permute-start(f32[2,136,128]{2,1,0:T(8,128)S(1)} %add.17), channel_id=1, source_target_pairs={{0,8},{4,12},{8,16},{12,20},{16,24},{20,28},{1,9},{5,13},{9,17},{1... | collective-permute-start | bytes 417800 | tf_op jit(solution)/shard_map/ppermute | solution.py:25
  87.5 0.0 copy-done.2
  87.5 0.1 add_divide_fusion
  87.6 2.8 %collective-permute-done.1 = f32[2,136,128]{2,1,0:T(8,128)S(1)} collective-permute-done((f32[2,136,128]{2,1,0:T(8,128)S(1)}, f32[2,136,128]{2,1,0:T(8,128)S(1)}, u32[]{:S(2)}, u32[]{:S(2)}) %collective-permute-start.1) | collective-permute-done | bytes 139296 | tf_op jit(solution)/shard_map/ppermute | solution.py:25
  90.4 4.2 %collective-permute-start.2 = (f32[2,136,128]{2,1,0:T(8,128)S(1)}, f32[2,136,128]{2,1,0:T(8,128)S(1)}, u32[]{:S(2)}, u32[]{:S(2)}) collective-permute-start(f32[2,136,128]{2,1,0:T(8,128)S(1)} %add.18), channel_id=1, source_target_pairs={{0,16},{4,20},{8,24},{12,28},{1,17},{5,21},{9,25},{13,29},{2,18},{... | collective-permute-start | bytes 417800 | tf_op jit(solution)/shard_map/ppermute | solution.py:25
  94.6 0.6 fusion
  95.2 4.5 %collective-permute-done.2 = f32[2,136,128]{2,1,0:T(8,128)S(1)} collective-permute-done((f32[2,136,128]{2,1,0:T(8,128)S(1)}, f32[2,136,128]{2,1,0:T(8,128)S(1)}, u32[]{:S(2)}, u32[]{:S(2)}) %collective-permute-start.2) | collective-permute-done | bytes 139296 | tf_op jit(solution)/shard_map/ppermute | solution.py:25
  99.7 1.6 add_subtract_fusion.s_ref
  101.3 36.7 %shard_map.85 = bf16[4,512,512]{2,1,0:T(8,128)(2,1)} custom-call(s32[10]{0:T(128)} %constant.18.clone.qi_ref, s32[10]{0:T(128)} %constant.19.clone.kj_ref, f32[4]{0:T(128)} %get-tuple-element.10.gate_ref, bf16[4,512,512]{2,1,0:T(8,128)(2,1)} %copy-done.1, bf16[4,512,512]{2,1,0:T(8,128)(2,1)} %all_to_all.25.k_ref.v_ref, ...), custom_call_target="tpu_custom_call" | custom-call | tf_op jit(solution)/shard_map/pallas_call | solution.py:197
  138.0 0.0 all-to-all-done.3.q_ref
  138.0 0.0 copy-start
  138.0 1.3 copy-done
  139.3 6.6 %all-to-all-start.2 = ((bf16[4,512,512]{2,1,0:T(8,128)(2,1)}), bf16[4,512,512]{2,1,0:T(8,128)(2,1)}, u32[]{:S(2)}, u32[]{:S(2)}) async-start(bf16[4,512,512]{2,1,0:T(8,128)(2,1)} %shard_map.85), calls=%async_computation.2 | async-start | bytes 4194304 | tf_op jit(solution)/shard_map/all_to_all | solution.py:231
  145.8 36.7 %shard_map.86 = bf16[4,512,512]{2,1,0:T(8,128)(2,1)} custom-call(s32[10]{0:T(128)} %constant.18.clone.qi_ref, s32[10]{0:T(128)} %constant.19.clone.kj_ref, f32[4]{0:T(128)} %get-tuple-element.9.gate_ref, bf16[4,512,512]{2,1,0:T(8,128)(2,1)} %copy-done, bf16[4,512,512]{2,1,0:T(8,128)(2,1)} %all_to_all.25.k_ref.v_ref, ...), custom_call_target="tpu_custom_call" | custom-call | tf_op jit(solution)/shard_map/pallas_call | solution.py:197
  182.6 0.0 all-to-all-done.2.refs_0_
  182.6 28.5 %all_to_all.26.refs_1_ = bf16[4,512,512]{2,1,0:T(8,128)(2,1)} all-to-all(bf16[4,512,512]{2,1,0:T(8,128)(2,1)} %shard_map.86), channel_id=1, replica_groups=mesh['seq'=8,'head'=4] {'head'}, dimensions={0} | all-to-all | bytes 4194304 | tf_op jit(solution)/shard_map/all_to_all | solution.py:231
  211.0 4.7 %shard_map.87 = bf16[512,4096]{1,0:T(8,128)(2,1)} custom-call(bf16[4,512,512]{2,1,0:T(8,128)(2,1)} %all-to-all-done.2.refs_0_, bf16[4,512,512]{2,1,0:T(8,128)(2,1)} %all_to_all.26.refs_1_), custom_call_target="tpu_custom_call" | custom-call | tf_op jit(solution)/shard_map/pallas_call | solution.py:215
  (1 shorter events, 0.0 us)
Async XLA Ops:
  4.7 28.2 %all-to-all-start = ((bf16[4,512,512]{2,1,0:T(8,128)(2,1)}), bf16[4,512,512]{2,1,0:T(8,128)(2,1)S(1)}, u32[]{:S(2)}, u32[]{:S(2)}) async-start(bf16[4,512,512]{2,1,0:T(8,128)(2,1)} %get-tuple-element.7), calls=%async_computation | async-start | bytes 4194304 | tf_op jit(solution)/shard_map/all_to_all | solution.py:231
  32.9 30.1 %copy-start.1 = (bf16[4,512,512]{2,1,0:T(8,128)(2,1)}, bf16[4,512,512]{2,1,0:T(8,128)(2,1)S(1)}, u32[]{:S(2)}) copy-start(bf16[4,512,512]{2,1,0:T(8,128)(2,1)S(1)} %all-to-all-done.q_ref) | copy-start | bytes 6291460
  63.1 74.9 %all-to-all-start.3 = ((bf16[4,512,512]{2,1,0:T(8,128)(2,1)}), bf16[4,512,512]{2,1,0:T(8,128)(2,1)S(1)}, u32[]{:S(2)}, u32[]{:S(2)}) async-start(bf16[4,512,512]{2,1,0:T(8,128)(2,1)} %get-tuple-element.8), calls=%async_computation.3 | async-start | bytes 4194304 | tf_op jit(solution)/shard_map/all_to_all | solution.py:231
  68.5 19.0 %copy-start.2 = (f32[32]{0:T(128)S(1)}, f32[32]{0:T(128)}, u32[]{:S(2)}) copy-start(f32[32]{0:T(128)} %param.11) | copy-start | bytes 388
  75.4 7.9 %collective-permute-start = (f32[2,136,128]{2,1,0:T(8,128)}, f32[2,136,128]{2,1,0:T(8,128)S(1)}, u32[]{:S(2)}, u32[]{:S(2)}) collective-permute-start(f32[2,136,128]{2,1,0:T(8,128)} %shard_map.84), channel_id=1, source_target_pairs={{0,4},{4,8},{8,12},{12,16},{16,20},{20,24},{24,28},{1,5},{5,9},{9,... | collective-permute-start | bytes 417800 | tf_op jit(solution)/shard_map/ppermute | solution.py:25
  84.2 6.1 %collective-permute-start.1 = (f32[2,136,128]{2,1,0:T(8,128)S(1)}, f32[2,136,128]{2,1,0:T(8,128)S(1)}, u32[]{:S(2)}, u32[]{:S(2)}) collective-permute-start(f32[2,136,128]{2,1,0:T(8,128)S(1)} %add.17), channel_id=1, source_target_pairs={{0,8},{4,12},{8,16},{12,20},{16,24},{20,28},{1,9},{5,13},{9,17},{1... | collective-permute-start | bytes 417800 | tf_op jit(solution)/shard_map/ppermute | solution.py:25
  90.4 9.3 %collective-permute-start.2 = (f32[2,136,128]{2,1,0:T(8,128)S(1)}, f32[2,136,128]{2,1,0:T(8,128)S(1)}, u32[]{:S(2)}, u32[]{:S(2)}) collective-permute-start(f32[2,136,128]{2,1,0:T(8,128)S(1)} %add.18), channel_id=1, source_target_pairs={{0,16},{4,20},{8,24},{12,28},{1,17},{5,21},{9,25},{13,29},{2,18},{... | collective-permute-start | bytes 417800 | tf_op jit(solution)/shard_map/ppermute | solution.py:25
  138.0 1.3 copy-start
  139.3 43.3 %all-to-all-start.2 = ((bf16[4,512,512]{2,1,0:T(8,128)(2,1)}), bf16[4,512,512]{2,1,0:T(8,128)(2,1)}, u32[]{:S(2)}, u32[]{:S(2)}) async-start(bf16[4,512,512]{2,1,0:T(8,128)(2,1)} %shard_map.85), calls=%async_computation.2 | async-start | bytes 4194304 | tf_op jit(solution)/shard_map/all_to_all | solution.py:231

commit v4 on v3

--- a/solution.py
+++ b/solution.py
@@ -25,42 +25,35 @@
     return lax.ppermute(value, axis, [(source, source + steps) for source in range(count - steps)])
 
 
-def split_kernel(q_ref, *out_refs):
-    width = out_refs[0].shape[-1]
-    for head, out_ref in enumerate(out_refs):
-        out_ref[...] = q_ref[:, head * width : (head + 1) * width]
-
-
-def split_queries(queries, parts, kv_here):
+def split_kernel(q_ref, k_ref, v_ref, first_ref, *out_refs):
+    kv_cols = k_ref.shape[-1]
+    width = out_refs[0].shape[-1] if out_refs else first_ref.shape[-1] - 2 * kv_cols
+    first_ref[:, :kv_cols] = k_ref[...]
+    first_ref[:, kv_cols : 2 * kv_cols] = v_ref[...]
+    first_ref[:, 2 * kv_cols :] = q_ref[:, :width]
+    for piece, out_ref in enumerate(out_refs):
+        out_ref[...] = q_ref[:, (piece + 1) * width : (piece + 2) * width]
+
+
+def split_inputs(queries, keys, values, parts, width):
     tokens_here, cols = queries.shape
     group_cols = cols // parts
-    width = group_cols // kv_here
-    shape = jax.ShapeDtypeStruct((parts, tokens_here, width), queries.dtype)
+    kv_cols = keys.shape[1] // parts
+    pieces = group_cols // width
+    first = jax.ShapeDtypeStruct((parts, tokens_here, 2 * kv_cols + width), queries.dtype)
+    rest = jax.ShapeDtypeStruct((parts, tokens_here, width), queries.dtype)
     return pl.pallas_call(
         split_kernel,
         grid=(parts,),
-        in_specs=[pl.BlockSpec((tokens_here, group_cols), lambda p: (0, p))],
-        out_specs=[pl.BlockSpec((None, tokens_here, width), lambda p: (p, 0, 0))] * kv_here,
-        out_shape=[shape] * kv_here,
-    )(queries)
-
-
-def pair_kernel(k_ref, v_ref, o_ref):
-    width = k_ref.shape[-1]
-    o_ref[:, :width] = k_ref[...]
-    o_ref[:, width:] = v_ref[...]
-
-
-def split_keys_values(keys, values, parts):
-    tokens_here, cols = keys.shape
-    group_cols = cols // parts
-    return pl.pallas_call(
-        pair_kernel,
-        grid=(parts,),
-        in_specs=[pl.BlockSpec((tokens_here, group_cols), lambda p: (0, p))] * 2,
-        out_specs=pl.BlockSpec((None, tokens_here, 2 * group_cols), lambda p: (p, 0, 0)),
-        out_shape=jax.ShapeDtypeStruct((parts, tokens_here, 2 * group_cols), keys.dtype),
-    )(keys, values)
+        in_specs=[
+            pl.BlockSpec((tokens_here, group_cols), lambda p: (0, p)),
+            pl.BlockSpec((tokens_here, kv_cols), lambda p: (0, p)),
+            pl.BlockSpec((tokens_here, kv_cols), lambda p: (0, p)),
+        ],
+        out_specs=[pl.BlockSpec((None, tokens_here, 2 * kv_cols + width), lambda p: (p, 0, 0))]
+        + [pl.BlockSpec((None, tokens_here, width), lambda p: (p, 0, 0))] * (pieces - 1),
+        out_shape=[first] + [rest] * (pieces - 1),
+    )(queries, keys, values)
 
 
 def delta_kernel(k_ref, v_ref, o_ref):
@@ -77,22 +70,27 @@
     o_ref[HD : HD + 1, :] += jnp.sum(key_feature, axis=0, keepdims=True)
 
 
-def segment_deltas(kv_local, kv_here):
-    parts, tokens_here, _ = kv_local.shape
+def local_deltas(keys, values):
+    tokens_here, cols = keys.shape
+    kv_heads = cols // HD
     return pl.pallas_call(
         delta_kernel,
-        grid=(kv_here, parts),
-        in_specs=[
-            pl.BlockSpec((None, tokens_here, HD), lambda g, t: (t, 0, g)),
-            pl.BlockSpec((None, tokens_here, HD), lambda g, t: (t, 0, kv_here + g)),
-        ],
+        grid=(kv_heads, 1),
+        in_specs=[pl.BlockSpec((tokens_here, HD), lambda g, t: (0, g))] * 2,
         out_specs=pl.BlockSpec((None, STATE_ROWS, HD), lambda g, t: (g, 0, 0)),
-        out_shape=jax.ShapeDtypeStruct((kv_here, STATE_ROWS, HD), jnp.float32),
+        out_shape=jax.ShapeDtypeStruct((kv_heads, STATE_ROWS, HD), jnp.float32),
         compiler_params=pltpu.CompilerParams(dimension_semantics=("arbitrary", "arbitrary")),
-    )(kv_local, kv_local)
-
-
-def earlier_sum(delta):
+    )(keys, values)
+
+
+def before_states(keys, values, kv_here):
+    total = local_deltas(keys, values)
+    parts = lax.axis_size("head")
+    steps = 1
+    while steps < parts:
+        total = total + lax.ppermute(total, "head", [(p, p ^ steps) for p in range(parts)])
+        steps *= 2
+    delta = lax.dynamic_slice_in_dim(total, lax.axis_index("head") * kv_here, kv_here)
     count = lax.axis_size("seq")
     total = delta
     steps = 1
@@ -171,8 +169,8 @@
             ).astype(o_ref.dtype)
 
 
-def attend(query_rows, kv_local, state, mixing, head, kv_here):
-    parts, block, width = query_rows.shape
+def attend(query_rows, q_col, kv_local, state, mixing, head, kv_here, width):
+    parts, block, _ = query_rows.shape
     group_size = width // HD
     pairs = [(i, j) for i in range(parts) for j in range(i + 1)]
     q_index = jnp.asarray(np.array([p[0] for p in pairs], np.int32))
@@ -182,7 +180,7 @@
         grid=(len(pairs),),
         in_specs=[
             pl.BlockSpec(memory_space=pltpu.SMEM),
-            pl.BlockSpec((None, block, width), lambda t, qi, kj: (qi[t], 0, 0)),
+            pl.BlockSpec((None, block, width), lambda t, qi, kj: (qi[t], 0, q_col)),
             pl.BlockSpec((None, block, HD), lambda t, qi, kj: (kj[t], 0, head)),
             pl.BlockSpec((None, block, HD), lambda t, qi, kj: (kj[t], 0, kv_here + head)),
             pl.BlockSpec((None, STATE_ROWS, HD), lambda t, qi, kj: (head, 0, 0)),
@@ -197,7 +195,7 @@
     return pl.pallas_call(
         functools.partial(flash_kernel, group_size=group_size),
         grid_spec=grid_spec,
-        out_shape=jax.ShapeDtypeStruct(query_rows.shape, jnp.bfloat16),
+        out_shape=jax.ShapeDtypeStruct((parts, block, width), jnp.bfloat16),
         compiler_params=pltpu.CompilerParams(dimension_semantics=("arbitrary",)),
     )(q_index, k_index, mixing, query_rows, kv_local, kv_local, state)
 
@@ -205,19 +203,19 @@
 def merge_kernel(*refs):
     in_refs, out_ref = refs[:-1], refs[-1]
     width = in_refs[0].shape[-1]
-    for head, in_ref in enumerate(in_refs):
-        out_ref[:, head * width : (head + 1) * width] = in_ref[...]
-
-
-def merge_heads(returned):
+    for piece, in_ref in enumerate(in_refs):
+        out_ref[:, piece * width : (piece + 1) * width] = in_ref[...]
+
+
+def merge_pieces(returned):
     parts, tokens_here, width = returned[0].shape
-    kv_here = len(returned)
+    pieces = len(returned)
     return pl.pallas_call(
         merge_kernel,
         grid=(parts,),
-        in_specs=[pl.BlockSpec((None, tokens_here, width), lambda p: (p, 0, 0))] * kv_here,
-        out_specs=pl.BlockSpec((tokens_here, kv_here * width), lambda p: (0, p)),
-        out_shape=jax.ShapeDtypeStruct((tokens_here, parts * kv_here * width), returned[0].dtype),
+        in_specs=[pl.BlockSpec((None, tokens_here, width), lambda p: (p, 0, 0))] * pieces,
+        out_specs=pl.BlockSpec((tokens_here, pieces * width), lambda p: (0, p)),
+        out_shape=jax.ShapeDtypeStruct((tokens_here, parts * pieces * width), returned[0].dtype),
     )(*returned)
 
 
@@ -226,23 +224,31 @@
     head_place = lax.axis_index("head")
     kv_here = keys.shape[1] // (parts * HD)
     group_size = queries.shape[1] // keys.shape[1]
+    width = 2 * HD if group_size % 2 == 0 else HD
+    per_head = group_size * HD // width
 
     def exchange(blocks):
         return lax.all_to_all(blocks, "head", split_axis=0, concat_axis=0, tiled=True)
 
-    kv_local = exchange(split_keys_values(keys, values, parts))
-    state = earlier_sum(segment_deltas(kv_local, kv_here))
-    query_parts = split_queries(queries, parts, kv_here)
+    state = before_states(keys, values, kv_here)
+    sent = split_inputs(queries, keys, values, parts, width)
+    kv_local = exchange(sent[0])
     gate_here = lax.dynamic_slice_in_dim(
         gate_logit, head_place * kv_here * group_size, kv_here * group_size
     )
-    mixing = jax.nn.sigmoid(gate_here).reshape(kv_here, group_size)
+    mixing = jax.nn.sigmoid(gate_here).reshape(kv_here * per_head, width // HD)
+    kv_blocks = 2 * kv_here * HD // width
     returned = []
-    for head in range(kv_here):
-        query_rows = exchange(query_parts[head])
-        attended = attend(query_rows, kv_local, state, mixing[head], head, kv_here)
+    for piece in range(kv_here * per_head):
+        if piece == 0:
+            query_rows, q_col = kv_local, kv_blocks
+        else:
+            query_rows, q_col = exchange(sent[piece]), 0
+        attended = attend(
+            query_rows, q_col, kv_local, state, mixing[piece], piece // per_head, kv_here, width
+        )
         returned.append(exchange(attended))
-    return merge_heads(returned)
+    return merge_pieces(returned)
 
 
 def solution(mesh):

time: 219 us -> 244 us (1.11)
  starting transfers between devices: 27 us -> 38.9 us
  Pallas kernels: 93.5 us -> 103 us
  waiting for transfers between devices: 32 us -> 40.4 us
  blocking collectives: 58.6 us -> 53.3 us
    pallas_call x2 -> x4, Pallas kernels: 73.4 us -> 85.6 us  [attend(): pl.pallas_call(functools.partial(flash_kernel, group_size=group_size), gr...]
    all_to_all x3 -> x5, starting transfers between devices: 16.5 us -> 27.9 us  [exchange(): lax.all_to_all(blocks, 'head', split_axis=0, concat_axis=0, tiled=True)]
    ppermute x0 -> x2, waiting for transfers between devices: none -> 7.26 us  [before_states(): lax.ppermute(total, 'head', [(p, p ^ steps) for p in range(parts)])]
    all_to_all x2 -> x3, blocking collectives: 58.6 us -> 53.3 us  [exchange(): lax.all_to_all(blocks, 'head', split_axis=0, concat_axis=0, tiled=True)]
    all_to_all x3 -> x5, waiting for transfers between devices: 20 us -> 23.8 us  [exchange(): lax.all_to_all(blocks, 'head', split_axis=0, concat_axis=0, tiled=True)]
    add x2 -> x4, other arithmetic: 0.95 us -> 3.86 us  [the longest x2 2.91 us: before_states(): total + lax.ppermute(total, 'head', [(p, p ^ steps) for p in range(parts)])]
    ppermute x3, waiting for transfers between devices: 12 us -> 9.34 us  [shifted(): lax.ppermute(value, axis, [(source, source + steps) for source in range(c...]
    pallas_call x4 -> x3, Pallas kernels: 20.1 us -> 17.7 us  [the longest x1 7.05 us: local_deltas(): pl.pallas_call(delta_kernel, grid=(kv_heads, 1), in_specs=[pl.BlockSpec((...]
  transfers between devices with their start and end apart: 6 -> 10, of which waited for: 4 -> 6; matrix products, arithmetic and copies ran while one was open for 1% -> 2% of each run, Pallas kernels for 39% -> 38%
where the time goes in v4:
time: 244 us; the launch traced here: 241 us
  Pallas kernels  103 us (42%)
  blocking collectives  53.3 us (22%)
  waiting for transfers between devices  40.4 us (17%)
  starting transfers between devices  38.9 us (16%)
  other arithmetic  4.62 us (2%)
    pallas_call x4, Pallas kernels, attend(): pl.pallas_call(functools.partial(flash_kernel, group_size=group_size), gr...  85.6 us
    all_to_all x3, blocking collectives, exchange(): lax.all_to_all(blocks, 'head', split_axis=0, concat_axis=0, tiled=True)  53.3 us
    all_to_all x5, starting transfers between devices, exchange(): lax.all_to_all(blocks, 'head', split_axis=0, concat_axis=0, tiled=True)  27.9 us
    all_to_all x5, waiting for transfers between devices, exchange(): lax.all_to_all(blocks, 'head', split_axis=0, concat_axis=0, tiled=True)  23.8 us
    ppermute x3, starting transfers between devices, shifted(): lax.ppermute(value, axis, [(source, source + steps) for source in range(c...  10.5 us
    ppermute x3, waiting for transfers between devices, shifted(): lax.ppermute(value, axis, [(source, source + steps) for source in range(c...  9.34 us
    ppermute x2, waiting for transfers between devices, before_states(): lax.ppermute(total, 'head', [(p, p ^ steps) for p in range(parts)])  7.26 us
    pallas_call x1, Pallas kernels, local_deltas(): pl.pallas_call(delta_kernel, grid=(kv_heads, 1), in_specs=[pl.BlockSpec((...  7.05 us
  transfers between devices with their start and end apart: 10, of which 6 were waited for; matrix products, arithmetic and copies ran while one was open for 2% of the time, Pallas kernels for 38%

profile of v4, /device:TPU:13, one launch (start us, length us, event | category | flops | bytes accessed | tf_op | source)
XLA Modules:
  0.0 241.4 jit_solution(14564994809187777891)
XLA Ops:
  0.0 5.9 %shard_map.118 = (bf16[4,512,768]{2,1,0:T(8,128)(2,1)}, bf16[4,512,256]{2,1,0:T(8,128)(2,1)}, bf16[4,512,256]{2,1,0:T(8,128)(2,1)}, bf16[4,512,256]{2,1,0:T(8,128)(2,1)}) custom-call(bf16[512,4096]{1,0:T(8,128)(2,1)} %q_ref.1, bf16[512,1024]{1,0:T(8,128)(2,1)} %k_ref.3, bf16[512,1024]{1,0:T(8,128)(2,1)} %v_ref.3), custom_call_target="tpu_custom_call" | custom-call | tf_op jit(solution)/shard_map/pallas_call | solution.py:45
  5.9 17.7 %all_to_all.40.q_ref = bf16[4,512,256]{2,1,0:T(8,128)(2,1)} all-to-all(bf16[4,512,256]{2,1,0:T(8,128)(2,1)} %get-tuple-element.10), channel_id=1, replica_groups=mesh['seq'=8,'head'=4] {'head'}, dimensions={0} | all-to-all | bytes 2097152 | tf_op jit(solution)/shard_map/all_to_all | solution.py:231
  23.5 18.8 %all_to_all.41.q_ref = bf16[4,512,256]{2,1,0:T(8,128)(2,1)} all-to-all(bf16[4,512,256]{2,1,0:T(8,128)(2,1)} %get-tuple-element.11), channel_id=1, replica_groups=mesh['seq'=8,'head'=4] {'head'}, dimensions={0} | all-to-all | bytes 2097152 | tf_op jit(solution)/shard_map/all_to_all | solution.py:231
  42.3 5.6 %all-to-all-start = ((bf16[4,512,768]{2,1,0:T(8,128)(2,1)}), bf16[4,512,768]{2,1,0:T(8,128)(2,1)S(1)}, u32[]{:S(2)}, u32[]{:S(2)}) async-start(bf16[4,512,768]{2,1,0:T(8,128)(2,1)} %get-tuple-element.9), calls=%async_computation | async-start | bytes 6291456 | tf_op jit(solution)/shard_map/all_to_all | solution.py:231
  47.9 0.0 copy-start.4
  47.9 7.0 %shard_map.119 = f32[8,136,128]{2,1,0:T(8,128)} custom-call(bf16[512,1024]{1,0:T(8,128)(2,1)} %k_ref.3, bf16[512,1024]{1,0:T(8,128)(2,1)} %v_ref.3), custom_call_target="tpu_custom_call" | custom-call | tf_op jit(solution)/shard_map/pallas_call | solution.py:76
  54.9 0.4 collective-permute-start
  55.3 1.8 collective-permute-done
  57.1 1.9 add.26
  59.0 0.1 collective-permute-start.1
  59.1 23.8 %all-to-all-done.q_ref.k_ref.v_ref = bf16[4,512,768]{2,1,0:T(8,128)(2,1)S(1)} async-done(((bf16[4,512,768]{2,1,0:T(8,128)(2,1)}), bf16[4,512,768]{2,1,0:T(8,128)(2,1)S(1)}, u32[]{:S(2)}, u32[]{:S(2)}) %all-to-all-start) | async-done | bytes 3145760 | tf_op jit(solution)/shard_map/all_to_all | solution.py:231
  82.9 0.0 copy-start
  82.9 6.6 %all-to-all-start.6 = ((bf16[4,512,256]{2,1,0:T(8,128)(2,1)}), bf16[4,512,256]{2,1,0:T(8,128)(2,1)}, u32[]{:S(2)}, u32[]{:S(2)}) async-start(bf16[4,512,256]{2,1,0:T(8,128)(2,1)} %get-tuple-element.12), calls=%async_computation.6 | async-start | bytes 2097152 | tf_op jit(solution)/shard_map/all_to_all | solution.py:231
  89.5 5.5 %collective-permute-done.1 = f32[8,136,128]{2,1,0:T(8,128)} collective-permute-done((f32[8,136,128]{2,1,0:T(8,128)}, f32[8,136,128]{2,1,0:T(8,128)}, u32[]{:S(2)}, u32[]{:S(2)}) %collective-permute-start.1) | collective-permute-done | bytes 557088 | tf_op jit(solution)/shard_map/ppermute | solution.py:91
  94.9 1.0 dynamic-slice_add_fusion
  95.9 3.1 %collective-permute-start.2 = (f32[2,136,128]{2,1,0:T(8,128)S(1)}, f32[2,136,128]{2,1,0:T(8,128)S(1)}, u32[]{:S(2)}, u32[]{:S(2)}) collective-permute-start(f32[2,136,128]{2,1,0:T(8,128)S(1)} %dynamic-slice_add_fusion), channel_id=1, source_target_pairs={{0,4},{4,8},{8,12},{12,16},{16,20},{20,24},{24,28},{1,5},{5,9},{9,... | collective-permute-start | bytes 417800 | tf_op jit(solution)/shard_map/ppermute | solution.py:25
  99.1 4.1 %collective-permute-done.2 = f32[2,136,128]{2,1,0:T(8,128)S(1)} collective-permute-done((f32[2,136,128]{2,1,0:T(8,128)S(1)}, f32[2,136,128]{2,1,0:T(8,128)S(1)}, u32[]{:S(2)}, u32[]{:S(2)}) %collective-permute-start.2) | collective-permute-done | bytes 139296 | tf_op jit(solution)/shard_map/ppermute | solution.py:25
  103.2 3.2 %collective-permute-start.3 = (f32[2,136,128]{2,1,0:T(8,128)S(1)}, f32[2,136,128]{2,1,0:T(8,128)}, u32[]{:S(2)}, u32[]{:S(2)}) collective-permute-start(f32[2,136,128]{2,1,0:T(8,128)S(1)} %add.29), channel_id=1, source_target_pairs={{0,8},{4,12},{8,16},{12,20},{16,24},{20,28},{1,9},{5,13},{9,17},{1... | collective-permute-start | bytes 417800 | tf_op jit(solution)/shard_map/ppermute | solution.py:25
  106.4 0.0 copy-done.4
  106.4 0.1 add_divide_fusion
  106.5 2.6 %collective-permute-done.3 = f32[2,136,128]{2,1,0:T(8,128)} collective-permute-done((f32[2,136,128]{2,1,0:T(8,128)S(1)}, f32[2,136,128]{2,1,0:T(8,128)}, u32[]{:S(2)}, u32[]{:S(2)}) %collective-permute-start.3) | collective-permute-done | bytes 139296 | tf_op jit(solution)/shard_map/ppermute | solution.py:25
  109.1 0.9 add.30
  110.0 4.2 %collective-permute-start.4 = (f32[2,136,128]{2,1,0:T(8,128)S(1)}, f32[2,136,128]{2,1,0:T(8,128)S(1)}, u32[]{:S(2)}, u32[]{:S(2)}) collective-permute-start(f32[2,136,128]{2,1,0:T(8,128)S(1)} %add.30), channel_id=1, source_target_pairs={{0,16},{4,20},{8,24},{12,28},{1,17},{5,21},{9,25},{13,29},{2,18},{... | collective-permute-start | bytes 417800 | tf_op jit(solution)/shard_map/ppermute | solution.py:25
  114.2 0.7 fusion
  114.9 2.7 %collective-permute-done.4 = f32[2,136,128]{2,1,0:T(8,128)S(1)} collective-permute-done((f32[2,136,128]{2,1,0:T(8,128)S(1)}, f32[2,136,128]{2,1,0:T(8,128)S(1)}, u32[]{:S(2)}, u32[]{:S(2)}) %collective-permute-start.4) | collective-permute-done | bytes 139296 | tf_op jit(solution)/shard_map/ppermute | solution.py:25
  117.6 0.7 add_subtract_fusion.s_ref
  118.2 0.0 copy-done
  118.2 21.4 %shard_map.120 = bf16[4,512,256]{2,1,0:T(8,128)(2,1)} custom-call(s32[10]{0:T(128)} %constant.20.clone.qi_ref, s32[10]{0:T(128)} %constant.21.clone.kj_ref, f32[2]{0:T(128)} %get-tuple-element.16.gate_ref, bf16[4,512,768]{2,1,0:T(8,128)(2,1)} %copy-done, bf16[4,512,768]{2,1,0:T(8,128)(2,1)} %copy-done, bf16[4,512,768]{2,1,0:T(8,128)(2,1)} %copy-done, ...), custom_call_target="tpu_custom_call" | custom-call | tf_op jit(solution)/shard_map/pallas_call | solution.py:195
  139.7 0.0 all-to-all-done.6.q_ref
  139.7 8.5 %all-to-all-start.1 = ((bf16[4,512,256]{2,1,0:T(8,128)(2,1)}), bf16[4,512,256]{2,1,0:T(8,128)(2,1)S(1)}, u32[]{:S(2)}, u32[]{:S(2)}) async-start(bf16[4,512,256]{2,1,0:T(8,128)(2,1)} %shard_map.120), calls=%async_computation.1 | async-start | bytes 2097152 | tf_op jit(solution)/shard_map/all_to_all | solution.py:231
  148.2 21.4 %shard_map.121 = bf16[4,512,256]{2,1,0:T(8,128)(2,1)} custom-call(s32[10]{0:T(128)} %constant.20.clone.qi_ref, s32[10]{0:T(128)} %constant.21.clone.kj_ref, f32[2]{0:T(128)} %get-tuple-element.15.gate_ref, bf16[4,512,256]{2,1,0:T(8,128)(2,1)} %all_to_all.40.q_ref, bf16[4,512,768]{2,1,0:T(8,128)(2,1)} %copy-done, bf16[4,512,768]{2,1,0:T(8,128)(2,1)} %copy-done, ...), custom_call_target="tpu_custom_call" | custom-call | tf_op jit(solution)/shard_map/pallas_call | solution.py:195
  169.6 0.0 all-to-all-done.1.refs_0_
  169.6 0.0 copy-start.1
  169.6 3.7 %all-to-all-start.3 = ((bf16[4,512,256]{2,1,0:T(8,128)(2,1)}), bf16[4,512,256]{2,1,0:T(8,128)(2,1)S(1)}, u32[]{:S(2)}, u32[]{:S(2)}) async-start(bf16[4,512,256]{2,1,0:T(8,128)(2,1)} %shard_map.121), calls=%async_computation.3 | async-start | bytes 2097152 | tf_op jit(solution)/shard_map/all_to_all | solution.py:231
  173.3 21.4 %shard_map.122 = bf16[4,512,256]{2,1,0:T(8,128)(2,1)} custom-call(s32[10]{0:T(128)} %constant.20.clone.qi_ref, s32[10]{0:T(128)} %constant.21.clone.kj_ref, f32[2]{0:T(128)} %get-tuple-element.14.gate_ref, bf16[4,512,256]{2,1,0:T(8,128)(2,1)} %all_to_all.41.q_ref, bf16[4,512,768]{2,1,0:T(8,128)(2,1)} %copy-done, bf16[4,512,768]{2,1,0:T(8,128)(2,1)} %copy-done, ...), custom_call_target="tpu_custom_call" | custom-call | tf_op jit(solution)/shard_map/pallas_call | solution.py:195
  194.7 0.0 copy-done.1
  194.7 0.0 all-to-all-done.3.refs_1_
  194.7 0.0 copy-start.2
  194.7 3.5 %all-to-all-start.5 = ((bf16[4,512,256]{2,1,0:T(8,128)(2,1)}), bf16[4,512,256]{2,1,0:T(8,128)(2,1)S(1)}, u32[]{:S(2)}, u32[]{:S(2)}) async-start(bf16[4,512,256]{2,1,0:T(8,128)(2,1)} %shard_map.122), calls=%async_computation.5 | async-start | bytes 2097152 | tf_op jit(solution)/shard_map/all_to_all | solution.py:231
  198.3 21.4 %shard_map.123 = bf16[4,512,256]{2,1,0:T(8,128)(2,1)} custom-call(s32[10]{0:T(128)} %constant.20.clone.qi_ref, s32[10]{0:T(128)} %constant.21.clone.kj_ref, f32[2]{0:T(128)} %get-tuple-element.13.gate_ref, bf16[4,512,256]{2,1,0:T(8,128)(2,1)} %all-to-all-done.6.q_ref, bf16[4,512,768]{2,1,0:T(8,128)(2,1)} %copy-done, bf16[4,512,768]{2,1,0:T(8,128)(2,1)} %copy-done, ...), custom_call_target="tpu_custom_call" | custom-call | tf_op jit(solution)/shard_map/pallas_call | solution.py:195
  219.7 0.0 copy-done.2
  219.7 0.0 all-to-all-done.5.refs_2_
  219.7 0.0 copy-start.3
  219.7 16.9 %all_to_all.42.refs_3_ = bf16[4,512,256]{2,1,0:T(8,128)(2,1)} all-to-all(bf16[4,512,256]{2,1,0:T(8,128)(2,1)} %shard_map.123), channel_id=1, replica_groups=mesh['seq'=8,'head'=4] {'head'}, dimensions={0} | all-to-all | bytes 2097152 | tf_op jit(solution)/shard_map/all_to_all | solution.py:231
  236.6 0.0 copy-done.3
  236.6 4.8 %shard_map.124 = bf16[512,4096]{1,0:T(8,128)(2,1)} custom-call(bf16[4,512,256]{2,1,0:T(8,128)(2,1)} %copy-done.1, bf16[4,512,256]{2,1,0:T(8,128)(2,1)} %copy-done.2, bf16[4,512,256]{2,1,0:T(8,128)(2,1)} %copy-done.3, bf16[4,512,256]{2,1,0:T(8,128)(2,1)} %all_to_all.42.refs_3_), custom_call_target="tpu_custom_call" | custom-call | tf_op jit(solution)/shard_map/pallas_call | solution.py:213
  (1 shorter events, 0.0 us)
Async XLA Ops:
  42.3 40.6 %all-to-all-start = ((bf16[4,512,768]{2,1,0:T(8,128)(2,1)}), bf16[4,512,768]{2,1,0:T(8,128)(2,1)S(1)}, u32[]{:S(2)}, u32[]{:S(2)}) async-start(bf16[4,512,768]{2,1,0:T(8,128)(2,1)} %get-tuple-element.9), calls=%async_computation | async-start | bytes 6291456 | tf_op jit(solution)/shard_map/all_to_all | solution.py:231
  47.9 58.5 %copy-start.4 = (f32[32]{0:T(128)S(1)}, f32[32]{0:T(128)}, u32[]{:S(2)}) copy-start(f32[32]{0:T(128)} %param.15) | copy-start | bytes 388
  54.9 2.2 collective-permute-start
  59.0 35.9 %collective-permute-start.1 = (f32[8,136,128]{2,1,0:T(8,128)}, f32[8,136,128]{2,1,0:T(8,128)}, u32[]{:S(2)}, u32[]{:S(2)}) collective-permute-start(f32[8,136,128]{2,1,0:T(8,128)} %add.26), channel_id=1, source_target_pairs={{0,2},{1,3},{2,0},{3,1},{4,6},{5,7},{6,4},{7,5},{8,10},{9,11},{10,... | collective-permute-start | bytes 1671176 | tf_op jit(solution)/shard_map/ppermute | solution.py:91
  82.9 35.3 %copy-start = (bf16[4,512,768]{2,1,0:T(8,128)(2,1)}, bf16[4,512,768]{2,1,0:T(8,128)(2,1)S(1)}, u32[]{:S(2)}) copy-start(bf16[4,512,768]{2,1,0:T(8,128)(2,1)S(1)} %all-to-all-done.q_ref.k_ref.v_ref) | copy-start | bytes 9437188
  82.9 56.8 %all-to-all-start.6 = ((bf16[4,512,256]{2,1,0:T(8,128)(2,1)}), bf16[4,512,256]{2,1,0:T(8,128)(2,1)}, u32[]{:S(2)}, u32[]{:S(2)}) async-start(bf16[4,512,256]{2,1,0:T(8,128)(2,1)} %get-tuple-element.12), calls=%async_computation.6 | async-start | bytes 2097152 | tf_op jit(solution)/shard_map/all_to_all | solution.py:231
  95.9 7.2 %collective-permute-start.2 = (f32[2,136,128]{2,1,0:T(8,128)S(1)}, f32[2,136,128]{2,1,0:T(8,128)S(1)}, u32[]{:S(2)}, u32[]{:S(2)}) collective-permute-start(f32[2,136,128]{2,1,0:T(8,128)S(1)} %dynamic-slice_add_fusion), channel_id=1, source_target_pairs={{0,4},{4,8},{8,12},{12,16},{16,20},{20,24},{24,28},{1,5},{5,9},{9,... | collective-permute-start | bytes 417800 | tf_op jit(solution)/shard_map/ppermute | solution.py:25
  103.2 5.9 %collective-permute-start.3 = (f32[2,136,128]{2,1,0:T(8,128)S(1)}, f32[2,136,128]{2,1,0:T(8,128)}, u32[]{:S(2)}, u32[]{:S(2)}) collective-permute-start(f32[2,136,128]{2,1,0:T(8,128)S(1)} %add.29), channel_id=1, source_target_pairs={{0,8},{4,12},{8,16},{12,20},{16,24},{20,28},{1,9},{5,13},{9,17},{1... | collective-permute-start | bytes 417800 | tf_op jit(solution)/shard_map/ppermute | solution.py:25
  110.0 7.6 %collective-permute-start.4 = (f32[2,136,128]{2,1,0:T(8,128)S(1)}, f32[2,136,128]{2,1,0:T(8,128)S(1)}, u32[]{:S(2)}, u32[]{:S(2)}) collective-permute-start(f32[2,136,128]{2,1,0:T(8,128)S(1)} %add.30), channel_id=1, source_target_pairs={{0,16},{4,20},{8,24},{12,28},{1,17},{5,21},{9,25},{13,29},{2,18},{... | collective-permute-start | bytes 417800 | tf_op jit(solution)/shard_map/ppermute | solution.py:25
  139.7 29.9 %all-to-all-start.1 = ((bf16[4,512,256]{2,1,0:T(8,128)(2,1)}), bf16[4,512,256]{2,1,0:T(8,128)(2,1)S(1)}, u32[]{:S(2)}, u32[]{:S(2)}) async-start(bf16[4,512,256]{2,1,0:T(8,128)(2,1)} %shard_map.120), calls=%async_computation.1 | async-start | bytes 2097152 | tf_op jit(solution)/shard_map/all_to_all | solution.py:231
  169.6 25.1 %copy-start.1 = (bf16[4,512,256]{2,1,0:T(8,128)(2,1)}, bf16[4,512,256]{2,1,0:T(8,128)(2,1)S(1)}, u32[]{:S(2)}) copy-start(bf16[4,512,256]{2,1,0:T(8,128)(2,1)S(1)} %all-to-all-done.1.refs_0_) | copy-start | bytes 3145732
  169.6 25.1 %all-to-all-start.3 = ((bf16[4,512,256]{2,1,0:T(8,128)(2,1)}), bf16[4,512,256]{2,1,0:T(8,128)(2,1)S(1)}, u32[]{:S(2)}, u32[]{:S(2)}) async-start(bf16[4,512,256]{2,1,0:T(8,128)(2,1)} %shard_map.121), calls=%async_computation.3 | async-start | bytes 2097152 | tf_op jit(solution)/shard_map/all_to_all | solution.py:231
  194.7 25.0 %copy-start.2 = (bf16[4,512,256]{2,1,0:T(8,128)(2,1)}, bf16[4,512,256]{2,1,0:T(8,128)(2,1)S(1)}, u32[]{:S(2)}) copy-start(bf16[4,512,256]{2,1,0:T(8,128)(2,1)S(1)} %all-to-all-done.3.refs_1_) | copy-start | bytes 3145732
  194.7 24.9 %all-to-all-start.5 = ((bf16[4,512,256]{2,1,0:T(8,128)(2,1)}), bf16[4,512,256]{2,1,0:T(8,128)(2,1)S(1)}, u32[]{:S(2)}, u32[]{:S(2)}) async-start(bf16[4,512,256]{2,1,0:T(8,128)(2,1)} %shard_map.122), calls=%async_computation.5 | async-start | bytes 2097152 | tf_op jit(solution)/shard_map/all_to_all | solution.py:231
  219.7 16.9 %copy-start.3 = (bf16[4,512,256]{2,1,0:T(8,128)(2,1)}, bf16[4,512,256]{2,1,0:T(8,128)(2,1)S(1)}, u32[]{:S(2)}) copy-start(bf16[4,512,256]{2,1,0:T(8,128)(2,1)S(1)} %all-to-all-done.5.refs_2_) | copy-start | bytes 3145732

commit v5 on v4

v5 whole, which is shorter than its diff:
```python
import functools

import jax
import jax.numpy as jnp
import numpy as np
from jax import lax
from jax.experimental import pallas as pl
from jax.experimental.pallas import tpu as pltpu
from jax.sharding import PartitionSpec as P

HQ = 32
KVH = 8
HD = 128
SEG = 2048
LANES = 128
STATE_ROWS = HD + 8


def feature(inputs):
    return jnp.where(inputs > 0, inputs + 1.0, jnp.exp(jnp.minimum(inputs, 0.0)))


def shifted(value, axis, steps):
    count = lax.axis_size(axis)
    return lax.ppermute(value, axis, [(source, source + steps) for source in range(count - steps)])


def split_kernel(core_ref, q_keep, k_keep, v_keep, q_send, k_send, v_send, keep_ref, send_ref):
    q_cols = q_keep.shape[-1]
    k_cols = k_keep.shape[-1]
    for q_ref, k_ref, v_ref, o_ref in ((q_keep, k_keep, v_keep, keep_ref), (q_send, k_send, v_send, send_ref)):
        o_ref[:, :q_cols] = q_ref[...]
        o_ref[:, q_cols : q_cols + k_cols] = k_ref[...]
        o_ref[:, q_cols + k_cols :] = v_ref[...]


def split_inputs(queries, keys, values, core):
    tokens_here, q_all = queries.shape
    q_cols = q_all // 2
    k_cols = keys.shape[1] // 2
    keep_map = lambda i, c: (0, c[0])
    send_map = lambda i, c: (0, 1 - c[0])
    shape = jax.ShapeDtypeStruct((tokens_here, q_cols + 2 * k_cols), queries.dtype)
    grid_spec = pltpu.PrefetchScalarGridSpec(
        num_scalar_prefetch=1,
        grid=(1,),
        in_specs=[
            pl.BlockSpec((tokens_here, q_cols), keep_map),
            pl.BlockSpec((tokens_here, k_cols), keep_map),
            pl.BlockSpec((tokens_here, k_cols), keep_map),
            pl.BlockSpec((tokens_here, q_cols), send_map),
            pl.BlockSpec((tokens_here, k_cols), send_map),
            pl.BlockSpec((tokens_here, k_cols), send_map),
        ],
        out_specs=[pl.BlockSpec((tokens_here, q_cols + 2 * k_cols), lambda i, c: (0, 0))] * 2,
    )
    return pl.pallas_call(
        split_kernel, grid_spec=grid_spec, out_shape=[shape, shape]
    )(core.reshape(1), queries, keys, values, queries, keys, values)


def delta_kernel(k_ref, v_ref, o_ref):
    @pl.when(pl.program_id(1) == 0)
    def _init():
        o_ref[...] = jnp.zeros(o_ref.shape, jnp.float32)

    key_feature = feature(k_ref[...].astype(jnp.float32))
    value_data = v_ref[...].astype(jnp.float32)
    o_ref[:HD, :] += jnp.dot(
        key_feature.T, value_data, precision=lax.Precision.HIGHEST,
        preferred_element_type=jnp.float32,
    )
    o_ref[HD : HD + 1, :] += jnp.sum(key_feature, axis=0, keepdims=True)


def local_deltas(keys, values):
    tokens_here, cols = keys.shape
    kv_heads = cols // HD
    return pl.pallas_call(
        delta_kernel,
        grid=(kv_heads, 1),
        in_specs=[pl.BlockSpec((tokens_here, HD), lambda g, t: (0, g))] * 2,
        out_specs=pl.BlockSpec((None, STATE_ROWS, HD), lambda g, t: (g, 0, 0)),
        out_shape=jax.ShapeDtypeStruct((kv_heads, STATE_ROWS, HD), jnp.float32),
        compiler_params=pltpu.CompilerParams(dimension_semantics=("arbitrary", "arbitrary")),
    )(keys, values)


def before_states(keys, values, core, kv_group):
    total = local_deltas(keys, values)
    parts = lax.axis_size("head")
    keep = lax.dynamic_slice_in_dim(total, core * kv_group, kv_group)
    send = lax.dynamic_slice_in_dim(total, (1 - core) * kv_group, kv_group)
    total = keep + lax.ppermute(send, "head", [(p, p ^ 1) for p in range(parts)])
    steps = 2
    while steps < parts:
        total = total + lax.ppermute(total, "head", [(p, p ^ steps) for p in range(parts)])
        steps *= 2
    delta = total
    count = lax.axis_size("seq")
    steps = 1
    while steps < count:
        total = total + shifted(total, "seq", steps)
        steps *= 2
    return total - delta


def flash_kernel(
    qp_ref, kp_ref, op_ref, first_ref, last_ref, valid_ref, gate_ref, q_ref, k_ref, v_ref, s_ref,
    o_ref, m_sc, l_sc, acc_sc, *, group_size
):
    kv_head = pl.program_id(0)
    step_at = pl.program_id(1)
    first = first_ref[step_at] == 1
    last = last_ref[step_at] == 1
    valid = valid_ref[step_at] == 1
    block = q_ref.shape[0]
    score_scale = HD ** (-0.5)

    @pl.when(valid & first)
    def _init():
        m_sc[...] = jnp.full(m_sc.shape, -jnp.inf, jnp.float32)
        l_sc[...] = jnp.zeros(l_sc.shape, jnp.float32)
        acc_sc[...] = jnp.zeros(acc_sc.shape, jnp.float32)

    def step(masked):
        key_rows = k_ref[...]
        value_rows = v_ref[...]
        if masked:
            rows = lax.broadcasted_iota(jnp.int32, (block, block), 0)
            cols = lax.broadcasted_iota(jnp.int32, (block, block), 1)
            allowed = cols <= rows
        for head in range(group_size):
            lanes = slice(head * HD, (head + 1) * HD)
            scores = (
                lax.dot_general(
                    q_ref[:, lanes], key_rows, (((1,), (1,)), ((), ())),
                    preferred_element_type=jnp.float32,
                )
                * score_scale
            )
            if masked:
                scores = jnp.where(allowed, scores, -1e30)
            m_prev = m_sc[head]
            m_new = jnp.maximum(m_prev, jnp.max(scores, axis=-1, keepdims=True))
            probs = jnp.exp(scores - m_new[:, :1])
            alpha = jnp.exp(m_prev - m_new)
            l_sc[head] = alpha * l_sc[head] + jnp.sum(probs, axis=-1, keepdims=True)
            acc_sc[:, lanes] = alpha * acc_sc[:, lanes] + jnp.dot(
                probs.astype(jnp.bfloat16), value_rows, preferred_element_type=jnp.float32
            )
            m_sc[head] = m_new

    @pl.when(valid & jnp.logical_not(last))
    def _full():
        step(False)

    @pl.when(valid & last)
    def _last():
        step(True)
        memory = s_ref[:HD, :]
        normalizer = s_ref[HD : HD + 1, :]
        for head in range(group_size):
            lanes = slice(head * HD, (head + 1) * HD)
            local_part = acc_sc[:, lanes] / l_sc[head]
            query_feature = feature(q_ref[:, lanes].astype(jnp.float32))
            numerator = jnp.dot(
                query_feature, memory, precision=lax.Precision.HIGHEST,
                preferred_element_type=jnp.float32,
            )
            denominator = jnp.maximum(
                jnp.sum(query_feature * normalizer, axis=-1, keepdims=True), 1.0
            )
            mixing = gate_ref[kv_head * group_size + head]
            o_ref[:, lanes] = (
                mixing * (numerator / denominator) + (1.0 - mixing) * local_part
            ).astype(o_ref.dtype)


def pair_tables(chips, chip, core):
    longest = 4 * chips - 1
    tables = np.zeros((chips, 2, 6, longest), np.int32)
    for y in range(chips):
        for c in range(2):
            steps = []
            for a in range(2):
                for j in range(2 * y + a + 1):
                    k_pos = 2 * (chips - 1 - y + j // 2) + ((j % 2) ^ c)
                    steps.append((a ^ c, k_pos, a ^ c, int(j == 0), int(j == 2 * y + a), 1))
            while len(steps) < longest:
                steps.append(steps[-1][:5] + (0,))
            tables[y, c] = np.array(steps, np.int32).T
    return jnp.asarray(tables)[chip, core]


def attend(query_rows, kv_rows, state, mixing, tables, group_size):
    _, block, q_cols = query_rows.shape
    kv_group = kv_rows.shape[-1] // (2 * HD)
    width = group_size * HD
    steps = tables.shape[-1]
    grid_spec = pltpu.PrefetchScalarGridSpec(
        num_scalar_prefetch=6,
        grid=(kv_group, steps),
        in_specs=[
            pl.BlockSpec(memory_space=pltpu.SMEM),
            pl.BlockSpec((None, block, width), lambda g, t, qp, kp, op, f, l, v: (qp[t], 0, g)),
            pl.BlockSpec((None, block, HD), lambda g, t, qp, kp, op, f, l, v: (kp[t], 0, g)),
            pl.BlockSpec(
                (None, block, HD), lambda g, t, qp, kp, op, f, l, v: (kp[t], 0, kv_group + g)
            ),
            pl.BlockSpec((None, STATE_ROWS, HD), lambda g, t, qp, kp, op, f, l, v: (g, 0, 0)),
        ],
        out_specs=pl.BlockSpec((None, block, width), lambda g, t, qp, kp, op, f, l, v: (op[t], 0, g)),
        scratch_shapes=[
            pltpu.VMEM((group_size, block, LANES), jnp.float32),
            pltpu.VMEM((group_size, block, LANES), jnp.float32),
            pltpu.VMEM((block, width), jnp.float32),
        ],
    )
    return pl.pallas_call(
        functools.partial(flash_kernel, group_size=group_size),
        grid_spec=grid_spec,
        out_shape=jax.ShapeDtypeStruct((2, block, q_cols), jnp.bfloat16),
        compiler_params=pltpu.CompilerParams(dimension_semantics=("arbitrary", "arbitrary")),
    )(*[tables[i] for i in range(6)], mixing, query_rows, kv_rows, kv_rows, state)


def merge_kernel(core_ref, own_ref, back_ref, o_ref):
    @pl.when(pl.program_id(0) == core_ref[0])
    def _own():
        o_ref[...] = own_ref[...]

    @pl.when(pl.program_id(0) != core_ref[0])
    def _back():
        o_ref[...] = back_ref[...]


def merge_halves(own, back, core):
    tokens_here, q_cols = back.shape
    grid_spec = pltpu.PrefetchScalarGridSpec(
        num_scalar_prefetch=1,
        grid=(2,),
        in_specs=[
            pl.BlockSpec((None, tokens_here, q_cols), lambda h, c: (0, 0, 0)),
            pl.BlockSpec((tokens_here, q_cols), lambda h, c: (0, 0)),
        ],
        out_specs=pl.BlockSpec((tokens_here, q_cols), lambda h, c: (0, h)),
    )
    return pl.pallas_call(
        merge_kernel,
        grid_spec=grid_spec,
        out_shape=jax.ShapeDtypeStruct((tokens_here, 2 * q_cols), back.dtype),
    )(core.reshape(1), own, back)


def body(queries, keys, values, gate_logit):
    parts = lax.axis_size("head")
    chips = parts // 2
    place = lax.axis_index("head")
    chip = place // 2
    core = place % 2
    q_cols = queries.shape[1] // 2
    k_cols = keys.shape[1] // 2
    kv_group = k_cols // HD
    group_size = queries.shape[1] // keys.shape[1]
    sibling = [(p, p ^ 1) for p in range(parts)]

    state = before_states(keys, values, core, kv_group)
    keep, send = split_inputs(queries, keys, values, core)
    recv = lax.ppermute(send, "head", sibling)
    query_rows = jnp.stack([keep[:, :q_cols], recv[:, :q_cols]])
    kv_chip = jnp.stack([keep[:, q_cols:], recv[:, q_cols:]])
    kv_parts = [
        lax.ppermute(kv_chip, "head", [(p, p + 2 * s) for p in range(parts - 2 * s)])
        for s in range(chips - 1, 0, -1)
    ]
    kv_rows = jnp.concatenate(kv_parts + [kv_chip], axis=0)
    gate_here = lax.dynamic_slice_in_dim(gate_logit, core * kv_group * group_size, kv_group * group_size)
    mixing = jax.nn.sigmoid(gate_here)
    attended = attend(query_rows, kv_rows, state, mixing, pair_tables(chips, chip, core), group_size)
    back = lax.ppermute(attended[1], "head", sibling)
    return merge_halves(attended, back, core)


def solution(mesh):
    in_specs = (P(("seq", "head"), None), P(("seq", "head"), None), P(("seq", "head"), None), P())
    out_specs = P(("seq", "head"), None)
    return jax.shard_map(body, mesh=mesh, in_specs=in_specs, out_specs=out_specs, check_vma=False)
```

time: 244 us -> 202 us (0.83)
  blocking collectives: 53.3 us -> 0 us
  starting transfers between devices: 38.9 us -> 14.7 us
  waiting for transfers between devices: 40.4 us -> 53.7 us
  local copies, waits for them, and re-layouts: 0.69 us -> 11.3 us
  Pallas kernels: 103 us -> 112 us
  other arithmetic: 4.62 us -> 9.81 us
    all_to_all x3 -> x0, blocking collectives: 53.3 us -> none  [exchange(): lax.all_to_all(blocks, 'head', split_axis=0, concat_axis=0, tiled=True)]
    ppermute x0 -> x4, waiting for transfers between devices: none -> 30.6 us  [the longest x1 25.3 us: body(): lax.ppermute(kv_chip, 'head', [(p, p + 2 * s) for p in range(parts - 2 *...]
    all_to_all x5 -> x0, starting transfers between devices: 27.9 us -> none  [exchange(): lax.all_to_all(blocks, 'head', split_axis=0, concat_axis=0, tiled=True)]
    all_to_all x5 -> x0, waiting for transfers between devices: 23.8 us -> none  [exchange(): lax.all_to_all(blocks, 'head', split_axis=0, concat_axis=0, tiled=True)]
    pallas_call x4 -> x1, Pallas kernels: 85.6 us -> 95 us  [attend(): pl.pallas_call(functools.partial(flash_kernel, group_size=group_size), gr...]
    ppermute x3, waiting for transfers between devices: 9.34 us -> 15.1 us  [shifted(): lax.ppermute(value, axis, [(source, source + steps) for source in range(c...]
    another operation x0 -> x4, local copies, waits for them, and re-layouts: none -> 5.77 us  [the longest x2 3.18 us: body(): query_rows = jnp.stack([keep[:, :q_cols], recv[:, :q_cols]])]
    ppermute x0 -> x4, starting transfers between devices: none -> 5.29 us  [the longest x1 3.13 us: body(): back = lax.ppermute(attended[1], 'head', sibling)]
  transfers between devices with their start and end apart: 10 -> 8, of which waited for: 6 -> 6; matrix products, arithmetic and copies ran while one was open for 2% -> 7% of each run, Pallas kernels for 38% -> 3%
where the time goes in v5:
time: 202 us
  Pallas kernels  112 us (55%)
  waiting for transfers between devices  53.7 us (27%)
  starting transfers between devices  14.7 us (7%)
  local copies, waits for them, and re-layouts  11.3 us (6%)
  other arithmetic  9.81 us (5%)
    pallas_call x1, Pallas kernels, attend(): pl.pallas_call(functools.partial(flash_kernel, group_size=group_size), gr...  95 us
    ppermute x1, waiting for transfers between devices, body(): lax.ppermute(kv_chip, 'head', [(p, p + 2 * s) for p in range(parts - 2 *...  25.3 us
    ppermute x3, waiting for transfers between devices, shifted(): lax.ppermute(value, axis, [(source, source + steps) for source in range(c...  15.1 us
    ppermute x3, starting transfers between devices, shifted(): lax.ppermute(value, axis, [(source, source + steps) for source in range(c...  9.17 us
    ppermute x1, waiting for transfers between devices, before_states(): lax.ppermute(total, 'head', [(p, p ^ steps) for p in range(parts)])  7.9 us
    pallas_call x1, Pallas kernels, local_deltas(): pl.pallas_call(delta_kernel, grid=(kv_heads, 1), in_specs=[pl.BlockSpec((...  7.03 us
    pallas_call x1, Pallas kernels, split_inputs(): pl.pallas_call(split_kernel, grid_spec=grid_spec, out_shape=[shape, shape])  5.69 us
    pallas_call x1, Pallas kernels, merge_halves(): pl.pallas_call(merge_kernel, grid_spec=grid_spec, out_shape=jax.ShapeDtyp...  4.37 us
  transfers between devices with their start and end apart: 8, of which 6 were waited for; matrix products, arithmetic and copies ran while one was open for 7% of the time, Pallas kernels for 3%

profile of v5, /device:TPU:13, one launch (start us, length us, event | category | flops | bytes accessed | tf_op | source)
XLA Modules:
  0.0 201.6 jit_solution(14658846567349106200)
XLA Ops:
  0.0 5.7 %shard_map.55 = (bf16[512,3072]{1,0:T(8,128)(2,1)}, bf16[512,3072]{1,0:T(8,128)(2,1)}) custom-call(s32[1]{0:T(128)} %bitcast.core_ref, bf16[512,4096]{1,0:T(8,128)(2,1)} %q_send.1, bf16[512,1024]{1,0:T(8,128)(2,1)} %k_ref.1, bf16[512,1024]{1,0:T(8,128)(2,1)} %v_ref.1, bf16[512,4096]{1,0:T(8,128)(2,1)} %q_send.1, bf16[512,1024]{1,0:T(8,128)(2,1)} %k_ref.1, ...), custom_call_target="tpu_custom_call" | custom-call | tf_op jit(solution)/shard_map/pallas_call | solution.py:57
  5.7 0.7 collective-permute-start
  6.4 7.0 %shard_map.56 = f32[8,136,128]{2,1,0:T(8,128)} custom-call(bf16[512,1024]{1,0:T(8,128)(2,1)} %k_ref.1, bf16[512,1024]{1,0:T(8,128)(2,1)} %v_ref.1), custom_call_target="tpu_custom_call" | custom-call | tf_op jit(solution)/shard_map/pallas_call | solution.py:79
  13.4 1.0 constant_dynamic-slice_fusion
  14.4 0.1 collective-permute-start.2
  14.5 1.5 collective-permute-done.2
  16.0 1.0 dynamic-slice_add_fusion
  17.0 0.3 collective-permute-start.3
  17.3 7.9 %collective-permute-done.3 = f32[4,136,128]{2,1,0:T(8,128)S(1)} collective-permute-done((f32[4,136,128]{2,1,0:T(8,128)S(1)}, f32[4,136,128]{2,1,0:T(8,128)S(1)}, u32[]{:S(2)}, u32[]{:S(2)}) %collective-permute-start.3) | collective-permute-done | bytes 278560 | tf_op jit(solution)/shard_map/ppermute | solution.py:97
  25.2 3.1 %collective-permute-start.4 = (f32[4,136,128]{2,1,0:T(8,128)S(1)}, f32[4,136,128]{2,1,0:T(8,128)S(1)}, u32[]{:S(2)}, u32[]{:S(2)}) collective-permute-start(f32[4,136,128]{2,1,0:T(8,128)S(1)} %add.46), channel_id=1, source_target_pairs={{0,4},{4,8},{8,12},{12,16},{16,20},{20,24},{24,28},{1,5},{5,9},{9,... | collective-permute-start | bytes 835592 | tf_op jit(solution)/shard_map/ppermute | solution.py:25
  28.3 1.3 slice_bitcast_fusion.4
  29.6 5.6 %collective-permute-done.4 = f32[4,136,128]{2,1,0:T(8,128)S(1)} collective-permute-done((f32[4,136,128]{2,1,0:T(8,128)S(1)}, f32[4,136,128]{2,1,0:T(8,128)S(1)}, u32[]{:S(2)}, u32[]{:S(2)}) %collective-permute-start.4) | collective-permute-done | bytes 278560 | tf_op jit(solution)/shard_map/ppermute | solution.py:25
  35.2 0.0 copy-start.1
  35.2 3.5 %collective-permute-start.5 = (f32[4,136,128]{2,1,0:T(8,128)S(1)}, f32[4,136,128]{2,1,0:T(8,128)S(1)}, u32[]{:S(2)}, u32[]{:S(2)}) collective-permute-start(f32[4,136,128]{2,1,0:T(8,128)S(1)} %add.47), channel_id=1, source_target_pairs={{0,8},{4,12},{8,16},{12,20},{16,24},{20,28},{1,9},{5,13},{9,17},{1... | collective-permute-start | bytes 835592 | tf_op jit(solution)/shard_map/ppermute | solution.py:25
  38.7 0.0 collective-permute-done
  38.7 1.3 slice_bitcast_fusion.3
  40.0 1.5 pad_maximum_fusion.2
  41.6 0.0 copy-start.3
  41.6 1.4 collective-permute-start.1
  43.0 0.0 copy-done.1
  43.0 1.5 slice_bitcast_fusion.2
  44.5 0.0 copy-start
  44.5 0.8 constant_dynamic-slice_fusion.1
  45.3 0.0 collective-permute-done.5
  45.3 2.6 %collective-permute-start.6 = (f32[4,136,128]{2,1,0:T(8,128)S(1)}, f32[4,136,128]{2,1,0:T(8,128)S(1)}, u32[]{:S(2)}, u32[]{:S(2)}) collective-permute-start(f32[4,136,128]{2,1,0:T(8,128)S(1)} %add.48), channel_id=1, source_target_pairs={{0,16},{4,20},{8,24},{12,28},{1,17},{5,21},{9,25},{13,29},{2,18},{... | collective-permute-start | bytes 835592 | tf_op jit(solution)/shard_map/ppermute | solution.py:25
  48.0 0.0 copy-done.3
  48.0 0.6 add_divide_fusion.gate_ref
  48.6 0.6 slice_bitcast_fusion.5
  49.2 9.5 %collective-permute-done.6 = f32[4,136,128]{2,1,0:T(8,128)S(1)} collective-permute-done((f32[4,136,128]{2,1,0:T(8,128)S(1)}, f32[4,136,128]{2,1,0:T(8,128)S(1)}, u32[]{:S(2)}, u32[]{:S(2)}) %collective-permute-start.6) | collective-permute-done | bytes 278560 | tf_op jit(solution)/shard_map/ppermute | solution.py:25
  58.7 0.8 add_subtract_fusion.s_ref
  59.5 1.7 slice_bitcast_fusion.1
  61.2 0.0 copy-done
  61.2 2.4 %pad_maximum_fusion.q_ref = bf16[2,512,2048]{2,1,0:T(8,128)(2,1)} fusion(bf16[1,512,2048]{2,1,0:T(8,128)(2,1)S(1)} %slice_bitcast_fusion.1, bf16[1,512,2048]{2,1,0:T(8,128)(2,1)S(1)} %copy-done), kind=kLoop, calls=%fused_computation | loop fusion | flops 2097152 | bytes 8388608 | tf_op jit(solution)/shard_map/stack | solution.py:271
  63.6 25.3 %collective-permute-done.1 = bf16[2,512,1024]{2,1,0:T(8,128)(2,1)} collective-permute-done((bf16[2,512,1024]{2,1,0:T(8,128)(2,1)}, bf16[2,512,1024]{2,1,0:T(8,128)(2,1)}, u32[]{:S(2)}, u32[]{:S(2)}) %collective-permute-start.1) | collective-permute-done | bytes 2097184 | tf_op jit(solution)/shard_map/ppermute | solution.py:274
  88.9 3.4 %pad_maximum_fusion.1.k_ref.v_ref = bf16[4,512,1024]{2,1,0:T(8,128)(2,1)} fusion(bf16[1,512,1024]{2,1,0:T(8,128)(2,1)S(1)} %slice_bitcast_fusion.3, bf16[1,512,1024]{2,1,0:T(8,128)(2,1)S(1)} %slice_bitcast_fusion.4, bf16[2,512,1024]{2,1,0:T(8,128)(2,1)} %collective-permute-done.1), kind=kLoop, calls=%fused_computation.1 | loop fusion | flops 4194304 | bytes 8388608 | tf_op jit(solution)/shard_map/concatenate | solution.py:277
  92.3 95.0 %shard_map.57.own_ref = bf16[2,512,2048]{2,1,0:T(8,128)(2,1)} custom-call(s32[7]{0:T(128)} %get-tuple-element.14.qp_ref, s32[7]{0:T(128)} %get-tuple-element.13.kp_ref, s32[7]{0:T(128)} %get-tuple-element.12.op_ref, s32[7]{0:T(128)} %get-tuple-element.11.first_ref, s32[7]{0:T(128)} %get-tuple-element.10.last_ref, s32[7]{0:T(128)} %get-tuple-element.9.valid_ref, ...), custom_call_target="tpu_custom_call" | custom-call | tf_op jit(solution)/shard_map/pallas_call | solution.py:220
  187.3 1.7 slice_bitcast_fusion
  189.0 3.1 %collective-permute-start.7 = (bf16[512,2048]{1,0:T(8,128)(2,1)S(1)}, bf16[512,2048]{1,0:T(8,128)(2,1)S(1)}, u32[]{:S(2)}, u32[]{:S(2)}) collective-permute-start(bf16[512,2048]{1,0:T(8,128)(2,1)S(1)} %slice_bitcast_fusion), channel_id=1, source_target_pairs={{0,1},{1,0},{2,3},{3,2},{4,5},{5,4},{6,7},{7,6},{8,9},{9,8},{10,11... | collective-permute-start | bytes 6291464 | tf_op jit(solution)/shard_map/ppermute | solution.py:281
  192.1 3.8 %collective-permute-done.7.back_ref = bf16[512,2048]{1,0:T(8,128)(2,1)S(1)} collective-permute-done((bf16[512,2048]{1,0:T(8,128)(2,1)S(1)}, bf16[512,2048]{1,0:T(8,128)(2,1)S(1)}, u32[]{:S(2)}, u32[]{:S(2)}) %collective-permute-start.7) | collective-permute-done | bytes 2097184 | tf_op jit(solution)/shard_map/ppermute | solution.py:281
  195.9 0.0 copy-start.2
  195.9 1.3 copy-done.2
  197.3 4.4 %shard_map.58 = bf16[512,4096]{1,0:T(8,128)(2,1)} custom-call(s32[1]{0:T(128)} %bitcast.core_ref, bf16[2,512,2048]{2,1,0:T(8,128)(2,1)} %shard_map.57.own_ref, bf16[512,2048]{1,0:T(8,128)(2,1)} %copy-done.2), custom_call_target="tpu_custom_call" | custom-call | tf_op jit(solution)/shard_map/pallas_call | solution.py:249
  (3 shorter events, 0.1 us)
Async XLA Ops:
  5.7 33.0 %collective-permute-start = (bf16[512,3072]{1,0:T(8,128)(2,1)}, bf16[512,3072]{1,0:T(8,128)(2,1)}, u32[]{:S(2)}, u32[]{:S(2)}) collective-permute-start(bf16[512,3072]{1,0:T(8,128)(2,1)} %get-tuple-element.8), channel_id=1, source_target_pairs={{0,1},{1,0},{2,3},{3,2},{4,5},{5,4},{6,7},{7,6},{8,9},{9,8},{10,11... | collective-permute-start | bytes 9437192 | tf_op jit(solution)/shard_map/ppermute | solution.py:270
  14.4 1.6 collective-permute-start.2
  17.0 8.2 %collective-permute-start.3 = (f32[4,136,128]{2,1,0:T(8,128)S(1)}, f32[4,136,128]{2,1,0:T(8,128)S(1)}, u32[]{:S(2)}, u32[]{:S(2)}) collective-permute-start(f32[4,136,128]{2,1,0:T(8,128)S(1)} %dynamic-slice_add_fusion), channel_id=1, source_target_pairs={{0,2},{1,3},{2,0},{3,1},{4,6},{5,7},{6,4},{7,5},{8,10},{9,11},{10,... | collective-permute-start | bytes 835592 | tf_op jit(solution)/shard_map/ppermute | solution.py:97
  25.2 10.0 %collective-permute-start.4 = (f32[4,136,128]{2,1,0:T(8,128)S(1)}, f32[4,136,128]{2,1,0:T(8,128)S(1)}, u32[]{:S(2)}, u32[]{:S(2)}) collective-permute-start(f32[4,136,128]{2,1,0:T(8,128)S(1)} %add.46), channel_id=1, source_target_pairs={{0,4},{4,8},{8,12},{12,16},{16,20},{20,24},{24,28},{1,5},{5,9},{9,... | collective-permute-start | bytes 835592 | tf_op jit(solution)/shard_map/ppermute | solution.py:25
  35.2 7.8 %copy-start.1 = (bf16[512,3072]{1,0:T(8,128)(2,1)S(1)}, bf16[512,3072]{1,0:T(8,128)(2,1)}, u32[]{:S(2)}) copy-start(bf16[512,3072]{1,0:T(8,128)(2,1)} %get-tuple-element.7) | copy-start | bytes 9437188
  35.2 10.1 %collective-permute-start.5 = (f32[4,136,128]{2,1,0:T(8,128)S(1)}, f32[4,136,128]{2,1,0:T(8,128)S(1)}, u32[]{:S(2)}, u32[]{:S(2)}) collective-permute-start(f32[4,136,128]{2,1,0:T(8,128)S(1)} %add.47), channel_id=1, source_target_pairs={{0,8},{4,12},{8,16},{12,20},{16,24},{20,28},{1,9},{5,13},{9,17},{1... | collective-permute-start | bytes 835592 | tf_op jit(solution)/shard_map/ppermute | solution.py:25
  41.6 6.4 %copy-start.3 = (f32[32]{0:T(128)S(1)}, f32[32]{0:T(128)}, u32[]{:S(2)}) copy-start(f32[32]{0:T(128)} %param.8) | copy-start | bytes 388
  41.6 47.3 %collective-permute-start.1 = (bf16[2,512,1024]{2,1,0:T(8,128)(2,1)}, bf16[2,512,1024]{2,1,0:T(8,128)(2,1)}, u32[]{:S(2)}, u32[]{:S(2)}) collective-permute-start(bf16[2,512,1024]{2,1,0:T(8,128)(2,1)} %pad_maximum_fusion.2), channel_id=1, source_target_pairs={{0,2},{1,3},{4,6},{5,7},{8,10},{9,11},{12,14},{13,15},{16,18},{17,... | collective-permute-start | bytes 6291464 | tf_op jit(solution)/shard_map/ppermute | solution.py:274
  44.5 16.7 %copy-start = (bf16[1,512,2048]{2,1,0:T(8,128)(2,1)S(1)}, bf16[1,512,2048]{2,1,0:T(8,128)(2,1)}, u32[]{:S(2)}) copy-start(bf16[1,512,2048]{2,1,0:T(8,128)(2,1)} %slice_bitcast_fusion.2) | copy-start | bytes 6291460
  45.3 13.4 %collective-permute-start.6 = (f32[4,136,128]{2,1,0:T(8,128)S(1)}, f32[4,136,128]{2,1,0:T(8,128)S(1)}, u32[]{:S(2)}, u32[]{:S(2)}) collective-permute-start(f32[4,136,128]{2,1,0:T(8,128)S(1)} %add.48), channel_id=1, source_target_pairs={{0,16},{4,20},{8,24},{12,28},{1,17},{5,21},{9,25},{13,29},{2,18},{... | collective-permute-start | bytes 835592 | tf_op jit(solution)/shard_map/ppermute | solution.py:25
  189.0 6.9 %collective-permute-start.7 = (bf16[512,2048]{1,0:T(8,128)(2,1)S(1)}, bf16[512,2048]{1,0:T(8,128)(2,1)S(1)}, u32[]{:S(2)}, u32[]{:S(2)}) collective-permute-start(bf16[512,2048]{1,0:T(8,128)(2,1)S(1)} %slice_bitcast_fusion), channel_id=1, source_target_pairs={{0,1},{1,0},{2,3},{3,2},{4,5},{5,4},{6,7},{7,6},{8,9},{9,8},{10,11... | collective-permute-start | bytes 6291464 | tf_op jit(solution)/shard_map/ppermute | solution.py:281
  195.9 1.3 copy-start.2

commit v6 on v5

--- a/solution.py
+++ b/solution.py
@@ -25,13 +25,15 @@
     return lax.ppermute(value, axis, [(source, source + steps) for source in range(count - steps)])
 
 
-def split_kernel(core_ref, q_keep, k_keep, v_keep, q_send, k_send, v_send, keep_ref, send_ref):
-    q_cols = q_keep.shape[-1]
+def split_kernel(core_ref, q_keep, k_keep, v_keep, q_send, k_send, v_send, *out_refs):
     k_cols = k_keep.shape[-1]
-    for q_ref, k_ref, v_ref, o_ref in ((q_keep, k_keep, v_keep, keep_ref), (q_send, k_send, v_send, send_ref)):
-        o_ref[:, :q_cols] = q_ref[...]
-        o_ref[:, q_cols : q_cols + k_cols] = k_ref[...]
-        o_ref[:, q_cols + k_cols :] = v_ref[...]
+    keep_q, keep_kv, send_q, send_kv = out_refs
+    keep_q[...] = q_keep[...]
+    keep_kv[:, :k_cols] = k_keep[...]
+    keep_kv[:, k_cols:] = v_keep[...]
+    send_q[...] = q_send[...]
+    send_kv[:, :k_cols] = k_send[...]
+    send_kv[:, k_cols:] = v_send[...]
 
 
 def split_inputs(queries, keys, values, core):
@@ -40,7 +42,8 @@
     k_cols = keys.shape[1] // 2
     keep_map = lambda i, c: (0, c[0])
     send_map = lambda i, c: (0, 1 - c[0])
-    shape = jax.ShapeDtypeStruct((tokens_here, q_cols + 2 * k_cols), queries.dtype)
+    q_shape = jax.ShapeDtypeStruct((tokens_here, q_cols), queries.dtype)
+    kv_shape = jax.ShapeDtypeStruct((tokens_here, 2 * k_cols), keys.dtype)
     grid_spec = pltpu.PrefetchScalarGridSpec(
         num_scalar_prefetch=1,
         grid=(1,),
@@ -52,10 +55,14 @@
             pl.BlockSpec((tokens_here, k_cols), send_map),
             pl.BlockSpec((tokens_here, k_cols), send_map),
         ],
-        out_specs=[pl.BlockSpec((tokens_here, q_cols + 2 * k_cols), lambda i, c: (0, 0))] * 2,
-    )
-    return pl.pallas_call(
-        split_kernel, grid_spec=grid_spec, out_shape=[shape, shape]
+        out_specs=[
+            pl.BlockSpec((tokens_here, q_cols), lambda i, c: (0, 0)),
+            pl.BlockSpec((tokens_here, 2 * k_cols), lambda i, c: (0, 0)),
+        ]
+        * 2,
+    )
+    return pl.pallas_call(
+        split_kernel, grid_spec=grid_spec, out_shape=[q_shape, kv_shape] * 2
     )(core.reshape(1), queries, keys, values, queries, keys, values)
 
 
@@ -259,22 +266,23 @@
     place = lax.axis_index("head")
     chip = place // 2
     core = place % 2
-    q_cols = queries.shape[1] // 2
     k_cols = keys.shape[1] // 2
     kv_group = k_cols // HD
     group_size = queries.shape[1] // keys.shape[1]
     sibling = [(p, p ^ 1) for p in range(parts)]
 
     state = before_states(keys, values, core, kv_group)
-    keep, send = split_inputs(queries, keys, values, core)
-    recv = lax.ppermute(send, "head", sibling)
-    query_rows = jnp.stack([keep[:, :q_cols], recv[:, :q_cols]])
-    kv_chip = jnp.stack([keep[:, q_cols:], recv[:, q_cols:]])
-    kv_parts = [
-        lax.ppermute(kv_chip, "head", [(p, p + 2 * s) for p in range(parts - 2 * s)])
-        for s in range(chips - 1, 0, -1)
-    ]
-    kv_rows = jnp.concatenate(kv_parts + [kv_chip], axis=0)
+    keep_q, keep_kv, send_q, send_kv = split_inputs(queries, keys, values, core)
+    kv_parts = []
+    for s in range(chips - 1, 0, -1):
+        kv_parts.append(lax.ppermute(keep_kv, "head", [(p, p + 2 * s) for p in range(parts - 2 * s)]))
+        kv_parts.append(
+            lax.ppermute(send_kv, "head", [(p, (p + 2 * s) ^ 1) for p in range(parts - 2 * s)])
+        )
+    recv_q = lax.ppermute(send_q, "head", sibling)
+    recv_kv = lax.ppermute(send_kv, "head", sibling)
+    query_rows = jnp.stack([keep_q, recv_q])
+    kv_rows = jnp.stack(kv_parts + [keep_kv, recv_kv])
     gate_here = lax.dynamic_slice_in_dim(gate_logit, core * kv_group * group_size, kv_group * group_size)
     mixing = jax.nn.sigmoid(gate_here)
     attended = attend(query_rows, kv_rows, state, mixing, pair_tables(chips, chip, core), group_size)

time: 202 us -> 217 us (1.074)
  waiting for transfers between devices: 53.7 us -> 69.3 us
  local copies, waits for them, and re-layouts: 11.3 us -> 5.34 us
  starting transfers between devices: 14.7 us -> 19.3 us
    ppermute x1, waiting for transfers between devices: 7.9 us -> 47.3 us  [before_states(): lax.ppermute(total, 'head', [(p, p ^ steps) for p in range(parts)])]
    ppermute x2 -> x4, waiting for transfers between devices: 25.3 us -> 0.01 us  [the longest x1 0.01 us: body(): lax.ppermute(keep_kv, 'head', [(p, p + 2 * s) for p in range(parts - 2 *...]
    another operation x4 -> x0, local copies, waits for them, and re-layouts: 5.77 us -> none  [the longest x2 3.18 us: body(): query_rows = jnp.stack([keep[:, :q_cols], recv[:, :q_cols]])]
    ppermute x1, starting transfers between devices: 0.28 us -> 4.17 us  [before_states(): lax.ppermute(total, 'head', [(p, p ^ steps) for p in range(parts)])]
    concatenate x1 -> x0, other arithmetic: 3.43 us -> none  [body(): kv_rows = jnp.concatenate(kv_parts + [kv_chip], axis=0)]
    ppermute x3, waiting for transfers between devices: 15.1 us -> 18.2 us  [shifted(): lax.ppermute(value, axis, [(source, source + steps) for source in range(c...]
    ppermute x1, starting transfers between devices: 3.13 us -> 0.72 us  [body(): back = lax.ppermute(attended[1], 'head', sibling)]
    another operation x2, other arithmetic: 3.92 us -> 6.1 us  [the longest x1 3.73 us: body(): kv_rows = jnp.stack(kv_parts + [keep_kv, recv_kv])]
  transfers between devices with their start and end apart: 8 -> 10, of which waited for: 6 -> 5; matrix products, arithmetic and copies ran while one was open for 7% -> 4% of each run, Pallas kernels for 3% -> 3%
where the time goes in v6:
time: 217 us; the launch traced here: 216 us
  Pallas kernels  112 us (52%)
  waiting for transfers between devices  69.3 us (32%)
  starting transfers between devices  19.3 us (9%)
  other arithmetic  9.59 us (4%)
  local copies, waits for them, and re-layouts  5.34 us (2%)
    pallas_call x1, Pallas kernels, attend(): pl.pallas_call(functools.partial(flash_kernel, group_size=group_size), gr...  94.9 us
    ppermute x1, waiting for transfers between devices, before_states(): lax.ppermute(total, 'head', [(p, p ^ steps) for p in range(parts)])  47.3 us
    ppermute x3, waiting for transfers between devices, shifted(): lax.ppermute(value, axis, [(source, source + steps) for source in range(c...  18.2 us
    ppermute x3, starting transfers between devices, shifted(): lax.ppermute(value, axis, [(source, source + steps) for source in range(c...  10.6 us
    pallas_call x1, Pallas kernels, local_deltas(): pl.pallas_call(delta_kernel, grid=(kv_heads, 1), in_specs=[pl.BlockSpec((...  7.03 us
    pallas_call x1, Pallas kernels, split_inputs(): pl.pallas_call(split_kernel, grid_spec=grid_spec, out_shape=[q_shape, kv_...  5.57 us
    pallas_call x1, Pallas kernels, merge_halves(): pl.pallas_call(merge_kernel, grid_spec=grid_spec, out_shape=jax.ShapeDtyp...  4.37 us
  transfers between devices with their start and end apart: 10, of which 5 were waited for; matrix products, arithmetic and copies ran while one was open for 4% of the time, Pallas kernels for 3%

profile of v6, /device:TPU:13, one launch (start us, length us, event | category | flops | bytes accessed | tf_op | source)
XLA Modules:
  0.0 215.6 jit_solution(14544166734863247727)
XLA Ops:
  0.0 5.6 %shard_map.55 = (bf16[512,2048]{1,0:T(8,128)(2,1)}, bf16[512,1024]{1,0:T(8,128)(2,1)}, bf16[512,2048]{1,0:T(8,128)(2,1)}, bf16[512,1024]{1,0:T(8,128)(2,1)}) custom-call(s32[1]{0:T(128)} %bitcast.core_ref, bf16[512,4096]{1,0:T(8,128)(2,1)} %q_send.1, bf16[512,1024]{1,0:T(8,128)(2,1)} %k_ref.1, bf16[512,1024]{1,0:T(8,128)(2,1)} %v_ref.1, ...), custom_call_target="tpu_custom_call" | custom-call | tf_op jit(solution)/shard_map/pallas_call | solution.py:64
  5.6 0.0 copy-start.3
  5.6 0.0 copy-start.2
  5.6 0.7 collective-permute-start
  6.3 7.0 %shard_map.56 = f32[8,136,128]{2,1,0:T(8,128)} custom-call(bf16[512,1024]{1,0:T(8,128)(2,1)} %k_ref.1, bf16[512,1024]{1,0:T(8,128)(2,1)} %v_ref.1), custom_call_target="tpu_custom_call" | custom-call | tf_op jit(solution)/shard_map/pallas_call | solution.py:86
  13.3 1.0 constant_dynamic-slice_fusion
  14.3 0.2 collective-permute-start.4
  14.4 0.4 collective-permute-start.3
  14.8 1.3 collective-permute-start.2
  16.1 1.3 collective-permute-start.1
  17.4 0.0 collective-permute-done.4
  17.4 1.1 dynamic-slice_add_fusion
  18.5 4.2 %collective-permute-start.5 = (f32[4,136,128]{2,1,0:T(8,128)S(1)}, f32[4,136,128]{2,1,0:T(8,128)S(1)}, u32[]{:S(2)}, u32[]{:S(2)}) collective-permute-start(f32[4,136,128]{2,1,0:T(8,128)S(1)} %dynamic-slice_add_fusion), channel_id=1, source_target_pairs={{0,2},{1,3},{2,0},{3,1},{4,6},{5,7},{6,4},{7,5},{8,10},{9,11},{10,... | collective-permute-start | bytes 835592 | tf_op jit(solution)/shard_map/ppermute | solution.py:104
  22.7 47.3 %collective-permute-done.5 = f32[4,136,128]{2,1,0:T(8,128)S(1)} collective-permute-done((f32[4,136,128]{2,1,0:T(8,128)S(1)}, f32[4,136,128]{2,1,0:T(8,128)S(1)}, u32[]{:S(2)}, u32[]{:S(2)}) %collective-permute-start.5) | collective-permute-done | bytes 278560 | tf_op jit(solution)/shard_map/ppermute | solution.py:104
  70.0 3.1 %collective-permute-start.6 = (f32[4,136,128]{2,1,0:T(8,128)S(1)}, f32[4,136,128]{2,1,0:T(8,128)}, u32[]{:S(2)}, u32[]{:S(2)}) collective-permute-start(f32[4,136,128]{2,1,0:T(8,128)S(1)} %add.46), channel_id=1, source_target_pairs={{0,4},{4,8},{8,12},{12,16},{16,20},{20,24},{24,28},{1,5},{5,9},{9,... | collective-permute-start | bytes 835592 | tf_op jit(solution)/shard_map/ppermute | solution.py:25
  73.2 0.7 constant_dynamic-slice_fusion.1
  73.9 6.2 %collective-permute-done.6 = f32[4,136,128]{2,1,0:T(8,128)} collective-permute-done((f32[4,136,128]{2,1,0:T(8,128)S(1)}, f32[4,136,128]{2,1,0:T(8,128)}, u32[]{:S(2)}, u32[]{:S(2)}) %collective-permute-start.6) | collective-permute-done | bytes 278560 | tf_op jit(solution)/shard_map/ppermute | solution.py:25
  80.1 1.0 add.47
  81.1 3.2 %collective-permute-start.7 = (f32[4,136,128]{2,1,0:T(8,128)S(1)}, f32[4,136,128]{2,1,0:T(8,128)S(1)}, u32[]{:S(2)}, u32[]{:S(2)}) collective-permute-start(f32[4,136,128]{2,1,0:T(8,128)S(1)} %add.47), channel_id=1, source_target_pairs={{0,8},{4,12},{8,16},{12,20},{16,24},{20,28},{1,9},{5,13},{9,17},{1... | collective-permute-start | bytes 835592 | tf_op jit(solution)/shard_map/ppermute | solution.py:25
  84.3 0.0 copy-done.3
  84.3 0.6 add_divide_fusion.gate_ref
  85.0 0.6 slice_bitcast_fusion.1
  85.6 3.7 %collective-permute-done.7 = f32[4,136,128]{2,1,0:T(8,128)S(1)} collective-permute-done((f32[4,136,128]{2,1,0:T(8,128)S(1)}, f32[4,136,128]{2,1,0:T(8,128)S(1)}, u32[]{:S(2)}, u32[]{:S(2)}) %collective-permute-start.7) | collective-permute-done | bytes 278560 | tf_op jit(solution)/shard_map/ppermute | solution.py:25
  89.3 4.2 %collective-permute-start.8 = (f32[4,136,128]{2,1,0:T(8,128)S(1)}, f32[4,136,128]{2,1,0:T(8,128)S(1)}, u32[]{:S(2)}, u32[]{:S(2)}) collective-permute-start(f32[4,136,128]{2,1,0:T(8,128)S(1)} %add.48), channel_id=1, source_target_pairs={{0,16},{4,20},{8,24},{12,28},{1,17},{5,21},{9,25},{13,29},{2,18},{... | collective-permute-start | bytes 835592 | tf_op jit(solution)/shard_map/ppermute | solution.py:25
  93.6 0.0 collective-permute-done.1
  93.6 0.0 collective-permute-done.3
  93.6 0.0 collective-permute-done.2
  93.6 0.0 copy-done.2
  93.6 0.0 copy-start
  93.6 3.7 %pad_maximum_fusion.1.k_ref.v_ref = bf16[4,512,1024]{2,1,0:T(8,128)(2,1)} fusion(bf16[1,512,1024]{2,1,0:T(8,128)(2,1)} %bitcast.12, bf16[1,512,1024]{2,1,0:T(8,128)(2,1)S(1)} %bitcast.23, bf16[1,512,1024]{2,1,0:T(8,128)(2,1)} %bitcast.10, bf16[1,512,1024]{2,1,0:T(8,128)(2,1)} %bitcast.9), kind=kLoop, calls=%fused_computation.1 | loop fusion | flops 6291456 | bytes 8388608 | tf_op jit(solution)/shard_map/stack | solution.py:285
  97.4 8.3 %collective-permute-done.8 = f32[4,136,128]{2,1,0:T(8,128)S(1)} collective-permute-done((f32[4,136,128]{2,1,0:T(8,128)S(1)}, f32[4,136,128]{2,1,0:T(8,128)S(1)}, u32[]{:S(2)}, u32[]{:S(2)}) %collective-permute-start.8) | collective-permute-done | bytes 278560 | tf_op jit(solution)/shard_map/ppermute | solution.py:25
  105.6 0.8 add_subtract_fusion.s_ref
  106.4 0.0 collective-permute-done
  106.4 0.0 copy-done
  106.4 2.4 %pad_maximum_fusion.q_ref = bf16[2,512,2048]{2,1,0:T(8,128)(2,1)} fusion(bf16[1,512,2048]{2,1,0:T(8,128)(2,1)S(1)} %bitcast.22, bf16[1,512,2048]{2,1,0:T(8,128)(2,1)S(1)} %bitcast.21), kind=kLoop, calls=%fused_computation | loop fusion | flops 2097152 | bytes 8388608 | tf_op jit(solution)/shard_map/stack | solution.py:284
  108.8 94.9 %shard_map.57.own_ref = bf16[2,512,2048]{2,1,0:T(8,128)(2,1)} custom-call(s32[7]{0:T(128)} %get-tuple-element.18.qp_ref, s32[7]{0:T(128)} %get-tuple-element.17.kp_ref, s32[7]{0:T(128)} %get-tuple-element.16.op_ref, s32[7]{0:T(128)} %get-tuple-element.15.first_ref, s32[7]{0:T(128)} %get-tuple-element.14.last_ref, s32[7]{0:T(128)} %get-tuple-element.13.valid_ref, ...), custom_call_target="tpu_custom_call" | custom-call | tf_op jit(solution)/shard_map/pallas_call | solution.py:227
  203.7 1.7 slice_bitcast_fusion
  205.4 0.7 collective-permute-start.9
  206.2 3.8 %collective-permute-done.9.back_ref = bf16[512,2048]{1,0:T(8,128)(2,1)S(1)} collective-permute-done((bf16[512,2048]{1,0:T(8,128)(2,1)S(1)}, bf16[512,2048]{1,0:T(8,128)(2,1)S(1)}, u32[]{:S(2)}, u32[]{:S(2)}) %collective-permute-start.9) | collective-permute-done | bytes 2097184 | tf_op jit(solution)/shard_map/ppermute | solution.py:289
  209.9 0.0 copy-start.1
  209.9 1.3 copy-done.1
  211.3 4.4 %shard_map.58 = bf16[512,4096]{1,0:T(8,128)(2,1)} custom-call(s32[1]{0:T(128)} %bitcast.core_ref, bf16[2,512,2048]{2,1,0:T(8,128)(2,1)} %shard_map.57.own_ref, bf16[512,2048]{1,0:T(8,128)(2,1)} %copy-done.1), custom_call_target="tpu_custom_call" | custom-call | tf_op jit(solution)/shard_map/pallas_call | solution.py:256
  (2 shorter events, 0.1 us)
Async XLA Ops:
  5.6 78.8 %copy-start.3 = (f32[32]{0:T(128)S(1)}, f32[32]{0:T(128)}, u32[]{:S(2)}) copy-start(f32[32]{0:T(128)} %param.8) | copy-start | bytes 388
  5.6 88.0 %copy-start.2 = (bf16[512,1024]{1,0:T(8,128)(2,1)S(1)}, bf16[512,1024]{1,0:T(8,128)(2,1)}, u32[]{:S(2)}) copy-start(bf16[512,1024]{1,0:T(8,128)(2,1)} %get-tuple-element.11) | copy-start | bytes 3145732
  5.6 100.8 %collective-permute-start = (bf16[512,2048]{1,0:T(8,128)(2,1)}, bf16[512,2048]{1,0:T(8,128)(2,1)S(1)}, u32[]{:S(2)}, u32[]{:S(2)}) collective-permute-start(bf16[512,2048]{1,0:T(8,128)(2,1)} %get-tuple-element.10), channel_id=1, source_target_pairs={{0,1},{1,0},{2,3},{3,2},{4,5},{5,4},{6,7},{7,6},{8,9},{9,8},{10,11... | collective-permute-start | bytes 6291464 | tf_op jit(solution)/shard_map/ppermute | solution.py:282
  14.3 3.2 %collective-permute-start.4 = (f32[4,136,128]{2,1,0:T(8,128)S(1)}, f32[4,136,128]{2,1,0:T(8,128)}, u32[]{:S(2)}, u32[]{:S(2)}) collective-permute-start(f32[4,136,128]{2,1,0:T(8,128)S(1)} %constant_dynamic-slice_fusion), channel_id=1, source_target_pairs={{0,1},{1,0},{2,3},{3,2},{4,5},{5,4},{6,7},{7,6},{8,9},{9,8},{10,11... | collective-permute-start | bytes 835592 | tf_op jit(solution)/shard_map/ppermute | solution.py:101
  14.4 79.2 %collective-permute-start.3 = (bf16[512,1024]{1,0:T(8,128)(2,1)}, bf16[512,1024]{1,0:T(8,128)(2,1)}, u32[]{:S(2)}, u32[]{:S(2)}) collective-permute-start(bf16[512,1024]{1,0:T(8,128)(2,1)} %get-tuple-element.12), channel_id=1, source_target_pairs={{0,1},{1,0},{2,3},{3,2},{4,5},{5,4},{6,7},{7,6},{8,9},{9,8},{10,11... | collective-permute-start | bytes 3145736 | tf_op jit(solution)/shard_map/ppermute | solution.py:283
  14.8 78.8 %collective-permute-start.2 = (bf16[512,1024]{1,0:T(8,128)(2,1)}, bf16[512,1024]{1,0:T(8,128)(2,1)}, u32[]{:S(2)}, u32[]{:S(2)}) collective-permute-start(bf16[512,1024]{1,0:T(8,128)(2,1)} %get-tuple-element.12), channel_id=1, source_target_pairs={{0,3},{1,2},{4,7},{5,6},{8,11},{9,10},{12,15},{13,14},{16,19},{17,... | collective-permute-start | bytes 3145736 | tf_op jit(solution)/shard_map/ppermute | solution.py:280
  16.1 77.5 %collective-permute-start.1 = (bf16[512,1024]{1,0:T(8,128)(2,1)}, bf16[512,1024]{1,0:T(8,128)(2,1)}, u32[]{:S(2)}, u32[]{:S(2)}) collective-permute-start(bf16[512,1024]{1,0:T(8,128)(2,1)} %get-tuple-element.11), channel_id=1, source_target_pairs={{0,2},{1,3},{4,6},{5,7},{8,10},{9,11},{12,14},{13,15},{16,18},{17,... | collective-permute-start | bytes 3145736 | tf_op jit(solution)/shard_map/ppermute | solution.py:278
  18.5 51.5 %collective-permute-start.5 = (f32[4,136,128]{2,1,0:T(8,128)S(1)}, f32[4,136,128]{2,1,0:T(8,128)S(1)}, u32[]{:S(2)}, u32[]{:S(2)}) collective-permute-start(f32[4,136,128]{2,1,0:T(8,128)S(1)} %dynamic-slice_add_fusion), channel_id=1, source_target_pairs={{0,2},{1,3},{2,0},{3,1},{4,6},{5,7},{6,4},{7,5},{8,10},{9,11},{10,... | collective-permute-start | bytes 835592 | tf_op jit(solution)/shard_map/ppermute | solution.py:104
  70.0 10.1 %collective-permute-start.6 = (f32[4,136,128]{2,1,0:T(8,128)S(1)}, f32[4,136,128]{2,1,0:T(8,128)}, u32[]{:S(2)}, u32[]{:S(2)}) collective-permute-start(f32[4,136,128]{2,1,0:T(8,128)S(1)} %add.46), channel_id=1, source_target_pairs={{0,4},{4,8},{8,12},{12,16},{16,20},{20,24},{24,28},{1,5},{5,9},{9,... | collective-permute-start | bytes 835592 | tf_op jit(solution)/shard_map/ppermute | solution.py:25
  81.1 8.2 %collective-permute-start.7 = (f32[4,136,128]{2,1,0:T(8,128)S(1)}, f32[4,136,128]{2,1,0:T(8,128)S(1)}, u32[]{:S(2)}, u32[]{:S(2)}) collective-permute-start(f32[4,136,128]{2,1,0:T(8,128)S(1)} %add.47), channel_id=1, source_target_pairs={{0,8},{4,12},{8,16},{12,20},{16,24},{20,28},{1,9},{5,13},{9,17},{1... | collective-permute-start | bytes 835592 | tf_op jit(solution)/shard_map/ppermute | solution.py:25
  89.3 16.3 %collective-permute-start.8 = (f32[4,136,128]{2,1,0:T(8,128)S(1)}, f32[4,136,128]{2,1,0:T(8,128)S(1)}, u32[]{:S(2)}, u32[]{:S(2)}) collective-permute-start(f32[4,136,128]{2,1,0:T(8,128)S(1)} %add.48), channel_id=1, source_target_pairs={{0,16},{4,20},{8,24},{12,28},{1,17},{5,21},{9,25},{13,29},{2,18},{... | collective-permute-start | bytes 835592 | tf_op jit(solution)/shard_map/ppermute | solution.py:25
  93.6 12.8 %copy-start = (bf16[512,2048]{1,0:T(8,128)(2,1)S(1)}, bf16[512,2048]{1,0:T(8,128)(2,1)}, u32[]{:S(2)}) copy-start(bf16[512,2048]{1,0:T(8,128)(2,1)} %get-tuple-element.9) | copy-start | bytes 6291460
  205.4 4.5 %collective-permute-start.9 = (bf16[512,2048]{1,0:T(8,128)(2,1)S(1)}, bf16[512,2048]{1,0:T(8,128)(2,1)S(1)}, u32[]{:S(2)}, u32[]{:S(2)}) collective-permute-start(bf16[512,2048]{1,0:T(8,128)(2,1)S(1)} %slice_bitcast_fusion), channel_id=1, source_target_pairs={{0,1},{1,0},{2,3},{3,2},{4,5},{5,4},{6,7},{7,6},{8,9},{9,8},{10,11... | collective-permute-start | bytes 6291464 | tf_op jit(solution)/shard_map/ppermute | solution.py:289
  209.9 1.3 copy-start.1

commit v7 on v6

--- a/solution.py
+++ b/solution.py
@@ -113,10 +113,9 @@
 
 
 def flash_kernel(
-    qp_ref, kp_ref, op_ref, first_ref, last_ref, valid_ref, gate_ref, q_ref, k_ref, v_ref, s_ref,
+    qp_ref, kp_ref, op_ref, first_ref, last_ref, valid_ref, q_ref, k_ref, v_ref,
     o_ref, m_sc, l_sc, acc_sc, *, group_size
 ):
-    kv_head = pl.program_id(0)
     step_at = pl.program_id(1)
     first = first_ref[step_at] == 1
     last = last_ref[step_at] == 1
@@ -165,23 +164,48 @@
     @pl.when(valid & last)
     def _last():
         step(True)
-        memory = s_ref[:HD, :]
-        normalizer = s_ref[HD : HD + 1, :]
         for head in range(group_size):
             lanes = slice(head * HD, (head + 1) * HD)
-            local_part = acc_sc[:, lanes] / l_sc[head]
-            query_feature = feature(q_ref[:, lanes].astype(jnp.float32))
-            numerator = jnp.dot(
-                query_feature, memory, precision=lax.Precision.HIGHEST,
-                preferred_element_type=jnp.float32,
-            )
-            denominator = jnp.maximum(
-                jnp.sum(query_feature * normalizer, axis=-1, keepdims=True), 1.0
-            )
-            mixing = gate_ref[kv_head * group_size + head]
-            o_ref[:, lanes] = (
-                mixing * (numerator / denominator) + (1.0 - mixing) * local_part
-            ).astype(o_ref.dtype)
+            o_ref[:, lanes] = acc_sc[:, lanes] / l_sc[head]
+
+
+def mix_kernel(gate_ref, q_ref, local_ref, s_ref, o_ref, *, group_size):
+    kv_head = pl.program_id(1)
+    memory = s_ref[:HD, :]
+    normalizer = s_ref[HD : HD + 1, :]
+    for head in range(group_size):
+        lanes = slice(head * HD, (head + 1) * HD)
+        query_feature = feature(q_ref[:, lanes].astype(jnp.float32))
+        numerator = jnp.dot(
+            query_feature, memory, precision=lax.Precision.HIGHEST,
+            preferred_element_type=jnp.float32,
+        )
+        denominator = jnp.maximum(
+            jnp.sum(query_feature * normalizer, axis=-1, keepdims=True), 1.0
+        )
+        mixing = gate_ref[kv_head * group_size + head]
+        o_ref[:, lanes] = (
+            mixing * (numerator / denominator) + (1.0 - mixing) * local_ref[:, lanes]
+        ).astype(o_ref.dtype)
+
+
+def mix(query_rows, local_part, state, mixing, group_size):
+    positions, block, q_cols = query_rows.shape
+    width = group_size * HD
+    kv_group = q_cols // width
+    row_map = lambda a, g: (a, 0, g)
+    return pl.pallas_call(
+        functools.partial(mix_kernel, group_size=group_size),
+        grid=(positions, kv_group),
+        in_specs=[
+            pl.BlockSpec(memory_space=pltpu.SMEM),
+            pl.BlockSpec((None, block, width), row_map),
+            pl.BlockSpec((None, block, width), row_map),
+            pl.BlockSpec((None, STATE_ROWS, HD), lambda a, g: (g, 0, 0)),
+        ],
+        out_specs=pl.BlockSpec((None, block, width), row_map),
+        out_shape=jax.ShapeDtypeStruct(query_rows.shape, jnp.bfloat16),
+    )(mixing, query_rows, local_part, state)
 
 
 def pair_tables(chips, chip, core):
@@ -200,7 +224,7 @@
     return jnp.asarray(tables)[chip, core]
 
 
-def attend(query_rows, kv_rows, state, mixing, tables, group_size):
+def attend(query_rows, kv_rows, tables, group_size):
     _, block, q_cols = query_rows.shape
     kv_group = kv_rows.shape[-1] // (2 * HD)
     width = group_size * HD
@@ -209,13 +233,11 @@
         num_scalar_prefetch=6,
         grid=(kv_group, steps),
         in_specs=[
-            pl.BlockSpec(memory_space=pltpu.SMEM),
             pl.BlockSpec((None, block, width), lambda g, t, qp, kp, op, f, l, v: (qp[t], 0, g)),
             pl.BlockSpec((None, block, HD), lambda g, t, qp, kp, op, f, l, v: (kp[t], 0, g)),
             pl.BlockSpec(
                 (None, block, HD), lambda g, t, qp, kp, op, f, l, v: (kp[t], 0, kv_group + g)
             ),
-            pl.BlockSpec((None, STATE_ROWS, HD), lambda g, t, qp, kp, op, f, l, v: (g, 0, 0)),
         ],
         out_specs=pl.BlockSpec((None, block, width), lambda g, t, qp, kp, op, f, l, v: (op[t], 0, g)),
         scratch_shapes=[
@@ -227,9 +249,9 @@
     return pl.pallas_call(
         functools.partial(flash_kernel, group_size=group_size),
         grid_spec=grid_spec,
-        out_shape=jax.ShapeDtypeStruct((2, block, q_cols), jnp.bfloat16),
+        out_shape=jax.ShapeDtypeStruct((2, block, q_cols), jnp.float32),
         compiler_params=pltpu.CompilerParams(dimension_semantics=("arbitrary", "arbitrary")),
-    )(*[tables[i] for i in range(6)], mixing, query_rows, kv_rows, kv_rows, state)
+    )(*[tables[i] for i in range(6)], query_rows, kv_rows, kv_rows)
 
 
 def merge_kernel(core_ref, own_ref, back_ref, o_ref):
@@ -285,7 +307,8 @@
     kv_rows = jnp.stack(kv_parts + [keep_kv, recv_kv])
     gate_here = lax.dynamic_slice_in_dim(gate_logit, core * kv_group * group_size, kv_group * group_size)
     mixing = jax.nn.sigmoid(gate_here)
-    attended = attend(query_rows, kv_rows, state, mixing, pair_tables(chips, chip, core), group_size)
+    local_part = attend(query_rows, kv_rows, pair_tables(chips, chip, core), group_size)
+    attended = mix(query_rows, local_part, state, mixing, group_size)
     back = lax.ppermute(attended[1], "head", sibling)
     return merge_halves(attended, back, core)
 

time: 217 us -> 221 us (1.018)
  Pallas kernels: 112 us -> 116 us
    pallas_call x0 -> x1, Pallas kernels: none -> 13.4 us  [mix(): pl.pallas_call(functools.partial(mix_kernel, group_size=group_size), grid...]
    pallas_call x1, Pallas kernels: 94.9 us -> 85.4 us  [attend(): pl.pallas_call(functools.partial(flash_kernel, group_size=group_size), gr...]
where the time goes in v7:
time: 221 us; the launch traced here: 220 us
  Pallas kernels  116 us (52%)
  waiting for transfers between devices  69.4 us (31%)
  starting transfers between devices  19.3 us (9%)
  other arithmetic  9.63 us (4%)
  local copies, waits for them, and re-layouts  5.35 us (2%)
    pallas_call x1, Pallas kernels, attend(): pl.pallas_call(functools.partial(flash_kernel, group_size=group_size), gr...  85.4 us
    ppermute x1, waiting for transfers between devices, before_states(): lax.ppermute(total, 'head', [(p, p ^ steps) for p in range(parts)])  47.4 us
    ppermute x3, waiting for transfers between devices, shifted(): lax.ppermute(value, axis, [(source, source + steps) for source in range(c...  18.2 us
    pallas_call x1, Pallas kernels, mix(): pl.pallas_call(functools.partial(mix_kernel, group_size=group_size), grid...  13.4 us
    ppermute x3, starting transfers between devices, shifted(): lax.ppermute(value, axis, [(source, source + steps) for source in range(c...  10.5 us
    pallas_call x1, Pallas kernels, local_deltas(): pl.pallas_call(delta_kernel, grid=(kv_heads, 1), in_specs=[pl.BlockSpec((...  7.01 us
    pallas_call x1, Pallas kernels, split_inputs(): pl.pallas_call(split_kernel, grid_spec=grid_spec, out_shape=[q_shape, kv_...  5.58 us
  transfers between devices with their start and end apart: 10, of which 5 were waited for; matrix products, arithmetic and copies ran while one was open for 4% of the time, Pallas kernels for 3%

profile of v7, /device:TPU:13, one launch (start us, length us, event | category | flops | bytes accessed | tf_op | source)
XLA Modules:
  0.0 219.6 jit_solution(13529602972525192292)
XLA Ops:
  0.0 5.6 %shard_map.55 = (bf16[512,2048]{1,0:T(8,128)(2,1)}, bf16[512,1024]{1,0:T(8,128)(2,1)}, bf16[512,2048]{1,0:T(8,128)(2,1)}, bf16[512,1024]{1,0:T(8,128)(2,1)}) custom-call(s32[1]{0:T(128)} %bitcast.core_ref, bf16[512,4096]{1,0:T(8,128)(2,1)} %q_send.1, bf16[512,1024]{1,0:T(8,128)(2,1)} %k_ref.1, bf16[512,1024]{1,0:T(8,128)(2,1)} %v_ref.1, ...), custom_call_target="tpu_custom_call" | custom-call | tf_op jit(solution)/shard_map/pallas_call | solution.py:64
  5.6 0.0 copy-start.3
  5.6 0.0 copy-start.2
  5.6 0.7 collective-permute-start
  6.3 7.0 %shard_map.57 = f32[8,136,128]{2,1,0:T(8,128)} custom-call(bf16[512,1024]{1,0:T(8,128)(2,1)} %k_ref.1, bf16[512,1024]{1,0:T(8,128)(2,1)} %v_ref.1), custom_call_target="tpu_custom_call" | custom-call | tf_op jit(solution)/shard_map/pallas_call | solution.py:86
  13.3 1.0 constant_dynamic-slice_fusion
  14.2 0.2 collective-permute-start.4
  14.4 0.4 collective-permute-start.3
  14.8 1.3 collective-permute-start.2
  16.1 1.3 collective-permute-start.1
  17.4 0.0 collective-permute-done.4
  17.4 1.1 dynamic-slice_add_fusion
  18.5 4.1 %collective-permute-start.5 = (f32[4,136,128]{2,1,0:T(8,128)S(1)}, f32[4,136,128]{2,1,0:T(8,128)S(1)}, u32[]{:S(2)}, u32[]{:S(2)}) collective-permute-start(f32[4,136,128]{2,1,0:T(8,128)S(1)} %dynamic-slice_add_fusion), channel_id=1, source_target_pairs={{0,2},{1,3},{2,0},{3,1},{4,6},{5,7},{6,4},{7,5},{8,10},{9,11},{10,... | collective-permute-start | bytes 835592 | tf_op jit(solution)/shard_map/ppermute | solution.py:104
  22.6 47.4 %collective-permute-done.5 = f32[4,136,128]{2,1,0:T(8,128)S(1)} collective-permute-done((f32[4,136,128]{2,1,0:T(8,128)S(1)}, f32[4,136,128]{2,1,0:T(8,128)S(1)}, u32[]{:S(2)}, u32[]{:S(2)}) %collective-permute-start.5) | collective-permute-done | bytes 278560 | tf_op jit(solution)/shard_map/ppermute | solution.py:104
  70.0 3.1 %collective-permute-start.6 = (f32[4,136,128]{2,1,0:T(8,128)S(1)}, f32[4,136,128]{2,1,0:T(8,128)}, u32[]{:S(2)}, u32[]{:S(2)}) collective-permute-start(f32[4,136,128]{2,1,0:T(8,128)S(1)} %add.46), channel_id=1, source_target_pairs={{0,4},{4,8},{8,12},{12,16},{16,20},{20,24},{24,28},{1,5},{5,9},{9,... | collective-permute-start | bytes 835592 | tf_op jit(solution)/shard_map/ppermute | solution.py:25
  73.2 0.7 constant_dynamic-slice_fusion.1
  73.9 6.3 %collective-permute-done.6 = f32[4,136,128]{2,1,0:T(8,128)} collective-permute-done((f32[4,136,128]{2,1,0:T(8,128)S(1)}, f32[4,136,128]{2,1,0:T(8,128)}, u32[]{:S(2)}, u32[]{:S(2)}) %collective-permute-start.6) | collective-permute-done | bytes 278560 | tf_op jit(solution)/shard_map/ppermute | solution.py:25
  80.1 1.0 add.47
  81.1 3.2 %collective-permute-start.7 = (f32[4,136,128]{2,1,0:T(8,128)S(1)}, f32[4,136,128]{2,1,0:T(8,128)S(1)}, u32[]{:S(2)}, u32[]{:S(2)}) collective-permute-start(f32[4,136,128]{2,1,0:T(8,128)S(1)} %add.47), channel_id=1, source_target_pairs={{0,8},{4,12},{8,16},{12,20},{16,24},{20,28},{1,9},{5,13},{9,17},{1... | collective-permute-start | bytes 835592 | tf_op jit(solution)/shard_map/ppermute | solution.py:25
  84.3 0.0 copy-done.3
  84.3 0.6 add_divide_fusion.gate_ref
  84.9 0.6 slice_bitcast_fusion.1
  85.5 3.8 %collective-permute-done.7 = f32[4,136,128]{2,1,0:T(8,128)S(1)} collective-permute-done((f32[4,136,128]{2,1,0:T(8,128)S(1)}, f32[4,136,128]{2,1,0:T(8,128)S(1)}, u32[]{:S(2)}, u32[]{:S(2)}) %collective-permute-start.7) | collective-permute-done | bytes 278560 | tf_op jit(solution)/shard_map/ppermute | solution.py:25
  89.3 4.2 %collective-permute-start.8 = (f32[4,136,128]{2,1,0:T(8,128)S(1)}, f32[4,136,128]{2,1,0:T(8,128)S(1)}, u32[]{:S(2)}, u32[]{:S(2)}) collective-permute-start(f32[4,136,128]{2,1,0:T(8,128)S(1)} %add.48), channel_id=1, source_target_pairs={{0,16},{4,20},{8,24},{12,28},{1,17},{5,21},{9,25},{13,29},{2,18},{... | collective-permute-start | bytes 835592 | tf_op jit(solution)/shard_map/ppermute | solution.py:25
  93.6 0.0 collective-permute-done.3
  93.6 0.0 collective-permute-done.2
  93.6 0.0 collective-permute-done.1
  93.6 0.0 copy-done.2
  93.6 0.0 copy-start
  93.6 3.7 %pad_maximum_fusion.1.k_ref.v_ref = bf16[4,512,1024]{2,1,0:T(8,128)(2,1)} fusion(bf16[1,512,1024]{2,1,0:T(8,128)(2,1)} %bitcast.12, bf16[1,512,1024]{2,1,0:T(8,128)(2,1)S(1)} %bitcast.23, bf16[1,512,1024]{2,1,0:T(8,128)(2,1)} %bitcast.10, bf16[1,512,1024]{2,1,0:T(8,128)(2,1)} %bitcast.9), kind=kLoop, calls=%fused_computation.1 | loop fusion | flops 6291456 | bytes 8388608 | tf_op jit(solution)/shard_map/stack | solution.py:307
  97.4 8.2 %collective-permute-done.8 = f32[4,136,128]{2,1,0:T(8,128)S(1)} collective-permute-done((f32[4,136,128]{2,1,0:T(8,128)S(1)}, f32[4,136,128]{2,1,0:T(8,128)S(1)}, u32[]{:S(2)}, u32[]{:S(2)}) %collective-permute-start.8) | collective-permute-done | bytes 278560 | tf_op jit(solution)/shard_map/ppermute | solution.py:25
  105.6 0.8 add_subtract_fusion.s_ref
  106.4 0.0 collective-permute-done
  106.4 0.0 copy-done
  106.4 2.4 %pad_maximum_fusion.q_ref = bf16[2,512,2048]{2,1,0:T(8,128)(2,1)} fusion(bf16[1,512,2048]{2,1,0:T(8,128)(2,1)S(1)} %bitcast.22, bf16[1,512,2048]{2,1,0:T(8,128)(2,1)S(1)} %bitcast.21), kind=kLoop, calls=%fused_computation | loop fusion | flops 2097152 | bytes 8388608 | tf_op jit(solution)/shard_map/stack | solution.py:306
  108.8 85.4 %shard_map.56.local_ref = f32[2,512,2048]{2,1,0:T(8,128)} custom-call(s32[7]{0:T(128)} %get-tuple-element.18.qp_ref, s32[7]{0:T(128)} %get-tuple-element.17.kp_ref, s32[7]{0:T(128)} %get-tuple-element.16.op_ref, s32[7]{0:T(128)} %get-tuple-element.15.first_ref, s32[7]{0:T(128)} %get-tuple-element.14.last_ref, s32[7]{0:T(128)} %get-tuple-element.13.valid_ref, ...), custom_call_target="tpu_custom_call" | custom-call | tf_op jit(solution)/shard_map/pallas_call | solution.py:249
  194.2 13.4 %shard_map.58.own_ref = bf16[2,512,2048]{2,1,0:T(8,128)(2,1)} custom-call(f32[16]{0:T(128)} %add_divide_fusion.gate_ref, bf16[2,512,2048]{2,1,0:T(8,128)(2,1)} %pad_maximum_fusion.q_ref, f32[2,512,2048]{2,1,0:T(8,128)} %shard_map.56.local_ref, f32[4,136,128]{2,1,0:T(8,128)} %add_subtract_fusion.s_ref), custom_call_target="tpu_custom_call" | custom-call | tf_op jit(solution)/shard_map/pallas_call | solution.py:197
  207.5 1.7 slice_bitcast_fusion
  209.3 0.8 collective-permute-start.9
  210.1 3.8 %collective-permute-done.9.back_ref = bf16[512,2048]{1,0:T(8,128)(2,1)S(1)} collective-permute-done((bf16[512,2048]{1,0:T(8,128)(2,1)S(1)}, bf16[512,2048]{1,0:T(8,128)(2,1)S(1)}, u32[]{:S(2)}, u32[]{:S(2)}) %collective-permute-start.9) | collective-permute-done | bytes 2097184 | tf_op jit(solution)/shard_map/ppermute | solution.py:312
  213.9 0.0 copy-start.1
  213.9 1.3 copy-done.1
  215.2 4.4 %shard_map.59 = bf16[512,4096]{1,0:T(8,128)(2,1)} custom-call(s32[1]{0:T(128)} %bitcast.core_ref, bf16[2,512,2048]{2,1,0:T(8,128)(2,1)} %shard_map.58.own_ref, bf16[512,2048]{1,0:T(8,128)(2,1)} %copy-done.1), custom_call_target="tpu_custom_call" | custom-call | tf_op jit(solution)/shard_map/pallas_call | solution.py:278
  (2 shorter events, 0.1 us)
Async XLA Ops:
  5.6 78.7 %copy-start.3 = (f32[32]{0:T(128)S(1)}, f32[32]{0:T(128)}, u32[]{:S(2)}) copy-start(f32[32]{0:T(128)} %param.8) | copy-start | bytes 388
  5.6 88.0 %copy-start.2 = (bf16[512,1024]{1,0:T(8,128)(2,1)S(1)}, bf16[512,1024]{1,0:T(8,128)(2,1)}, u32[]{:S(2)}) copy-start(bf16[512,1024]{1,0:T(8,128)(2,1)} %get-tuple-element.11) | copy-start | bytes 3145732
  5.6 100.8 %collective-permute-start = (bf16[512,2048]{1,0:T(8,128)(2,1)}, bf16[512,2048]{1,0:T(8,128)(2,1)S(1)}, u32[]{:S(2)}, u32[]{:S(2)}) collective-permute-start(bf16[512,2048]{1,0:T(8,128)(2,1)} %get-tuple-element.10), channel_id=1, source_target_pairs={{0,1},{1,0},{2,3},{3,2},{4,5},{5,4},{6,7},{7,6},{8,9},{9,8},{10,11... | collective-permute-start | bytes 6291464 | tf_op jit(solution)/shard_map/ppermute | solution.py:304
  14.2 3.2 %collective-permute-start.4 = (f32[4,136,128]{2,1,0:T(8,128)S(1)}, f32[4,136,128]{2,1,0:T(8,128)}, u32[]{:S(2)}, u32[]{:S(2)}) collective-permute-start(f32[4,136,128]{2,1,0:T(8,128)S(1)} %constant_dynamic-slice_fusion), channel_id=1, source_target_pairs={{0,1},{1,0},{2,3},{3,2},{4,5},{5,4},{6,7},{7,6},{8,9},{9,8},{10,11... | collective-permute-start | bytes 835592 | tf_op jit(solution)/shard_map/ppermute | solution.py:101
  14.4 79.1 %collective-permute-start.3 = (bf16[512,1024]{1,0:T(8,128)(2,1)}, bf16[512,1024]{1,0:T(8,128)(2,1)}, u32[]{:S(2)}, u32[]{:S(2)}) collective-permute-start(bf16[512,1024]{1,0:T(8,128)(2,1)} %get-tuple-element.12), channel_id=1, source_target_pairs={{0,1},{1,0},{2,3},{3,2},{4,5},{5,4},{6,7},{7,6},{8,9},{9,8},{10,11... | collective-permute-start | bytes 3145736 | tf_op jit(solution)/shard_map/ppermute | solution.py:305
  14.8 78.8 %collective-permute-start.2 = (bf16[512,1024]{1,0:T(8,128)(2,1)}, bf16[512,1024]{1,0:T(8,128)(2,1)}, u32[]{:S(2)}, u32[]{:S(2)}) collective-permute-start(bf16[512,1024]{1,0:T(8,128)(2,1)} %get-tuple-element.12), channel_id=1, source_target_pairs={{0,3},{1,2},{4,7},{5,6},{8,11},{9,10},{12,15},{13,14},{16,19},{17,... | collective-permute-start | bytes 3145736 | tf_op jit(solution)/shard_map/ppermute | solution.py:302
  16.1 77.5 %collective-permute-start.1 = (bf16[512,1024]{1,0:T(8,128)(2,1)}, bf16[512,1024]{1,0:T(8,128)(2,1)}, u32[]{:S(2)}, u32[]{:S(2)}) collective-permute-start(bf16[512,1024]{1,0:T(8,128)(2,1)} %get-tuple-element.11), channel_id=1, source_target_pairs={{0,2},{1,3},{4,6},{5,7},{8,10},{9,11},{12,14},{13,15},{16,18},{17,... | collective-permute-start | bytes 3145736 | tf_op jit(solution)/shard_map/ppermute | solution.py:300
  18.5 51.5 %collective-permute-start.5 = (f32[4,136,128]{2,1,0:T(8,128)S(1)}, f32[4,136,128]{2,1,0:T(8,128)S(1)}, u32[]{:S(2)}, u32[]{:S(2)}) collective-permute-start(f32[4,136,128]{2,1,0:T(8,128)S(1)} %dynamic-slice_add_fusion), channel_id=1, source_target_pairs={{0,2},{1,3},{2,0},{3,1},{4,6},{5,7},{6,4},{7,5},{8,10},{9,11},{10,... | collective-permute-start | bytes 835592 | tf_op jit(solution)/shard_map/ppermute | solution.py:104
  70.0 10.1 %collective-permute-start.6 = (f32[4,136,128]{2,1,0:T(8,128)S(1)}, f32[4,136,128]{2,1,0:T(8,128)}, u32[]{:S(2)}, u32[]{:S(2)}) collective-permute-start(f32[4,136,128]{2,1,0:T(8,128)S(1)} %add.46), channel_id=1, source_target_pairs={{0,4},{4,8},{8,12},{12,16},{16,20},{20,24},{24,28},{1,5},{5,9},{9,... | collective-permute-start | bytes 835592 | tf_op jit(solution)/shard_map/ppermute | solution.py:25
  81.1 8.2 %collective-permute-start.7 = (f32[4,136,128]{2,1,0:T(8,128)S(1)}, f32[4,136,128]{2,1,0:T(8,128)S(1)}, u32[]{:S(2)}, u32[]{:S(2)}) collective-permute-start(f32[4,136,128]{2,1,0:T(8,128)S(1)} %add.47), channel_id=1, source_target_pairs={{0,8},{4,12},{8,16},{12,20},{16,24},{20,28},{1,9},{5,13},{9,17},{1... | collective-permute-start | bytes 835592 | tf_op jit(solution)/shard_map/ppermute | solution.py:25
  89.3 16.3 %collective-permute-start.8 = (f32[4,136,128]{2,1,0:T(8,128)S(1)}, f32[4,136,128]{2,1,0:T(8,128)S(1)}, u32[]{:S(2)}, u32[]{:S(2)}) collective-permute-start(f32[4,136,128]{2,1,0:T(8,128)S(1)} %add.48), channel_id=1, source_target_pairs={{0,16},{4,20},{8,24},{12,28},{1,17},{5,21},{9,25},{13,29},{2,18},{... | collective-permute-start | bytes 835592 | tf_op jit(solution)/shard_map/ppermute | solution.py:25
  93.6 12.8 %copy-start = (bf16[512,2048]{1,0:T(8,128)(2,1)S(1)}, bf16[512,2048]{1,0:T(8,128)(2,1)}, u32[]{:S(2)}) copy-start(bf16[512,2048]{1,0:T(8,128)(2,1)} %get-tuple-element.9) | copy-start | bytes 6291460
  209.3 4.6 %collective-permute-start.9 = (bf16[512,2048]{1,0:T(8,128)(2,1)S(1)}, bf16[512,2048]{1,0:T(8,128)(2,1)S(1)}, u32[]{:S(2)}, u32[]{:S(2)}) collective-permute-start(bf16[512,2048]{1,0:T(8,128)(2,1)S(1)} %slice_bitcast_fusion), channel_id=1, source_target_pairs={{0,1},{1,0},{2,3},{3,2},{4,5},{5,4},{6,7},{7,6},{8,9},{9,8},{10,11... | collective-permute-start | bytes 6291464 | tf_op jit(solution)/shard_map/ppermute | solution.py:312
  213.9 1.3 copy-start.1

commit v8 on v6

--- a/solution.py
+++ b/solution.py
@@ -93,7 +93,7 @@
     )(keys, values)
 
 
-def before_states(keys, values, core, kv_group):
+def chip_states(keys, values, core, kv_group):
     total = local_deltas(keys, values)
     parts = lax.axis_size("head")
     keep = lax.dynamic_slice_in_dim(total, core * kv_group, kv_group)
@@ -103,8 +103,12 @@
     while steps < parts:
         total = total + lax.ppermute(total, "head", [(p, p ^ steps) for p in range(parts)])
         steps *= 2
-    delta = total
+    return total
+
+
+def earlier_states(delta):
     count = lax.axis_size("seq")
+    total = delta
     steps = 1
     while steps < count:
         total = total + shifted(total, "seq", steps)
@@ -271,8 +275,10 @@
     group_size = queries.shape[1] // keys.shape[1]
     sibling = [(p, p ^ 1) for p in range(parts)]
 
-    state = before_states(keys, values, core, kv_group)
+    delta = chip_states(keys, values, core, kv_group)
     keep_q, keep_kv, send_q, send_kv = split_inputs(queries, keys, values, core)
+    delta, keep_kv, send_kv = lax.optimization_barrier((delta, keep_kv, send_kv))
+    state = earlier_states(delta)
     kv_parts = []
     for s in range(chips - 1, 0, -1):
         kv_parts.append(lax.ppermute(keep_kv, "head", [(p, p + 2 * s) for p in range(parts - 2 * s)]))

time: 217 us -> 189 us (0.87)
  waiting for transfers between devices: 69.3 us -> 46.7 us
  starting transfers between devices: 19.3 us -> 15.9 us
    ppermute x2, waiting for transfers between devices: 47.3 us -> 7.54 us  [the longest x1 7.54 us: chip_states(): lax.ppermute(total, 'head', [(p, p ^ steps) for p in range(parts)])]
    ppermute x1, waiting for transfers between devices: 0.01 us -> 18.4 us  [body(): lax.ppermute(send_kv, 'head', [(p, p + 2 * s ^ 1) for p in range(parts -...]
    ppermute x2, starting transfers between devices: 4.33 us -> 1.02 us  [the longest x1 0.73 us: chip_states(): lax.ppermute(send, 'head', [(p, p ^ 1) for p in range(parts)])]
  transfers between devices with their start and end apart: 10 -> 10, of which waited for: 5 -> 6; matrix products, arithmetic and copies ran while one was open for 4% -> 4% of each run, Pallas kernels for 3% -> 3%
where the time goes in v8:
time: 189 us; the launch traced here: 188 us
  Pallas kernels  112 us (59%)
  waiting for transfers between devices  46.7 us (25%)
  starting transfers between devices  15.9 us (8%)
  other arithmetic  7.81 us (4%)
  local copies, waits for them, and re-layouts  5.33 us (3%)
    pallas_call x1, Pallas kernels, attend(): pl.pallas_call(functools.partial(flash_kernel, group_size=group_size), gr...  94.9 us
    ppermute x1, waiting for transfers between devices, body(): lax.ppermute(send_kv, 'head', [(p, p + 2 * s ^ 1) for p in range(parts -...  18.4 us
    ppermute x3, waiting for transfers between devices, shifted(): lax.ppermute(value, axis, [(source, source + steps) for source in range(c...  16.7 us
    ppermute x3, starting transfers between devices, shifted(): lax.ppermute(value, axis, [(source, source + steps) for source in range(c...  10.6 us
    ppermute x1, waiting for transfers between devices, chip_states(): lax.ppermute(total, 'head', [(p, p ^ steps) for p in range(parts)])  7.54 us
    pallas_call x1, Pallas kernels, local_deltas(): pl.pallas_call(delta_kernel, grid=(kv_heads, 1), in_specs=[pl.BlockSpec((...  7.04 us
    pallas_call x1, Pallas kernels, split_inputs(): pl.pallas_call(split_kernel, grid_spec=grid_spec, out_shape=[q_shape, kv_...  5.62 us
    pallas_call x1, Pallas kernels, merge_halves(): pl.pallas_call(merge_kernel, grid_spec=grid_spec, out_shape=jax.ShapeDtyp...  4.37 us
  transfers between devices with their start and end apart: 10, of which 6 were waited for; matrix products, arithmetic and copies ran while one was open for 4% of the time, Pallas kernels for 3%

profile of v8, /device:TPU:13, one launch (start us, length us, event | category | flops | bytes accessed | tf_op | source)
XLA Modules:
  0.0 187.9 jit_solution(6938884741301658839)
XLA Ops:
  0.0 7.0 %shard_map.56 = f32[8,136,128]{2,1,0:T(8,128)} custom-call(bf16[512,1024]{1,0:T(8,128)(2,1)} %k_ref.1, bf16[512,1024]{1,0:T(8,128)(2,1)} %v_ref.1), custom_call_target="tpu_custom_call" | custom-call | tf_op jit(solution)/shard_map/pallas_call | solution.py:86
  7.0 1.0 constant_dynamic-slice_fusion
  8.0 0.7 collective-permute-start.1
  8.7 0.0 copy-start
  8.8 0.0 copy-start.3
  8.8 5.6 %shard_map.55 = (bf16[512,2048]{1,0:T(8,128)(2,1)}, bf16[512,1024]{1,0:T(8,128)(2,1)}, bf16[512,2048]{1,0:T(8,128)(2,1)}, bf16[512,1024]{1,0:T(8,128)(2,1)}) custom-call(s32[1]{0:T(128)} %bitcast.core_ref, bf16[512,4096]{1,0:T(8,128)(2,1)} %q_send.1, bf16[512,1024]{1,0:T(8,128)(2,1)} %k_ref.1, bf16[512,1024]{1,0:T(8,128)(2,1)} %v_ref.1, ...), custom_call_target="tpu_custom_call" | custom-call | tf_op jit(solution)/shard_map/pallas_call | solution.py:64
  14.4 0.0 collective-permute-start
  14.4 0.0 collective-permute-done.1
  14.4 0.0 copy-done
  14.4 0.3 collective-permute-start.2
  14.7 7.5 %collective-permute-done.2 = f32[4,136,128]{2,1,0:T(8,128)S(1)} collective-permute-done((f32[4,136,128]{2,1,0:T(8,128)S(1)}, f32[4,136,128]{2,1,0:T(8,128)S(1)}, u32[]{:S(2)}, u32[]{:S(2)}) %collective-permute-start.2) | collective-permute-done | bytes 278560 | tf_op jit(solution)/shard_map/ppermute | solution.py:104
  22.3 3.1 %collective-permute-start.6 = (f32[4,136,128]{2,1,0:T(8,128)S(1)}, f32[4,136,128]{2,1,0:T(8,128)S(1)}, u32[]{:S(2)}, u32[]{:S(2)}) collective-permute-start(f32[4,136,128]{2,1,0:T(8,128)S(1)} %add.46), channel_id=1, source_target_pairs={{0,4},{4,8},{8,12},{12,16},{16,20},{20,24},{24,28},{1,5},{5,9},{9,... | collective-permute-start | bytes 835592 | tf_op jit(solution)/shard_map/ppermute | solution.py:25
  25.4 1.3 collective-permute-start.3
  26.7 1.7 collective-permute-start.5
  28.4 1.3 collective-permute-start.4
  29.7 2.3 %collective-permute-done.6 = f32[4,136,128]{2,1,0:T(8,128)S(1)} collective-permute-done((f32[4,136,128]{2,1,0:T(8,128)S(1)}, f32[4,136,128]{2,1,0:T(8,128)S(1)}, u32[]{:S(2)}, u32[]{:S(2)}) %collective-permute-start.6) | collective-permute-done | bytes 278560 | tf_op jit(solution)/shard_map/ppermute | solution.py:25
  32.0 3.2 %collective-permute-start.7 = (f32[4,136,128]{2,1,0:T(8,128)S(1)}, f32[4,136,128]{2,1,0:T(8,128)S(1)}, u32[]{:S(2)}, u32[]{:S(2)}) collective-permute-start(f32[4,136,128]{2,1,0:T(8,128)S(1)} %add.47), channel_id=1, source_target_pairs={{0,8},{4,12},{8,16},{12,20},{16,24},{20,28},{1,9},{5,13},{9,17},{1... | collective-permute-start | bytes 835592 | tf_op jit(solution)/shard_map/ppermute | solution.py:25
  35.2 0.7 constant_dynamic-slice_fusion.1
  35.9 4.0 %collective-permute-done.7 = f32[4,136,128]{2,1,0:T(8,128)S(1)} collective-permute-done((f32[4,136,128]{2,1,0:T(8,128)S(1)}, f32[4,136,128]{2,1,0:T(8,128)S(1)}, u32[]{:S(2)}, u32[]{:S(2)}) %collective-permute-start.7) | collective-permute-done | bytes 278560 | tf_op jit(solution)/shard_map/ppermute | solution.py:25
  39.9 4.2 %collective-permute-start.8 = (f32[4,136,128]{2,1,0:T(8,128)S(1)}, f32[4,136,128]{2,1,0:T(8,128)S(1)}, u32[]{:S(2)}, u32[]{:S(2)}) collective-permute-start(f32[4,136,128]{2,1,0:T(8,128)S(1)} %add.48), channel_id=1, source_target_pairs={{0,16},{4,20},{8,24},{12,28},{1,17},{5,21},{9,25},{13,29},{2,18},{... | collective-permute-start | bytes 835592 | tf_op jit(solution)/shard_map/ppermute | solution.py:25
  44.2 0.0 copy-done.3
  44.2 0.6 add_divide_fusion.gate_ref
  44.8 0.6 slice_bitcast_fusion.1
  45.4 10.4 %collective-permute-done.8 = f32[4,136,128]{2,1,0:T(8,128)S(1)} collective-permute-done((f32[4,136,128]{2,1,0:T(8,128)S(1)}, f32[4,136,128]{2,1,0:T(8,128)S(1)}, u32[]{:S(2)}, u32[]{:S(2)}) %collective-permute-start.8) | collective-permute-done | bytes 278560 | tf_op jit(solution)/shard_map/ppermute | solution.py:25
  55.8 0.8 add_subtract_fusion.s_ref
  56.6 0.0 collective-permute-done.3
  56.6 0.0 collective-permute-done.5
  56.6 18.4 %collective-permute-done.4 = bf16[512,1024]{1,0:T(8,128)(2,1)} collective-permute-done((bf16[512,1024]{1,0:T(8,128)(2,1)}, bf16[512,1024]{1,0:T(8,128)(2,1)}, u32[]{:S(2)}, u32[]{:S(2)}) %collective-permute-start.4) | collective-permute-done | bytes 1048608 | tf_op jit(solution)/shard_map/ppermute | solution.py:286
  75.0 0.0 copy-start.1
  75.0 3.9 %pad_maximum_fusion.1.k_ref.v_ref = bf16[4,512,1024]{2,1,0:T(8,128)(2,1)} fusion(bf16[1,512,1024]{2,1,0:T(8,128)(2,1)} %bitcast.12, bf16[1,512,1024]{2,1,0:T(8,128)(2,1)} %bitcast.23, bf16[1,512,1024]{2,1,0:T(8,128)(2,1)} %bitcast.10, bf16[1,512,1024]{2,1,0:T(8,128)(2,1)} %bitcast.9), kind=kLoop, calls=%fused_computation.1 | loop fusion | flops 6291456 | bytes 8388608 | tf_op jit(solution)/shard_map/stack | solution.py:291
  78.9 0.0 collective-permute-done
  78.9 0.0 copy-done.1
  78.9 2.4 %pad_maximum_fusion.q_ref = bf16[2,512,2048]{2,1,0:T(8,128)(2,1)} fusion(bf16[1,512,2048]{2,1,0:T(8,128)(2,1)S(1)} %bitcast.22, bf16[1,512,2048]{2,1,0:T(8,128)(2,1)S(1)} %bitcast.21), kind=kLoop, calls=%fused_computation | loop fusion | flops 2097152 | bytes 8388608 | tf_op jit(solution)/shard_map/stack | solution.py:290
  81.3 94.9 %shard_map.57.own_ref = bf16[2,512,2048]{2,1,0:T(8,128)(2,1)} custom-call(s32[7]{0:T(128)} %get-tuple-element.24.qp_ref, s32[7]{0:T(128)} %get-tuple-element.23.kp_ref, s32[7]{0:T(128)} %get-tuple-element.22.op_ref, s32[7]{0:T(128)} %get-tuple-element.21.first_ref, s32[7]{0:T(128)} %get-tuple-element.20.last_ref, s32[7]{0:T(128)} %get-tuple-element.19.valid_ref, ...), custom_call_target="tpu_custom_call" | custom-call | tf_op jit(solution)/shard_map/pallas_call | solution.py:231
  176.2 1.7 slice_bitcast_fusion
  177.9 0.1 collective-permute-start.9
  178.0 4.1 %collective-permute-done.9.back_ref = bf16[512,2048]{1,0:T(8,128)(2,1)S(1)} collective-permute-done((bf16[512,2048]{1,0:T(8,128)(2,1)S(1)}, bf16[512,2048]{1,0:T(8,128)(2,1)S(1)}, u32[]{:S(2)}, u32[]{:S(2)}) %collective-permute-start.9) | collective-permute-done | bytes 2097184 | tf_op jit(solution)/shard_map/ppermute | solution.py:295
  182.2 0.0 copy-start.2
  182.2 1.3 copy-done.2
  183.5 4.4 %shard_map.58 = bf16[512,4096]{1,0:T(8,128)(2,1)} custom-call(s32[1]{0:T(128)} %bitcast.core_ref, bf16[2,512,2048]{2,1,0:T(8,128)(2,1)} %shard_map.57.own_ref, bf16[512,2048]{1,0:T(8,128)(2,1)} %copy-done.2), custom_call_target="tpu_custom_call" | custom-call | tf_op jit(solution)/shard_map/pallas_call | solution.py:260
  (4 shorter events, 0.1 us)
Async XLA Ops:
  8.0 6.4 %collective-permute-start.1 = (f32[4,136,128]{2,1,0:T(8,128)S(1)}, f32[4,136,128]{2,1,0:T(8,128)S(1)}, u32[]{:S(2)}, u32[]{:S(2)}) collective-permute-start(f32[4,136,128]{2,1,0:T(8,128)S(1)} %constant_dynamic-slice_fusion), channel_id=1, source_target_pairs={{0,1},{1,0},{2,3},{3,2},{4,5},{5,4},{6,7},{7,6},{8,9},{9,8},{10,11... | collective-permute-start | bytes 835592 | tf_op jit(solution)/shard_map/ppermute | solution.py:101
  8.7 5.7 %copy-start = (f32[8,136,128]{2,1,0:T(8,128)S(1)}, f32[8,136,128]{2,1,0:T(8,128)}, u32[]{:S(2)}) copy-start(f32[8,136,128]{2,1,0:T(8,128)} %shard_map.56) | copy-start | bytes 1671172
  8.8 35.4 %copy-start.3 = (f32[32]{0:T(128)S(1)}, f32[32]{0:T(128)}, u32[]{:S(2)}) copy-start(f32[32]{0:T(128)} %param.8) | copy-start | bytes 388
  14.4 64.5 %collective-permute-start = (bf16[512,2048]{1,0:T(8,128)(2,1)}, bf16[512,2048]{1,0:T(8,128)(2,1)S(1)}, u32[]{:S(2)}, u32[]{:S(2)}) collective-permute-start(bf16[512,2048]{1,0:T(8,128)(2,1)} %get-tuple-element.13), channel_id=1, source_target_pairs={{0,1},{1,0},{2,3},{3,2},{4,5},{5,4},{6,7},{7,6},{8,9},{9,8},{10,11... | collective-permute-start | bytes 6291464 | tf_op jit(solution)/shard_map/ppermute | solution.py:288
  14.4 7.8 %collective-permute-start.2 = (f32[4,136,128]{2,1,0:T(8,128)S(1)}, f32[4,136,128]{2,1,0:T(8,128)S(1)}, u32[]{:S(2)}, u32[]{:S(2)}) collective-permute-start(f32[4,136,128]{2,1,0:T(8,128)S(1)} %dynamic-slice_add_fusion), channel_id=1, source_target_pairs={{0,2},{1,3},{2,0},{3,1},{4,6},{5,7},{6,4},{7,5},{8,10},{9,11},{10,... | collective-permute-start | bytes 835592 | tf_op jit(solution)/shard_map/ppermute | solution.py:104
  22.3 9.6 %collective-permute-start.6 = (f32[4,136,128]{2,1,0:T(8,128)S(1)}, f32[4,136,128]{2,1,0:T(8,128)S(1)}, u32[]{:S(2)}, u32[]{:S(2)}) collective-permute-start(f32[4,136,128]{2,1,0:T(8,128)S(1)} %add.46), channel_id=1, source_target_pairs={{0,4},{4,8},{8,12},{12,16},{16,20},{20,24},{24,28},{1,5},{5,9},{9,... | collective-permute-start | bytes 835592 | tf_op jit(solution)/shard_map/ppermute | solution.py:25
  25.4 31.2 %collective-permute-start.3 = (bf16[512,1024]{1,0:T(8,128)(2,1)}, bf16[512,1024]{1,0:T(8,128)(2,1)}, u32[]{:S(2)}, u32[]{:S(2)}) collective-permute-start(bf16[512,1024]{1,0:T(8,128)(2,1)} %get-tuple-element.16), channel_id=1, source_target_pairs={{0,2},{1,3},{4,6},{5,7},{8,10},{9,11},{12,14},{13,15},{16,18},{17,... | collective-permute-start | bytes 3145736 | tf_op jit(solution)/shard_map/ppermute | solution.py:284
  26.7 29.9 %collective-permute-start.5 = (bf16[512,1024]{1,0:T(8,128)(2,1)}, bf16[512,1024]{1,0:T(8,128)(2,1)}, u32[]{:S(2)}, u32[]{:S(2)}) collective-permute-start(bf16[512,1024]{1,0:T(8,128)(2,1)} %get-tuple-element.17), channel_id=1, source_target_pairs={{0,1},{1,0},{2,3},{3,2},{4,5},{5,4},{6,7},{7,6},{8,9},{9,8},{10,11... | collective-permute-start | bytes 3145736 | tf_op jit(solution)/shard_map/ppermute | solution.py:289
  28.4 46.6 %collective-permute-start.4 = (bf16[512,1024]{1,0:T(8,128)(2,1)}, bf16[512,1024]{1,0:T(8,128)(2,1)}, u32[]{:S(2)}, u32[]{:S(2)}) collective-permute-start(bf16[512,1024]{1,0:T(8,128)(2,1)} %get-tuple-element.17), channel_id=1, source_target_pairs={{0,3},{1,2},{4,7},{5,6},{8,11},{9,10},{12,15},{13,14},{16,19},{17,... | collective-permute-start | bytes 3145736 | tf_op jit(solution)/shard_map/ppermute | solution.py:286
  32.0 7.9 %collective-permute-start.7 = (f32[4,136,128]{2,1,0:T(8,128)S(1)}, f32[4,136,128]{2,1,0:T(8,128)S(1)}, u32[]{:S(2)}, u32[]{:S(2)}) collective-permute-start(f32[4,136,128]{2,1,0:T(8,128)S(1)} %add.47), channel_id=1, source_target_pairs={{0,8},{4,12},{8,16},{12,20},{16,24},{20,28},{1,9},{5,13},{9,17},{1... | collective-permute-start | bytes 835592 | tf_op jit(solution)/shard_map/ppermute | solution.py:25
  39.9 15.9 %collective-permute-start.8 = (f32[4,136,128]{2,1,0:T(8,128)S(1)}, f32[4,136,128]{2,1,0:T(8,128)S(1)}, u32[]{:S(2)}, u32[]{:S(2)}) collective-permute-start(f32[4,136,128]{2,1,0:T(8,128)S(1)} %add.48), channel_id=1, source_target_pairs={{0,16},{4,20},{8,24},{12,28},{1,17},{5,21},{9,25},{13,29},{2,18},{... | collective-permute-start | bytes 835592 | tf_op jit(solution)/shard_map/ppermute | solution.py:25
  75.0 3.9 %copy-start.1 = (bf16[512,2048]{1,0:T(8,128)(2,1)S(1)}, bf16[512,2048]{1,0:T(8,128)(2,1)}, u32[]{:S(2)}) copy-start(bf16[512,2048]{1,0:T(8,128)(2,1)} %get-tuple-element.12) | copy-start | bytes 6291460
  177.9 4.2 %collective-permute-start.9 = (bf16[512,2048]{1,0:T(8,128)(2,1)S(1)}, bf16[512,2048]{1,0:T(8,128)(2,1)S(1)}, u32[]{:S(2)}, u32[]{:S(2)}) collective-permute-start(bf16[512,2048]{1,0:T(8,128)(2,1)S(1)} %slice_bitcast_fusion), channel_id=1, source_target_pairs={{0,1},{1,0},{2,3},{3,2},{4,5},{5,4},{6,7},{7,6},{8,9},{9,8},{10,11... | collective-permute-start | bytes 6291464 | tf_op jit(solution)/shard_map/ppermute | solution.py:295
  182.2 1.3 copy-start.2

commit v9 on v8

--- a/solution.py
+++ b/solution.py
@@ -116,59 +116,84 @@
     return total - delta
 
 
-def flash_kernel(
-    qp_ref, kp_ref, op_ref, first_ref, last_ref, valid_ref, gate_ref, q_ref, k_ref, v_ref, s_ref,
-    o_ref, m_sc, l_sc, acc_sc, *, group_size
-):
-    kv_head = pl.program_id(0)
-    step_at = pl.program_id(1)
-    first = first_ref[step_at] == 1
-    last = last_ref[step_at] == 1
-    valid = valid_ref[step_at] == 1
+def online_step(q_ref, k_ref, v_ref, m_sc, l_sc, acc_sc, group_size, masked):
     block = q_ref.shape[0]
     score_scale = HD ** (-0.5)
-
-    @pl.when(valid & first)
+    key_rows = k_ref[...]
+    value_rows = v_ref[...]
+    if masked:
+        rows = lax.broadcasted_iota(jnp.int32, (block, block), 0)
+        cols = lax.broadcasted_iota(jnp.int32, (block, block), 1)
+        allowed = cols <= rows
+    for head in range(group_size):
+        lanes = slice(head * HD, (head + 1) * HD)
+        scores = (
+            lax.dot_general(
+                q_ref[:, lanes], key_rows, (((1,), (1,)), ((), ())),
+                preferred_element_type=jnp.float32,
+            )
+            * score_scale
+        )
+        if masked:
+            scores = jnp.where(allowed, scores, -1e30)
+        m_prev = m_sc[head]
+        m_new = jnp.maximum(m_prev, jnp.max(scores, axis=-1, keepdims=True))
+        probs = jnp.exp(scores - m_new[:, :1])
+        alpha = jnp.exp(m_prev - m_new)
+        l_sc[head] = alpha * l_sc[head] + jnp.sum(probs, axis=-1, keepdims=True)
+        acc_sc[:, lanes] = alpha * acc_sc[:, lanes] + jnp.dot(
+            probs.astype(jnp.bfloat16), value_rows, preferred_element_type=jnp.float32
+        )
+        m_sc[head] = m_new
+
+
+def near_kernel(qp_ref, kp_ref, first_ref, diag_ref, q_ref, k_ref, v_ref, acc_ref, ml_ref,
+                m_sc, l_sc, acc_sc, *, group_size):
+    step_at = pl.program_id(1)
+
+    @pl.when(first_ref[step_at] == 1)
     def _init():
         m_sc[...] = jnp.full(m_sc.shape, -jnp.inf, jnp.float32)
         l_sc[...] = jnp.zeros(l_sc.shape, jnp.float32)
         acc_sc[...] = jnp.zeros(acc_sc.shape, jnp.float32)
 
-    def step(masked):
-        key_rows = k_ref[...]
-        value_rows = v_ref[...]
-        if masked:
-            rows = lax.broadcasted_iota(jnp.int32, (block, block), 0)
-            cols = lax.broadcasted_iota(jnp.int32, (block, block), 1)
-            allowed = cols <= rows
+    @pl.when(diag_ref[step_at] == 0)
+    def _full():
+        online_step(q_ref, k_ref, v_ref, m_sc, l_sc, acc_sc, group_size, False)
+
+    @pl.when(diag_ref[step_at] == 1)
+    def _diag():
+        online_step(q_ref, k_ref, v_ref, m_sc, l_sc, acc_sc, group_size, True)
+        acc_ref[...] = acc_sc[...]
+        lane = lax.broadcasted_iota(jnp.int32, ml_ref.shape, 1)
+        packed = jnp.zeros(ml_ref.shape, jnp.float32)
         for head in range(group_size):
-            lanes = slice(head * HD, (head + 1) * HD)
-            scores = (
-                lax.dot_general(
-                    q_ref[:, lanes], key_rows, (((1,), (1,)), ((), ())),
-                    preferred_element_type=jnp.float32,
-                )
-                * score_scale
+            packed = jnp.where(lane == head, m_sc[head], packed)
+            packed = jnp.where(lane == group_size + head, l_sc[head], packed)
+        ml_ref[...] = packed
+
+
+def far_kernel(qp_ref, kp_ref, first_ref, last_ref, valid_ref, gate_ref, q_ref, k_ref, v_ref,
+               s_ref, acc_in, ml_in, o_ref, m_sc, l_sc, acc_sc, *, group_size):
+    kv_head = pl.program_id(0)
+    step_at = pl.program_id(1)
+
+    @pl.when(first_ref[step_at] == 1)
+    def _init():
+        packed = ml_in[...]
+        for head in range(group_size):
+            m_sc[head] = jnp.broadcast_to(packed[:, head : head + 1], m_sc.shape[1:])
+            l_sc[head] = jnp.broadcast_to(
+                packed[:, group_size + head : group_size + head + 1], l_sc.shape[1:]
             )
-            if masked:
-                scores = jnp.where(allowed, scores, -1e30)
-            m_prev = m_sc[head]
-            m_new = jnp.maximum(m_prev, jnp.max(scores, axis=-1, keepdims=True))
-            probs = jnp.exp(scores - m_new[:, :1])
-            alpha = jnp.exp(m_prev - m_new)
-            l_sc[head] = alpha * l_sc[head] + jnp.sum(probs, axis=-1, keepdims=True)
-            acc_sc[:, lanes] = alpha * acc_sc[:, lanes] + jnp.dot(
-                probs.astype(jnp.bfloat16), value_rows, preferred_element_type=jnp.float32
-            )
-            m_sc[head] = m_new
-
-    @pl.when(valid & jnp.logical_not(last))
-    def _full():
-        step(False)
-
-    @pl.when(valid & last)
+        acc_sc[...] = acc_in[...]
+
+    @pl.when(valid_ref[step_at] == 1)
+    def _step():
+        online_step(q_ref, k_ref, v_ref, m_sc, l_sc, acc_sc, group_size, False)
+
+    @pl.when(last_ref[step_at] == 1)
     def _last():
-        step(True)
         memory = s_ref[:HD, :]
         normalizer = s_ref[HD : HD + 1, :]
         for head in range(group_size):
@@ -188,52 +213,86 @@
             ).astype(o_ref.dtype)
 
 
-def pair_tables(chips, chip, core):
-    longest = 4 * chips - 1
-    tables = np.zeros((chips, 2, 6, longest), np.int32)
+def near_tables(core):
+    tables = np.array(
+        [[[c, 1 ^ c, 1 ^ c], [c, c, 1 ^ c], [1, 1, 0], [1, 0, 1]] for c in range(2)], np.int32
+    )
+    return jnp.asarray(tables)[core]
+
+
+def far_tables(chips, chip, core):
+    per_block = max(1, 2 * (chips - 1))
+    tables = np.zeros((chips, 2, 5, 2 * per_block), np.int32)
     for y in range(chips):
         for c in range(2):
             steps = []
             for a in range(2):
-                for j in range(2 * y + a + 1):
-                    k_pos = 2 * (chips - 1 - y + j // 2) + ((j % 2) ^ c)
-                    steps.append((a ^ c, k_pos, a ^ c, int(j == 0), int(j == 2 * y + a), 1))
-            while len(steps) < longest:
-                steps.append(steps[-1][:5] + (0,))
+                k_pos = 0
+                for j in range(per_block):
+                    valid = int(j < 2 * y)
+                    if valid:
+                        k_pos = 2 * (chips - 1 - y + j // 2) + ((j % 2) ^ c)
+                    steps.append((a ^ c, k_pos, int(j == 0), int(j == per_block - 1), valid))
             tables[y, c] = np.array(steps, np.int32).T
     return jnp.asarray(tables)[chip, core]
 
 
-def attend(query_rows, kv_rows, state, mixing, tables, group_size):
+def attend(query_rows, near_kv, far_kv, state, mixing, chips, chip, core, group_size):
     _, block, q_cols = query_rows.shape
-    kv_group = kv_rows.shape[-1] // (2 * HD)
+    kv_group = near_kv.shape[-1] // (2 * HD)
     width = group_size * HD
-    steps = tables.shape[-1]
-    grid_spec = pltpu.PrefetchScalarGridSpec(
-        num_scalar_prefetch=6,
-        grid=(kv_group, steps),
+    scratch = [
+        pltpu.VMEM((group_size, block, LANES), jnp.float32),
+        pltpu.VMEM((group_size, block, LANES), jnp.float32),
+        pltpu.VMEM((block, width), jnp.float32),
+    ]
+    params = pltpu.CompilerParams(dimension_semantics=("arbitrary", "arbitrary"))
+    near = near_tables(core)
+    near_spec = pltpu.PrefetchScalarGridSpec(
+        num_scalar_prefetch=4,
+        grid=(kv_group, near.shape[-1]),
+        in_specs=[
+            pl.BlockSpec((None, block, width), lambda g, t, qp, kp, f, d: (qp[t], 0, g)),
+            pl.BlockSpec((None, block, HD), lambda g, t, qp, kp, f, d: (kp[t], 0, g)),
+            pl.BlockSpec((None, block, HD), lambda g, t, qp, kp, f, d: (kp[t], 0, kv_group + g)),
+        ],
+        out_specs=[
+            pl.BlockSpec((None, block, width), lambda g, t, qp, kp, f, d: (qp[t], 0, g)),
+            pl.BlockSpec((None, None, block, LANES), lambda g, t, qp, kp, f, d: (g, qp[t], 0, 0)),
+        ],
+        scratch_shapes=scratch,
+    )
+    acc, ml = pl.pallas_call(
+        functools.partial(near_kernel, group_size=group_size),
+        grid_spec=near_spec,
+        out_shape=[
+            jax.ShapeDtypeStruct((2, block, q_cols), jnp.float32),
+            jax.ShapeDtypeStruct((kv_group, 2, block, LANES), jnp.float32),
+        ],
+        compiler_params=params,
+    )(*[near[i] for i in range(4)], query_rows, near_kv, near_kv)
+    far = far_tables(chips, chip, core)
+    far_spec = pltpu.PrefetchScalarGridSpec(
+        num_scalar_prefetch=5,
+        grid=(kv_group, far.shape[-1]),
         in_specs=[
             pl.BlockSpec(memory_space=pltpu.SMEM),
-            pl.BlockSpec((None, block, width), lambda g, t, qp, kp, op, f, l, v: (qp[t], 0, g)),
-            pl.BlockSpec((None, block, HD), lambda g, t, qp, kp, op, f, l, v: (kp[t], 0, g)),
-            pl.BlockSpec(
-                (None, block, HD), lambda g, t, qp, kp, op, f, l, v: (kp[t], 0, kv_group + g)
-            ),
-            pl.BlockSpec((None, STATE_ROWS, HD), lambda g, t, qp, kp, op, f, l, v: (g, 0, 0)),
-        ],
-        out_specs=pl.BlockSpec((None, block, width), lambda g, t, qp, kp, op, f, l, v: (op[t], 0, g)),
-        scratch_shapes=[
-            pltpu.VMEM((group_size, block, LANES), jnp.float32),
-            pltpu.VMEM((group_size, block, LANES), jnp.float32),
-            pltpu.VMEM((block, width), jnp.float32),
-        ],
+            pl.BlockSpec((None, block, width), lambda g, t, qp, kp, f, l, v: (qp[t], 0, g)),
+            pl.BlockSpec((None, block, HD), lambda g, t, qp, kp, f, l, v: (kp[t], 0, g)),
+            pl.BlockSpec((None, block, HD), lambda g, t, qp, kp, f, l, v: (kp[t], 0, kv_group + g)),
+            pl.BlockSpec((None, STATE_ROWS, HD), lambda g, t, qp, kp, f, l, v: (g, 0, 0)),
+            pl.BlockSpec((None, block, width), lambda g, t, qp, kp, f, l, v: (qp[t], 0, g)),
+            pl.BlockSpec((None, None, block, LANES), lambda g, t, qp, kp, f, l, v: (g, qp[t], 0, 0)),
+        ],
+        out_specs=pl.BlockSpec((None, block, width), lambda g, t, qp, kp, f, l, v: (qp[t], 0, g)),
+        scratch_shapes=scratch,
     )
     return pl.pallas_call(
-        functools.partial(flash_kernel, group_size=group_size),
-        grid_spec=grid_spec,
+        functools.partial(far_kernel, group_size=group_size),
+        grid_spec=far_spec,
         out_shape=jax.ShapeDtypeStruct((2, block, q_cols), jnp.bfloat16),
-        compiler_params=pltpu.CompilerParams(dimension_semantics=("arbitrary", "arbitrary")),
-    )(*[tables[i] for i in range(6)], mixing, query_rows, kv_rows, kv_rows, state)
+        compiler_params=params,
+    )(*[far[i] for i in range(5)], mixing, query_rows, far_kv, far_kv, state, acc, ml)
 
 
 def merge_kernel(core_ref, own_ref, back_ref, o_ref):
@@ -288,10 +347,11 @@
     recv_q = lax.ppermute(send_q, "head", sibling)
     recv_kv = lax.ppermute(send_kv, "head", sibling)
     query_rows = jnp.stack([keep_q, recv_q])
-    kv_rows = jnp.stack(kv_parts + [keep_kv, recv_kv])
+    near_kv = jnp.stack([keep_kv, recv_kv])
+    far_kv = jnp.stack(kv_parts) if kv_parts else near_kv
     gate_here = lax.dynamic_slice_in_dim(gate_logit, core * kv_group * group_size, kv_group * group_size)
     mixing = jax.nn.sigmoid(gate_here)
-    attended = attend(query_rows, kv_rows, state, mixing, pair_tables(chips, chip, core), group_size)
+    attended = attend(query_rows, near_kv, far_kv, state, mixing, chips, chip, core, group_size)
     back = lax.ppermute(attended[1], "head", sibling)
     return merge_halves(attended, back, core)
 

time: 189 us -> 201 us (1.063)
  Pallas kernels: 112 us -> 122 us
  other arithmetic: 7.81 us -> 9.93 us
    ppermute x1, waiting for transfers between devices: 18.4 us -> 0.01 us  [body(): lax.ppermute(send_kv, 'head', [(p, p + 2 * s ^ 1) for p in range(parts -...]
    ppermute x1, waiting for transfers between devices: 0.01 us -> 17.6 us  [body(): lax.ppermute(keep_kv, 'head', [(p, p + 2 * s) for p in range(parts - 2 *...]
    pallas_call x1 -> x2, Pallas kernels: 94.9 us -> 105 us  [the longest x1 65.6 us: attend(): pl.pallas_call(functools.partial(far_kernel, group_size=group_size), grid...]
    another operation x1 -> x2, other arithmetic: 3.89 us -> 6.04 us  [the longest x1 3.24 us: body(): far_kv = jnp.stack(kv_parts) if kv_parts else near_kv]
  transfers between devices with their start and end apart: 10 -> 10, of which waited for: 6 -> 6; matrix products, arithmetic and copies ran while one was open for 4% -> 5% of each run, Pallas kernels for 3% -> 3%
where the time goes in v9:
time: 201 us; the launch traced here: 200 us
  Pallas kernels  122 us (61%)
  waiting for transfers between devices  45 us (22%)
  starting transfers between devices  16.9 us (8%)
  other arithmetic  9.93 us (5%)
  local copies, waits for them, and re-layouts  5.93 us (3%)
    pallas_call x1, Pallas kernels, attend(): pl.pallas_call(functools.partial(far_kernel, group_size=group_size), grid...  65.6 us
    pallas_call x1, Pallas kernels, attend(): pl.pallas_call(functools.partial(near_kernel, group_size=group_size), gri...  39.7 us
    ppermute x1, waiting for transfers between devices, body(): lax.ppermute(keep_kv, 'head', [(p, p + 2 * s) for p in range(parts - 2 *...  17.6 us
    ppermute x3, waiting for transfers between devices, shifted(): lax.ppermute(value, axis, [(source, source + steps) for source in range(c...  16.1 us
    ppermute x3, starting transfers between devices, shifted(): lax.ppermute(value, axis, [(source, source + steps) for source in range(c...  10.6 us
    ppermute x1, waiting for transfers between devices, chip_states(): lax.ppermute(total, 'head', [(p, p ^ steps) for p in range(parts)])  7.52 us
    pallas_call x1, Pallas kernels, local_deltas(): pl.pallas_call(delta_kernel, grid=(kv_heads, 1), in_specs=[pl.BlockSpec((...  7.03 us
    pallas_call x1, Pallas kernels, split_inputs(): pl.pallas_call(split_kernel, grid_spec=grid_spec, out_shape=[q_shape, kv_...  5.63 us
  transfers between devices with their start and end apart: 10, of which 6 were waited for; matrix products, arithmetic and copies ran while one was open for 5% of the time, Pallas kernels for 3%

profile of v9, /device:TPU:13, one launch (start us, length us, event | category | flops | bytes accessed | tf_op | source)
XLA Modules:
  0.0 200.2 jit_solution(4217374762096840622)
XLA Ops:
  0.0 7.0 %shard_map.65 = f32[8,136,128]{2,1,0:T(8,128)} custom-call(bf16[512,1024]{1,0:T(8,128)(2,1)} %k_ref.1, bf16[512,1024]{1,0:T(8,128)(2,1)} %v_ref.1), custom_call_target="tpu_custom_call" | custom-call | tf_op jit(solution)/shard_map/pallas_call | solution.py:86
  7.0 1.0 constant_dynamic-slice_fusion.1
  8.0 0.7 collective-permute-start.1
  8.7 0.0 copy-start
  8.7 5.6 %shard_map.64 = (bf16[512,2048]{1,0:T(8,128)(2,1)}, bf16[512,1024]{1,0:T(8,128)(2,1)}, bf16[512,2048]{1,0:T(8,128)(2,1)}, bf16[512,1024]{1,0:T(8,128)(2,1)}) custom-call(s32[1]{0:T(128)} %bitcast.core_ref, bf16[512,4096]{1,0:T(8,128)(2,1)} %q_send.1, bf16[512,1024]{1,0:T(8,128)(2,1)} %k_ref.1, bf16[512,1024]{1,0:T(8,128)(2,1)} %v_ref.1, ...), custom_call_target="tpu_custom_call" | custom-call | tf_op jit(solution)/shard_map/pallas_call | solution.py:64
  14.4 0.0 copy-start.4
  14.4 0.0 copy-start.5
  14.4 0.0 collective-permute-start
  14.4 0.0 collective-permute-done.1
  14.4 0.0 copy-done
  14.5 0.3 collective-permute-start.2
  14.8 7.5 %collective-permute-done.2 = f32[4,136,128]{2,1,0:T(8,128)S(1)} collective-permute-done((f32[4,136,128]{2,1,0:T(8,128)S(1)}, f32[4,136,128]{2,1,0:T(8,128)S(1)}, u32[]{:S(2)}, u32[]{:S(2)}) %collective-permute-start.2) | collective-permute-done | bytes 278560 | tf_op jit(solution)/shard_map/ppermute | solution.py:104
  22.3 3.1 %collective-permute-start.5 = (f32[4,136,128]{2,1,0:T(8,128)S(1)}, f32[4,136,128]{2,1,0:T(8,128)S(1)}, u32[]{:S(2)}, u32[]{:S(2)}) collective-permute-start(f32[4,136,128]{2,1,0:T(8,128)S(1)} %add.47), channel_id=1, source_target_pairs={{0,4},{4,8},{8,12},{12,16},{16,20},{20,24},{24,28},{1,5},{5,9},{9,... | collective-permute-start | bytes 835592 | tf_op jit(solution)/shard_map/ppermute | solution.py:25
  25.4 1.7 collective-permute-start.8
  27.1 0.7 constant_dynamic-slice_fusion.2
  27.8 1.3 collective-permute-start.4
  29.1 1.3 collective-permute-start.3
  30.4 1.5 collective-permute-done.5
  32.0 3.2 %collective-permute-start.6 = (f32[4,136,128]{2,1,0:T(8,128)S(1)}, f32[4,136,128]{2,1,0:T(8,128)S(1)}, u32[]{:S(2)}, u32[]{:S(2)}) collective-permute-start(f32[4,136,128]{2,1,0:T(8,128)S(1)} %add.48), channel_id=1, source_target_pairs={{0,8},{4,12},{8,16},{12,20},{16,24},{20,28},{1,9},{5,13},{9,17},{1... | collective-permute-start | bytes 835592 | tf_op jit(solution)/shard_map/ppermute | solution.py:25
  35.2 0.0 copy-done.4
  35.2 0.0 copy-start.3
  35.2 0.6 slice_bitcast_fusion.1
  35.8 4.1 %collective-permute-done.6 = f32[4,136,128]{2,1,0:T(8,128)S(1)} collective-permute-done((f32[4,136,128]{2,1,0:T(8,128)S(1)}, f32[4,136,128]{2,1,0:T(8,128)S(1)}, u32[]{:S(2)}, u32[]{:S(2)}) %collective-permute-start.6) | collective-permute-done | bytes 278560 | tf_op jit(solution)/shard_map/ppermute | solution.py:25
  39.9 4.2 %collective-permute-start.7 = (f32[4,136,128]{2,1,0:T(8,128)S(1)}, f32[4,136,128]{2,1,0:T(8,128)S(1)}, u32[]{:S(2)}, u32[]{:S(2)}) collective-permute-start(f32[4,136,128]{2,1,0:T(8,128)S(1)} %add.49), channel_id=1, source_target_pairs={{0,16},{4,20},{8,24},{12,28},{1,17},{5,21},{9,25},{13,29},{2,18},{... | collective-permute-start | bytes 835592 | tf_op jit(solution)/shard_map/ppermute | solution.py:25
  44.1 0.0 copy-done.5
  44.2 0.6 add_divide_fusion.gate_ref
  44.8 0.6 slice_bitcast_fusion.5
  45.4 10.5 %collective-permute-done.7 = f32[4,136,128]{2,1,0:T(8,128)S(1)} collective-permute-done((f32[4,136,128]{2,1,0:T(8,128)S(1)}, f32[4,136,128]{2,1,0:T(8,128)S(1)}, u32[]{:S(2)}, u32[]{:S(2)}) %collective-permute-start.7) | collective-permute-done | bytes 278560 | tf_op jit(solution)/shard_map/ppermute | solution.py:25
  55.8 0.7 add_subtract_fusion.s_ref
  56.6 0.0 collective-permute-done.8
  56.6 0.0 copy-done.3
  56.6 2.8 %pad_maximum_fusion.2.k_ref.v_ref = bf16[2,512,1024]{2,1,0:T(8,128)(2,1)} fusion(bf16[1,512,1024]{2,1,0:T(8,128)(2,1)} %bitcast.15, bf16[1,512,1024]{2,1,0:T(8,128)(2,1)S(1)} %bitcast.29), kind=kLoop, calls=%fused_computation.3 | loop fusion | flops 1048576 | bytes 4194304 | tf_op jit(solution)/shard_map/stack | solution.py:350
  59.4 17.6 %collective-permute-done.3 = bf16[512,1024]{1,0:T(8,128)(2,1)} collective-permute-done((bf16[512,1024]{1,0:T(8,128)(2,1)}, bf16[512,1024]{1,0:T(8,128)(2,1)}, u32[]{:S(2)}, u32[]{:S(2)}) %collective-permute-start.3) | collective-permute-done | bytes 1048608 | tf_op jit(solution)/shard_map/ppermute | solution.py:343
  77.0 0.0 collective-permute-done.4
  77.0 0.0 copy-start.1
  77.0 3.2 %pad_maximum_fusion.1.k_ref.v_ref = bf16[2,512,1024]{2,1,0:T(8,128)(2,1)} fusion(bf16[1,512,1024]{2,1,0:T(8,128)(2,1)} %bitcast.9, bf16[1,512,1024]{2,1,0:T(8,128)(2,1)} %bitcast.8), kind=kLoop, calls=%fused_computation.2 | loop fusion | flops 1048576 | bytes 4194304 | tf_op jit(solution)/shard_map/stack | solution.py:351
  80.2 0.0 collective-permute-done
  80.2 0.0 copy-done.1
  80.2 2.4 %pad_maximum_fusion.q_ref = bf16[2,512,2048]{2,1,0:T(8,128)(2,1)} fusion(bf16[1,512,2048]{2,1,0:T(8,128)(2,1)S(1)} %bitcast.28, bf16[1,512,2048]{2,1,0:T(8,128)(2,1)S(1)} %bitcast.27), kind=kLoop, calls=%fused_computation | loop fusion | flops 2097152 | bytes 8388608 | tf_op jit(solution)/shard_map/stack | solution.py:349
  82.6 39.7 %shard_map.66 = (f32[2,512,2048]{2,1,0:T(8,128)}, f32[4,2,512,128]{3,2,1,0:T(8,128)}) custom-call(s32[3]{0:T(128)} %get-tuple-element.31.qp_ref, s32[3]{0:T(128)} %get-tuple-element.30.kp_ref, s32[3]{0:T(128)} %get-tuple-element.29.first_ref, s32[3]{0:T(128)} %get-tuple-element.28.diag_ref, bf16[2,512,2048]{2,1,0:T(8,128)(2,1)} %pad_maximum_fusion.q_ref, ...), custom_call_target="tpu_custom_call" | custom-call | tf_op jit(solution)/shard_map/pallas_call | solution.py:265
  122.3 65.6 %shard_map.67.own_ref = bf16[2,512,2048]{2,1,0:T(8,128)(2,1)} custom-call(s32[4]{0:T(128)} %get-tuple-element.27.qp_ref, s32[4]{0:T(128)} %get-tuple-element.26.kp_ref, s32[4]{0:T(128)} %get-tuple-element.25.first_ref, s32[4]{0:T(128)} %get-tuple-element.24.last_ref, s32[4]{0:T(128)} %get-tuple-element.23.valid_ref, f32[16]{0:T(128)} %add_divide_fusion.gate_ref, ...), custom_call_target="tpu_custom_call" | custom-call | tf_op jit(solution)/shard_map/pallas_call | solution.py:290
  187.9 1.7 slice_bitcast_fusion
  189.7 1.1 collective-permute-start.9
  190.7 3.8 %collective-permute-done.9.back_ref = bf16[512,2048]{1,0:T(8,128)(2,1)S(1)} collective-permute-done((bf16[512,2048]{1,0:T(8,128)(2,1)S(1)}, bf16[512,2048]{1,0:T(8,128)(2,1)S(1)}, u32[]{:S(2)}, u32[]{:S(2)}) %collective-permute-start.9) | collective-permute-done | bytes 2097184 | tf_op jit(solution)/shard_map/ppermute | solution.py:355
  194.5 0.0 copy-start.2
  194.5 1.3 copy-done.2
  195.9 4.4 %shard_map.68 = bf16[512,4096]{1,0:T(8,128)(2,1)} custom-call(s32[1]{0:T(128)} %bitcast.core_ref, bf16[2,512,2048]{2,1,0:T(8,128)(2,1)} %shard_map.67.own_ref, bf16[512,2048]{1,0:T(8,128)(2,1)} %copy-done.2), custom_call_target="tpu_custom_call" | custom-call | tf_op jit(solution)/shard_map/pallas_call | solution.py:319
  (5 shorter events, 0.1 us)
Async XLA Ops:
  8.0 6.4 %collective-permute-start.1 = (f32[4,136,128]{2,1,0:T(8,128)S(1)}, f32[4,136,128]{2,1,0:T(8,128)S(1)}, u32[]{:S(2)}, u32[]{:S(2)}) collective-permute-start(f32[4,136,128]{2,1,0:T(8,128)S(1)} %constant_dynamic-slice_fusion.1), channel_id=1, source_target_pairs={{0,1},{1,0},{2,3},{3,2},{4,5},{5,4},{6,7},{7,6},{8,9},{9,8},{10,11... | collective-permute-start | bytes 835592 | tf_op jit(solution)/shard_map/ppermute | solution.py:101
  8.7 5.7 %copy-start = (f32[8,136,128]{2,1,0:T(8,128)S(1)}, f32[8,136,128]{2,1,0:T(8,128)}, u32[]{:S(2)}) copy-start(f32[8,136,128]{2,1,0:T(8,128)} %shard_map.65) | copy-start | bytes 1671172
  14.4 20.8 %copy-start.4 = (s32[2,4,3]{2,1,0:T(4,128)S(1)}, s32[2,4,3]{2,1,0:T(4,128)}, u32[]{:S(2)}) copy-start(s32[2,4,3]{2,1,0:T(4,128)} %constant.44.clone) | copy-start | bytes 292
  14.4 29.8 %copy-start.5 = (f32[32]{0:T(128)S(1)}, f32[32]{0:T(128)}, u32[]{:S(2)}) copy-start(f32[32]{0:T(128)} %param.9) | copy-start | bytes 388
  14.4 65.9 %collective-permute-start = (bf16[512,2048]{1,0:T(8,128)(2,1)}, bf16[512,2048]{1,0:T(8,128)(2,1)S(1)}, u32[]{:S(2)}, u32[]{:S(2)}) collective-permute-start(bf16[512,2048]{1,0:T(8,128)(2,1)} %get-tuple-element.15), channel_id=1, source_target_pairs={{0,1},{1,0},{2,3},{3,2},{4,5},{5,4},{6,7},{7,6},{8,9},{9,8},{10,11... | collective-permute-start | bytes 6291464 | tf_op jit(solution)/shard_map/ppermute | solution.py:347
  14.5 7.8 %collective-permute-start.2 = (f32[4,136,128]{2,1,0:T(8,128)S(1)}, f32[4,136,128]{2,1,0:T(8,128)S(1)}, u32[]{:S(2)}, u32[]{:S(2)}) collective-permute-start(f32[4,136,128]{2,1,0:T(8,128)S(1)} %dynamic-slice_add_fusion), channel_id=1, source_target_pairs={{0,2},{1,3},{2,0},{3,1},{4,6},{5,7},{6,4},{7,5},{8,10},{9,11},{10,... | collective-permute-start | bytes 835592 | tf_op jit(solution)/shard_map/ppermute | solution.py:104
  22.3 9.6 %collective-permute-start.5 = (f32[4,136,128]{2,1,0:T(8,128)S(1)}, f32[4,136,128]{2,1,0:T(8,128)S(1)}, u32[]{:S(2)}, u32[]{:S(2)}) collective-permute-start(f32[4,136,128]{2,1,0:T(8,128)S(1)} %add.47), channel_id=1, source_target_pairs={{0,4},{4,8},{8,12},{12,16},{16,20},{20,24},{24,28},{1,5},{5,9},{9,... | collective-permute-start | bytes 835592 | tf_op jit(solution)/shard_map/ppermute | solution.py:25
  25.4 31.1 %collective-permute-start.8 = (bf16[512,1024]{1,0:T(8,128)(2,1)}, bf16[512,1024]{1,0:T(8,128)(2,1)}, u32[]{:S(2)}, u32[]{:S(2)}) collective-permute-start(bf16[512,1024]{1,0:T(8,128)(2,1)} %get-tuple-element.19), channel_id=1, source_target_pairs={{0,1},{1,0},{2,3},{3,2},{4,5},{5,4},{6,7},{7,6},{8,9},{9,8},{10,11... | collective-permute-start | bytes 3145736 | tf_op jit(solution)/shard_map/ppermute | solution.py:348
  27.8 49.2 %collective-permute-start.4 = (bf16[512,1024]{1,0:T(8,128)(2,1)}, bf16[512,1024]{1,0:T(8,128)(2,1)}, u32[]{:S(2)}, u32[]{:S(2)}) collective-permute-start(bf16[512,1024]{1,0:T(8,128)(2,1)} %get-tuple-element.19), channel_id=1, source_target_pairs={{0,3},{1,2},{4,7},{5,6},{8,11},{9,10},{12,15},{13,14},{16,19},{17,... | collective-permute-start | bytes 3145736 | tf_op jit(solution)/shard_map/ppermute | solution.py:345
  29.1 47.9 %collective-permute-start.3 = (bf16[512,1024]{1,0:T(8,128)(2,1)}, bf16[512,1024]{1,0:T(8,128)(2,1)}, u32[]{:S(2)}, u32[]{:S(2)}) collective-permute-start(bf16[512,1024]{1,0:T(8,128)(2,1)} %get-tuple-element.18), channel_id=1, source_target_pairs={{0,2},{1,3},{4,6},{5,7},{8,10},{9,11},{12,14},{13,15},{16,18},{17,... | collective-permute-start | bytes 3145736 | tf_op jit(solution)/shard_map/ppermute | solution.py:343
  32.0 7.9 %collective-permute-start.6 = (f32[4,136,128]{2,1,0:T(8,128)S(1)}, f32[4,136,128]{2,1,0:T(8,128)S(1)}, u32[]{:S(2)}, u32[]{:S(2)}) collective-permute-start(f32[4,136,128]{2,1,0:T(8,128)S(1)} %add.48), channel_id=1, source_target_pairs={{0,8},{4,12},{8,16},{12,20},{16,24},{20,28},{1,9},{5,13},{9,17},{1... | collective-permute-start | bytes 835592 | tf_op jit(solution)/shard_map/ppermute | solution.py:25
  35.2 21.4 %copy-start.3 = (bf16[512,1024]{1,0:T(8,128)(2,1)S(1)}, bf16[512,1024]{1,0:T(8,128)(2,1)}, u32[]{:S(2)}) copy-start(bf16[512,1024]{1,0:T(8,128)(2,1)} %get-tuple-element.18) | copy-start | bytes 3145732
  39.9 15.9 %collective-permute-start.7 = (f32[4,136,128]{2,1,0:T(8,128)S(1)}, f32[4,136,128]{2,1,0:T(8,128)S(1)}, u32[]{:S(2)}, u32[]{:S(2)}) collective-permute-start(f32[4,136,128]{2,1,0:T(8,128)S(1)} %add.49), channel_id=1, source_target_pairs={{0,16},{4,20},{8,24},{12,28},{1,17},{5,21},{9,25},{13,29},{2,18},{... | collective-permute-start | bytes 835592 | tf_op jit(solution)/shard_map/ppermute | solution.py:25
  77.0 3.2 %copy-start.1 = (bf16[512,2048]{1,0:T(8,128)(2,1)S(1)}, bf16[512,2048]{1,0:T(8,128)(2,1)}, u32[]{:S(2)}) copy-start(bf16[512,2048]{1,0:T(8,128)(2,1)} %get-tuple-element.14) | copy-start | bytes 6291460
  189.7 4.8 %collective-permute-start.9 = (bf16[512,2048]{1,0:T(8,128)(2,1)S(1)}, bf16[512,2048]{1,0:T(8,128)(2,1)S(1)}, u32[]{:S(2)}, u32[]{:S(2)}) collective-permute-start(bf16[512,2048]{1,0:T(8,128)(2,1)S(1)} %slice_bitcast_fusion), channel_id=1, source_target_pairs={{0,1},{1,0},{2,3},{3,2},{4,5},{5,4},{6,7},{7,6},{8,9},{9,8},{10,11... | collective-permute-start | bytes 6291464 | tf_op jit(solution)/shard_map/ppermute | solution.py:355
  194.5 1.3 copy-start.2

commit v10 on v9

--- a/solution.py
+++ b/solution.py
@@ -262,9 +262,15 @@
         ],
         scratch_shapes=scratch,
     )
+    pair_flops = 4 * block * block * HD * group_size * kv_group
+    pair_exps = block * block * group_size * kv_group
     acc, ml = pl.pallas_call(
         functools.partial(near_kernel, group_size=group_size),
         grid_spec=near_spec,
+        cost_estimate=pl.CostEstimate(
+            flops=3 * pair_flops, transcendentals=3 * pair_exps,
+            bytes_accessed=int(query_rows.size * 6 + near_kv.size * 2),
+        ),
         out_shape=[
             jax.ShapeDtypeStruct((2, block, q_cols), jnp.float32),
             jax.ShapeDtypeStruct((kv_group, 2, block, LANES), jnp.float32),
@@ -287,9 +293,14 @@
         out_specs=pl.BlockSpec((None, block, width), lambda g, t, qp, kp, f, l, v: (qp[t], 0, g)),
         scratch_shapes=scratch,
     )
+    far_pairs = far.shape[-1]
     return pl.pallas_call(
         functools.partial(far_kernel, group_size=group_size),
         grid_spec=far_spec,
+        cost_estimate=pl.CostEstimate(
+            flops=far_pairs * pair_flops, transcendentals=far_pairs * pair_exps,
+            bytes_accessed=int(query_rows.size * 8 + far_kv.size * 2),
+        ),
         out_shape=jax.ShapeDtypeStruct((2, block, q_cols), jnp.bfloat16),
         compiler_params=params,
     )(*[far[i] for i in range(5)], mixing, query_rows, far_kv, far_kv, state, acc, ml)
@@ -336,7 +347,11 @@
 
     delta = chip_states(keys, values, core, kv_group)
     keep_q, keep_kv, send_q, send_kv = split_inputs(queries, keys, values, core)
-    delta, keep_kv, send_kv = lax.optimization_barrier((delta, keep_kv, send_kv))
+    recv_q = lax.ppermute(send_q, "head", sibling)
+    recv_kv = lax.ppermute(send_kv, "head", sibling)
+    delta, keep_kv, send_kv, recv_q, recv_kv = lax.optimization_barrier(
+        (delta, keep_kv, send_kv, recv_q, recv_kv)
+    )
     state = earlier_states(delta)
     kv_parts = []
     for s in range(chips - 1, 0, -1):
@@ -344,8 +359,6 @@
         kv_parts.append(
             lax.ppermute(send_kv, "head", [(p, (p + 2 * s) ^ 1) for p in range(parts - 2 * s)])
         )
-    recv_q = lax.ppermute(send_q, "head", sibling)
-    recv_kv = lax.ppermute(send_kv, "head", sibling)
     query_rows = jnp.stack([keep_q, recv_q])
     near_kv = jnp.stack([keep_kv, recv_kv])
     far_kv = jnp.stack(kv_parts) if kv_parts else near_kv

time: 201 us -> 173 us (0.86)
  waiting for transfers between devices: 45 us -> 14.1 us
  other arithmetic: 9.93 us -> 12.4 us
    ppermute x1, waiting for transfers between devices: 17.6 us -> 0.01 us  [body(): lax.ppermute(keep_kv, 'head', [(p, p + 2 * s) for p in range(parts - 2 *...]
    ppermute x3, waiting for transfers between devices: 16.1 us -> 2.81 us  [shifted(): lax.ppermute(value, axis, [(source, source + steps) for source in range(c...]
    ppermute x1, starting transfers between devices: 1.05 us -> 3.11 us  [body(): back = lax.ppermute(attended[1], 'head', sibling)]
  transfers between devices with their start and end apart: 10 -> 10, of which waited for: 6 -> 4; matrix products, arithmetic and copies ran while one was open for 5% -> 7% of each run, Pallas kernels for 3% -> 27%
where the time goes in v10:
time: 173 us; the launch traced here: 171 us
  Pallas kernels  122 us (71%)
  starting transfers between devices  16.1 us (9%)
  waiting for transfers between devices  14.1 us (8%)
  other arithmetic  12.4 us (7%)
  local copies, waits for them, and re-layouts  6.09 us (4%)
    pallas_call x1, Pallas kernels, attend(): pl.pallas_call(functools.partial(far_kernel, group_size=group_size), grid...  65.6 us
    pallas_call x1, Pallas kernels, attend(): pl.pallas_call(functools.partial(near_kernel, group_size=group_size), gri...  39.7 us
    ppermute x3, starting transfers between devices, shifted(): lax.ppermute(value, axis, [(source, source + steps) for source in range(c...  8.83 us
    pallas_call x1, Pallas kernels, local_deltas(): pl.pallas_call(delta_kernel, grid=(kv_heads, 1), in_specs=[pl.BlockSpec((...  7.08 us
    ppermute x1, waiting for transfers between devices, chip_states(): lax.ppermute(total, 'head', [(p, p ^ steps) for p in range(parts)])  7.03 us
    pallas_call x1, Pallas kernels, split_inputs(): pl.pallas_call(split_kernel, grid_spec=grid_spec, out_shape=[q_shape, kv_...  5.57 us
    pallas_call x1, Pallas kernels, merge_halves(): pl.pallas_call(merge_kernel, grid_spec=grid_spec, out_shape=jax.ShapeDtyp...  4.37 us
    another operation x1, other arithmetic, body(): query_rows = jnp.stack([keep_q, recv_q])  4.08 us
  transfers between devices with their start and end apart: 10, of which 4 were waited for; matrix products, arithmetic and copies ran while one was open for 7% of the time, Pallas kernels for 27%

profile of v10, /device:TPU:13, one launch (start us, length us, event | category | flops | bytes accessed | tf_op | source)
XLA Modules:
  0.0 171.1 jit_solution(5681635971345601499)
XLA Ops:
  0.0 5.6 %shard_map.64 = (bf16[512,2048]{1,0:T(8,128)(2,1)}, bf16[512,1024]{1,0:T(8,128)(2,1)}, bf16[512,2048]{1,0:T(8,128)(2,1)}, bf16[512,1024]{1,0:T(8,128)(2,1)}) custom-call(s32[1]{0:T(128)} %bitcast.core_ref, bf16[512,4096]{1,0:T(8,128)(2,1)} %q_send.1, bf16[512,1024]{1,0:T(8,128)(2,1)} %k_ref.1, bf16[512,1024]{1,0:T(8,128)(2,1)} %v_ref.1, ...), custom_call_target="tpu_custom_call" | custom-call | tf_op jit(solution)/shard_map/pallas_call | solution.py:64
  5.6 0.0 copy-start.3
  5.6 0.7 collective-permute-start.2
  6.3 0.1 collective-permute-start.3
  6.3 0.0 copy-start.4
  6.3 7.1 %shard_map.65 = f32[8,136,128]{2,1,0:T(8,128)} custom-call(bf16[512,1024]{1,0:T(8,128)(2,1)} %k_ref.1, bf16[512,1024]{1,0:T(8,128)(2,1)} %v_ref.1), custom_call_target="tpu_custom_call" | custom-call | tf_op jit(solution)/shard_map/pallas_call | solution.py:86
  13.4 0.0 copy-start
  13.4 1.1 constant_dynamic-slice_fusion.1
  14.5 0.5 collective-permute-start
  15.0 0.7 constant_dynamic-slice_fusion.2
  15.7 0.5 collective-permute-done
  16.2 1.0 dynamic-slice_add_fusion
  17.2 0.3 collective-permute-start.1
  17.5 0.0 copy-done.3
  17.5 0.6 slice_bitcast_fusion.1
  18.1 7.0 %collective-permute-done.1 = f32[4,136,128]{2,1,0:T(8,128)S(1)} collective-permute-done((f32[4,136,128]{2,1,0:T(8,128)S(1)}, f32[4,136,128]{2,1,0:T(8,128)S(1)}, u32[]{:S(2)}, u32[]{:S(2)}) %collective-permute-start.1) | collective-permute-done | bytes 278560 | tf_op jit(solution)/shard_map/ppermute | solution.py:104
  25.2 0.0 collective-permute-done.3
  25.2 0.0 collective-permute-done.2
  25.2 3.1 %collective-permute-start.6 = (f32[4,136,128]{2,1,0:T(8,128)S(1)}, f32[4,136,128]{2,1,0:T(8,128)S(1)}, u32[]{:S(2)}, u32[]{:S(2)}) collective-permute-start(f32[4,136,128]{2,1,0:T(8,128)S(1)} %add.47), channel_id=1, source_target_pairs={{0,4},{4,8},{8,12},{12,16},{16,20},{20,24},{24,28},{1,5},{5,9},{9,... | collective-permute-start | bytes 835592 | tf_op jit(solution)/shard_map/ppermute | solution.py:25
  28.3 0.0 copy-done.4
  28.4 0.6 add_divide_fusion.gate_ref
  29.0 0.6 slice_bitcast_fusion.5
  29.6 1.3 collective-permute-start.5
  30.8 1.3 collective-permute-start.4
  32.1 2.8 %collective-permute-done.6 = f32[4,136,128]{2,1,0:T(8,128)S(1)} collective-permute-done((f32[4,136,128]{2,1,0:T(8,128)S(1)}, f32[4,136,128]{2,1,0:T(8,128)S(1)}, u32[]{:S(2)}, u32[]{:S(2)}) %collective-permute-start.6) | collective-permute-done | bytes 278560 | tf_op jit(solution)/shard_map/ppermute | solution.py:25
  35.0 3.2 %collective-permute-start.7 = (f32[4,136,128]{2,1,0:T(8,128)S(1)}, f32[4,136,128]{2,1,0:T(8,128)S(1)}, u32[]{:S(2)}, u32[]{:S(2)}) collective-permute-start(f32[4,136,128]{2,1,0:T(8,128)S(1)} %add.48), channel_id=1, source_target_pairs={{0,8},{4,12},{8,16},{12,20},{16,24},{20,28},{1,9},{5,13},{9,17},{1... | collective-permute-start | bytes 835592 | tf_op jit(solution)/shard_map/ppermute | solution.py:25
  38.2 0.0 copy-done
  38.2 0.0 copy-start.2
  38.2 4.1 %pad_maximum_fusion.q_ref = bf16[2,512,2048]{2,1,0:T(8,128)(2,1)} fusion(bf16[1,512,2048]{2,1,0:T(8,128)(2,1)} %bitcast.7, bf16[1,512,2048]{2,1,0:T(8,128)(2,1)S(1)} %bitcast.27), kind=kLoop, calls=%fused_computation | loop fusion | flops 2097152 | bytes 8388608 | tf_op jit(solution)/shard_map/stack | solution.py:362
  42.3 0.0 copy-done.2
  42.3 2.8 %pad_maximum_fusion.2.k_ref.v_ref = bf16[2,512,1024]{2,1,0:T(8,128)(2,1)} fusion(bf16[1,512,1024]{2,1,0:T(8,128)(2,1)} %bitcast.15, bf16[1,512,1024]{2,1,0:T(8,128)(2,1)S(1)} %bitcast.28), kind=kLoop, calls=%fused_computation.3 | loop fusion | flops 1048576 | bytes 4194304 | tf_op jit(solution)/shard_map/stack | solution.py:363
  45.1 0.0 collective-permute-done.7
  45.1 2.5 %collective-permute-start.8 = (f32[4,136,128]{2,1,0:T(8,128)S(1)}, f32[4,136,128]{2,1,0:T(8,128)S(1)}, u32[]{:S(2)}, u32[]{:S(2)}) collective-permute-start(f32[4,136,128]{2,1,0:T(8,128)S(1)} %add.49), channel_id=1, source_target_pairs={{0,16},{4,20},{8,24},{12,28},{1,17},{5,21},{9,25},{13,29},{2,18},{... | collective-permute-start | bytes 835592 | tf_op jit(solution)/shard_map/ppermute | solution.py:25
  47.7 39.7 %shard_map.66 = (f32[2,512,2048]{2,1,0:T(8,128)}, f32[4,2,512,128]{3,2,1,0:T(8,128)}) custom-call(s32[3]{0:T(128)} %get-tuple-element.35.qp_ref, s32[3]{0:T(128)} %get-tuple-element.34.kp_ref, s32[3]{0:T(128)} %get-tuple-element.33.first_ref, s32[3]{0:T(128)} %get-tuple-element.32.diag_ref, bf16[2,512,2048]{2,1,0:T(8,128)(2,1)} %pad_maximum_fusion.q_ref, ...), custom_call_target="tpu_custom_call" | custom-call | flops 6442450944 | bytes 14680064 | tf_op jit(solution)/shard_map/pallas_call | solution.py:267
  87.3 0.0 collective-permute-done.8
  87.3 0.7 add_subtract_fusion.s_ref
  88.1 0.0 collective-permute-done.5
  88.1 0.0 collective-permute-done.4
  88.1 3.0 %pad_maximum_fusion.1.k_ref.v_ref = bf16[2,512,1024]{2,1,0:T(8,128)(2,1)} fusion(bf16[1,512,1024]{2,1,0:T(8,128)(2,1)} %bitcast.9, bf16[1,512,1024]{2,1,0:T(8,128)(2,1)} %bitcast.8), kind=kLoop, calls=%fused_computation.2 | loop fusion | flops 1048576 | bytes 4194304 | tf_op jit(solution)/shard_map/stack | solution.py:364
  91.1 65.6 %shard_map.67.own_ref = bf16[2,512,2048]{2,1,0:T(8,128)(2,1)} custom-call(s32[4]{0:T(128)} %get-tuple-element.31.qp_ref, s32[4]{0:T(128)} %get-tuple-element.30.kp_ref, s32[4]{0:T(128)} %get-tuple-element.29.first_ref, s32[4]{0:T(128)} %get-tuple-element.28.last_ref, s32[4]{0:T(128)} %get-tuple-element.27.valid_ref, f32[16]{0:T(128)} %add_divide_fusion.gate_ref, ...), custom_call_target="tpu_custom_call" | custom-call | flops 8589934592 | bytes 18874368 | tf_op jit(solution)/shard_map/pallas_call | solution.py:297
  156.8 1.7 %slice_bitcast_fusion = bf16[512,2048]{1,0:T(8,128)(2,1)S(1)} fusion(bf16[2,512,2048]{2,1,0:T(8,128)(2,1)} %shard_map.67.own_ref), kind=kLoop, calls=%fused_computation.1 | loop fusion | bytes 4194304 | tf_op jit(solution)/shard_map/squeeze | solution.py:368
  158.5 3.1 %collective-permute-start.9 = (bf16[512,2048]{1,0:T(8,128)(2,1)S(1)}, bf16[512,2048]{1,0:T(8,128)(2,1)S(1)}, u32[]{:S(2)}, u32[]{:S(2)}) collective-permute-start(bf16[512,2048]{1,0:T(8,128)(2,1)S(1)} %slice_bitcast_fusion), channel_id=1, source_target_pairs={{0,1},{1,0},{2,3},{3,2},{4,5},{5,4},{6,7},{7,6},{8,9},{9,8},{10,11... | collective-permute-start | bytes 6291464 | tf_op jit(solution)/shard_map/ppermute | solution.py:368
  161.6 3.8 %collective-permute-done.9.back_ref = bf16[512,2048]{1,0:T(8,128)(2,1)S(1)} collective-permute-done((bf16[512,2048]{1,0:T(8,128)(2,1)S(1)}, bf16[512,2048]{1,0:T(8,128)(2,1)S(1)}, u32[]{:S(2)}, u32[]{:S(2)}) %collective-permute-start.9) | collective-permute-done | bytes 2097184 | tf_op jit(solution)/shard_map/ppermute | solution.py:368
  165.4 0.0 copy-start.1
  165.4 1.3 copy-done.1
  166.7 4.4 %shard_map.68 = bf16[512,4096]{1,0:T(8,128)(2,1)} custom-call(s32[1]{0:T(128)} %bitcast.core_ref, bf16[2,512,2048]{2,1,0:T(8,128)(2,1)} %shard_map.67.own_ref, bf16[512,2048]{1,0:T(8,128)(2,1)} %copy-done.1), custom_call_target="tpu_custom_call" | custom-call | tf_op jit(solution)/shard_map/pallas_call | solution.py:330
  (4 shorter events, 0.1 us)
Async XLA Ops:
  5.6 11.9 %copy-start.3 = (s32[2,4,3]{2,1,0:T(4,128)S(1)}, s32[2,4,3]{2,1,0:T(4,128)}, u32[]{:S(2)}) copy-start(s32[2,4,3]{2,1,0:T(4,128)} %constant.44.clone) | copy-start | bytes 292
  5.6 19.6 %collective-permute-start.2 = (bf16[512,2048]{1,0:T(8,128)(2,1)}, bf16[512,2048]{1,0:T(8,128)(2,1)}, u32[]{:S(2)}, u32[]{:S(2)}) collective-permute-start(bf16[512,2048]{1,0:T(8,128)(2,1)} %get-tuple-element.19), channel_id=1, source_target_pairs={{0,1},{1,0},{2,3},{3,2},{4,5},{5,4},{6,7},{7,6},{8,9},{9,8},{10,11... | collective-permute-start | bytes 6291464 | tf_op jit(solution)/shard_map/ppermute | solution.py:350
  6.3 18.9 %collective-permute-start.3 = (bf16[512,1024]{1,0:T(8,128)(2,1)}, bf16[512,1024]{1,0:T(8,128)(2,1)}, u32[]{:S(2)}, u32[]{:S(2)}) collective-permute-start(bf16[512,1024]{1,0:T(8,128)(2,1)} %get-tuple-element.22), channel_id=1, source_target_pairs={{0,1},{1,0},{2,3},{3,2},{4,5},{5,4},{6,7},{7,6},{8,9},{9,8},{10,11... | collective-permute-start | bytes 3145736 | tf_op jit(solution)/shard_map/ppermute | solution.py:351
  6.3 22.0 %copy-start.4 = (f32[32]{0:T(128)S(1)}, f32[32]{0:T(128)}, u32[]{:S(2)}) copy-start(f32[32]{0:T(128)} %param.9) | copy-start | bytes 388
  13.4 24.8 %copy-start = (bf16[512,2048]{1,0:T(8,128)(2,1)S(1)}, bf16[512,2048]{1,0:T(8,128)(2,1)}, u32[]{:S(2)}) copy-start(bf16[512,2048]{1,0:T(8,128)(2,1)} %get-tuple-element.16) | copy-start | bytes 6291460
  14.5 1.7 collective-permute-start
  17.2 7.9 %collective-permute-start.1 = (f32[4,136,128]{2,1,0:T(8,128)S(1)}, f32[4,136,128]{2,1,0:T(8,128)S(1)}, u32[]{:S(2)}, u32[]{:S(2)}) collective-permute-start(f32[4,136,128]{2,1,0:T(8,128)S(1)} %dynamic-slice_add_fusion), channel_id=1, source_target_pairs={{0,2},{1,3},{2,0},{3,1},{4,6},{5,7},{6,4},{7,5},{8,10},{9,11},{10,... | collective-permute-start | bytes 835592 | tf_op jit(solution)/shard_map/ppermute | solution.py:104
  25.2 9.7 %collective-permute-start.6 = (f32[4,136,128]{2,1,0:T(8,128)S(1)}, f32[4,136,128]{2,1,0:T(8,128)S(1)}, u32[]{:S(2)}, u32[]{:S(2)}) collective-permute-start(f32[4,136,128]{2,1,0:T(8,128)S(1)} %add.47), channel_id=1, source_target_pairs={{0,4},{4,8},{8,12},{12,16},{16,20},{20,24},{24,28},{1,5},{5,9},{9,... | collective-permute-start | bytes 835592 | tf_op jit(solution)/shard_map/ppermute | solution.py:25
  29.6 58.5 %collective-permute-start.5 = (bf16[512,1024]{1,0:T(8,128)(2,1)}, bf16[512,1024]{1,0:T(8,128)(2,1)}, u32[]{:S(2)}, u32[]{:S(2)}) collective-permute-start(bf16[512,1024]{1,0:T(8,128)(2,1)} %get-tuple-element.22), channel_id=1, source_target_pairs={{0,3},{1,2},{4,7},{5,6},{8,11},{9,10},{12,15},{13,14},{16,19},{17,... | collective-permute-start | bytes 3145736 | tf_op jit(solution)/shard_map/ppermute | solution.py:360
  30.8 57.3 %collective-permute-start.4 = (bf16[512,1024]{1,0:T(8,128)(2,1)}, bf16[512,1024]{1,0:T(8,128)(2,1)}, u32[]{:S(2)}, u32[]{:S(2)}) collective-permute-start(bf16[512,1024]{1,0:T(8,128)(2,1)} %get-tuple-element.21), channel_id=1, source_target_pairs={{0,2},{1,3},{4,6},{5,7},{8,10},{9,11},{12,14},{13,15},{16,18},{17,... | collective-permute-start | bytes 3145736 | tf_op jit(solution)/shard_map/ppermute | solution.py:358
  35.0 10.1 %collective-permute-start.7 = (f32[4,136,128]{2,1,0:T(8,128)S(1)}, f32[4,136,128]{2,1,0:T(8,128)S(1)}, u32[]{:S(2)}, u32[]{:S(2)}) collective-permute-start(f32[4,136,128]{2,1,0:T(8,128)S(1)} %add.48), channel_id=1, source_target_pairs={{0,8},{4,12},{8,16},{12,20},{16,24},{20,28},{1,9},{5,13},{9,17},{1... | collective-permute-start | bytes 835592 | tf_op jit(solution)/shard_map/ppermute | solution.py:25
  38.2 4.1 %copy-start.2 = (bf16[512,1024]{1,0:T(8,128)(2,1)S(1)}, bf16[512,1024]{1,0:T(8,128)(2,1)}, u32[]{:S(2)}) copy-start(bf16[512,1024]{1,0:T(8,128)(2,1)} %get-tuple-element.21) | copy-start | bytes 3145732
  45.1 42.2 %collective-permute-start.8 = (f32[4,136,128]{2,1,0:T(8,128)S(1)}, f32[4,136,128]{2,1,0:T(8,128)S(1)}, u32[]{:S(2)}, u32[]{:S(2)}) collective-permute-start(f32[4,136,128]{2,1,0:T(8,128)S(1)} %add.49), channel_id=1, source_target_pairs={{0,16},{4,20},{8,24},{12,28},{1,17},{5,21},{9,25},{13,29},{2,18},{... | collective-permute-start | bytes 835592 | tf_op jit(solution)/shard_map/ppermute | solution.py:25
  158.5 6.9 %collective-permute-start.9 = (bf16[512,2048]{1,0:T(8,128)(2,1)S(1)}, bf16[512,2048]{1,0:T(8,128)(2,1)S(1)}, u32[]{:S(2)}, u32[]{:S(2)}) collective-permute-start(bf16[512,2048]{1,0:T(8,128)(2,1)S(1)} %slice_bitcast_fusion), channel_id=1, source_target_pairs={{0,1},{1,0},{2,3},{3,2},{4,5},{5,4},{6,7},{7,6},{8,9},{9,8},{10,11... | collective-permute-start | bytes 6291464 | tf_op jit(solution)/shard_map/ppermute | solution.py:368
  165.4 1.3 copy-start.1

commit v11 on v10

--- a/solution.py
+++ b/solution.py
@@ -120,30 +120,26 @@
     block = q_ref.shape[0]
     score_scale = HD ** (-0.5)
     key_rows = k_ref[...]
-    value_rows = v_ref[...]
+    value_rows = jnp.concatenate([v_ref[...], jnp.ones((block, LANES), v_ref.dtype)], axis=1)
     if masked:
         rows = lax.broadcasted_iota(jnp.int32, (block, block), 0)
         cols = lax.broadcasted_iota(jnp.int32, (block, block), 1)
         allowed = cols <= rows
     for head in range(group_size):
         lanes = slice(head * HD, (head + 1) * HD)
-        scores = (
-            lax.dot_general(
-                q_ref[:, lanes], key_rows, (((1,), (1,)), ((), ())),
-                preferred_element_type=jnp.float32,
-            )
-            * score_scale
+        scores = lax.dot_general(
+            q_ref[:, lanes], key_rows, (((1,), (1,)), ((), ())),
+            preferred_element_type=jnp.float32,
         )
         if masked:
             scores = jnp.where(allowed, scores, -1e30)
         m_prev = m_sc[head]
-        m_new = jnp.maximum(m_prev, jnp.max(scores, axis=-1, keepdims=True))
-        probs = jnp.exp(scores - m_new[:, :1])
+        m_new = jnp.maximum(m_prev, jnp.max(scores, axis=-1, keepdims=True) * score_scale)
+        probs = jnp.exp(scores * score_scale - m_new[:, :1])
         alpha = jnp.exp(m_prev - m_new)
-        l_sc[head] = alpha * l_sc[head] + jnp.sum(probs, axis=-1, keepdims=True)
-        acc_sc[:, lanes] = alpha * acc_sc[:, lanes] + jnp.dot(
-            probs.astype(jnp.bfloat16), value_rows, preferred_element_type=jnp.float32
-        )
+        both = jnp.dot(probs.astype(jnp.bfloat16), value_rows, preferred_element_type=jnp.float32)
+        l_sc[head] = alpha * l_sc[head] + both[:, HD:]
+        acc_sc[:, lanes] = alpha * acc_sc[:, lanes] + both[:, :HD]
         m_sc[head] = m_new
 
 

time: 173 us -> 156 us (0.902)
  Pallas kernels: 122 us -> 105 us
    pallas_call x1, Pallas kernels: 65.6 us -> 56.7 us  [attend(): pl.pallas_call(functools.partial(far_kernel, group_size=group_size), grid...]
    pallas_call x1, Pallas kernels: 39.7 us -> 31.7 us  [attend(): pl.pallas_call(functools.partial(near_kernel, group_size=group_size), gri...]
  transfers between devices with their start and end apart: 10 -> 10, of which waited for: 4 -> 4; matrix products, arithmetic and copies ran while one was open for 7% -> 8% of each run, Pallas kernels for 27% -> 25%
where the time goes in v11:
time: 156 us; the launch traced here: 154 us
  Pallas kernels  105 us (67%)
  starting transfers between devices  16.1 us (10%)
  waiting for transfers between devices  14.1 us (9%)
  other arithmetic  12.4 us (8%)
  local copies, waits for them, and re-layouts  6.09 us (4%)
    pallas_call x1, Pallas kernels, attend(): pl.pallas_call(functools.partial(far_kernel, group_size=group_size), grid...  56.7 us
    pallas_call x1, Pallas kernels, attend(): pl.pallas_call(functools.partial(near_kernel, group_size=group_size), gri...  31.7 us
    ppermute x3, starting transfers between devices, shifted(): lax.ppermute(value, axis, [(source, source + steps) for source in range(c...  8.83 us
    pallas_call x1, Pallas kernels, local_deltas(): pl.pallas_call(delta_kernel, grid=(kv_heads, 1), in_specs=[pl.BlockSpec((...  7.08 us
    ppermute x1, waiting for transfers between devices, chip_states(): lax.ppermute(total, 'head', [(p, p ^ steps) for p in range(parts)])  7.03 us
    pallas_call x1, Pallas kernels, split_inputs(): pl.pallas_call(split_kernel, grid_spec=grid_spec, out_shape=[q_shape, kv_...  5.57 us
    pallas_call x1, Pallas kernels, merge_halves(): pl.pallas_call(merge_kernel, grid_spec=grid_spec, out_shape=jax.ShapeDtyp...  4.37 us
    another operation x1, other arithmetic, body(): query_rows = jnp.stack([keep_q, recv_q])  4.08 us
  transfers between devices with their start and end apart: 10, of which 4 were waited for; matrix products, arithmetic and copies ran while one was open for 8% of the time, Pallas kernels for 25%

profile of v11, /device:TPU:13, one launch (start us, length us, event | category | flops | bytes accessed | tf_op | source)
XLA Modules:
  0.0 154.2 jit_solution(326795580275778687)
XLA Ops:
  0.0 5.6 %shard_map.64 = (bf16[512,2048]{1,0:T(8,128)(2,1)}, bf16[512,1024]{1,0:T(8,128)(2,1)}, bf16[512,2048]{1,0:T(8,128)(2,1)}, bf16[512,1024]{1,0:T(8,128)(2,1)}) custom-call(s32[1]{0:T(128)} %bitcast.core_ref, bf16[512,4096]{1,0:T(8,128)(2,1)} %q_send.1, bf16[512,1024]{1,0:T(8,128)(2,1)} %k_ref.1, bf16[512,1024]{1,0:T(8,128)(2,1)} %v_ref.1, ...), custom_call_target="tpu_custom_call" | custom-call | tf_op jit(solution)/shard_map/pallas_call | solution.py:64
  5.6 0.0 copy-start.3
  5.6 0.7 collective-permute-start.2
  6.3 0.1 collective-permute-start.3
  6.3 0.0 copy-start.4
  6.3 7.1 %shard_map.65 = f32[8,136,128]{2,1,0:T(8,128)} custom-call(bf16[512,1024]{1,0:T(8,128)(2,1)} %k_ref.1, bf16[512,1024]{1,0:T(8,128)(2,1)} %v_ref.1), custom_call_target="tpu_custom_call" | custom-call | tf_op jit(solution)/shard_map/pallas_call | solution.py:86
  13.4 0.0 copy-start
  13.4 1.1 constant_dynamic-slice_fusion.1
  14.5 0.5 collective-permute-start
  15.0 0.7 constant_dynamic-slice_fusion.2
  15.7 0.5 collective-permute-done
  16.2 1.0 dynamic-slice_add_fusion
  17.2 0.3 collective-permute-start.1
  17.5 0.0 copy-done.3
  17.5 0.6 slice_bitcast_fusion.1
  18.1 7.0 %collective-permute-done.1 = f32[4,136,128]{2,1,0:T(8,128)S(1)} collective-permute-done((f32[4,136,128]{2,1,0:T(8,128)S(1)}, f32[4,136,128]{2,1,0:T(8,128)S(1)}, u32[]{:S(2)}, u32[]{:S(2)}) %collective-permute-start.1) | collective-permute-done | bytes 278560 | tf_op jit(solution)/shard_map/ppermute | solution.py:104
  25.2 0.0 collective-permute-done.3
  25.2 0.0 collective-permute-done.2
  25.2 3.1 %collective-permute-start.6 = (f32[4,136,128]{2,1,0:T(8,128)S(1)}, f32[4,136,128]{2,1,0:T(8,128)S(1)}, u32[]{:S(2)}, u32[]{:S(2)}) collective-permute-start(f32[4,136,128]{2,1,0:T(8,128)S(1)} %add.47), channel_id=1, source_target_pairs={{0,4},{4,8},{8,12},{12,16},{16,20},{20,24},{24,28},{1,5},{5,9},{9,... | collective-permute-start | bytes 835592 | tf_op jit(solution)/shard_map/ppermute | solution.py:25
  28.3 0.0 copy-done.4
  28.4 0.6 add_divide_fusion.gate_ref
  29.0 0.6 slice_bitcast_fusion.5
  29.6 1.3 collective-permute-start.5
  30.8 1.3 collective-permute-start.4
  32.1 2.8 %collective-permute-done.6 = f32[4,136,128]{2,1,0:T(8,128)S(1)} collective-permute-done((f32[4,136,128]{2,1,0:T(8,128)S(1)}, f32[4,136,128]{2,1,0:T(8,128)S(1)}, u32[]{:S(2)}, u32[]{:S(2)}) %collective-permute-start.6) | collective-permute-done | bytes 278560 | tf_op jit(solution)/shard_map/ppermute | solution.py:25
  35.0 3.2 %collective-permute-start.7 = (f32[4,136,128]{2,1,0:T(8,128)S(1)}, f32[4,136,128]{2,1,0:T(8,128)S(1)}, u32[]{:S(2)}, u32[]{:S(2)}) collective-permute-start(f32[4,136,128]{2,1,0:T(8,128)S(1)} %add.48), channel_id=1, source_target_pairs={{0,8},{4,12},{8,16},{12,20},{16,24},{20,28},{1,9},{5,13},{9,17},{1... | collective-permute-start | bytes 835592 | tf_op jit(solution)/shard_map/ppermute | solution.py:25
  38.2 0.0 copy-done
  38.2 0.0 copy-start.2
  38.2 4.1 %pad_maximum_fusion.q_ref = bf16[2,512,2048]{2,1,0:T(8,128)(2,1)} fusion(bf16[1,512,2048]{2,1,0:T(8,128)(2,1)} %bitcast.7, bf16[1,512,2048]{2,1,0:T(8,128)(2,1)S(1)} %bitcast.27), kind=kLoop, calls=%fused_computation | loop fusion | flops 2097152 | bytes 8388608 | tf_op jit(solution)/shard_map/stack | solution.py:358
  42.3 0.0 copy-done.2
  42.3 2.8 %pad_maximum_fusion.2.k_ref.v_ref = bf16[2,512,1024]{2,1,0:T(8,128)(2,1)} fusion(bf16[1,512,1024]{2,1,0:T(8,128)(2,1)} %bitcast.15, bf16[1,512,1024]{2,1,0:T(8,128)(2,1)S(1)} %bitcast.28), kind=kLoop, calls=%fused_computation.3 | loop fusion | flops 1048576 | bytes 4194304 | tf_op jit(solution)/shard_map/stack | solution.py:359
  45.1 0.0 collective-permute-done.7
  45.1 2.5 %collective-permute-start.8 = (f32[4,136,128]{2,1,0:T(8,128)S(1)}, f32[4,136,128]{2,1,0:T(8,128)S(1)}, u32[]{:S(2)}, u32[]{:S(2)}) collective-permute-start(f32[4,136,128]{2,1,0:T(8,128)S(1)} %add.49), channel_id=1, source_target_pairs={{0,16},{4,20},{8,24},{12,28},{1,17},{5,21},{9,25},{13,29},{2,18},{... | collective-permute-start | bytes 835592 | tf_op jit(solution)/shard_map/ppermute | solution.py:25
  47.7 31.7 %shard_map.66 = (f32[2,512,2048]{2,1,0:T(8,128)}, f32[4,2,512,128]{3,2,1,0:T(8,128)}) custom-call(s32[3]{0:T(128)} %get-tuple-element.35.qp_ref, s32[3]{0:T(128)} %get-tuple-element.34.kp_ref, s32[3]{0:T(128)} %get-tuple-element.33.first_ref, s32[3]{0:T(128)} %get-tuple-element.32.diag_ref, bf16[2,512,2048]{2,1,0:T(8,128)(2,1)} %pad_maximum_fusion.q_ref, ...), custom_call_target="tpu_custom_call" | custom-call | flops 6442450944 | bytes 14680064 | tf_op jit(solution)/shard_map/pallas_call | solution.py:263
  79.4 0.0 collective-permute-done.8
  79.4 0.7 add_subtract_fusion.s_ref
  80.1 0.0 collective-permute-done.5
  80.1 0.0 collective-permute-done.4
  80.1 3.0 %pad_maximum_fusion.1.k_ref.v_ref = bf16[2,512,1024]{2,1,0:T(8,128)(2,1)} fusion(bf16[1,512,1024]{2,1,0:T(8,128)(2,1)} %bitcast.9, bf16[1,512,1024]{2,1,0:T(8,128)(2,1)} %bitcast.8), kind=kLoop, calls=%fused_computation.2 | loop fusion | flops 1048576 | bytes 4194304 | tf_op jit(solution)/shard_map/stack | solution.py:360
  83.2 56.7 %shard_map.67.own_ref = bf16[2,512,2048]{2,1,0:T(8,128)(2,1)} custom-call(s32[4]{0:T(128)} %get-tuple-element.31.qp_ref, s32[4]{0:T(128)} %get-tuple-element.30.kp_ref, s32[4]{0:T(128)} %get-tuple-element.29.first_ref, s32[4]{0:T(128)} %get-tuple-element.28.last_ref, s32[4]{0:T(128)} %get-tuple-element.27.valid_ref, f32[16]{0:T(128)} %add_divide_fusion.gate_ref, ...), custom_call_target="tpu_custom_call" | custom-call | flops 8589934592 | bytes 18874368 | tf_op jit(solution)/shard_map/pallas_call | solution.py:293
  139.8 1.7 %slice_bitcast_fusion = bf16[512,2048]{1,0:T(8,128)(2,1)S(1)} fusion(bf16[2,512,2048]{2,1,0:T(8,128)(2,1)} %shard_map.67.own_ref), kind=kLoop, calls=%fused_computation.1 | loop fusion | bytes 4194304 | tf_op jit(solution)/shard_map/squeeze | solution.py:364
  141.6 3.1 %collective-permute-start.9 = (bf16[512,2048]{1,0:T(8,128)(2,1)S(1)}, bf16[512,2048]{1,0:T(8,128)(2,1)S(1)}, u32[]{:S(2)}, u32[]{:S(2)}) collective-permute-start(bf16[512,2048]{1,0:T(8,128)(2,1)S(1)} %slice_bitcast_fusion), channel_id=1, source_target_pairs={{0,1},{1,0},{2,3},{3,2},{4,5},{5,4},{6,7},{7,6},{8,9},{9,8},{10,11... | collective-permute-start | bytes 6291464 | tf_op jit(solution)/shard_map/ppermute | solution.py:364
  144.7 3.8 %collective-permute-done.9.back_ref = bf16[512,2048]{1,0:T(8,128)(2,1)S(1)} collective-permute-done((bf16[512,2048]{1,0:T(8,128)(2,1)S(1)}, bf16[512,2048]{1,0:T(8,128)(2,1)S(1)}, u32[]{:S(2)}, u32[]{:S(2)}) %collective-permute-start.9) | collective-permute-done | bytes 2097184 | tf_op jit(solution)/shard_map/ppermute | solution.py:364
  148.5 0.0 copy-start.1
  148.5 1.3 copy-done.1
  149.8 4.4 %shard_map.68 = bf16[512,4096]{1,0:T(8,128)(2,1)} custom-call(s32[1]{0:T(128)} %bitcast.core_ref, bf16[2,512,2048]{2,1,0:T(8,128)(2,1)} %shard_map.67.own_ref, bf16[512,2048]{1,0:T(8,128)(2,1)} %copy-done.1), custom_call_target="tpu_custom_call" | custom-call | tf_op jit(solution)/shard_map/pallas_call | solution.py:326
  (4 shorter events, 0.1 us)
Async XLA Ops:
  5.6 11.9 %copy-start.3 = (s32[2,4,3]{2,1,0:T(4,128)S(1)}, s32[2,4,3]{2,1,0:T(4,128)}, u32[]{:S(2)}) copy-start(s32[2,4,3]{2,1,0:T(4,128)} %constant.44.clone) | copy-start | bytes 292
  5.6 19.6 %collective-permute-start.2 = (bf16[512,2048]{1,0:T(8,128)(2,1)}, bf16[512,2048]{1,0:T(8,128)(2,1)}, u32[]{:S(2)}, u32[]{:S(2)}) collective-permute-start(bf16[512,2048]{1,0:T(8,128)(2,1)} %get-tuple-element.19), channel_id=1, source_target_pairs={{0,1},{1,0},{2,3},{3,2},{4,5},{5,4},{6,7},{7,6},{8,9},{9,8},{10,11... | collective-permute-start | bytes 6291464 | tf_op jit(solution)/shard_map/ppermute | solution.py:346
  6.3 18.9 %collective-permute-start.3 = (bf16[512,1024]{1,0:T(8,128)(2,1)}, bf16[512,1024]{1,0:T(8,128)(2,1)}, u32[]{:S(2)}, u32[]{:S(2)}) collective-permute-start(bf16[512,1024]{1,0:T(8,128)(2,1)} %get-tuple-element.22), channel_id=1, source_target_pairs={{0,1},{1,0},{2,3},{3,2},{4,5},{5,4},{6,7},{7,6},{8,9},{9,8},{10,11... | collective-permute-start | bytes 3145736 | tf_op jit(solution)/shard_map/ppermute | solution.py:347
  6.3 22.0 %copy-start.4 = (f32[32]{0:T(128)S(1)}, f32[32]{0:T(128)}, u32[]{:S(2)}) copy-start(f32[32]{0:T(128)} %param.9) | copy-start | bytes 388
  13.4 24.8 %copy-start = (bf16[512,2048]{1,0:T(8,128)(2,1)S(1)}, bf16[512,2048]{1,0:T(8,128)(2,1)}, u32[]{:S(2)}) copy-start(bf16[512,2048]{1,0:T(8,128)(2,1)} %get-tuple-element.16) | copy-start | bytes 6291460
  14.5 1.7 %collective-permute-start = (f32[4,136,128]{2,1,0:T(8,128)S(1)}, f32[4,136,128]{2,1,0:T(8,128)S(1)}, u32[]{:S(2)}, u32[]{:S(2)}) collective-permute-start(f32[4,136,128]{2,1,0:T(8,128)S(1)} %constant_dynamic-slice_fusion.1), channel_id=1, source_target_pairs={{0,1},{1,0},{2,3},{3,2},{4,5},{5,4},{6,7},{7,6},{8,9},{9,8},{10,11... | collective-permute-start | bytes 835592 | tf_op jit(solution)/shard_map/ppermute | solution.py:101
  17.2 7.9 %collective-permute-start.1 = (f32[4,136,128]{2,1,0:T(8,128)S(1)}, f32[4,136,128]{2,1,0:T(8,128)S(1)}, u32[]{:S(2)}, u32[]{:S(2)}) collective-permute-start(f32[4,136,128]{2,1,0:T(8,128)S(1)} %dynamic-slice_add_fusion), channel_id=1, source_target_pairs={{0,2},{1,3},{2,0},{3,1},{4,6},{5,7},{6,4},{7,5},{8,10},{9,11},{10,... | collective-permute-start | bytes 835592 | tf_op jit(solution)/shard_map/ppermute | solution.py:104
  25.2 9.7 %collective-permute-start.6 = (f32[4,136,128]{2,1,0:T(8,128)S(1)}, f32[4,136,128]{2,1,0:T(8,128)S(1)}, u32[]{:S(2)}, u32[]{:S(2)}) collective-permute-start(f32[4,136,128]{2,1,0:T(8,128)S(1)} %add.47), channel_id=1, source_target_pairs={{0,4},{4,8},{8,12},{12,16},{16,20},{20,24},{24,28},{1,5},{5,9},{9,... | collective-permute-start | bytes 835592 | tf_op jit(solution)/shard_map/ppermute | solution.py:25
  29.6 50.6 %collective-permute-start.5 = (bf16[512,1024]{1,0:T(8,128)(2,1)}, bf16[512,1024]{1,0:T(8,128)(2,1)}, u32[]{:S(2)}, u32[]{:S(2)}) collective-permute-start(bf16[512,1024]{1,0:T(8,128)(2,1)} %get-tuple-element.22), channel_id=1, source_target_pairs={{0,3},{1,2},{4,7},{5,6},{8,11},{9,10},{12,15},{13,14},{16,19},{17,... | collective-permute-start | bytes 3145736 | tf_op jit(solution)/shard_map/ppermute | solution.py:356
  30.8 49.3 %collective-permute-start.4 = (bf16[512,1024]{1,0:T(8,128)(2,1)}, bf16[512,1024]{1,0:T(8,128)(2,1)}, u32[]{:S(2)}, u32[]{:S(2)}) collective-permute-start(bf16[512,1024]{1,0:T(8,128)(2,1)} %get-tuple-element.21), channel_id=1, source_target_pairs={{0,2},{1,3},{4,6},{5,7},{8,10},{9,11},{12,14},{13,15},{16,18},{17,... | collective-permute-start | bytes 3145736 | tf_op jit(solution)/shard_map/ppermute | solution.py:354
  35.0 10.1 %collective-permute-start.7 = (f32[4,136,128]{2,1,0:T(8,128)S(1)}, f32[4,136,128]{2,1,0:T(8,128)S(1)}, u32[]{:S(2)}, u32[]{:S(2)}) collective-permute-start(f32[4,136,128]{2,1,0:T(8,128)S(1)} %add.48), channel_id=1, source_target_pairs={{0,8},{4,12},{8,16},{12,20},{16,24},{20,28},{1,9},{5,13},{9,17},{1... | collective-permute-start | bytes 835592 | tf_op jit(solution)/shard_map/ppermute | solution.py:25
  38.2 4.1 %copy-start.2 = (bf16[512,1024]{1,0:T(8,128)(2,1)S(1)}, bf16[512,1024]{1,0:T(8,128)(2,1)}, u32[]{:S(2)}) copy-start(bf16[512,1024]{1,0:T(8,128)(2,1)} %get-tuple-element.21) | copy-start | bytes 3145732
  45.1 34.2 %collective-permute-start.8 = (f32[4,136,128]{2,1,0:T(8,128)S(1)}, f32[4,136,128]{2,1,0:T(8,128)S(1)}, u32[]{:S(2)}, u32[]{:S(2)}) collective-permute-start(f32[4,136,128]{2,1,0:T(8,128)S(1)} %add.49), channel_id=1, source_target_pairs={{0,16},{4,20},{8,24},{12,28},{1,17},{5,21},{9,25},{13,29},{2,18},{... | collective-permute-start | bytes 835592 | tf_op jit(solution)/shard_map/ppermute | solution.py:25
  141.6 6.9 %collective-permute-start.9 = (bf16[512,2048]{1,0:T(8,128)(2,1)S(1)}, bf16[512,2048]{1,0:T(8,128)(2,1)S(1)}, u32[]{:S(2)}, u32[]{:S(2)}) collective-permute-start(bf16[512,2048]{1,0:T(8,128)(2,1)S(1)} %slice_bitcast_fusion), channel_id=1, source_target_pairs={{0,1},{1,0},{2,3},{3,2},{4,5},{5,4},{6,7},{7,6},{8,9},{9,8},{10,11... | collective-permute-start | bytes 6291464 | tf_op jit(solution)/shard_map/ppermute | solution.py:364
  148.5 1.3 copy-start.1

commit v12 on v11

--- a/solution.py
+++ b/solution.py
@@ -67,29 +67,23 @@
 
 
 def delta_kernel(k_ref, v_ref, o_ref):
-    @pl.when(pl.program_id(1) == 0)
-    def _init():
-        o_ref[...] = jnp.zeros(o_ref.shape, jnp.float32)
-
-    key_feature = feature(k_ref[...].astype(jnp.float32))
-    value_data = v_ref[...].astype(jnp.float32)
-    o_ref[:HD, :] += jnp.dot(
-        key_feature.T, value_data, precision=lax.Precision.HIGHEST,
-        preferred_element_type=jnp.float32,
-    )
-    o_ref[HD : HD + 1, :] += jnp.sum(key_feature, axis=0, keepdims=True)
+    for head in range(o_ref.shape[0]):
+        lanes = slice(head * HD, (head + 1) * HD)
+        key_feature = feature(k_ref[:, lanes].astype(jnp.float32))
+        value_data = v_ref[:, lanes].astype(jnp.float32)
+        o_ref[head, :HD, :] = jnp.dot(
+            key_feature.T, value_data, precision=lax.Precision.HIGHEST,
+            preferred_element_type=jnp.float32,
+        )
+        o_ref[head, HD:, :] = jnp.zeros((STATE_ROWS - HD, HD), jnp.float32)
+        o_ref[head, HD : HD + 1, :] = jnp.sum(key_feature, axis=0, keepdims=True)
 
 
 def local_deltas(keys, values):
-    tokens_here, cols = keys.shape
-    kv_heads = cols // HD
+    kv_heads = keys.shape[1] // HD
     return pl.pallas_call(
         delta_kernel,
-        grid=(kv_heads, 1),
-        in_specs=[pl.BlockSpec((tokens_here, HD), lambda g, t: (0, g))] * 2,
-        out_specs=pl.BlockSpec((None, STATE_ROWS, HD), lambda g, t: (g, 0, 0)),
         out_shape=jax.ShapeDtypeStruct((kv_heads, STATE_ROWS, HD), jnp.float32),
-        compiler_params=pltpu.CompilerParams(dimension_semantics=("arbitrary", "arbitrary")),
     )(keys, values)
 
 
@@ -143,9 +137,12 @@
         m_sc[head] = m_new
 
 
-def near_kernel(qp_ref, kp_ref, first_ref, diag_ref, q_ref, k_ref, v_ref, acc_ref, ml_ref,
-                m_sc, l_sc, acc_sc, *, group_size):
+def near_kernel(qs_ref, ks_ref, first_ref, diag_ref, q_keep, q_recv, k_keep, v_keep, k_recv,
+                v_recv, acc_ref, ml_ref, m_sc, l_sc, acc_sc, *, group_size):
     step_at = pl.program_id(1)
+    q_src = qs_ref[step_at]
+    k_src = ks_ref[step_at]
+    diag = diag_ref[step_at] == 1
 
     @pl.when(first_ref[step_at] == 1)
     def _init():
@@ -153,13 +150,19 @@
         l_sc[...] = jnp.zeros(l_sc.shape, jnp.float32)
         acc_sc[...] = jnp.zeros(acc_sc.shape, jnp.float32)
 
-    @pl.when(diag_ref[step_at] == 0)
-    def _full():
-        online_step(q_ref, k_ref, v_ref, m_sc, l_sc, acc_sc, group_size, False)
-
-    @pl.when(diag_ref[step_at] == 1)
-    def _diag():
-        online_step(q_ref, k_ref, v_ref, m_sc, l_sc, acc_sc, group_size, True)
+    sources = ((q_keep, k_keep, v_keep), (q_recv, k_recv, v_recv))
+    for q_at in range(2):
+        for k_at in range(2):
+            masked = q_at == k_at
+
+            @pl.when((q_src == q_at) & (k_src == k_at) & (diag == masked))
+            def _step():
+                q_ref = sources[q_at][0]
+                online_step(q_ref, sources[k_at][1], sources[k_at][2], m_sc, l_sc, acc_sc,
+                            group_size, masked)
+
+    @pl.when(diag)
+    def _save():
         acc_ref[...] = acc_sc[...]
         lane = lax.broadcasted_iota(jnp.int32, ml_ref.shape, 1)
         packed = jnp.zeros(ml_ref.shape, jnp.float32)
@@ -169,8 +172,8 @@
         ml_ref[...] = packed
 
 
-def far_kernel(qp_ref, kp_ref, first_ref, last_ref, valid_ref, gate_ref, q_ref, k_ref, v_ref,
-               s_ref, acc_in, ml_in, o_ref, m_sc, l_sc, acc_sc, *, group_size):
+def far_kernel(qp_ref, kp_ref, first_ref, last_ref, valid_ref, gate_ref, q_keep, q_recv, k_ref,
+               v_ref, s_ref, acc_in, ml_in, o_ref, m_sc, l_sc, acc_sc, *, group_size):
     kv_head = pl.program_id(0)
     step_at = pl.program_id(1)
 
@@ -184,29 +187,36 @@
             )
         acc_sc[...] = acc_in[...]
 
-    @pl.when(valid_ref[step_at] == 1)
-    def _step():
-        online_step(q_ref, k_ref, v_ref, m_sc, l_sc, acc_sc, group_size, False)
-
-    @pl.when(last_ref[step_at] == 1)
-    def _last():
-        memory = s_ref[:HD, :]
-        normalizer = s_ref[HD : HD + 1, :]
-        for head in range(group_size):
-            lanes = slice(head * HD, (head + 1) * HD)
-            local_part = acc_sc[:, lanes] / l_sc[head]
-            query_feature = feature(q_ref[:, lanes].astype(jnp.float32))
-            numerator = jnp.dot(
-                query_feature, memory, precision=lax.Precision.HIGHEST,
-                preferred_element_type=jnp.float32,
-            )
-            denominator = jnp.maximum(
-                jnp.sum(query_feature * normalizer, axis=-1, keepdims=True), 1.0
-            )
-            mixing = gate_ref[kv_head * group_size + head]
-            o_ref[:, lanes] = (
-                mixing * (numerator / denominator) + (1.0 - mixing) * local_part
-            ).astype(o_ref.dtype)
+    for q_at, q_ref in enumerate((q_keep, q_recv)):
+        chosen = qp_ref[step_at] == q_at
+
+        @pl.when(chosen & (valid_ref[step_at] == 1))
+        def _step():
+            online_step(q_ref, k_ref, v_ref, m_sc, l_sc, acc_sc, group_size, False)
+
+        @pl.when(chosen & (last_ref[step_at] == 1))
+        def _last():
+            finish(q_ref, s_ref, gate_ref, o_ref, acc_sc, l_sc, kv_head, group_size)
+
+
+def finish(q_ref, s_ref, gate_ref, o_ref, acc_sc, l_sc, kv_head, group_size):
+    memory = s_ref[:HD, :]
+    normalizer = s_ref[HD : HD + 1, :]
+    for head in range(group_size):
+        lanes = slice(head * HD, (head + 1) * HD)
+        local_part = acc_sc[:, lanes] / l_sc[head]
+        query_feature = feature(q_ref[:, lanes].astype(jnp.float32))
+        numerator = jnp.dot(
+            query_feature, memory, precision=lax.Precision.HIGHEST,
+            preferred_element_type=jnp.float32,
+        )
+        denominator = jnp.maximum(
+            jnp.sum(query_feature * normalizer, axis=-1, keepdims=True), 1.0
+        )
+        mixing = gate_ref[kv_head * group_size + head]
+        o_ref[:, lanes] = (
+            mixing * (numerator / denominator) + (1.0 - mixing) * local_part
+        ).astype(o_ref.dtype)
 
 
 def near_tables(core):
@@ -233,9 +243,9 @@
     return jnp.asarray(tables)[chip, core]
 
 
-def attend(query_rows, near_kv, far_kv, state, mixing, chips, chip, core, group_size):
-    _, block, q_cols = query_rows.shape
-    kv_group = near_kv.shape[-1] // (2 * HD)
+def attend(keep_q, recv_q, keep_kv, recv_kv, far_kv, state, mixing, chips, chip, core, group_size):
+    block, q_cols = keep_q.shape
+    kv_group = keep_kv.shape[-1] // (2 * HD)
     width = group_size * HD
     scratch = [
         pltpu.VMEM((group_size, block, LANES), jnp.float32),
@@ -244,17 +254,16 @@
     ]
     params = pltpu.CompilerParams(dimension_semantics=("arbitrary", "arbitrary"))
     near = near_tables(core)
+    q_spec = pl.BlockSpec((block, width), lambda g, t, *_: (0, g))
+    k_spec = pl.BlockSpec((block, HD), lambda g, t, *_: (0, g))
+    v_spec = pl.BlockSpec((block, HD), lambda g, t, *_: (0, kv_group + g))
     near_spec = pltpu.PrefetchScalarGridSpec(
         num_scalar_prefetch=4,
         grid=(kv_group, near.shape[-1]),
-        in_specs=[
-            pl.BlockSpec((None, block, width), lambda g, t, qp, kp, f, d: (qp[t], 0, g)),
-            pl.BlockSpec((None, block, HD), lambda g, t, qp, kp, f, d: (kp[t], 0, g)),
-            pl.BlockSpec((None, block, HD), lambda g, t, qp, kp, f, d: (kp[t], 0, kv_group + g)),
-        ],
+        in_specs=[q_spec, q_spec, k_spec, v_spec, k_spec, v_spec],
         out_specs=[
-            pl.BlockSpec((None, block, width), lambda g, t, qp, kp, f, d: (qp[t], 0, g)),
-            pl.BlockSpec((None, None, block, LANES), lambda g, t, qp, kp, f, d: (g, qp[t], 0, 0)),
+            pl.BlockSpec((None, block, width), lambda g, t, qs, ks, f, d: (qs[t], 0, g)),
+            pl.BlockSpec((None, None, block, LANES), lambda g, t, qs, ks, f, d: (g, qs[t], 0, 0)),
         ],
         scratch_shapes=scratch,
     )
@@ -265,21 +274,22 @@
         grid_spec=near_spec,
         cost_estimate=pl.CostEstimate(
             flops=3 * pair_flops, transcendentals=3 * pair_exps,
-            bytes_accessed=int(query_rows.size * 6 + near_kv.size * 2),
+            bytes_accessed=int(keep_q.size * 12 + keep_kv.size * 4),
         ),
         out_shape=[
             jax.ShapeDtypeStruct((2, block, q_cols), jnp.float32),
             jax.ShapeDtypeStruct((kv_group, 2, block, LANES), jnp.float32),
         ],
         compiler_params=params,
-    )(*[near[i] for i in range(4)], query_rows, near_kv, near_kv)
+    )(*[near[i] for i in range(4)], keep_q, recv_q, keep_kv, keep_kv, recv_kv, recv_kv)
     far = far_tables(chips, chip, core)
     far_spec = pltpu.PrefetchScalarGridSpec(
         num_scalar_prefetch=5,
         grid=(kv_group, far.shape[-1]),
         in_specs=[
             pl.BlockSpec(memory_space=pltpu.SMEM),
-            pl.BlockSpec((None, block, width), lambda g, t, qp, kp, f, l, v: (qp[t], 0, g)),
+            q_spec,
+            q_spec,
             pl.BlockSpec((None, block, HD), lambda g, t, qp, kp, f, l, v: (kp[t], 0, g)),
             pl.BlockSpec((None, block, HD), lambda g, t, qp, kp, f, l, v: (kp[t], 0, kv_group + g)),
             pl.BlockSpec((None, STATE_ROWS, HD), lambda g, t, qp, kp, f, l, v: (g, 0, 0)),
@@ -295,11 +305,11 @@
         grid_spec=far_spec,
         cost_estimate=pl.CostEstimate(
             flops=far_pairs * pair_flops, transcendentals=far_pairs * pair_exps,
-            bytes_accessed=int(query_rows.size * 8 + far_kv.size * 2),
+            bytes_accessed=int(keep_q.size * 16 + far_kv.size * 2),
         ),
         out_shape=jax.ShapeDtypeStruct((2, block, q_cols), jnp.bfloat16),
         compiler_params=params,
-    )(*[far[i] for i in range(5)], mixing, query_rows, far_kv, far_kv, state, acc, ml)
+    )(*[far[i] for i in range(5)], mixing, keep_q, recv_q, far_kv, far_kv, state, acc, ml)
 
 
 def merge_kernel(core_ref, own_ref, back_ref, o_ref):
@@ -355,12 +365,12 @@
         kv_parts.append(
             lax.ppermute(send_kv, "head", [(p, (p + 2 * s) ^ 1) for p in range(parts - 2 * s)])
         )
-    query_rows = jnp.stack([keep_q, recv_q])
-    near_kv = jnp.stack([keep_kv, recv_kv])
-    far_kv = jnp.stack(kv_parts) if kv_parts else near_kv
+    far_kv = jnp.stack(kv_parts) if kv_parts else jnp.stack([keep_kv, recv_kv])
     gate_here = lax.dynamic_slice_in_dim(gate_logit, core * kv_group * group_size, kv_group * group_size)
     mixing = jax.nn.sigmoid(gate_here)
-    attended = attend(query_rows, near_kv, far_kv, state, mixing, chips, chip, core, group_size)
+    attended = attend(
+        keep_q, recv_q, keep_kv, recv_kv, far_kv, state, mixing, chips, chip, core, group_size
+    )
     back = lax.ppermute(attended[1], "head", sibling)
     return merge_halves(attended, back, core)
 

time: 156 us -> 159 us (1.019)
  waiting for transfers between devices: 14.1 us -> 27.6 us
  other arithmetic: 12.4 us -> 4.03 us
    ppermute x1, waiting for transfers between devices: 0.01 us -> 8.45 us  [body(): lax.ppermute(keep_kv, 'head', [(p, p + 2 * s) for p in range(parts - 2 *...]
    another operation x3 -> x1, other arithmetic: 9.92 us -> 1.52 us  [body(): far_kv = jnp.stack(kv_parts) if kv_parts else jnp.stack([keep_kv, recv_kv])]
    ppermute x3, waiting for transfers between devices: 2.81 us -> 6.87 us  [shifted(): lax.ppermute(value, axis, [(source, source + steps) for source in range(c...]
    ppermute x1, starting transfers between devices: 3.11 us -> 0.07 us  [body(): back = lax.ppermute(attended[1], 'head', sibling)]
    pallas_call x1, Pallas kernels: 7.08 us -> 4.49 us  [local_deltas(): pl.pallas_call(delta_kernel, out_shape=jax.ShapeDtypeStruct((kv_heads, ST...]
    ppermute x3, starting transfers between devices: 8.83 us -> 10.7 us  [shifted(): lax.ppermute(value, axis, [(source, source + steps) for source in range(c...]
  transfers between devices with their start and end apart: 10 -> 10, of which waited for: 4 -> 6; matrix products, arithmetic and copies ran while one was open for 8% -> 3% of each run, Pallas kernels for 25% -> 23%
where the time goes in v12:
time: 159 us; the launch traced here: 158 us
  Pallas kernels  104 us (65%)
  waiting for transfers between devices  27.6 us (17%)
  starting transfers between devices  14.9 us (9%)
  local copies, waits for them, and re-layouts  7.26 us (5%)
  other arithmetic  4.03 us (3%)
    pallas_call x1, Pallas kernels, attend(): pl.pallas_call(functools.partial(far_kernel, group_size=group_size), grid...  57.3 us
    pallas_call x1, Pallas kernels, attend(): pl.pallas_call(functools.partial(near_kernel, group_size=group_size), gri...  32.5 us
    ppermute x3, starting transfers between devices, shifted(): lax.ppermute(value, axis, [(source, source + steps) for source in range(c...  10.7 us
    ppermute x1, waiting for transfers between devices, body(): lax.ppermute(keep_kv, 'head', [(p, p + 2 * s) for p in range(parts - 2 *...  8.45 us
    ppermute x1, waiting for transfers between devices, chip_states(): lax.ppermute(total, 'head', [(p, p ^ steps) for p in range(parts)])  6.96 us
    ppermute x3, waiting for transfers between devices, shifted(): lax.ppermute(value, axis, [(source, source + steps) for source in range(c...  6.87 us
    pallas_call x1, Pallas kernels, split_inputs(): pl.pallas_call(split_kernel, grid_spec=grid_spec, out_shape=[q_shape, kv_...  5.55 us
    pallas_call x1, Pallas kernels, local_deltas(): pl.pallas_call(delta_kernel, out_shape=jax.ShapeDtypeStruct((kv_heads, ST...  4.49 us
  transfers between devices with their start and end apart: 10, of which 6 were waited for; matrix products, arithmetic and copies ran while one was open for 3% of the time, Pallas kernels for 23%

profile of v12, /device:TPU:13, one launch (start us, length us, event | category | flops | bytes accessed | tf_op | source)
XLA Modules:
  0.0 158.1 jit_solution(14723612551844734832)
XLA Ops:
  0.0 5.6 %shard_map.64 = (bf16[512,2048]{1,0:T(8,128)(2,1)}, bf16[512,1024]{1,0:T(8,128)(2,1)}, bf16[512,2048]{1,0:T(8,128)(2,1)}, bf16[512,1024]{1,0:T(8,128)(2,1)}) custom-call(s32[1]{0:T(128)} %bitcast.core_ref, bf16[512,4096]{1,0:T(8,128)(2,1)} %q_send.1, bf16[512,1024]{1,0:T(8,128)(2,1)} %k_ref.1, bf16[512,1024]{1,0:T(8,128)(2,1)} %v_ref.1, ...), custom_call_target="tpu_custom_call" | custom-call | tf_op jit(solution)/shard_map/pallas_call | solution.py:64
  5.6 0.7 collective-permute-start.2
  6.2 0.0 collective-permute-start.3
  6.2 0.0 copy-start.1
  6.2 4.5 %shard_map.65 = f32[8,136,128]{2,1,0:T(8,128)} custom-call(bf16[512,1024]{1,0:T(8,128)(2,1)} %k_ref.1, bf16[512,1024]{1,0:T(8,128)(2,1)} %v_ref.1), custom_call_target="tpu_custom_call" | custom-call | tf_op jit(solution)/shard_map/pallas_call | solution.py:84
  10.7 0.0 copy-start.3
  10.7 1.0 constant_dynamic-slice_fusion.1
  11.7 0.6 collective-permute-start
  12.3 1.2 collective-permute-done
  13.5 1.0 dynamic-slice_add_fusion
  14.5 0.3 collective-permute-start.1
  14.8 0.7 constant_dynamic-slice_fusion.2
  15.4 7.0 %collective-permute-done.1 = f32[4,136,128]{2,1,0:T(8,128)S(1)} collective-permute-done((f32[4,136,128]{2,1,0:T(8,128)S(1)}, f32[4,136,128]{2,1,0:T(8,128)S(1)}, u32[]{:S(2)}, u32[]{:S(2)}) %collective-permute-start.1) | collective-permute-done | bytes 278560 | tf_op jit(solution)/shard_map/ppermute | solution.py:98
  22.4 0.0 collective-permute-done.3.k_recv.v_recv
  22.5 0.0 collective-permute-done.2.q_recv
  22.5 0.0 copy-start.2
  22.5 1.3 copy-done.2
  23.8 3.1 %collective-permute-start.6 = (f32[4,136,128]{2,1,0:T(8,128)S(1)}, f32[4,136,128]{2,1,0:T(8,128)S(1)}, u32[]{:S(2)}, u32[]{:S(2)}) collective-permute-start(f32[4,136,128]{2,1,0:T(8,128)S(1)} %add.47), channel_id=1, source_target_pairs={{0,4},{4,8},{8,12},{12,16},{16,20},{20,24},{24,28},{1,5},{5,9},{9,... | collective-permute-start | bytes 835592 | tf_op jit(solution)/shard_map/ppermute | solution.py:25
  26.9 0.0 copy-done.1
  27.0 0.6 slice_bitcast_fusion.5
  27.6 6.0 %collective-permute-done.6 = f32[4,136,128]{2,1,0:T(8,128)S(1)} collective-permute-done((f32[4,136,128]{2,1,0:T(8,128)S(1)}, f32[4,136,128]{2,1,0:T(8,128)S(1)}, u32[]{:S(2)}, u32[]{:S(2)}) %collective-permute-start.6) | collective-permute-done | bytes 278560 | tf_op jit(solution)/shard_map/ppermute | solution.py:25
  33.6 3.2 %collective-permute-start.7 = (f32[4,136,128]{2,1,0:T(8,128)S(1)}, f32[4,136,128]{2,1,0:T(8,128)S(1)}, u32[]{:S(2)}, u32[]{:S(2)}) collective-permute-start(f32[4,136,128]{2,1,0:T(8,128)S(1)} %add.48), channel_id=1, source_target_pairs={{0,8},{4,12},{8,16},{12,20},{16,24},{20,28},{1,9},{5,13},{9,17},{1... | collective-permute-start | bytes 835592 | tf_op jit(solution)/shard_map/ppermute | solution.py:25
  36.8 0.0 copy-done.3
  36.8 0.7 add_divide_fusion.gate_ref
  37.5 1.3 collective-permute-start.5
  38.8 1.3 collective-permute-start.4
  40.1 0.6 slice_bitcast_fusion.1
  40.6 0.9 collective-permute-done.7
  41.5 4.4 %collective-permute-start.8 = (f32[4,136,128]{2,1,0:T(8,128)S(1)}, f32[4,136,128]{2,1,0:T(8,128)S(1)}, u32[]{:S(2)}, u32[]{:S(2)}) collective-permute-start(f32[4,136,128]{2,1,0:T(8,128)S(1)} %add.49), channel_id=1, source_target_pairs={{0,16},{4,20},{8,24},{12,28},{1,17},{5,21},{9,25},{13,29},{2,18},{... | collective-permute-start | bytes 835592 | tf_op jit(solution)/shard_map/ppermute | solution.py:25
  46.0 32.5 %shard_map.66 = (f32[2,512,2048]{2,1,0:T(8,128)}, f32[4,2,512,128]{3,2,1,0:T(8,128)}) custom-call(s32[3]{0:T(128)} %get-tuple-element.35.qs_ref, s32[3]{0:T(128)} %get-tuple-element.34.ks_ref, s32[3]{0:T(128)} %get-tuple-element.33.first_ref, s32[3]{0:T(128)} %get-tuple-element.32.diag_ref, bf16[512,2048]{1,0:T(8,128)(2,1)} %get-tuple-element.16.q_keep, ...), custom_call_target="tpu_custom_call" | custom-call | flops 6442450944 | bytes 14680064 | tf_op jit(solution)/shard_map/pallas_call | solution.py:272
  78.4 0.0 collective-permute-done.8
  78.4 0.8 add_subtract_fusion.s_ref
  79.2 0.0 collective-permute-done.5
  79.2 8.5 %collective-permute-done.4 = bf16[512,1024]{1,0:T(8,128)(2,1)S(1)} collective-permute-done((bf16[512,1024]{1,0:T(8,128)(2,1)}, bf16[512,1024]{1,0:T(8,128)(2,1)S(1)}, u32[]{:S(2)}, u32[]{:S(2)}) %collective-permute-start.4) | collective-permute-done | bytes 1048608 | tf_op jit(solution)/shard_map/ppermute | solution.py:364
  87.6 1.5 pad_maximum_fusion.k_ref.v_ref
  89.2 57.3 %shard_map.67.own_ref = bf16[2,512,2048]{2,1,0:T(8,128)(2,1)} custom-call(s32[4]{0:T(128)} %get-tuple-element.31.qp_ref, s32[4]{0:T(128)} %get-tuple-element.30.kp_ref, s32[4]{0:T(128)} %get-tuple-element.29.first_ref, s32[4]{0:T(128)} %get-tuple-element.28.last_ref, s32[4]{0:T(128)} %get-tuple-element.27.valid_ref, f32[16]{0:T(128)} %add_divide_fusion.gate_ref, ...), custom_call_target="tpu_custom_call" | custom-call | flops 8589934592 | bytes 18874368 | tf_op jit(solution)/shard_map/pallas_call | solution.py:303
  146.4 1.7 %slice_bitcast_fusion = bf16[512,2048]{1,0:T(8,128)(2,1)S(1)} fusion(bf16[2,512,2048]{2,1,0:T(8,128)(2,1)} %shard_map.67.own_ref), kind=kLoop, calls=%fused_computation | loop fusion | bytes 4194304 | tf_op jit(solution)/shard_map/squeeze | solution.py:374
  148.2 0.1 collective-permute-start.9
  148.2 4.1 %collective-permute-done.9.back_ref = bf16[512,2048]{1,0:T(8,128)(2,1)S(1)} collective-permute-done((bf16[512,2048]{1,0:T(8,128)(2,1)S(1)}, bf16[512,2048]{1,0:T(8,128)(2,1)S(1)}, u32[]{:S(2)}, u32[]{:S(2)}) %collective-permute-start.9) | collective-permute-done | bytes 2097184 | tf_op jit(solution)/shard_map/ppermute | solution.py:374
  152.4 0.0 copy-start
  152.4 1.3 copy-done
  153.7 4.4 %shard_map.68 = bf16[512,4096]{1,0:T(8,128)(2,1)} custom-call(s32[1]{0:T(128)} %bitcast.core_ref, bf16[2,512,2048]{2,1,0:T(8,128)(2,1)} %shard_map.67.own_ref, bf16[512,2048]{1,0:T(8,128)(2,1)} %copy-done), custom_call_target="tpu_custom_call" | custom-call | tf_op jit(solution)/shard_map/pallas_call | solution.py:336
  (4 shorter events, 0.1 us)
Async XLA Ops:
  5.6 16.9 %collective-permute-start.2 = (bf16[512,2048]{1,0:T(8,128)(2,1)}, bf16[512,2048]{1,0:T(8,128)(2,1)S(1)}, u32[]{:S(2)}, u32[]{:S(2)}) collective-permute-start(bf16[512,2048]{1,0:T(8,128)(2,1)} %get-tuple-element.19), channel_id=1, source_target_pairs={{0,1},{1,0},{2,3},{3,2},{4,5},{5,4},{6,7},{7,6},{8,9},{9,8},{10,11... | collective-permute-start | bytes 6291464 | tf_op jit(solution)/shard_map/ppermute | solution.py:356
  6.2 16.2 %collective-permute-start.3 = (bf16[512,1024]{1,0:T(8,128)(2,1)}, bf16[512,1024]{1,0:T(8,128)(2,1)}, u32[]{:S(2)}, u32[]{:S(2)}) collective-permute-start(bf16[512,1024]{1,0:T(8,128)(2,1)} %get-tuple-element.22), channel_id=1, source_target_pairs={{0,1},{1,0},{2,3},{3,2},{4,5},{5,4},{6,7},{7,6},{8,9},{9,8},{10,11... | collective-permute-start | bytes 3145736 | tf_op jit(solution)/shard_map/ppermute | solution.py:357
  6.2 20.7 %copy-start.1 = (s32[2,4,3]{2,1,0:T(4,128)S(1)}, s32[2,4,3]{2,1,0:T(4,128)}, u32[]{:S(2)}) copy-start(s32[2,4,3]{2,1,0:T(4,128)} %constant.44.clone) | copy-start | bytes 292
  10.7 26.1 %copy-start.3 = (f32[32]{0:T(128)S(1)}, f32[32]{0:T(128)}, u32[]{:S(2)}) copy-start(f32[32]{0:T(128)} %param.9) | copy-start | bytes 388
  11.7 1.8 %collective-permute-start = (f32[4,136,128]{2,1,0:T(8,128)S(1)}, f32[4,136,128]{2,1,0:T(8,128)S(1)}, u32[]{:S(2)}, u32[]{:S(2)}) collective-permute-start(f32[4,136,128]{2,1,0:T(8,128)S(1)} %constant_dynamic-slice_fusion.1), channel_id=1, source_target_pairs={{0,1},{1,0},{2,3},{3,2},{4,5},{5,4},{6,7},{7,6},{8,9},{9,8},{10,11... | collective-permute-start | bytes 835592 | tf_op jit(solution)/shard_map/ppermute | solution.py:95
  14.5 7.9 %collective-permute-start.1 = (f32[4,136,128]{2,1,0:T(8,128)S(1)}, f32[4,136,128]{2,1,0:T(8,128)S(1)}, u32[]{:S(2)}, u32[]{:S(2)}) collective-permute-start(f32[4,136,128]{2,1,0:T(8,128)S(1)} %dynamic-slice_add_fusion), channel_id=1, source_target_pairs={{0,2},{1,3},{2,0},{3,1},{4,6},{5,7},{6,4},{7,5},{8,10},{9,11},{10,... | collective-permute-start | bytes 835592 | tf_op jit(solution)/shard_map/ppermute | solution.py:98
  22.5 1.3 copy-start.2
  23.8 9.7 %collective-permute-start.6 = (f32[4,136,128]{2,1,0:T(8,128)S(1)}, f32[4,136,128]{2,1,0:T(8,128)S(1)}, u32[]{:S(2)}, u32[]{:S(2)}) collective-permute-start(f32[4,136,128]{2,1,0:T(8,128)S(1)} %add.47), channel_id=1, source_target_pairs={{0,4},{4,8},{8,12},{12,16},{16,20},{20,24},{24,28},{1,5},{5,9},{9,... | collective-permute-start | bytes 835592 | tf_op jit(solution)/shard_map/ppermute | solution.py:25
  33.6 7.9 %collective-permute-start.7 = (f32[4,136,128]{2,1,0:T(8,128)S(1)}, f32[4,136,128]{2,1,0:T(8,128)S(1)}, u32[]{:S(2)}, u32[]{:S(2)}) collective-permute-start(f32[4,136,128]{2,1,0:T(8,128)S(1)} %add.48), channel_id=1, source_target_pairs={{0,8},{4,12},{8,16},{12,20},{16,24},{20,28},{1,9},{5,13},{9,17},{1... | collective-permute-start | bytes 835592 | tf_op jit(solution)/shard_map/ppermute | solution.py:25
  37.5 41.7 %collective-permute-start.5 = (bf16[512,1024]{1,0:T(8,128)(2,1)}, bf16[512,1024]{1,0:T(8,128)(2,1)S(1)}, u32[]{:S(2)}, u32[]{:S(2)}) collective-permute-start(bf16[512,1024]{1,0:T(8,128)(2,1)} %get-tuple-element.22), channel_id=1, source_target_pairs={{0,3},{1,2},{4,7},{5,6},{8,11},{9,10},{12,15},{13,14},{16,19},{17,... | collective-permute-start | bytes 3145736 | tf_op jit(solution)/shard_map/ppermute | solution.py:366
  38.8 48.9 %collective-permute-start.4 = (bf16[512,1024]{1,0:T(8,128)(2,1)}, bf16[512,1024]{1,0:T(8,128)(2,1)S(1)}, u32[]{:S(2)}, u32[]{:S(2)}) collective-permute-start(bf16[512,1024]{1,0:T(8,128)(2,1)} %get-tuple-element.21.k_keep.v_keep), channel_id=1, source_target_pairs={{0,2},{1,3},{4,6},{5,7},{8,10},{9,11},{12,14},{13,15},{16,18},{17,... | collective-permute-start | bytes 3145736 | tf_op jit(solution)/shard_map/ppermute | solution.py:364
  41.5 36.9 %collective-permute-start.8 = (f32[4,136,128]{2,1,0:T(8,128)S(1)}, f32[4,136,128]{2,1,0:T(8,128)S(1)}, u32[]{:S(2)}, u32[]{:S(2)}) collective-permute-start(f32[4,136,128]{2,1,0:T(8,128)S(1)} %add.49), channel_id=1, source_target_pairs={{0,16},{4,20},{8,24},{12,28},{1,17},{5,21},{9,25},{13,29},{2,18},{... | collective-permute-start | bytes 835592 | tf_op jit(solution)/shard_map/ppermute | solution.py:25
  148.2 4.2 %collective-permute-start.9 = (bf16[512,2048]{1,0:T(8,128)(2,1)S(1)}, bf16[512,2048]{1,0:T(8,128)(2,1)S(1)}, u32[]{:S(2)}, u32[]{:S(2)}) collective-permute-start(bf16[512,2048]{1,0:T(8,128)(2,1)S(1)} %slice_bitcast_fusion), channel_id=1, source_target_pairs={{0,1},{1,0},{2,3},{3,2},{4,5},{5,4},{6,7},{7,6},{8,9},{9,8},{10,11... | collective-permute-start | bytes 6291464 | tf_op jit(solution)/shard_map/ppermute | solution.py:374
  152.4 1.3 copy-start

commit v13 on v12

--- a/solution.py
+++ b/solution.py
@@ -172,7 +172,7 @@
         ml_ref[...] = packed
 
 
-def far_kernel(qp_ref, kp_ref, first_ref, last_ref, valid_ref, gate_ref, q_keep, q_recv, k_ref,
+def far_kernel(qp_ref, kp_ref, first_ref, last_ref, valid_ref, off_ref, gate_ref, q_keep, q_recv, k_ref,
                v_ref, s_ref, acc_in, ml_in, o_ref, m_sc, l_sc, acc_sc, *, group_size):
     kv_head = pl.program_id(0)
     step_at = pl.program_id(1)
@@ -226,19 +226,18 @@
     return jnp.asarray(tables)[core]
 
 
-def far_tables(chips, chip, core):
+def far_tables(chips, chip, core, source):
     per_block = max(1, 2 * (chips - 1))
-    tables = np.zeros((chips, 2, 5, 2 * per_block), np.int32)
+    tables = np.zeros((chips, 2, 5, per_block), np.int32)
     for y in range(chips):
         for c in range(2):
             steps = []
-            for a in range(2):
-                k_pos = 0
-                for j in range(per_block):
-                    valid = int(j < 2 * y)
-                    if valid:
-                        k_pos = 2 * (chips - 1 - y + j // 2) + ((j % 2) ^ c)
-                    steps.append((a ^ c, k_pos, int(j == 0), int(j == per_block - 1), valid))
+            k_pos = 0
+            for j in range(per_block):
+                valid = int(j < 2 * y)
+                if valid:
+                    k_pos = 2 * (chips - 1 - y + j // 2) + ((j % 2) ^ c)
+                steps.append((source, k_pos, int(j == 0), int(j == per_block - 1), valid))
             tables[y, c] = np.array(steps, np.int32).T
     return jnp.asarray(tables)[chip, core]
 
@@ -282,62 +281,71 @@
         ],
         compiler_params=params,
     )(*[near[i] for i in range(4)], keep_q, recv_q, keep_kv, keep_kv, recv_kv, recv_kv)
-    far = far_tables(chips, chip, core)
-    far_spec = pltpu.PrefetchScalarGridSpec(
-        num_scalar_prefetch=5,
-        grid=(kv_group, far.shape[-1]),
-        in_specs=[
-            pl.BlockSpec(memory_space=pltpu.SMEM),
-            q_spec,
-            q_spec,
-            pl.BlockSpec((None, block, HD), lambda g, t, qp, kp, f, l, v: (kp[t], 0, g)),
-            pl.BlockSpec((None, block, HD), lambda g, t, qp, kp, f, l, v: (kp[t], 0, kv_group + g)),
-            pl.BlockSpec((None, STATE_ROWS, HD), lambda g, t, qp, kp, f, l, v: (g, 0, 0)),
-            pl.BlockSpec((None, block, width), lambda g, t, qp, kp, f, l, v: (qp[t], 0, g)),
-            pl.BlockSpec((None, None, block, LANES), lambda g, t, qp, kp, f, l, v: (g, qp[t], 0, 0)),
-        ],
-        out_specs=pl.BlockSpec((None, block, width), lambda g, t, qp, kp, f, l, v: (qp[t], 0, g)),
-        scratch_shapes=scratch,
-    )
-    far_pairs = far.shape[-1]
-    return pl.pallas_call(
-        functools.partial(far_kernel, group_size=group_size),
-        grid_spec=far_spec,
-        cost_estimate=pl.CostEstimate(
-            flops=far_pairs * pair_flops, transcendentals=far_pairs * pair_exps,
-            bytes_accessed=int(keep_q.size * 16 + far_kv.size * 2),
-        ),
-        out_shape=jax.ShapeDtypeStruct((2, block, q_cols), jnp.bfloat16),
-        compiler_params=params,
-    )(*[far[i] for i in range(5)], mixing, keep_q, recv_q, far_kv, far_kv, state, acc, ml)
-
-
-def merge_kernel(core_ref, own_ref, back_ref, o_ref):
-    @pl.when(pl.program_id(0) == core_ref[0])
-    def _own():
-        o_ref[...] = own_ref[...]
-
-    @pl.when(pl.program_id(0) != core_ref[0])
-    def _back():
-        o_ref[...] = back_ref[...]
-
-
-def merge_halves(own, back, core):
+    far_pairs = max(1, 2 * (chips - 1))
+
+    def far_call(source, out_cols, col_offset):
+        far = far_tables(chips, chip, core, source)
+        offset = jnp.reshape(col_offset, (1,)).astype(jnp.int32)
+        far_spec = pltpu.PrefetchScalarGridSpec(
+            num_scalar_prefetch=6,
+            grid=(kv_group, far.shape[-1]),
+            in_specs=[
+                pl.BlockSpec(memory_space=pltpu.SMEM),
+                q_spec,
+                q_spec,
+                pl.BlockSpec((None, block, HD), lambda g, t, qp, kp, f, l, v, o: (kp[t], 0, g)),
+                pl.BlockSpec(
+                    (None, block, HD), lambda g, t, qp, kp, f, l, v, o: (kp[t], 0, kv_group + g)
+                ),
+                pl.BlockSpec((None, STATE_ROWS, HD), lambda g, t, qp, kp, f, l, v, o: (g, 0, 0)),
+                pl.BlockSpec((None, block, width), lambda g, t, qp, kp, f, l, v, o: (qp[t], 0, g)),
+                pl.BlockSpec(
+                    (None, None, block, LANES), lambda g, t, qp, kp, f, l, v, o: (g, qp[t], 0, 0)
+                ),
+            ],
+            out_specs=pl.BlockSpec((block, width), lambda g, t, qp, kp, f, l, v, o: (0, o[0] + g)),
+            scratch_shapes=scratch,
+        )
+        return pl.pallas_call(
+            functools.partial(far_kernel, group_size=group_size),
+            grid_spec=far_spec,
+            cost_estimate=pl.CostEstimate(
+                flops=far_pairs * pair_flops // 2, transcendentals=far_pairs * pair_exps // 2,
+                bytes_accessed=int(keep_q.size * 8 + far_kv.size * 2),
+            ),
+            out_shape=jax.ShapeDtypeStruct((block, out_cols), jnp.bfloat16),
+            compiler_params=params,
+        )(*[far[i] for i in range(5)], offset, mixing, keep_q, recv_q, far_kv, far_kv, state, acc, ml)
+
+    sibling_part = far_call(1, q_cols, 0)
+    back = lax.ppermute(sibling_part, "head", [(p, p ^ 1) for p in range(lax.axis_size("head"))])
+    own_part = far_call(0, 2 * q_cols, core * kv_group)
+    return own_part, back
+
+
+def place_kernel(col_ref, full_ref, back_ref, o_ref):
+    o_ref[...] = back_ref[...]
+
+
+def place_back(own_part, back, core, kv_group):
     tokens_here, q_cols = back.shape
+    width = q_cols // kv_group
+    other = jnp.reshape((1 - core) * kv_group, (1,)).astype(jnp.int32)
     grid_spec = pltpu.PrefetchScalarGridSpec(
         num_scalar_prefetch=1,
-        grid=(2,),
+        grid=(kv_group,),
         in_specs=[
-            pl.BlockSpec((None, tokens_here, q_cols), lambda h, c: (0, 0, 0)),
-            pl.BlockSpec((tokens_here, q_cols), lambda h, c: (0, 0)),
+            pl.BlockSpec(memory_space=pl.ANY),
+            pl.BlockSpec((tokens_here, width), lambda g, c: (0, g)),
         ],
-        out_specs=pl.BlockSpec((tokens_here, q_cols), lambda h, c: (0, h)),
+        out_specs=pl.BlockSpec((tokens_here, width), lambda g, c: (0, c[0] + g)),
     )
     return pl.pallas_call(
-        merge_kernel,
+        place_kernel,
         grid_spec=grid_spec,
-        out_shape=jax.ShapeDtypeStruct((tokens_here, 2 * q_cols), back.dtype),
-    )(core.reshape(1), own, back)
+        out_shape=jax.ShapeDtypeStruct(own_part.shape, own_part.dtype),
+        input_output_aliases={1: 0},
+    )(other, own_part, back)
 
 
 def body(queries, keys, values, gate_logit):
@@ -368,11 +376,10 @@
     far_kv = jnp.stack(kv_parts) if kv_parts else jnp.stack([keep_kv, recv_kv])
     gate_here = lax.dynamic_slice_in_dim(gate_logit, core * kv_group * group_size, kv_group * group_size)
     mixing = jax.nn.sigmoid(gate_here)
-    attended = attend(
+    own_part, back = attend(
         keep_q, recv_q, keep_kv, recv_kv, far_kv, state, mixing, chips, chip, core, group_size
     )
-    back = lax.ppermute(attended[1], "head", sibling)
-    return merge_halves(attended, back, core)
+    return place_back(own_part, back, core, kv_group)
 
 
 def solution(mesh):

time: 159 us -> 156 us (0.981)
  waiting for transfers between devices: 27.6 us -> 23.6 us
  Pallas kernels: 104 us -> 107 us
  local copies, waits for them, and re-layouts: 7.26 us -> 4.86 us
    ppermute x1, waiting for transfers between devices: 4.15 us -> 0.01 us  [attend(): lax.ppermute(sibling_part, 'head', [(p, p ^ 1) for p in range(lax.axis_si...]
    pallas_call x2 -> x3, Pallas kernels: 61.6 us -> 64.3 us  [the longest x2 60.5 us: far_call(): pl.pallas_call(functools.partial(far_kernel, group_size=group_size), grid...]
  transfers between devices with their start and end apart: 10 -> 10, of which waited for: 6 -> 5; matrix products, arithmetic and copies ran while one was open for 3% -> 4% of each run, Pallas kernels for 23% -> 43%
where the time goes in v13:
time: 156 us
  Pallas kernels  107 us (69%)
  waiting for transfers between devices  23.6 us (15%)
  starting transfers between devices  14.9 us (10%)
  other arithmetic  5.55 us (4%)
  local copies, waits for them, and re-layouts  4.86 us (3%)
    pallas_call x2, Pallas kernels, far_call(): pl.pallas_call(functools.partial(far_kernel, group_size=group_size), grid...  60.5 us
    pallas_call x1, Pallas kernels, attend(): pl.pallas_call(functools.partial(near_kernel, group_size=group_size), gri...  32.4 us
    ppermute x3, starting transfers between devices, shifted(): lax.ppermute(value, axis, [(source, source + steps) for source in range(c...  10.7 us
    ppermute x1, waiting for transfers between devices, body(): lax.ppermute(keep_kv, 'head', [(p, p + 2 * s) for p in range(parts - 2 *...  8.55 us
    ppermute x1, waiting for transfers between devices, chip_states(): lax.ppermute(total, 'head', [(p, p ^ steps) for p in range(parts)])  6.94 us
    ppermute x3, waiting for transfers between devices, shifted(): lax.ppermute(value, axis, [(source, source + steps) for source in range(c...  6.87 us
    pallas_call x1, Pallas kernels, split_inputs(): pl.pallas_call(split_kernel, grid_spec=grid_spec, out_shape=[q_shape, kv_...  5.56 us
    pallas_call x1, Pallas kernels, local_deltas(): pl.pallas_call(delta_kernel, out_shape=jax.ShapeDtypeStruct((kv_heads, ST...  4.48 us
  transfers between devices with their start and end apart: 10, of which 5 were waited for; matrix products, arithmetic and copies ran while one was open for 4% of the time, Pallas kernels for 43%

profile of v13, /device:TPU:13, one launch (start us, length us, event | category | flops | bytes accessed | tf_op | source)
XLA Modules:
  0.0 155.7 jit_solution(4965048265908050562)
XLA Ops:
  0.0 5.6 %shard_map.73 = (bf16[512,2048]{1,0:T(8,128)(2,1)}, bf16[512,1024]{1,0:T(8,128)(2,1)}, bf16[512,2048]{1,0:T(8,128)(2,1)}, bf16[512,1024]{1,0:T(8,128)(2,1)}) custom-call(s32[1]{0:T(128)} %bitcast.7.core_ref, bf16[512,4096]{1,0:T(8,128)(2,1)} %q_send.1, bf16[512,1024]{1,0:T(8,128)(2,1)} %k_ref.1, bf16[512,1024]{1,0:T(8,128)(2,1)} %v_ref.1, ...), custom_call_target="tpu_custom_call" | custom-call | tf_op jit(solution)/shard_map/pallas_call | solution.py:64
  5.6 0.7 collective-permute-start.2
  6.2 0.0 collective-permute-start.3
  6.2 0.0 copy-start.2
  6.2 4.5 %shard_map.74 = f32[8,136,128]{2,1,0:T(8,128)} custom-call(bf16[512,1024]{1,0:T(8,128)(2,1)} %k_ref.1, bf16[512,1024]{1,0:T(8,128)(2,1)} %v_ref.1), custom_call_target="tpu_custom_call" | custom-call | tf_op jit(solution)/shard_map/pallas_call | solution.py:84
  10.7 0.0 copy-start.3
  10.7 1.0 constant_dynamic-slice_fusion.2
  11.7 0.6 collective-permute-start
  12.3 1.2 collective-permute-done
  13.5 1.0 dynamic-slice_add_fusion
  14.5 0.3 collective-permute-start.1
  14.8 0.7 constant_dynamic-slice_fusion
  15.5 6.9 %collective-permute-done.1 = f32[4,136,128]{2,1,0:T(8,128)S(1)} collective-permute-done((f32[4,136,128]{2,1,0:T(8,128)S(1)}, f32[4,136,128]{2,1,0:T(8,128)S(1)}, u32[]{:S(2)}, u32[]{:S(2)}) %collective-permute-start.1) | collective-permute-done | bytes 278560 | tf_op jit(solution)/shard_map/ppermute | solution.py:98
  22.4 0.0 collective-permute-done.3.k_recv.v_recv
  22.4 0.0 collective-permute-done.2.q_recv
  22.5 0.0 copy-start
  22.5 3.1 %collective-permute-start.6 = (f32[4,136,128]{2,1,0:T(8,128)S(1)}, f32[4,136,128]{2,1,0:T(8,128)S(1)}, u32[]{:S(2)}, u32[]{:S(2)}) collective-permute-start(f32[4,136,128]{2,1,0:T(8,128)S(1)} %add.49), channel_id=1, source_target_pairs={{0,4},{4,8},{8,12},{12,16},{16,20},{20,24},{24,28},{1,5},{5,9},{9,... | collective-permute-start | bytes 835592 | tf_op jit(solution)/shard_map/ppermute | solution.py:25
  25.6 0.0 copy-done.2
  25.6 0.6 slice_bitcast_fusion
  26.2 6.0 %collective-permute-done.6 = f32[4,136,128]{2,1,0:T(8,128)S(1)} collective-permute-done((f32[4,136,128]{2,1,0:T(8,128)S(1)}, f32[4,136,128]{2,1,0:T(8,128)S(1)}, u32[]{:S(2)}, u32[]{:S(2)}) %collective-permute-start.6) | collective-permute-done | bytes 278560 | tf_op jit(solution)/shard_map/ppermute | solution.py:25
  32.2 3.2 %collective-permute-start.7 = (f32[4,136,128]{2,1,0:T(8,128)S(1)}, f32[4,136,128]{2,1,0:T(8,128)S(1)}, u32[]{:S(2)}, u32[]{:S(2)}) collective-permute-start(f32[4,136,128]{2,1,0:T(8,128)S(1)} %add.50), channel_id=1, source_target_pairs={{0,8},{4,12},{8,16},{12,20},{16,24},{20,28},{1,9},{5,13},{9,17},{1... | collective-permute-start | bytes 835592 | tf_op jit(solution)/shard_map/ppermute | solution.py:25
  35.5 0.0 copy-done.3
  35.5 0.6 add_divide_fusion.gate_ref
  36.1 1.3 collective-permute-start.5
  37.4 1.3 collective-permute-start.4
  38.7 0.6 slice_bitcast_fusion.5
  39.3 0.9 collective-permute-done.7
  40.2 4.4 %collective-permute-start.8 = (f32[4,136,128]{2,1,0:T(8,128)S(1)}, f32[4,136,128]{2,1,0:T(8,128)S(1)}, u32[]{:S(2)}, u32[]{:S(2)}) collective-permute-start(f32[4,136,128]{2,1,0:T(8,128)S(1)} %add.51), channel_id=1, source_target_pairs={{0,16},{4,20},{8,24},{12,28},{1,17},{5,21},{9,25},{13,29},{2,18},{... | collective-permute-start | bytes 835592 | tf_op jit(solution)/shard_map/ppermute | solution.py:25
  44.6 0.0 copy-done
  44.6 32.4 %shard_map.75 = (f32[2,512,2048]{2,1,0:T(8,128)}, f32[4,2,512,128]{3,2,1,0:T(8,128)}) custom-call(s32[3]{0:T(128)} %get-tuple-element.40.qs_ref, s32[3]{0:T(128)} %get-tuple-element.39.ks_ref, s32[3]{0:T(128)} %get-tuple-element.38.first_ref, s32[3]{0:T(128)} %get-tuple-element.37.diag_ref, bf16[512,2048]{1,0:T(8,128)(2,1)} %get-tuple-element.16.q_keep, ...), custom_call_target="tpu_custom_call" | custom-call | flops 6442450944 | bytes 14680064 | tf_op jit(solution)/shard_map/pallas_call | solution.py:271
  77.1 0.0 collective-permute-done.8
  77.1 0.8 add_subtract_fusion.s_ref
  77.8 0.0 collective-permute-done.5
  77.8 8.5 %collective-permute-done.4 = bf16[512,1024]{1,0:T(8,128)(2,1)} collective-permute-done((bf16[512,1024]{1,0:T(8,128)(2,1)}, bf16[512,1024]{1,0:T(8,128)(2,1)}, u32[]{:S(2)}, u32[]{:S(2)}) %collective-permute-start.4) | collective-permute-done | bytes 1048608 | tf_op jit(solution)/shard_map/ppermute | solution.py:372
  86.4 3.1 %pad_maximum_fusion.k_ref.v_ref = bf16[2,512,1024]{2,1,0:T(8,128)(2,1)} fusion(bf16[1,512,1024]{2,1,0:T(8,128)(2,1)} %bitcast.9, bf16[1,512,1024]{2,1,0:T(8,128)(2,1)} %bitcast.8), kind=kLoop, calls=%fused_computation | loop fusion | flops 1048576 | bytes 4194304 | tf_op jit(solution)/shard_map/stack | solution.py:376
  89.5 30.3 %shard_map.77 = bf16[512,2048]{1,0:T(8,128)(2,1)} custom-call(s32[2]{0:T(128)} %get-tuple-element.31.qp_ref, s32[2]{0:T(128)} %get-tuple-element.30.kp_ref, s32[2]{0:T(128)} %get-tuple-element.29.first_ref, s32[2]{0:T(128)} %get-tuple-element.28.last_ref, s32[2]{0:T(128)} %get-tuple-element.27.valid_ref, s32[1]{0:T(128)} %constant.47.clone.1.off_ref, ...), custom_call_target="tpu_custom_call" | custom-call | flops 2147483648 | bytes 10485760 | tf_op jit(solution)/shard_map/pallas_call | solution.py:309
  119.7 0.0 collective-permute-start.9
  119.7 0.6 slice_bitcast_fusion.9
  120.3 30.3 %shard_map.76.full_ref = bf16[512,4096]{1,0:T(8,128)(2,1)} custom-call(s32[2]{0:T(128)} %get-tuple-element.36.qp_ref, s32[2]{0:T(128)} %get-tuple-element.35.kp_ref, s32[2]{0:T(128)} %get-tuple-element.34.first_ref, s32[2]{0:T(128)} %get-tuple-element.33.last_ref, s32[2]{0:T(128)} %get-tuple-element.32.valid_ref, s32[1]{0:T(128)} %bitcast.6.off_ref, ...), custom_call_target="tpu_custom_call" | custom-call | flops 2147483648 | bytes 10485760 | tf_op jit(solution)/shard_map/pallas_call | solution.py:309
  150.6 0.0 collective-permute-done.9.back_ref
  150.6 0.0 copy-start.1
  150.6 1.3 copy-done.1
  152.0 3.8 %shard_map.78 = bf16[512,4096]{1,0:T(8,128)(2,1)} custom-call(s32[1]{0:T(128)} %bitcast.col_ref, bf16[512,4096]{1,0:T(8,128)(2,1)} %shard_map.76.full_ref, bf16[512,2048]{1,0:T(8,128)(2,1)} %copy-done.1), custom_call_target="tpu_custom_call", output_to_operand_aliasing={{}: (1, {})} | custom-call | tf_op jit(solution)/shard_map/pallas_call | solution.py:343
  (4 shorter events, 0.1 us)
Async XLA Ops:
  5.6 16.9 %collective-permute-start.2 = (bf16[512,2048]{1,0:T(8,128)(2,1)}, bf16[512,2048]{1,0:T(8,128)(2,1)S(1)}, u32[]{:S(2)}, u32[]{:S(2)}) collective-permute-start(bf16[512,2048]{1,0:T(8,128)(2,1)} %get-tuple-element.19), channel_id=1, source_target_pairs={{0,1},{1,0},{2,3},{3,2},{4,5},{5,4},{6,7},{7,6},{8,9},{9,8},{10,11... | collective-permute-start | bytes 6291464 | tf_op jit(solution)/shard_map/ppermute | solution.py:364
  6.2 16.2 %collective-permute-start.3 = (bf16[512,1024]{1,0:T(8,128)(2,1)}, bf16[512,1024]{1,0:T(8,128)(2,1)}, u32[]{:S(2)}, u32[]{:S(2)}) collective-permute-start(bf16[512,1024]{1,0:T(8,128)(2,1)} %get-tuple-element.22), channel_id=1, source_target_pairs={{0,1},{1,0},{2,3},{3,2},{4,5},{5,4},{6,7},{7,6},{8,9},{9,8},{10,11... | collective-permute-start | bytes 3145736 | tf_op jit(solution)/shard_map/ppermute | solution.py:365
  6.2 19.4 %copy-start.2 = (s32[2,4,3]{2,1,0:T(4,128)S(1)}, s32[2,4,3]{2,1,0:T(4,128)}, u32[]{:S(2)}) copy-start(s32[2,4,3]{2,1,0:T(4,128)} %constant.48.clone) | copy-start | bytes 292
  10.7 24.7 %copy-start.3 = (f32[32]{0:T(128)S(1)}, f32[32]{0:T(128)}, u32[]{:S(2)}) copy-start(f32[32]{0:T(128)} %param.10) | copy-start | bytes 388
  11.7 1.8 %collective-permute-start = (f32[4,136,128]{2,1,0:T(8,128)S(1)}, f32[4,136,128]{2,1,0:T(8,128)S(1)}, u32[]{:S(2)}, u32[]{:S(2)}) collective-permute-start(f32[4,136,128]{2,1,0:T(8,128)S(1)} %constant_dynamic-slice_fusion.2), channel_id=1, source_target_pairs={{0,1},{1,0},{2,3},{3,2},{4,5},{5,4},{6,7},{7,6},{8,9},{9,8},{10,11... | collective-permute-start | bytes 835592 | tf_op jit(solution)/shard_map/ppermute | solution.py:95
  14.5 7.9 %collective-permute-start.1 = (f32[4,136,128]{2,1,0:T(8,128)S(1)}, f32[4,136,128]{2,1,0:T(8,128)S(1)}, u32[]{:S(2)}, u32[]{:S(2)}) collective-permute-start(f32[4,136,128]{2,1,0:T(8,128)S(1)} %dynamic-slice_add_fusion), channel_id=1, source_target_pairs={{0,2},{1,3},{2,0},{3,1},{4,6},{5,7},{6,4},{7,5},{8,10},{9,11},{10,... | collective-permute-start | bytes 835592 | tf_op jit(solution)/shard_map/ppermute | solution.py:98
  22.5 22.2 %copy-start = (bf16[512,2048]{1,0:T(8,128)(2,1)}, bf16[512,2048]{1,0:T(8,128)(2,1)S(1)}, u32[]{:S(2)}) copy-start(bf16[512,2048]{1,0:T(8,128)(2,1)S(1)} %collective-permute-done.2.q_recv) | copy-start | bytes 6291460
  22.5 9.7 %collective-permute-start.6 = (f32[4,136,128]{2,1,0:T(8,128)S(1)}, f32[4,136,128]{2,1,0:T(8,128)S(1)}, u32[]{:S(2)}, u32[]{:S(2)}) collective-permute-start(f32[4,136,128]{2,1,0:T(8,128)S(1)} %add.49), channel_id=1, source_target_pairs={{0,4},{4,8},{8,12},{12,16},{16,20},{20,24},{24,28},{1,5},{5,9},{9,... | collective-permute-start | bytes 835592 | tf_op jit(solution)/shard_map/ppermute | solution.py:25
  32.2 7.9 %collective-permute-start.7 = (f32[4,136,128]{2,1,0:T(8,128)S(1)}, f32[4,136,128]{2,1,0:T(8,128)S(1)}, u32[]{:S(2)}, u32[]{:S(2)}) collective-permute-start(f32[4,136,128]{2,1,0:T(8,128)S(1)} %add.50), channel_id=1, source_target_pairs={{0,8},{4,12},{8,16},{12,20},{16,24},{20,28},{1,9},{5,13},{9,17},{1... | collective-permute-start | bytes 835592 | tf_op jit(solution)/shard_map/ppermute | solution.py:25
  36.1 41.7 %collective-permute-start.5 = (bf16[512,1024]{1,0:T(8,128)(2,1)}, bf16[512,1024]{1,0:T(8,128)(2,1)}, u32[]{:S(2)}, u32[]{:S(2)}) collective-permute-start(bf16[512,1024]{1,0:T(8,128)(2,1)} %get-tuple-element.22), channel_id=1, source_target_pairs={{0,3},{1,2},{4,7},{5,6},{8,11},{9,10},{12,15},{13,14},{16,19},{17,... | collective-permute-start | bytes 3145736 | tf_op jit(solution)/shard_map/ppermute | solution.py:374
  37.4 49.0 %collective-permute-start.4 = (bf16[512,1024]{1,0:T(8,128)(2,1)}, bf16[512,1024]{1,0:T(8,128)(2,1)}, u32[]{:S(2)}, u32[]{:S(2)}) collective-permute-start(bf16[512,1024]{1,0:T(8,128)(2,1)} %get-tuple-element.21.k_keep.v_keep), channel_id=1, source_target_pairs={{0,2},{1,3},{4,6},{5,7},{8,10},{9,11},{12,14},{13,15},{16,18},{17,... | collective-permute-start | bytes 3145736 | tf_op jit(solution)/shard_map/ppermute | solution.py:372
  40.2 36.9 %collective-permute-start.8 = (f32[4,136,128]{2,1,0:T(8,128)S(1)}, f32[4,136,128]{2,1,0:T(8,128)S(1)}, u32[]{:S(2)}, u32[]{:S(2)}) collective-permute-start(f32[4,136,128]{2,1,0:T(8,128)S(1)} %add.51), channel_id=1, source_target_pairs={{0,16},{4,20},{8,24},{12,28},{1,17},{5,21},{9,25},{13,29},{2,18},{... | collective-permute-start | bytes 835592 | tf_op jit(solution)/shard_map/ppermute | solution.py:25
  119.7 30.9 %collective-permute-start.9 = (bf16[512,2048]{1,0:T(8,128)(2,1)}, bf16[512,2048]{1,0:T(8,128)(2,1)S(1)}, u32[]{:S(2)}, u32[]{:S(2)}) collective-permute-start(bf16[512,2048]{1,0:T(8,128)(2,1)} %shard_map.77), channel_id=1, source_target_pairs={{0,1},{1,0},{2,3},{3,2},{4,5},{5,4},{6,7},{7,6},{8,9},{9,8},{10,11... | collective-permute-start | bytes 6291464 | tf_op jit(solution)/shard_map/ppermute | solution.py:321
  150.6 1.3 copy-start.1

commit v14 on v13

--- a/solution.py
+++ b/solution.py
@@ -92,10 +92,11 @@
     parts = lax.axis_size("head")
     keep = lax.dynamic_slice_in_dim(total, core * kv_group, kv_group)
     send = lax.dynamic_slice_in_dim(total, (1 - core) * kv_group, kv_group)
-    total = keep + lax.ppermute(send, "head", [(p, p ^ 1) for p in range(parts)])
+    total = keep + lax.ppermute(send.astype(jnp.bfloat16), "head", [(p, p ^ 1) for p in range(parts)])
     steps = 2
     while steps < parts:
-        total = total + lax.ppermute(total, "head", [(p, p ^ steps) for p in range(parts)])
+        across = lax.ppermute(total.astype(jnp.bfloat16), "head", [(p, p ^ steps) for p in range(parts)])
+        total = total + across
         steps *= 2
     return total
 
@@ -105,7 +106,7 @@
     total = delta
     steps = 1
     while steps < count:
-        total = total + shifted(total, "seq", steps)
+        total = total + shifted(total.astype(jnp.bfloat16), "seq", steps)
         steps *= 2
     return total - delta
 

time: 156 us -> 152 us (0.974)
  waiting for transfers between devices: 23.6 us -> 19.3 us
    ppermute x3, waiting for transfers between devices: 6.87 us -> 2.96 us  [shifted(): lax.ppermute(value, axis, [(source, source + steps) for source in range(c...]
    ppermute x2, waiting for transfers between devices: 8.12 us -> 4.96 us  [the longest x1 3.96 us: chip_states(): lax.ppermute(total.astype(jnp.bfloat16), 'head', [(p, p ^ steps) for p in...]
    ppermute x1, waiting for transfers between devices: 8.55 us -> 11.4 us  [body(): lax.ppermute(keep_kv, 'head', [(p, p + 2 * s) for p in range(parts - 2 *...]
  transfers between devices with their start and end apart: 10 -> 10, of which waited for: 5 -> 4; matrix products, arithmetic and copies ran while one was open for 4% -> 5% of each run, Pallas kernels for 43% -> 44%
where the time goes in v14:
time: 152 us; the launch traced here: 151 us
  Pallas kernels  107 us (70%)
  waiting for transfers between devices  19.3 us (13%)
  starting transfers between devices  13.6 us (9%)
  other arithmetic  6.59 us (4%)
  local copies, waits for them, and re-layouts  4.84 us (3%)
    pallas_call x2, Pallas kernels, far_call(): pl.pallas_call(functools.partial(far_kernel, group_size=group_size), grid...  60.5 us
    pallas_call x1, Pallas kernels, attend(): pl.pallas_call(functools.partial(near_kernel, group_size=group_size), gri...  32.4 us
    ppermute x1, waiting for transfers between devices, body(): lax.ppermute(keep_kv, 'head', [(p, p + 2 * s) for p in range(parts - 2 *...  11.4 us
    ppermute x3, starting transfers between devices, shifted(): lax.ppermute(value, axis, [(source, source + steps) for source in range(c...  9.5 us
    pallas_call x1, Pallas kernels, split_inputs(): pl.pallas_call(split_kernel, grid_spec=grid_spec, out_shape=[q_shape, kv_...  5.56 us
    pallas_call x1, Pallas kernels, local_deltas(): pl.pallas_call(delta_kernel, out_shape=jax.ShapeDtypeStruct((kv_heads, ST...  4.49 us
    ppermute x1, waiting for transfers between devices, chip_states(): lax.ppermute(total.astype(jnp.bfloat16), 'head', [(p, p ^ steps) for p in...  3.96 us
    pallas_call x1, Pallas kernels, place_back(): pl.pallas_call(place_kernel, grid_spec=grid_spec, out_shape=jax.ShapeDtyp...  3.78 us
  transfers between devices with their start and end apart: 10, of which 4 were waited for; matrix products, arithmetic and copies ran while one was open for 5% of the time, Pallas kernels for 44%

profile of v14, /device:TPU:13, one launch (start us, length us, event | category | flops | bytes accessed | tf_op | source)
XLA Modules:
  0.0 151.3 jit_solution(13064291948008330487)
XLA Ops:
  0.0 5.6 %shard_map.73 = (bf16[512,2048]{1,0:T(8,128)(2,1)}, bf16[512,1024]{1,0:T(8,128)(2,1)}, bf16[512,2048]{1,0:T(8,128)(2,1)}, bf16[512,1024]{1,0:T(8,128)(2,1)}) custom-call(s32[1]{0:T(128)} %bitcast.7.core_ref, bf16[512,4096]{1,0:T(8,128)(2,1)} %q_send.1, bf16[512,1024]{1,0:T(8,128)(2,1)} %k_ref.1, bf16[512,1024]{1,0:T(8,128)(2,1)} %v_ref.1, ...), custom_call_target="tpu_custom_call" | custom-call | tf_op jit(solution)/shard_map/pallas_call | solution.py:64
  5.6 0.7 collective-permute-start.2
  6.2 0.0 collective-permute-start.3
  6.2 0.0 copy-start.2
  6.2 0.0 copy-start.3
  6.2 4.5 %shard_map.74 = f32[8,136,128]{2,1,0:T(8,128)} custom-call(bf16[512,1024]{1,0:T(8,128)(2,1)} %k_ref.1, bf16[512,1024]{1,0:T(8,128)(2,1)} %v_ref.1), custom_call_target="tpu_custom_call" | custom-call | tf_op jit(solution)/shard_map/pallas_call | solution.py:84
  10.7 1.0 dynamic-slice_convert_fusion
  11.7 0.6 collective-permute-start
  12.3 1.0 collective-permute-done
  13.3 1.0 fusion.2
  14.3 0.3 collective-permute-start.1
  14.6 0.7 constant_dynamic-slice_fusion
  15.3 4.0 %collective-permute-done.1 = bf16[4,136,128]{2,1,0:T(8,128)(2,1)S(1)} collective-permute-done((bf16[4,136,128]{2,1,0:T(8,128)(2,1)S(1)}, bf16[4,136,128]{2,1,0:T(8,128)(2,1)S(1)}, u32[]{:S(2)}, u32[]{:S(2)}) %collective-permute-start.1) | collective-permute-done | bytes 139296 | tf_op jit(solution)/shard_map/ppermute | solution.py:98
  19.2 1.0 convert_add_fusion.2
  20.2 0.0 collective-permute-done.3.k_recv.v_recv
  20.2 0.0 collective-permute-done.2.q_recv
  20.3 0.0 copy-start
  20.3 3.1 %collective-permute-start.6 = (bf16[4,136,128]{2,1,0:T(8,128)(2,1)S(1)}, bf16[4,136,128]{2,1,0:T(8,128)(2,1)S(1)}, u32[]{:S(2)}, u32[]{:S(2)}) collective-permute-start(bf16[4,136,128]{2,1,0:T(8,128)(2,1)S(1)} %convert_element_type.34), channel_id=1, source_target_pairs={{0,4},{4,8},{8,12},{12,16},{16,20},{20,24},{24,28},{1,5},{5,9},{9,... | collective-permute-start | bytes 417800 | tf_op jit(solution)/shard_map/ppermute | solution.py:25
  23.4 0.6 slice_bitcast_fusion
  24.0 0.0 copy-done.2
  24.0 3.0 %collective-permute-done.6 = bf16[4,136,128]{2,1,0:T(8,128)(2,1)S(1)} collective-permute-done((bf16[4,136,128]{2,1,0:T(8,128)(2,1)S(1)}, bf16[4,136,128]{2,1,0:T(8,128)(2,1)S(1)}, u32[]{:S(2)}, u32[]{:S(2)}) %collective-permute-start.6) | collective-permute-done | bytes 139296 | tf_op jit(solution)/shard_map/ppermute | solution.py:25
  27.0 3.2 %collective-permute-start.7 = (bf16[4,136,128]{2,1,0:T(8,128)(2,1)S(1)}, bf16[4,136,128]{2,1,0:T(8,128)(2,1)S(1)}, u32[]{:S(2)}, u32[]{:S(2)}) collective-permute-start(bf16[4,136,128]{2,1,0:T(8,128)(2,1)S(1)} %fusion), channel_id=1, source_target_pairs={{0,8},{4,12},{8,16},{12,20},{16,24},{20,28},{1,9},{5,13},{9,17},{1... | collective-permute-start | bytes 417800 | tf_op jit(solution)/shard_map/ppermute | solution.py:25
  30.2 0.6 slice_bitcast_fusion.5
  30.8 0.0 copy-done.3
  30.8 0.6 add_divide_fusion.gate_ref
  31.5 1.3 collective-permute-start.5
  32.7 1.3 collective-permute-start.4
  34.0 0.0 collective-permute-done.7
  34.1 0.1 fusion.1
  34.1 3.2 %collective-permute-start.8 = (bf16[4,136,128]{2,1,0:T(8,128)(2,1)S(1)}, bf16[4,136,128]{2,1,0:T(8,128)(2,1)S(1)}, u32[]{:S(2)}, u32[]{:S(2)}) collective-permute-start(bf16[4,136,128]{2,1,0:T(8,128)(2,1)S(1)} %fusion.1), channel_id=1, source_target_pairs={{0,16},{4,20},{8,24},{12,28},{1,17},{5,21},{9,25},{13,29},{2,18},{... | collective-permute-start | bytes 417800 | tf_op jit(solution)/shard_map/ppermute | solution.py:25
  37.3 0.0 copy-done
  37.3 32.4 %shard_map.75 = (f32[2,512,2048]{2,1,0:T(8,128)}, f32[4,2,512,128]{3,2,1,0:T(8,128)}) custom-call(s32[3]{0:T(128)} %get-tuple-element.40.qs_ref, s32[3]{0:T(128)} %get-tuple-element.39.ks_ref, s32[3]{0:T(128)} %get-tuple-element.38.first_ref, s32[3]{0:T(128)} %get-tuple-element.37.diag_ref, bf16[512,2048]{1,0:T(8,128)(2,1)} %get-tuple-element.16.q_keep, ...), custom_call_target="tpu_custom_call" | custom-call | flops 6442450944 | bytes 14680064 | tf_op jit(solution)/shard_map/pallas_call | solution.py:272
  69.7 0.0 collective-permute-done.8
  69.7 0.8 add_subtract_fusion.s_ref
  70.5 0.0 collective-permute-done.5
  70.5 11.4 %collective-permute-done.4 = bf16[512,1024]{1,0:T(8,128)(2,1)} collective-permute-done((bf16[512,1024]{1,0:T(8,128)(2,1)}, bf16[512,1024]{1,0:T(8,128)(2,1)}, u32[]{:S(2)}, u32[]{:S(2)}) %collective-permute-start.4) | collective-permute-done | bytes 1048608 | tf_op jit(solution)/shard_map/ppermute | solution.py:373
  82.0 3.1 %pad_maximum_fusion.k_ref.v_ref = bf16[2,512,1024]{2,1,0:T(8,128)(2,1)} fusion(bf16[1,512,1024]{2,1,0:T(8,128)(2,1)} %bitcast.9, bf16[1,512,1024]{2,1,0:T(8,128)(2,1)} %bitcast.8), kind=kLoop, calls=%fused_computation | loop fusion | flops 1048576 | bytes 4194304 | tf_op jit(solution)/shard_map/stack | solution.py:377
  85.0 30.3 %shard_map.77 = bf16[512,2048]{1,0:T(8,128)(2,1)} custom-call(s32[2]{0:T(128)} %get-tuple-element.31.qp_ref, s32[2]{0:T(128)} %get-tuple-element.30.kp_ref, s32[2]{0:T(128)} %get-tuple-element.29.first_ref, s32[2]{0:T(128)} %get-tuple-element.28.last_ref, s32[2]{0:T(128)} %get-tuple-element.27.valid_ref, s32[1]{0:T(128)} %constant.47.clone.1.off_ref, ...), custom_call_target="tpu_custom_call" | custom-call | flops 2147483648 | bytes 10485760 | tf_op jit(solution)/shard_map/pallas_call | solution.py:310
  115.3 0.0 collective-permute-start.9
  115.3 0.6 slice_bitcast_fusion.9
  115.9 30.3 %shard_map.76.full_ref = bf16[512,4096]{1,0:T(8,128)(2,1)} custom-call(s32[2]{0:T(128)} %get-tuple-element.36.qp_ref, s32[2]{0:T(128)} %get-tuple-element.35.kp_ref, s32[2]{0:T(128)} %get-tuple-element.34.first_ref, s32[2]{0:T(128)} %get-tuple-element.33.last_ref, s32[2]{0:T(128)} %get-tuple-element.32.valid_ref, s32[1]{0:T(128)} %bitcast.6.off_ref, ...), custom_call_target="tpu_custom_call" | custom-call | flops 2147483648 | bytes 10485760 | tf_op jit(solution)/shard_map/pallas_call | solution.py:310
  146.2 0.0 collective-permute-done.9.back_ref
  146.2 0.0 copy-start.1
  146.2 1.3 copy-done.1
  147.5 3.8 %shard_map.78 = bf16[512,4096]{1,0:T(8,128)(2,1)} custom-call(s32[1]{0:T(128)} %bitcast.col_ref, bf16[512,4096]{1,0:T(8,128)(2,1)} %shard_map.76.full_ref, bf16[512,2048]{1,0:T(8,128)(2,1)} %copy-done.1), custom_call_target="tpu_custom_call", output_to_operand_aliasing={{}: (1, {})} | custom-call | tf_op jit(solution)/shard_map/pallas_call | solution.py:344
  (3 shorter events, 0.1 us)
Async XLA Ops:
  5.6 14.7 %collective-permute-start.2 = (bf16[512,2048]{1,0:T(8,128)(2,1)}, bf16[512,2048]{1,0:T(8,128)(2,1)S(1)}, u32[]{:S(2)}, u32[]{:S(2)}) collective-permute-start(bf16[512,2048]{1,0:T(8,128)(2,1)} %get-tuple-element.19), channel_id=1, source_target_pairs={{0,1},{1,0},{2,3},{3,2},{4,5},{5,4},{6,7},{7,6},{8,9},{9,8},{10,11... | collective-permute-start | bytes 6291464 | tf_op jit(solution)/shard_map/ppermute | solution.py:365
  6.2 14.0 %collective-permute-start.3 = (bf16[512,1024]{1,0:T(8,128)(2,1)}, bf16[512,1024]{1,0:T(8,128)(2,1)}, u32[]{:S(2)}, u32[]{:S(2)}) collective-permute-start(bf16[512,1024]{1,0:T(8,128)(2,1)} %get-tuple-element.22), channel_id=1, source_target_pairs={{0,1},{1,0},{2,3},{3,2},{4,5},{5,4},{6,7},{7,6},{8,9},{9,8},{10,11... | collective-permute-start | bytes 3145736 | tf_op jit(solution)/shard_map/ppermute | solution.py:366
  6.2 17.8 %copy-start.2 = (s32[2,4,3]{2,1,0:T(4,128)S(1)}, s32[2,4,3]{2,1,0:T(4,128)}, u32[]{:S(2)}) copy-start(s32[2,4,3]{2,1,0:T(4,128)} %constant.48.clone) | copy-start | bytes 292
  6.2 24.6 %copy-start.3 = (f32[32]{0:T(128)S(1)}, f32[32]{0:T(128)}, u32[]{:S(2)}) copy-start(f32[32]{0:T(128)} %param.10) | copy-start | bytes 388
  11.7 1.6 %collective-permute-start = (bf16[4,136,128]{2,1,0:T(8,128)(2,1)S(1)}, bf16[4,136,128]{2,1,0:T(8,128)(2,1)S(1)}, u32[]{:S(2)}, u32[]{:S(2)}) collective-permute-start(bf16[4,136,128]{2,1,0:T(8,128)(2,1)S(1)} %dynamic-slice_convert_fusion), channel_id=1, source_target_pairs={{0,1},{1,0},{2,3},{3,2},{4,5},{5,4},{6,7},{7,6},{8,9},{9,8},{10,11... | collective-permute-start | bytes 417800 | tf_op jit(solution)/shard_map/ppermute | solution.py:95
  14.3 5.0 %collective-permute-start.1 = (bf16[4,136,128]{2,1,0:T(8,128)(2,1)S(1)}, bf16[4,136,128]{2,1,0:T(8,128)(2,1)S(1)}, u32[]{:S(2)}, u32[]{:S(2)}) collective-permute-start(bf16[4,136,128]{2,1,0:T(8,128)(2,1)S(1)} %fusion.2), channel_id=1, source_target_pairs={{0,2},{1,3},{2,0},{3,1},{4,6},{5,7},{6,4},{7,5},{8,10},{9,11},{10,... | collective-permute-start | bytes 417800 | tf_op jit(solution)/shard_map/ppermute | solution.py:98
  20.3 17.0 %copy-start = (bf16[512,2048]{1,0:T(8,128)(2,1)}, bf16[512,2048]{1,0:T(8,128)(2,1)S(1)}, u32[]{:S(2)}) copy-start(bf16[512,2048]{1,0:T(8,128)(2,1)S(1)} %collective-permute-done.2.q_recv) | copy-start | bytes 6291460
  20.3 6.7 %collective-permute-start.6 = (bf16[4,136,128]{2,1,0:T(8,128)(2,1)S(1)}, bf16[4,136,128]{2,1,0:T(8,128)(2,1)S(1)}, u32[]{:S(2)}, u32[]{:S(2)}) collective-permute-start(bf16[4,136,128]{2,1,0:T(8,128)(2,1)S(1)} %convert_element_type.34), channel_id=1, source_target_pairs={{0,4},{4,8},{8,12},{12,16},{16,20},{20,24},{24,28},{1,5},{5,9},{9,... | collective-permute-start | bytes 417800 | tf_op jit(solution)/shard_map/ppermute | solution.py:25
  27.0 7.0 %collective-permute-start.7 = (bf16[4,136,128]{2,1,0:T(8,128)(2,1)S(1)}, bf16[4,136,128]{2,1,0:T(8,128)(2,1)S(1)}, u32[]{:S(2)}, u32[]{:S(2)}) collective-permute-start(bf16[4,136,128]{2,1,0:T(8,128)(2,1)S(1)} %fusion), channel_id=1, source_target_pairs={{0,8},{4,12},{8,16},{12,20},{16,24},{20,28},{1,9},{5,13},{9,17},{1... | collective-permute-start | bytes 417800 | tf_op jit(solution)/shard_map/ppermute | solution.py:25
  31.5 39.1 %collective-permute-start.5 = (bf16[512,1024]{1,0:T(8,128)(2,1)}, bf16[512,1024]{1,0:T(8,128)(2,1)}, u32[]{:S(2)}, u32[]{:S(2)}) collective-permute-start(bf16[512,1024]{1,0:T(8,128)(2,1)} %get-tuple-element.22), channel_id=1, source_target_pairs={{0,3},{1,2},{4,7},{5,6},{8,11},{9,10},{12,15},{13,14},{16,19},{17,... | collective-permute-start | bytes 3145736 | tf_op jit(solution)/shard_map/ppermute | solution.py:375
  32.7 49.2 %collective-permute-start.4 = (bf16[512,1024]{1,0:T(8,128)(2,1)}, bf16[512,1024]{1,0:T(8,128)(2,1)}, u32[]{:S(2)}, u32[]{:S(2)}) collective-permute-start(bf16[512,1024]{1,0:T(8,128)(2,1)} %get-tuple-element.21.k_keep.v_keep), channel_id=1, source_target_pairs={{0,2},{1,3},{4,6},{5,7},{8,10},{9,11},{12,14},{13,15},{16,18},{17,... | collective-permute-start | bytes 3145736 | tf_op jit(solution)/shard_map/ppermute | solution.py:373
  34.1 35.6 %collective-permute-start.8 = (bf16[4,136,128]{2,1,0:T(8,128)(2,1)S(1)}, bf16[4,136,128]{2,1,0:T(8,128)(2,1)S(1)}, u32[]{:S(2)}, u32[]{:S(2)}) collective-permute-start(bf16[4,136,128]{2,1,0:T(8,128)(2,1)S(1)} %fusion.1), channel_id=1, source_target_pairs={{0,16},{4,20},{8,24},{12,28},{1,17},{5,21},{9,25},{13,29},{2,18},{... | collective-permute-start | bytes 417800 | tf_op jit(solution)/shard_map/ppermute | solution.py:25
  115.3 30.9 %collective-permute-start.9 = (bf16[512,2048]{1,0:T(8,128)(2,1)}, bf16[512,2048]{1,0:T(8,128)(2,1)S(1)}, u32[]{:S(2)}, u32[]{:S(2)}) collective-permute-start(bf16[512,2048]{1,0:T(8,128)(2,1)} %shard_map.77), channel_id=1, source_target_pairs={{0,1},{1,0},{2,3},{3,2},{4,5},{5,4},{6,7},{7,6},{8,9},{9,8},{10,11... | collective-permute-start | bytes 6291464 | tf_op jit(solution)/shard_map/ppermute | solution.py:322
  146.2 1.3 copy-start.1

commit v15 on v14

--- a/solution.py
+++ b/solution.py
@@ -173,8 +173,10 @@
         ml_ref[...] = packed
 
 
-def far_kernel(qp_ref, kp_ref, first_ref, last_ref, valid_ref, off_ref, gate_ref, q_keep, q_recv, k_ref,
-               v_ref, s_ref, acc_in, ml_in, o_ref, m_sc, l_sc, acc_sc, *, group_size):
+def far_kernel(qp_ref, kp_ref, first_ref, last_ref, valid_ref, off_ref, gate_ref, q_ref, *refs,
+               group_size):
+    kv_refs = refs[:-7]
+    s_ref, acc_in, ml_in, o_ref, m_sc, l_sc, acc_sc = refs[-7:]
     kv_head = pl.program_id(0)
     step_at = pl.program_id(1)
 
@@ -188,16 +190,15 @@
             )
         acc_sc[...] = acc_in[...]
 
-    for q_at, q_ref in enumerate((q_keep, q_recv)):
-        chosen = qp_ref[step_at] == q_at
-
-        @pl.when(chosen & (valid_ref[step_at] == 1))
+    for part in range(len(kv_refs) // 2):
+        @pl.when((kp_ref[step_at] == part) & (valid_ref[step_at] == 1))
         def _step():
-            online_step(q_ref, k_ref, v_ref, m_sc, l_sc, acc_sc, group_size, False)
-
-        @pl.when(chosen & (last_ref[step_at] == 1))
-        def _last():
-            finish(q_ref, s_ref, gate_ref, o_ref, acc_sc, l_sc, kv_head, group_size)
+            online_step(q_ref, kv_refs[2 * part], kv_refs[2 * part + 1], m_sc, l_sc, acc_sc,
+                        group_size, False)
+
+    @pl.when(last_ref[step_at] == 1)
+    def _last():
+        finish(q_ref, s_ref, gate_ref, o_ref, acc_sc, l_sc, kv_head, group_size)
 
 
 def finish(q_ref, s_ref, gate_ref, o_ref, acc_sc, l_sc, kv_head, group_size):
@@ -287,17 +288,15 @@
     def far_call(source, out_cols, col_offset):
         far = far_tables(chips, chip, core, source)
         offset = jnp.reshape(col_offset, (1,)).astype(jnp.int32)
+        part_specs = []
+        for _ in far_kv:
+            part_specs += [k_spec, v_spec]
         far_spec = pltpu.PrefetchScalarGridSpec(
             num_scalar_prefetch=6,
             grid=(kv_group, far.shape[-1]),
-            in_specs=[
-                pl.BlockSpec(memory_space=pltpu.SMEM),
-                q_spec,
-                q_spec,
-                pl.BlockSpec((None, block, HD), lambda g, t, qp, kp, f, l, v, o: (kp[t], 0, g)),
-                pl.BlockSpec(
-                    (None, block, HD), lambda g, t, qp, kp, f, l, v, o: (kp[t], 0, kv_group + g)
-                ),
+            in_specs=[pl.BlockSpec(memory_space=pltpu.SMEM), q_spec]
+            + part_specs
+            + [
                 pl.BlockSpec((None, STATE_ROWS, HD), lambda g, t, qp, kp, f, l, v, o: (g, 0, 0)),
                 pl.BlockSpec((None, block, width), lambda g, t, qp, kp, f, l, v, o: (qp[t], 0, g)),
                 pl.BlockSpec(
@@ -307,16 +306,20 @@
             out_specs=pl.BlockSpec((block, width), lambda g, t, qp, kp, f, l, v, o: (0, o[0] + g)),
             scratch_shapes=scratch,
         )
+        kv_args = []
+        for part in far_kv:
+            kv_args += [part, part]
         return pl.pallas_call(
             functools.partial(far_kernel, group_size=group_size),
             grid_spec=far_spec,
             cost_estimate=pl.CostEstimate(
                 flops=far_pairs * pair_flops // 2, transcendentals=far_pairs * pair_exps // 2,
-                bytes_accessed=int(keep_q.size * 8 + far_kv.size * 2),
+                bytes_accessed=int(keep_q.size * 8 + keep_kv.size * 2 * len(far_kv)),
             ),
             out_shape=jax.ShapeDtypeStruct((block, out_cols), jnp.bfloat16),
             compiler_params=params,
-        )(*[far[i] for i in range(5)], offset, mixing, keep_q, recv_q, far_kv, far_kv, state, acc, ml)
+        )(*[far[i] for i in range(5)], offset, mixing, (keep_q, recv_q)[source], *kv_args, state,
+          acc, ml)
 
     sibling_part = far_call(1, q_cols, 0)
     back = lax.ppermute(sibling_part, "head", [(p, p ^ 1) for p in range(lax.axis_size("head"))])
@@ -374,7 +377,7 @@
         kv_parts.append(
             lax.ppermute(send_kv, "head", [(p, (p + 2 * s) ^ 1) for p in range(parts - 2 * s)])
         )
-    far_kv = jnp.stack(kv_parts) if kv_parts else jnp.stack([keep_kv, recv_kv])
+    far_kv = kv_parts if kv_parts else [keep_kv, recv_kv]
     gate_here = lax.dynamic_slice_in_dim(gate_logit, core * kv_group * group_size, kv_group * group_size)
     mixing = jax.nn.sigmoid(gate_here)
     own_part, back = attend(

time: 152 us -> 149 us (0.980)
  other arithmetic: 6.59 us -> 3.5 us
    another operation x1 -> x0, other arithmetic: 3.07 us -> none  [body(): far_kv = jnp.stack(kv_parts) if kv_parts else jnp.stack([keep_kv, recv_kv])]
  transfers between devices with their start and end apart: 10 -> 10, of which waited for: 4 -> 4; matrix products, arithmetic and copies ran while one was open for 5% -> 5% of each run, Pallas kernels for 44% -> 45%
where the time goes in v15:
time: 149 us
  Pallas kernels  106 us (71%)
  waiting for transfers between devices  19.2 us (13%)
  starting transfers between devices  13.6 us (9%)
  local copies, waits for them, and re-layouts  5.69 us (4%)
  other arithmetic  3.5 us (2%)
    pallas_call x2, Pallas kernels, far_call(): pl.pallas_call(functools.partial(far_kernel, group_size=group_size), grid...  60 us
    pallas_call x1, Pallas kernels, attend(): pl.pallas_call(functools.partial(near_kernel, group_size=group_size), gri...  32.5 us
    ppermute x1, waiting for transfers between devices, body(): lax.ppermute(keep_kv, 'head', [(p, p + 2 * s) for p in range(parts - 2 *...  11.3 us
    ppermute x3, starting transfers between devices, shifted(): lax.ppermute(value, axis, [(source, source + steps) for source in range(c...  9.48 us
    pallas_call x1, Pallas kernels, split_inputs(): pl.pallas_call(split_kernel, grid_spec=grid_spec, out_shape=[q_shape, kv_...  5.57 us
    pallas_call x1, Pallas kernels, local_deltas(): pl.pallas_call(delta_kernel, out_shape=jax.ShapeDtypeStruct((kv_heads, ST...  4.49 us
    ppermute x1, waiting for transfers between devices, chip_states(): lax.ppermute(total.astype(jnp.bfloat16), 'head', [(p, p ^ steps) for p in...  3.96 us
    pallas_call x1, Pallas kernels, place_back(): pl.pallas_call(place_kernel, grid_spec=grid_spec, out_shape=jax.ShapeDtyp...  3.78 us
  transfers between devices with their start and end apart: 10, of which 4 were waited for; matrix products, arithmetic and copies ran while one was open for 5% of the time, Pallas kernels for 45%

profile of v15, /device:TPU:13, one launch (start us, length us, event | category | flops | bytes accessed | tf_op | source)
XLA Modules:
  0.0 148.5 jit_solution(1518251672375773119)
XLA Ops:
  0.0 5.6 %shard_map.73 = (bf16[512,2048]{1,0:T(8,128)(2,1)}, bf16[512,1024]{1,0:T(8,128)(2,1)}, bf16[512,2048]{1,0:T(8,128)(2,1)}, bf16[512,1024]{1,0:T(8,128)(2,1)}) custom-call(s32[1]{0:T(128)} %bitcast.7.core_ref, bf16[512,4096]{1,0:T(8,128)(2,1)} %q_send.1, bf16[512,1024]{1,0:T(8,128)(2,1)} %k_ref.1, bf16[512,1024]{1,0:T(8,128)(2,1)} %v_ref.1, ...), custom_call_target="tpu_custom_call" | custom-call | tf_op jit(solution)/shard_map/pallas_call | solution.py:64
  5.6 0.7 collective-permute-start.2
  6.2 0.0 collective-permute-start.3
  6.2 0.0 copy-start.4
  6.2 0.0 copy-start.5
  6.3 4.5 %shard_map.74 = f32[8,136,128]{2,1,0:T(8,128)} custom-call(bf16[512,1024]{1,0:T(8,128)(2,1)} %k_ref.1, bf16[512,1024]{1,0:T(8,128)(2,1)} %v_ref.1), custom_call_target="tpu_custom_call" | custom-call | tf_op jit(solution)/shard_map/pallas_call | solution.py:84
  10.7 1.0 dynamic-slice_convert_fusion
  11.7 0.6 collective-permute-start
  12.3 1.0 collective-permute-done
  13.3 1.0 fusion.2
  14.3 0.3 collective-permute-start.1
  14.6 0.7 constant_dynamic-slice_fusion
  15.3 4.0 %collective-permute-done.1 = bf16[4,136,128]{2,1,0:T(8,128)(2,1)S(1)} collective-permute-done((bf16[4,136,128]{2,1,0:T(8,128)(2,1)S(1)}, bf16[4,136,128]{2,1,0:T(8,128)(2,1)S(1)}, u32[]{:S(2)}, u32[]{:S(2)}) %collective-permute-start.1) | collective-permute-done | bytes 139296 | tf_op jit(solution)/shard_map/ppermute | solution.py:98
  19.2 1.0 convert_add_fusion.2
  20.2 0.0 collective-permute-done.3.k_recv.v_recv
  20.3 0.0 collective-permute-done.2.q_recv.q_ref
  20.3 0.0 copy-start.2
  20.3 3.1 %collective-permute-start.6 = (bf16[4,136,128]{2,1,0:T(8,128)(2,1)S(1)}, bf16[4,136,128]{2,1,0:T(8,128)(2,1)S(1)}, u32[]{:S(2)}, u32[]{:S(2)}) collective-permute-start(bf16[4,136,128]{2,1,0:T(8,128)(2,1)S(1)} %convert_element_type.34), channel_id=1, source_target_pairs={{0,4},{4,8},{8,12},{12,16},{16,20},{20,24},{24,28},{1,5},{5,9},{9,... | collective-permute-start | bytes 417800 | tf_op jit(solution)/shard_map/ppermute | solution.py:25
  23.4 0.6 slice_bitcast_fusion
  24.0 0.0 copy-done.4
  24.0 3.0 %collective-permute-done.6 = bf16[4,136,128]{2,1,0:T(8,128)(2,1)S(1)} collective-permute-done((bf16[4,136,128]{2,1,0:T(8,128)(2,1)S(1)}, bf16[4,136,128]{2,1,0:T(8,128)(2,1)S(1)}, u32[]{:S(2)}, u32[]{:S(2)}) %collective-permute-start.6) | collective-permute-done | bytes 139296 | tf_op jit(solution)/shard_map/ppermute | solution.py:25
  27.0 3.2 %collective-permute-start.7 = (bf16[4,136,128]{2,1,0:T(8,128)(2,1)S(1)}, bf16[4,136,128]{2,1,0:T(8,128)(2,1)S(1)}, u32[]{:S(2)}, u32[]{:S(2)}) collective-permute-start(bf16[4,136,128]{2,1,0:T(8,128)(2,1)S(1)} %fusion), channel_id=1, source_target_pairs={{0,8},{4,12},{8,16},{12,20},{16,24},{20,28},{1,9},{5,13},{9,17},{1... | collective-permute-start | bytes 417800 | tf_op jit(solution)/shard_map/ppermute | solution.py:25
  30.3 0.6 slice_bitcast_fusion.5
  30.9 0.0 copy-done.2
  30.9 0.0 copy-done.5
  30.9 0.6 add_divide_fusion.gate_ref
  31.5 1.3 collective-permute-start.5
  32.8 1.3 collective-permute-start.4
  34.1 0.0 collective-permute-done.7
  34.1 0.1 fusion.1
  34.1 3.2 %collective-permute-start.8 = (bf16[4,136,128]{2,1,0:T(8,128)(2,1)S(1)}, bf16[4,136,128]{2,1,0:T(8,128)(2,1)S(1)}, u32[]{:S(2)}, u32[]{:S(2)}) collective-permute-start(bf16[4,136,128]{2,1,0:T(8,128)(2,1)S(1)} %fusion.1), channel_id=1, source_target_pairs={{0,16},{4,20},{8,24},{12,28},{1,17},{5,21},{9,25},{13,29},{2,18},{... | collective-permute-start | bytes 417800 | tf_op jit(solution)/shard_map/ppermute | solution.py:25
  37.3 32.5 %shard_map.75 = (f32[2,512,2048]{2,1,0:T(8,128)}, f32[4,2,512,128]{3,2,1,0:T(8,128)}) custom-call(s32[3]{0:T(128)} %get-tuple-element.40.qs_ref, s32[3]{0:T(128)} %get-tuple-element.39.ks_ref, s32[3]{0:T(128)} %get-tuple-element.38.first_ref, s32[3]{0:T(128)} %get-tuple-element.37.diag_ref, bf16[512,2048]{1,0:T(8,128)(2,1)} %get-tuple-element.16.q_keep.q_ref, ...), custom_call_target="tpu_custom_call" | custom-call | flops 6442450944 | bytes 14680064 | tf_op jit(solution)/shard_map/pallas_call | solution.py:273
  69.8 0.0 collective-permute-done.8
  69.8 0.8 add_subtract_fusion.refs_4_
  70.6 0.0 collective-permute-done.5.refs_2_.refs_3_
  70.6 0.0 copy-start
  70.6 11.3 %collective-permute-done.4.refs_0_.refs_1_ = bf16[512,1024]{1,0:T(8,128)(2,1)S(1)} collective-permute-done((bf16[512,1024]{1,0:T(8,128)(2,1)}, bf16[512,1024]{1,0:T(8,128)(2,1)S(1)}, u32[]{:S(2)}, u32[]{:S(2)}) %collective-permute-start.4) | collective-permute-done | bytes 1048608 | tf_op jit(solution)/shard_map/ppermute | solution.py:376
  81.9 0.0 copy-start.1
  81.9 0.0 copy-done
  81.9 1.0 copy-done.1
  82.9 30.0 %shard_map.77 = bf16[512,2048]{1,0:T(8,128)(2,1)} custom-call(s32[2]{0:T(128)} %get-tuple-element.31.qp_ref, s32[2]{0:T(128)} %get-tuple-element.30.kp_ref, s32[2]{0:T(128)} %get-tuple-element.29.first_ref, s32[2]{0:T(128)} %get-tuple-element.28.last_ref, s32[2]{0:T(128)} %get-tuple-element.27.valid_ref, s32[1]{0:T(128)} %constant.47.clone.1.off_ref, ...), custom_call_target="tpu_custom_call" | custom-call | flops 2147483648 | bytes 10485760 | tf_op jit(solution)/shard_map/pallas_call | solution.py:312
  112.9 0.0 collective-permute-start.9
  112.9 0.6 slice_bitcast_fusion.9
  113.4 30.0 %shard_map.76.full_ref = bf16[512,4096]{1,0:T(8,128)(2,1)} custom-call(s32[2]{0:T(128)} %get-tuple-element.36.qp_ref, s32[2]{0:T(128)} %get-tuple-element.35.kp_ref, s32[2]{0:T(128)} %get-tuple-element.34.first_ref, s32[2]{0:T(128)} %get-tuple-element.33.last_ref, s32[2]{0:T(128)} %get-tuple-element.32.valid_ref, s32[1]{0:T(128)} %bitcast.6.off_ref, ...), custom_call_target="tpu_custom_call" | custom-call | flops 2147483648 | bytes 10485760 | tf_op jit(solution)/shard_map/pallas_call | solution.py:312
  143.4 0.0 collective-permute-done.9.back_ref
  143.4 0.0 copy-start.3
  143.4 1.3 copy-done.3
  144.8 3.8 %shard_map.78 = bf16[512,4096]{1,0:T(8,128)(2,1)} custom-call(s32[1]{0:T(128)} %bitcast.col_ref, bf16[512,4096]{1,0:T(8,128)(2,1)} %shard_map.76.full_ref, bf16[512,2048]{1,0:T(8,128)(2,1)} %copy-done.3), custom_call_target="tpu_custom_call", output_to_operand_aliasing={{}: (1, {})} | custom-call | tf_op jit(solution)/shard_map/pallas_call | solution.py:347
  (3 shorter events, 0.1 us)
Async XLA Ops:
  5.6 14.7 %collective-permute-start.2 = (bf16[512,2048]{1,0:T(8,128)(2,1)}, bf16[512,2048]{1,0:T(8,128)(2,1)S(1)}, u32[]{:S(2)}, u32[]{:S(2)}) collective-permute-start(bf16[512,2048]{1,0:T(8,128)(2,1)} %get-tuple-element.19), channel_id=1, source_target_pairs={{0,1},{1,0},{2,3},{3,2},{4,5},{5,4},{6,7},{7,6},{8,9},{9,8},{10,11... | collective-permute-start | bytes 6291464 | tf_op jit(solution)/shard_map/ppermute | solution.py:368
  6.2 14.0 %collective-permute-start.3 = (bf16[512,1024]{1,0:T(8,128)(2,1)}, bf16[512,1024]{1,0:T(8,128)(2,1)}, u32[]{:S(2)}, u32[]{:S(2)}) collective-permute-start(bf16[512,1024]{1,0:T(8,128)(2,1)} %get-tuple-element.21), channel_id=1, source_target_pairs={{0,1},{1,0},{2,3},{3,2},{4,5},{5,4},{6,7},{7,6},{8,9},{9,8},{10,11... | collective-permute-start | bytes 3145736 | tf_op jit(solution)/shard_map/ppermute | solution.py:369
  6.2 17.7 %copy-start.4 = (s32[2,4,3]{2,1,0:T(4,128)S(1)}, s32[2,4,3]{2,1,0:T(4,128)}, u32[]{:S(2)}) copy-start(s32[2,4,3]{2,1,0:T(4,128)} %constant.48.clone) | copy-start | bytes 292
  6.2 24.6 %copy-start.5 = (f32[32]{0:T(128)S(1)}, f32[32]{0:T(128)}, u32[]{:S(2)}) copy-start(f32[32]{0:T(128)} %param.10) | copy-start | bytes 388
  11.7 1.6 %collective-permute-start = (bf16[4,136,128]{2,1,0:T(8,128)(2,1)S(1)}, bf16[4,136,128]{2,1,0:T(8,128)(2,1)S(1)}, u32[]{:S(2)}, u32[]{:S(2)}) collective-permute-start(bf16[4,136,128]{2,1,0:T(8,128)(2,1)S(1)} %dynamic-slice_convert_fusion), channel_id=1, source_target_pairs={{0,1},{1,0},{2,3},{3,2},{4,5},{5,4},{6,7},{7,6},{8,9},{9,8},{10,11... | collective-permute-start | bytes 417800 | tf_op jit(solution)/shard_map/ppermute | solution.py:95
  14.3 5.0 %collective-permute-start.1 = (bf16[4,136,128]{2,1,0:T(8,128)(2,1)S(1)}, bf16[4,136,128]{2,1,0:T(8,128)(2,1)S(1)}, u32[]{:S(2)}, u32[]{:S(2)}) collective-permute-start(bf16[4,136,128]{2,1,0:T(8,128)(2,1)S(1)} %fusion.2), channel_id=1, source_target_pairs={{0,2},{1,3},{2,0},{3,1},{4,6},{5,7},{6,4},{7,5},{8,10},{9,11},{10,... | collective-permute-start | bytes 417800 | tf_op jit(solution)/shard_map/ppermute | solution.py:98
  20.3 10.6 %copy-start.2 = (bf16[512,2048]{1,0:T(8,128)(2,1)}, bf16[512,2048]{1,0:T(8,128)(2,1)S(1)}, u32[]{:S(2)}) copy-start(bf16[512,2048]{1,0:T(8,128)(2,1)S(1)} %collective-permute-done.2.q_recv.q_ref) | copy-start | bytes 6291460
  20.3 6.7 %collective-permute-start.6 = (bf16[4,136,128]{2,1,0:T(8,128)(2,1)S(1)}, bf16[4,136,128]{2,1,0:T(8,128)(2,1)S(1)}, u32[]{:S(2)}, u32[]{:S(2)}) collective-permute-start(bf16[4,136,128]{2,1,0:T(8,128)(2,1)S(1)} %convert_element_type.34), channel_id=1, source_target_pairs={{0,4},{4,8},{8,12},{12,16},{16,20},{20,24},{24,28},{1,5},{5,9},{9,... | collective-permute-start | bytes 417800 | tf_op jit(solution)/shard_map/ppermute | solution.py:25
  27.0 7.0 %collective-permute-start.7 = (bf16[4,136,128]{2,1,0:T(8,128)(2,1)S(1)}, bf16[4,136,128]{2,1,0:T(8,128)(2,1)S(1)}, u32[]{:S(2)}, u32[]{:S(2)}) collective-permute-start(bf16[4,136,128]{2,1,0:T(8,128)(2,1)S(1)} %fusion), channel_id=1, source_target_pairs={{0,8},{4,12},{8,16},{12,20},{16,24},{20,28},{1,9},{5,13},{9,17},{1... | collective-permute-start | bytes 417800 | tf_op jit(solution)/shard_map/ppermute | solution.py:25
  31.5 39.1 %collective-permute-start.5 = (bf16[512,1024]{1,0:T(8,128)(2,1)}, bf16[512,1024]{1,0:T(8,128)(2,1)S(1)}, u32[]{:S(2)}, u32[]{:S(2)}) collective-permute-start(bf16[512,1024]{1,0:T(8,128)(2,1)} %get-tuple-element.21), channel_id=1, source_target_pairs={{0,3},{1,2},{4,7},{5,6},{8,11},{9,10},{12,15},{13,14},{16,19},{17,... | collective-permute-start | bytes 3145736 | tf_op jit(solution)/shard_map/ppermute | solution.py:378
  32.8 49.1 %collective-permute-start.4 = (bf16[512,1024]{1,0:T(8,128)(2,1)}, bf16[512,1024]{1,0:T(8,128)(2,1)S(1)}, u32[]{:S(2)}, u32[]{:S(2)}) collective-permute-start(bf16[512,1024]{1,0:T(8,128)(2,1)} %get-tuple-element.20.k_keep.v_keep), channel_id=1, source_target_pairs={{0,2},{1,3},{4,6},{5,7},{8,10},{9,11},{12,14},{13,15},{16,18},{17,... | collective-permute-start | bytes 3145736 | tf_op jit(solution)/shard_map/ppermute | solution.py:376
  34.1 35.7 %collective-permute-start.8 = (bf16[4,136,128]{2,1,0:T(8,128)(2,1)S(1)}, bf16[4,136,128]{2,1,0:T(8,128)(2,1)S(1)}, u32[]{:S(2)}, u32[]{:S(2)}) collective-permute-start(bf16[4,136,128]{2,1,0:T(8,128)(2,1)S(1)} %fusion.1), channel_id=1, source_target_pairs={{0,16},{4,20},{8,24},{12,28},{1,17},{5,21},{9,25},{13,29},{2,18},{... | collective-permute-start | bytes 417800 | tf_op jit(solution)/shard_map/ppermute | solution.py:25
  70.6 11.3 %copy-start = (bf16[512,1024]{1,0:T(8,128)(2,1)}, bf16[512,1024]{1,0:T(8,128)(2,1)S(1)}, u32[]{:S(2)}) copy-start(bf16[512,1024]{1,0:T(8,128)(2,1)S(1)} %collective-permute-done.5.refs_2_.refs_3_) | copy-start | bytes 3145732
  81.9 1.0 copy-start.1
  112.9 30.6 %collective-permute-start.9 = (bf16[512,2048]{1,0:T(8,128)(2,1)}, bf16[512,2048]{1,0:T(8,128)(2,1)S(1)}, u32[]{:S(2)}, u32[]{:S(2)}) collective-permute-start(bf16[512,2048]{1,0:T(8,128)(2,1)} %shard_map.77), channel_id=1, source_target_pairs={{0,1},{1,0},{2,3},{3,2},{4,5},{5,4},{6,7},{7,6},{8,9},{9,8},{10,11... | collective-permute-start | bytes 6291464 | tf_op jit(solution)/shard_map/ppermute | solution.py:325
  143.4 1.3 copy-start.3

commit v16 on v15

--- a/solution.py
+++ b/solution.py
@@ -333,16 +333,15 @@
 
 def place_back(own_part, back, core, kv_group):
     tokens_here, q_cols = back.shape
-    width = q_cols // kv_group
-    other = jnp.reshape((1 - core) * kv_group, (1,)).astype(jnp.int32)
+    other = jnp.reshape(1 - core, (1,)).astype(jnp.int32)
     grid_spec = pltpu.PrefetchScalarGridSpec(
         num_scalar_prefetch=1,
-        grid=(kv_group,),
+        grid=(1,),
         in_specs=[
             pl.BlockSpec(memory_space=pl.ANY),
-            pl.BlockSpec((tokens_here, width), lambda g, c: (0, g)),
+            pl.BlockSpec((tokens_here, q_cols), lambda i, c: (0, 0)),
         ],
-        out_specs=pl.BlockSpec((tokens_here, width), lambda g, c: (0, c[0] + g)),
+        out_specs=pl.BlockSpec((tokens_here, q_cols), lambda i, c: (0, c[0])),
     )
     return pl.pallas_call(
         place_kernel,

time: 149 us -> 149 us (level)
  no operation moved by 1% of the time
where the time goes in v16:
time: 149 us; the launch traced here: 148 us
  Pallas kernels  106 us (71%)
  waiting for transfers between devices  19.2 us (13%)
  starting transfers between devices  13.6 us (9%)
  local copies, waits for them, and re-layouts  5.69 us (4%)
  other arithmetic  3.5 us (2%)
    pallas_call x2, Pallas kernels, far_call(): pl.pallas_call(functools.partial(far_kernel, group_size=group_size), grid...  60 us
    pallas_call x1, Pallas kernels, attend(): pl.pallas_call(functools.partial(near_kernel, group_size=group_size), gri...  32.5 us
    ppermute x1, waiting for transfers between devices, body(): lax.ppermute(keep_kv, 'head', [(p, p + 2 * s) for p in range(parts - 2 *...  11.3 us
    ppermute x3, starting transfers between devices, shifted(): lax.ppermute(value, axis, [(source, source + steps) for source in range(c...  9.48 us
    pallas_call x1, Pallas kernels, split_inputs(): pl.pallas_call(split_kernel, grid_spec=grid_spec, out_shape=[q_shape, kv_...  5.57 us
    pallas_call x1, Pallas kernels, local_deltas(): pl.pallas_call(delta_kernel, out_shape=jax.ShapeDtypeStruct((kv_heads, ST...  4.49 us
    ppermute x1, waiting for transfers between devices, chip_states(): lax.ppermute(total.astype(jnp.bfloat16), 'head', [(p, p ^ steps) for p in...  3.96 us
    pallas_call x1, Pallas kernels, place_back(): pl.pallas_call(place_kernel, grid_spec=grid_spec, out_shape=jax.ShapeDtyp...  3.04 us
  transfers between devices with their start and end apart: 10, of which 4 were waited for; matrix products, arithmetic and copies ran while one was open for 5% of the time, Pallas kernels for 45%

profile of v16, /device:TPU:13, one launch (start us, length us, event | category | flops | bytes accessed | tf_op | source)
XLA Modules:
  0.0 147.8 jit_solution(9348358702964154537)
XLA Ops:
  0.0 5.6 %shard_map.73 = (bf16[512,2048]{1,0:T(8,128)(2,1)}, bf16[512,1024]{1,0:T(8,128)(2,1)}, bf16[512,2048]{1,0:T(8,128)(2,1)}, bf16[512,1024]{1,0:T(8,128)(2,1)}) custom-call(s32[1]{0:T(128)} %bitcast.7.core_ref, bf16[512,4096]{1,0:T(8,128)(2,1)} %q_send.1, bf16[512,1024]{1,0:T(8,128)(2,1)} %k_ref.1, bf16[512,1024]{1,0:T(8,128)(2,1)} %v_ref.1, ...), custom_call_target="tpu_custom_call" | custom-call | tf_op jit(solution)/shard_map/pallas_call | solution.py:64
  5.6 0.7 collective-permute-start.2
  6.2 0.0 collective-permute-start.3
  6.2 0.0 copy-start.4
  6.2 0.0 copy-start.5
  6.3 4.5 %shard_map.74 = f32[8,136,128]{2,1,0:T(8,128)} custom-call(bf16[512,1024]{1,0:T(8,128)(2,1)} %k_ref.1, bf16[512,1024]{1,0:T(8,128)(2,1)} %v_ref.1), custom_call_target="tpu_custom_call" | custom-call | tf_op jit(solution)/shard_map/pallas_call | solution.py:84
  10.7 1.0 dynamic-slice_convert_fusion
  11.7 0.6 collective-permute-start
  12.3 1.0 collective-permute-done
  13.3 1.0 fusion.2
  14.3 0.3 collective-permute-start.1
  14.6 0.7 constant_dynamic-slice_fusion
  15.3 4.0 %collective-permute-done.1 = bf16[4,136,128]{2,1,0:T(8,128)(2,1)S(1)} collective-permute-done((bf16[4,136,128]{2,1,0:T(8,128)(2,1)S(1)}, bf16[4,136,128]{2,1,0:T(8,128)(2,1)S(1)}, u32[]{:S(2)}, u32[]{:S(2)}) %collective-permute-start.1) | collective-permute-done | bytes 139296 | tf_op jit(solution)/shard_map/ppermute | solution.py:98
  19.2 1.0 convert_add_fusion.2
  20.2 0.0 collective-permute-done.3.k_recv.v_recv
  20.3 0.0 collective-permute-done.2.q_recv.q_ref
  20.3 0.0 copy-start.2
  20.3 3.1 %collective-permute-start.6 = (bf16[4,136,128]{2,1,0:T(8,128)(2,1)S(1)}, bf16[4,136,128]{2,1,0:T(8,128)(2,1)S(1)}, u32[]{:S(2)}, u32[]{:S(2)}) collective-permute-start(bf16[4,136,128]{2,1,0:T(8,128)(2,1)S(1)} %convert_element_type.34), channel_id=1, source_target_pairs={{0,4},{4,8},{8,12},{12,16},{16,20},{20,24},{24,28},{1,5},{5,9},{9,... | collective-permute-start | bytes 417800 | tf_op jit(solution)/shard_map/ppermute | solution.py:25
  23.4 0.6 slice_bitcast_fusion
  24.0 0.0 copy-done.4
  24.0 3.0 %collective-permute-done.6 = bf16[4,136,128]{2,1,0:T(8,128)(2,1)S(1)} collective-permute-done((bf16[4,136,128]{2,1,0:T(8,128)(2,1)S(1)}, bf16[4,136,128]{2,1,0:T(8,128)(2,1)S(1)}, u32[]{:S(2)}, u32[]{:S(2)}) %collective-permute-start.6) | collective-permute-done | bytes 139296 | tf_op jit(solution)/shard_map/ppermute | solution.py:25
  27.0 3.2 %collective-permute-start.7 = (bf16[4,136,128]{2,1,0:T(8,128)(2,1)S(1)}, bf16[4,136,128]{2,1,0:T(8,128)(2,1)S(1)}, u32[]{:S(2)}, u32[]{:S(2)}) collective-permute-start(bf16[4,136,128]{2,1,0:T(8,128)(2,1)S(1)} %fusion), channel_id=1, source_target_pairs={{0,8},{4,12},{8,16},{12,20},{16,24},{20,28},{1,9},{5,13},{9,17},{1... | collective-permute-start | bytes 417800 | tf_op jit(solution)/shard_map/ppermute | solution.py:25
  30.3 0.6 slice_bitcast_fusion.5
  30.9 0.0 copy-done.2
  30.9 0.0 copy-done.5
  30.9 0.6 add_divide_fusion.gate_ref
  31.5 1.3 collective-permute-start.5
  32.8 1.3 collective-permute-start.4
  34.1 0.0 collective-permute-done.7
  34.1 0.1 fusion.1
  34.1 3.2 %collective-permute-start.8 = (bf16[4,136,128]{2,1,0:T(8,128)(2,1)S(1)}, bf16[4,136,128]{2,1,0:T(8,128)(2,1)S(1)}, u32[]{:S(2)}, u32[]{:S(2)}) collective-permute-start(bf16[4,136,128]{2,1,0:T(8,128)(2,1)S(1)} %fusion.1), channel_id=1, source_target_pairs={{0,16},{4,20},{8,24},{12,28},{1,17},{5,21},{9,25},{13,29},{2,18},{... | collective-permute-start | bytes 417800 | tf_op jit(solution)/shard_map/ppermute | solution.py:25
  37.3 32.5 %shard_map.75 = (f32[2,512,2048]{2,1,0:T(8,128)}, f32[4,2,512,128]{3,2,1,0:T(8,128)}) custom-call(s32[3]{0:T(128)} %get-tuple-element.40.qs_ref, s32[3]{0:T(128)} %get-tuple-element.39.ks_ref, s32[3]{0:T(128)} %get-tuple-element.38.first_ref, s32[3]{0:T(128)} %get-tuple-element.37.diag_ref, bf16[512,2048]{1,0:T(8,128)(2,1)} %get-tuple-element.16.q_keep.q_ref, ...), custom_call_target="tpu_custom_call" | custom-call | flops 6442450944 | bytes 14680064 | tf_op jit(solution)/shard_map/pallas_call | solution.py:273
  69.8 0.0 collective-permute-done.8
  69.8 0.8 add_subtract_fusion.refs_4_
  70.6 0.0 collective-permute-done.5.refs_2_.refs_3_
  70.6 0.0 copy-start
  70.6 11.3 %collective-permute-done.4.refs_0_.refs_1_ = bf16[512,1024]{1,0:T(8,128)(2,1)S(1)} collective-permute-done((bf16[512,1024]{1,0:T(8,128)(2,1)}, bf16[512,1024]{1,0:T(8,128)(2,1)S(1)}, u32[]{:S(2)}, u32[]{:S(2)}) %collective-permute-start.4) | collective-permute-done | bytes 1048608 | tf_op jit(solution)/shard_map/ppermute | solution.py:375
  81.9 0.0 copy-start.1
  81.9 0.0 copy-done
  81.9 1.0 copy-done.1
  82.9 30.0 %shard_map.77 = bf16[512,2048]{1,0:T(8,128)(2,1)} custom-call(s32[2]{0:T(128)} %get-tuple-element.31.qp_ref, s32[2]{0:T(128)} %get-tuple-element.30.kp_ref, s32[2]{0:T(128)} %get-tuple-element.29.first_ref, s32[2]{0:T(128)} %get-tuple-element.28.last_ref, s32[2]{0:T(128)} %get-tuple-element.27.valid_ref, s32[1]{0:T(128)} %constant.47.clone.1.off_ref, ...), custom_call_target="tpu_custom_call" | custom-call | flops 2147483648 | bytes 10485760 | tf_op jit(solution)/shard_map/pallas_call | solution.py:312
  112.9 0.0 collective-permute-start.9
  112.9 0.6 slice_bitcast_fusion.9
  113.4 30.0 %shard_map.76.full_ref = bf16[512,4096]{1,0:T(8,128)(2,1)} custom-call(s32[2]{0:T(128)} %get-tuple-element.36.qp_ref, s32[2]{0:T(128)} %get-tuple-element.35.kp_ref, s32[2]{0:T(128)} %get-tuple-element.34.first_ref, s32[2]{0:T(128)} %get-tuple-element.33.last_ref, s32[2]{0:T(128)} %get-tuple-element.32.valid_ref, s32[1]{0:T(128)} %bitcast.6.off_ref, ...), custom_call_target="tpu_custom_call" | custom-call | flops 2147483648 | bytes 10485760 | tf_op jit(solution)/shard_map/pallas_call | solution.py:312
  143.4 0.0 collective-permute-done.9.back_ref
  143.4 0.0 copy-start.3
  143.4 1.3 copy-done.3
  144.8 3.0 %shard_map.78 = bf16[512,4096]{1,0:T(8,128)(2,1)} custom-call(s32[1]{0:T(128)} %bitcast.col_ref, bf16[512,4096]{1,0:T(8,128)(2,1)} %shard_map.76.full_ref, bf16[512,2048]{1,0:T(8,128)(2,1)} %copy-done.3), custom_call_target="tpu_custom_call", output_to_operand_aliasing={{}: (1, {})} | custom-call | tf_op jit(solution)/shard_map/pallas_call | solution.py:346
  (3 shorter events, 0.1 us)
Async XLA Ops:
  5.6 14.7 %collective-permute-start.2 = (bf16[512,2048]{1,0:T(8,128)(2,1)}, bf16[512,2048]{1,0:T(8,128)(2,1)S(1)}, u32[]{:S(2)}, u32[]{:S(2)}) collective-permute-start(bf16[512,2048]{1,0:T(8,128)(2,1)} %get-tuple-element.19), channel_id=1, source_target_pairs={{0,1},{1,0},{2,3},{3,2},{4,5},{5,4},{6,7},{7,6},{8,9},{9,8},{10,11... | collective-permute-start | bytes 6291464 | tf_op jit(solution)/shard_map/ppermute | solution.py:367
  6.2 14.0 %collective-permute-start.3 = (bf16[512,1024]{1,0:T(8,128)(2,1)}, bf16[512,1024]{1,0:T(8,128)(2,1)}, u32[]{:S(2)}, u32[]{:S(2)}) collective-permute-start(bf16[512,1024]{1,0:T(8,128)(2,1)} %get-tuple-element.21), channel_id=1, source_target_pairs={{0,1},{1,0},{2,3},{3,2},{4,5},{5,4},{6,7},{7,6},{8,9},{9,8},{10,11... | collective-permute-start | bytes 3145736 | tf_op jit(solution)/shard_map/ppermute | solution.py:368
  6.2 17.7 %copy-start.4 = (s32[2,4,3]{2,1,0:T(4,128)S(1)}, s32[2,4,3]{2,1,0:T(4,128)}, u32[]{:S(2)}) copy-start(s32[2,4,3]{2,1,0:T(4,128)} %constant.48.clone) | copy-start | bytes 292
  6.2 24.6 %copy-start.5 = (f32[32]{0:T(128)S(1)}, f32[32]{0:T(128)}, u32[]{:S(2)}) copy-start(f32[32]{0:T(128)} %param.10) | copy-start | bytes 388
  11.7 1.6 %collective-permute-start = (bf16[4,136,128]{2,1,0:T(8,128)(2,1)S(1)}, bf16[4,136,128]{2,1,0:T(8,128)(2,1)S(1)}, u32[]{:S(2)}, u32[]{:S(2)}) collective-permute-start(bf16[4,136,128]{2,1,0:T(8,128)(2,1)S(1)} %dynamic-slice_convert_fusion), channel_id=1, source_target_pairs={{0,1},{1,0},{2,3},{3,2},{4,5},{5,4},{6,7},{7,6},{8,9},{9,8},{10,11... | collective-permute-start | bytes 417800 | tf_op jit(solution)/shard_map/ppermute | solution.py:95
  14.3 5.0 %collective-permute-start.1 = (bf16[4,136,128]{2,1,0:T(8,128)(2,1)S(1)}, bf16[4,136,128]{2,1,0:T(8,128)(2,1)S(1)}, u32[]{:S(2)}, u32[]{:S(2)}) collective-permute-start(bf16[4,136,128]{2,1,0:T(8,128)(2,1)S(1)} %fusion.2), channel_id=1, source_target_pairs={{0,2},{1,3},{2,0},{3,1},{4,6},{5,7},{6,4},{7,5},{8,10},{9,11},{10,... | collective-permute-start | bytes 417800 | tf_op jit(solution)/shard_map/ppermute | solution.py:98
  20.3 10.6 %copy-start.2 = (bf16[512,2048]{1,0:T(8,128)(2,1)}, bf16[512,2048]{1,0:T(8,128)(2,1)S(1)}, u32[]{:S(2)}) copy-start(bf16[512,2048]{1,0:T(8,128)(2,1)S(1)} %collective-permute-done.2.q_recv.q_ref) | copy-start | bytes 6291460
  20.3 6.7 %collective-permute-start.6 = (bf16[4,136,128]{2,1,0:T(8,128)(2,1)S(1)}, bf16[4,136,128]{2,1,0:T(8,128)(2,1)S(1)}, u32[]{:S(2)}, u32[]{:S(2)}) collective-permute-start(bf16[4,136,128]{2,1,0:T(8,128)(2,1)S(1)} %convert_element_type.34), channel_id=1, source_target_pairs={{0,4},{4,8},{8,12},{12,16},{16,20},{20,24},{24,28},{1,5},{5,9},{9,... | collective-permute-start | bytes 417800 | tf_op jit(solution)/shard_map/ppermute | solution.py:25
  27.0 7.0 %collective-permute-start.7 = (bf16[4,136,128]{2,1,0:T(8,128)(2,1)S(1)}, bf16[4,136,128]{2,1,0:T(8,128)(2,1)S(1)}, u32[]{:S(2)}, u32[]{:S(2)}) collective-permute-start(bf16[4,136,128]{2,1,0:T(8,128)(2,1)S(1)} %fusion), channel_id=1, source_target_pairs={{0,8},{4,12},{8,16},{12,20},{16,24},{20,28},{1,9},{5,13},{9,17},{1... | collective-permute-start | bytes 417800 | tf_op jit(solution)/shard_map/ppermute | solution.py:25
  31.5 39.1 %collective-permute-start.5 = (bf16[512,1024]{1,0:T(8,128)(2,1)}, bf16[512,1024]{1,0:T(8,128)(2,1)S(1)}, u32[]{:S(2)}, u32[]{:S(2)}) collective-permute-start(bf16[512,1024]{1,0:T(8,128)(2,1)} %get-tuple-element.21), channel_id=1, source_target_pairs={{0,3},{1,2},{4,7},{5,6},{8,11},{9,10},{12,15},{13,14},{16,19},{17,... | collective-permute-start | bytes 3145736 | tf_op jit(solution)/shard_map/ppermute | solution.py:377
  32.8 49.1 %collective-permute-start.4 = (bf16[512,1024]{1,0:T(8,128)(2,1)}, bf16[512,1024]{1,0:T(8,128)(2,1)S(1)}, u32[]{:S(2)}, u32[]{:S(2)}) collective-permute-start(bf16[512,1024]{1,0:T(8,128)(2,1)} %get-tuple-element.20.k_keep.v_keep), channel_id=1, source_target_pairs={{0,2},{1,3},{4,6},{5,7},{8,10},{9,11},{12,14},{13,15},{16,18},{17,... | collective-permute-start | bytes 3145736 | tf_op jit(solution)/shard_map/ppermute | solution.py:375
  34.1 35.7 %collective-permute-start.8 = (bf16[4,136,128]{2,1,0:T(8,128)(2,1)S(1)}, bf16[4,136,128]{2,1,0:T(8,128)(2,1)S(1)}, u32[]{:S(2)}, u32[]{:S(2)}) collective-permute-start(bf16[4,136,128]{2,1,0:T(8,128)(2,1)S(1)} %fusion.1), channel_id=1, source_target_pairs={{0,16},{4,20},{8,24},{12,28},{1,17},{5,21},{9,25},{13,29},{2,18},{... | collective-permute-start | bytes 417800 | tf_op jit(solution)/shard_map/ppermute | solution.py:25
  70.6 11.3 %copy-start = (bf16[512,1024]{1,0:T(8,128)(2,1)}, bf16[512,1024]{1,0:T(8,128)(2,1)S(1)}, u32[]{:S(2)}) copy-start(bf16[512,1024]{1,0:T(8,128)(2,1)S(1)} %collective-permute-done.5.refs_2_.refs_3_) | copy-start | bytes 3145732
  81.9 1.0 copy-start.1
  112.9 30.6 %collective-permute-start.9 = (bf16[512,2048]{1,0:T(8,128)(2,1)}, bf16[512,2048]{1,0:T(8,128)(2,1)S(1)}, u32[]{:S(2)}, u32[]{:S(2)}) collective-permute-start(bf16[512,2048]{1,0:T(8,128)(2,1)} %shard_map.77), channel_id=1, source_target_pairs={{0,1},{1,0},{2,3},{3,2},{4,5},{5,4},{6,7},{7,6},{8,9},{9,8},{10,11... | collective-permute-start | bytes 6291464 | tf_op jit(solution)/shard_map/ppermute | solution.py:325
  143.4 1.3 copy-start.3

commit v17 on v16

--- a/solution.py
+++ b/solution.py
@@ -25,10 +25,9 @@
     return lax.ppermute(value, axis, [(source, source + steps) for source in range(count - steps)])
 
 
-def split_kernel(core_ref, q_keep, k_keep, v_keep, q_send, k_send, v_send, *out_refs):
+def split_kernel(core_ref, k_keep, v_keep, q_send, k_send, v_send, *out_refs):
     k_cols = k_keep.shape[-1]
-    keep_q, keep_kv, send_q, send_kv = out_refs
-    keep_q[...] = q_keep[...]
+    keep_kv, send_q, send_kv = out_refs
     keep_kv[:, :k_cols] = k_keep[...]
     keep_kv[:, k_cols:] = v_keep[...]
     send_q[...] = q_send[...]
@@ -48,7 +47,6 @@
         num_scalar_prefetch=1,
         grid=(1,),
         in_specs=[
-            pl.BlockSpec((tokens_here, q_cols), keep_map),
             pl.BlockSpec((tokens_here, k_cols), keep_map),
             pl.BlockSpec((tokens_here, k_cols), keep_map),
             pl.BlockSpec((tokens_here, q_cols), send_map),
@@ -56,14 +54,14 @@
             pl.BlockSpec((tokens_here, k_cols), send_map),
         ],
         out_specs=[
+            pl.BlockSpec((tokens_here, 2 * k_cols), lambda i, c: (0, 0)),
             pl.BlockSpec((tokens_here, q_cols), lambda i, c: (0, 0)),
             pl.BlockSpec((tokens_here, 2 * k_cols), lambda i, c: (0, 0)),
-        ]
-        * 2,
+        ],
     )
     return pl.pallas_call(
-        split_kernel, grid_spec=grid_spec, out_shape=[q_shape, kv_shape] * 2
-    )(core.reshape(1), queries, keys, values, queries, keys, values)
+        split_kernel, grid_spec=grid_spec, out_shape=[kv_shape, q_shape, kv_shape]
+    )(core.reshape(1), keys, values, queries, keys, values)
 
 
 def delta_kernel(k_ref, v_ref, o_ref):
@@ -138,7 +136,7 @@
         m_sc[head] = m_new
 
 
-def near_kernel(qs_ref, ks_ref, first_ref, diag_ref, q_keep, q_recv, k_keep, v_keep, k_recv,
+def near_kernel(qs_ref, ks_ref, first_ref, diag_ref, off_ref, q_keep, q_recv, k_keep, v_keep, k_recv,
                 v_recv, acc_ref, ml_ref, m_sc, l_sc, acc_sc, *, group_size):
     step_at = pl.program_id(1)
     q_src = qs_ref[step_at]
@@ -244,8 +242,9 @@
     return jnp.asarray(tables)[chip, core]
 
 
-def attend(keep_q, recv_q, keep_kv, recv_kv, far_kv, state, mixing, chips, chip, core, group_size):
-    block, q_cols = keep_q.shape
+def attend(queries, recv_q, keep_kv, recv_kv, far_kv, state, mixing, chips, chip, core, group_size):
+    block, q_cols = recv_q.shape
+    keep_q = queries
     kv_group = keep_kv.shape[-1] // (2 * HD)
     width = group_size * HD
     scratch = [
@@ -255,16 +254,20 @@
     ]
     params = pltpu.CompilerParams(dimension_semantics=("arbitrary", "arbitrary"))
     near = near_tables(core)
+    q_offset = jnp.reshape(core * kv_group, (1,)).astype(jnp.int32)
     q_spec = pl.BlockSpec((block, width), lambda g, t, *_: (0, g))
+    own_q_spec = pl.BlockSpec((block, width), lambda g, t, *p: (0, p[-1][0] + g))
     k_spec = pl.BlockSpec((block, HD), lambda g, t, *_: (0, g))
     v_spec = pl.BlockSpec((block, HD), lambda g, t, *_: (0, kv_group + g))
     near_spec = pltpu.PrefetchScalarGridSpec(
-        num_scalar_prefetch=4,
+        num_scalar_prefetch=5,
         grid=(kv_group, near.shape[-1]),
-        in_specs=[q_spec, q_spec, k_spec, v_spec, k_spec, v_spec],
+        in_specs=[own_q_spec, q_spec, k_spec, v_spec, k_spec, v_spec],
         out_specs=[
-            pl.BlockSpec((None, block, width), lambda g, t, qs, ks, f, d: (qs[t], 0, g)),
-            pl.BlockSpec((None, None, block, LANES), lambda g, t, qs, ks, f, d: (g, qs[t], 0, 0)),
+            pl.BlockSpec((None, block, width), lambda g, t, qs, ks, f, d, o: (qs[t], 0, g)),
+            pl.BlockSpec(
+                (None, None, block, LANES), lambda g, t, qs, ks, f, d, o: (g, qs[t], 0, 0)
+            ),
         ],
         scratch_shapes=scratch,
     )
@@ -275,14 +278,14 @@
         grid_spec=near_spec,
         cost_estimate=pl.CostEstimate(
             flops=3 * pair_flops, transcendentals=3 * pair_exps,
-            bytes_accessed=int(keep_q.size * 12 + keep_kv.size * 4),
+            bytes_accessed=int(recv_q.size * 12 + keep_kv.size * 4),
         ),
         out_shape=[
             jax.ShapeDtypeStruct((2, block, q_cols), jnp.float32),
             jax.ShapeDtypeStruct((kv_group, 2, block, LANES), jnp.float32),
         ],
         compiler_params=params,
-    )(*[near[i] for i in range(4)], keep_q, recv_q, keep_kv, keep_kv, recv_kv, recv_kv)
+    )(*[near[i] for i in range(4)], q_offset, keep_q, recv_q, keep_kv, keep_kv, recv_kv, recv_kv)
     far_pairs = max(1, 2 * (chips - 1))
 
     def far_call(source, out_cols, col_offset):
@@ -294,7 +297,7 @@
         far_spec = pltpu.PrefetchScalarGridSpec(
             num_scalar_prefetch=6,
             grid=(kv_group, far.shape[-1]),
-            in_specs=[pl.BlockSpec(memory_space=pltpu.SMEM), q_spec]
+            in_specs=[pl.BlockSpec(memory_space=pltpu.SMEM), own_q_spec]
             + part_specs
             + [
                 pl.BlockSpec((None, STATE_ROWS, HD), lambda g, t, qp, kp, f, l, v, o: (g, 0, 0)),
@@ -314,7 +317,7 @@
             grid_spec=far_spec,
             cost_estimate=pl.CostEstimate(
                 flops=far_pairs * pair_flops // 2, transcendentals=far_pairs * pair_exps // 2,
-                bytes_accessed=int(keep_q.size * 8 + keep_kv.size * 2 * len(far_kv)),
+                bytes_accessed=int(recv_q.size * 8 + keep_kv.size * 2 * len(far_kv)),
             ),
             out_shape=jax.ShapeDtypeStruct((block, out_cols), jnp.bfloat16),
             compiler_params=params,
@@ -363,7 +366,7 @@
     sibling = [(p, p ^ 1) for p in range(parts)]
 
     delta = chip_states(keys, values, core, kv_group)
-    keep_q, keep_kv, send_q, send_kv = split_inputs(queries, keys, values, core)
+    keep_kv, send_q, send_kv = split_inputs(queries, keys, values, core)
     recv_q = lax.ppermute(send_q, "head", sibling)
     recv_kv = lax.ppermute(send_kv, "head", sibling)
     delta, keep_kv, send_kv, recv_q, recv_kv = lax.optimization_barrier(
@@ -380,7 +383,7 @@
     gate_here = lax.dynamic_slice_in_dim(gate_logit, core * kv_group * group_size, kv_group * group_size)
     mixing = jax.nn.sigmoid(gate_here)
     own_part, back = attend(
-        keep_q, recv_q, keep_kv, recv_kv, far_kv, state, mixing, chips, chip, core, group_size
+        queries, recv_q, keep_kv, recv_kv, far_kv, state, mixing, chips, chip, core, group_size
     )
     return place_back(own_part, back, core, kv_group)
 

time: 149 us -> 147 us (0.987)
  transfers between devices with their start and end apart: 10 -> 10, of which waited for: 4 -> 4; matrix products, arithmetic and copies ran while one was open for 5% -> 5% of each run, Pallas kernels for 45% -> 46%
where the time goes in v17:
time: 147 us
  Pallas kernels  105 us (71%)
  waiting for transfers between devices  19 us (13%)
  starting transfers between devices  13.6 us (9%)
  local copies, waits for them, and re-layouts  5.8 us (4%)
  other arithmetic  3.5 us (2%)
    pallas_call x2, Pallas kernels, far_call(): pl.pallas_call(functools.partial(far_kernel, group_size=group_size), grid...  60.1 us
    pallas_call x1, Pallas kernels, attend(): pl.pallas_call(functools.partial(near_kernel, group_size=group_size), gri...  32.7 us
    ppermute x1, waiting for transfers between devices, body(): lax.ppermute(keep_kv, 'head', [(p, p + 2 * s) for p in range(parts - 2 *...  11.1 us
    ppermute x3, starting transfers between devices, shifted(): lax.ppermute(value, axis, [(source, source + steps) for source in range(c...  9.48 us
    pallas_call x1, Pallas kernels, local_deltas(): pl.pallas_call(delta_kernel, out_shape=jax.ShapeDtypeStruct((kv_heads, ST...  4.49 us
    pallas_call x1, Pallas kernels, split_inputs(): pl.pallas_call(split_kernel, grid_spec=grid_spec, out_shape=[kv_shape, q_...  4.32 us
    ppermute x1, waiting for transfers between devices, chip_states(): lax.ppermute(total.astype(jnp.bfloat16), 'head', [(p, p ^ steps) for p in...  3.96 us
    pallas_call x1, Pallas kernels, place_back(): pl.pallas_call(place_kernel, grid_spec=grid_spec, out_shape=jax.ShapeDtyp...  3.04 us
  transfers between devices with their start and end apart: 10, of which 4 were waited for; matrix products, arithmetic and copies ran while one was open for 5% of the time, Pallas kernels for 46%

profile of v17, /device:TPU:13, one launch (start us, length us, event | category | flops | bytes accessed | tf_op | source)
XLA Modules:
  0.0 146.7 jit_solution(5053409728047513436)
XLA Ops:
  0.0 4.3 %shard_map.74 = (bf16[512,1024]{1,0:T(8,128)(2,1)}, bf16[512,2048]{1,0:T(8,128)(2,1)}, bf16[512,1024]{1,0:T(8,128)(2,1)}) custom-call(s32[1]{0:T(128)} %bitcast.7.core_ref, bf16[512,1024]{1,0:T(8,128)(2,1)} %k_send.1, bf16[512,1024]{1,0:T(8,128)(2,1)} %v_send.1, bf16[512,4096]{1,0:T(8,128)(2,1)} %q_ref.1, bf16[512,1024]{1,0:T(8,128)(2,1)} %k_send.1, ...), custom_call_target="tpu_custom_call" | custom-call | tf_op jit(solution)/shard_map/pallas_call | solution.py:62
  4.3 0.7 collective-permute-start.2
  5.0 0.0 collective-permute-start.3
  5.0 0.0 copy-start.4
  5.0 0.0 copy-start.5
  5.0 4.5 %shard_map.73 = f32[8,136,128]{2,1,0:T(8,128)} custom-call(bf16[512,1024]{1,0:T(8,128)(2,1)} %k_send.1, bf16[512,1024]{1,0:T(8,128)(2,1)} %v_send.1), custom_call_target="tpu_custom_call" | custom-call | tf_op jit(solution)/shard_map/pallas_call | solution.py:82
  9.5 1.0 dynamic-slice_convert_fusion
  10.5 0.6 collective-permute-start
  11.0 1.0 collective-permute-done
  12.0 1.0 fusion.2
  13.0 0.3 collective-permute-start.1
  13.3 0.7 constant_dynamic-slice_fusion
  14.0 4.0 %collective-permute-done.1 = bf16[4,136,128]{2,1,0:T(8,128)(2,1)S(1)} collective-permute-done((bf16[4,136,128]{2,1,0:T(8,128)(2,1)S(1)}, bf16[4,136,128]{2,1,0:T(8,128)(2,1)S(1)}, u32[]{:S(2)}, u32[]{:S(2)}) %collective-permute-start.1) | collective-permute-done | bytes 139296 | tf_op jit(solution)/shard_map/ppermute | solution.py:96
  18.0 1.0 convert_add_fusion.2
  19.0 0.0 collective-permute-done.3.k_recv.v_recv
  19.0 0.0 collective-permute-done.2.q_recv.q_ref
  19.0 0.0 copy-start.2
  19.1 3.1 %collective-permute-start.6 = (bf16[4,136,128]{2,1,0:T(8,128)(2,1)S(1)}, bf16[4,136,128]{2,1,0:T(8,128)(2,1)S(1)}, u32[]{:S(2)}, u32[]{:S(2)}) collective-permute-start(bf16[4,136,128]{2,1,0:T(8,128)(2,1)S(1)} %convert_element_type.34), channel_id=1, source_target_pairs={{0,4},{4,8},{8,12},{12,16},{16,20},{20,24},{24,28},{1,5},{5,9},{9,... | collective-permute-start | bytes 417800 | tf_op jit(solution)/shard_map/ppermute | solution.py:25
  22.2 0.6 slice_bitcast_fusion
  22.8 0.0 copy-done.4
  22.8 3.0 %collective-permute-done.6 = bf16[4,136,128]{2,1,0:T(8,128)(2,1)S(1)} collective-permute-done((bf16[4,136,128]{2,1,0:T(8,128)(2,1)S(1)}, bf16[4,136,128]{2,1,0:T(8,128)(2,1)S(1)}, u32[]{:S(2)}, u32[]{:S(2)}) %collective-permute-start.6) | collective-permute-done | bytes 139296 | tf_op jit(solution)/shard_map/ppermute | solution.py:25
  25.8 3.2 %collective-permute-start.7 = (bf16[4,136,128]{2,1,0:T(8,128)(2,1)S(1)}, bf16[4,136,128]{2,1,0:T(8,128)(2,1)S(1)}, u32[]{:S(2)}, u32[]{:S(2)}) collective-permute-start(bf16[4,136,128]{2,1,0:T(8,128)(2,1)S(1)} %fusion), channel_id=1, source_target_pairs={{0,8},{4,12},{8,16},{12,20},{16,24},{20,28},{1,9},{5,13},{9,17},{1... | collective-permute-start | bytes 417800 | tf_op jit(solution)/shard_map/ppermute | solution.py:25
  29.0 0.6 slice_bitcast_fusion.5
  29.6 0.0 copy-done.2
  29.6 0.0 copy-done.5
  29.6 0.6 add_divide_fusion.gate_ref
  30.2 1.3 collective-permute-start.5
  31.5 1.3 collective-permute-start.4
  32.8 0.0 collective-permute-done.7
  32.8 0.1 fusion.1
  32.9 3.2 %collective-permute-start.8 = (bf16[4,136,128]{2,1,0:T(8,128)(2,1)S(1)}, bf16[4,136,128]{2,1,0:T(8,128)(2,1)S(1)}, u32[]{:S(2)}, u32[]{:S(2)}) collective-permute-start(bf16[4,136,128]{2,1,0:T(8,128)(2,1)S(1)} %fusion.1), channel_id=1, source_target_pairs={{0,16},{4,20},{8,24},{12,28},{1,17},{5,21},{9,25},{13,29},{2,18},{... | collective-permute-start | bytes 417800 | tf_op jit(solution)/shard_map/ppermute | solution.py:25
  36.1 32.7 %shard_map.75 = (f32[2,512,2048]{2,1,0:T(8,128)}, f32[4,2,512,128]{3,2,1,0:T(8,128)}) custom-call(s32[3]{0:T(128)} %get-tuple-element.38.qs_ref, s32[3]{0:T(128)} %get-tuple-element.37.ks_ref, s32[3]{0:T(128)} %get-tuple-element.36.first_ref, s32[3]{0:T(128)} %get-tuple-element.35.diag_ref, s32[1]{0:T(128)} %bitcast.6.off_ref, bf16[512,4096]{1,0:T(8,128)(2,1)} %q_ref.1, ...), custom_call_target="tpu_custom_call" | custom-call | flops 6442450944 | bytes 14680064 | tf_op jit(solution)/shard_map/pallas_call | solution.py:276
  68.8 0.0 collective-permute-done.8
  68.8 0.8 add_subtract_fusion.refs_4_
  69.5 0.0 collective-permute-done.5.refs_2_.refs_3_
  69.5 0.0 copy-start
  69.5 11.1 %collective-permute-done.4.refs_0_.refs_1_ = bf16[512,1024]{1,0:T(8,128)(2,1)S(1)} collective-permute-done((bf16[512,1024]{1,0:T(8,128)(2,1)}, bf16[512,1024]{1,0:T(8,128)(2,1)S(1)}, u32[]{:S(2)}, u32[]{:S(2)}) %collective-permute-start.4) | collective-permute-done | bytes 1048608 | tf_op jit(solution)/shard_map/ppermute | solution.py:378
  80.6 0.0 copy-start.1
  80.6 0.0 copy-done
  80.6 1.0 copy-done.1
  81.6 30.1 %shard_map.77 = bf16[512,2048]{1,0:T(8,128)(2,1)} custom-call(s32[2]{0:T(128)} %get-tuple-element.29.qp_ref, s32[2]{0:T(128)} %get-tuple-element.28.kp_ref, s32[2]{0:T(128)} %get-tuple-element.27.first_ref, s32[2]{0:T(128)} %get-tuple-element.26.last_ref, s32[2]{0:T(128)} %get-tuple-element.25.valid_ref, s32[1]{0:T(128)} %constant.47.clone.1.off_ref, ...), custom_call_target="tpu_custom_call" | custom-call | flops 2147483648 | bytes 10485760 | tf_op jit(solution)/shard_map/pallas_call | solution.py:315
  111.7 0.0 collective-permute-start.9
  111.7 0.6 slice_bitcast_fusion.9
  112.3 30.1 %shard_map.76.full_ref = bf16[512,4096]{1,0:T(8,128)(2,1)} custom-call(s32[2]{0:T(128)} %get-tuple-element.34.qp_ref, s32[2]{0:T(128)} %get-tuple-element.33.kp_ref, s32[2]{0:T(128)} %get-tuple-element.32.first_ref, s32[2]{0:T(128)} %get-tuple-element.31.last_ref, s32[2]{0:T(128)} %get-tuple-element.30.valid_ref, s32[1]{0:T(128)} %bitcast.6.off_ref, ...), custom_call_target="tpu_custom_call" | custom-call | flops 2147483648 | bytes 10485760 | tf_op jit(solution)/shard_map/pallas_call | solution.py:315
  142.4 0.0 collective-permute-done.9.back_ref
  142.4 0.0 copy-start.3
  142.4 1.3 copy-done.3
  143.7 3.0 %shard_map.78 = bf16[512,4096]{1,0:T(8,128)(2,1)} custom-call(s32[1]{0:T(128)} %bitcast.col_ref, bf16[512,4096]{1,0:T(8,128)(2,1)} %shard_map.76.full_ref, bf16[512,2048]{1,0:T(8,128)(2,1)} %copy-done.3), custom_call_target="tpu_custom_call", output_to_operand_aliasing={{}: (1, {})} | custom-call | tf_op jit(solution)/shard_map/pallas_call | solution.py:349
  (3 shorter events, 0.1 us)
Async XLA Ops:
  4.3 14.7 %collective-permute-start.2 = (bf16[512,2048]{1,0:T(8,128)(2,1)}, bf16[512,2048]{1,0:T(8,128)(2,1)S(1)}, u32[]{:S(2)}, u32[]{:S(2)}) collective-permute-start(bf16[512,2048]{1,0:T(8,128)(2,1)} %get-tuple-element.17), channel_id=1, source_target_pairs={{0,1},{1,0},{2,3},{3,2},{4,5},{5,4},{6,7},{7,6},{8,9},{9,8},{10,11... | collective-permute-start | bytes 6291464 | tf_op jit(solution)/shard_map/ppermute | solution.py:370
  5.0 14.0 %collective-permute-start.3 = (bf16[512,1024]{1,0:T(8,128)(2,1)}, bf16[512,1024]{1,0:T(8,128)(2,1)}, u32[]{:S(2)}, u32[]{:S(2)}) collective-permute-start(bf16[512,1024]{1,0:T(8,128)(2,1)} %get-tuple-element.19), channel_id=1, source_target_pairs={{0,1},{1,0},{2,3},{3,2},{4,5},{5,4},{6,7},{7,6},{8,9},{9,8},{10,11... | collective-permute-start | bytes 3145736 | tf_op jit(solution)/shard_map/ppermute | solution.py:371
  5.0 17.8 %copy-start.4 = (s32[2,4,3]{2,1,0:T(4,128)S(1)}, s32[2,4,3]{2,1,0:T(4,128)}, u32[]{:S(2)}) copy-start(s32[2,4,3]{2,1,0:T(4,128)} %constant.48.clone) | copy-start | bytes 292
  5.0 24.6 %copy-start.5 = (f32[32]{0:T(128)S(1)}, f32[32]{0:T(128)}, u32[]{:S(2)}) copy-start(f32[32]{0:T(128)} %param.10) | copy-start | bytes 388
  10.5 1.6 %collective-permute-start = (bf16[4,136,128]{2,1,0:T(8,128)(2,1)S(1)}, bf16[4,136,128]{2,1,0:T(8,128)(2,1)S(1)}, u32[]{:S(2)}, u32[]{:S(2)}) collective-permute-start(bf16[4,136,128]{2,1,0:T(8,128)(2,1)S(1)} %dynamic-slice_convert_fusion), channel_id=1, source_target_pairs={{0,1},{1,0},{2,3},{3,2},{4,5},{5,4},{6,7},{7,6},{8,9},{9,8},{10,11... | collective-permute-start | bytes 417800 | tf_op jit(solution)/shard_map/ppermute | solution.py:93
  13.0 5.0 %collective-permute-start.1 = (bf16[4,136,128]{2,1,0:T(8,128)(2,1)S(1)}, bf16[4,136,128]{2,1,0:T(8,128)(2,1)S(1)}, u32[]{:S(2)}, u32[]{:S(2)}) collective-permute-start(bf16[4,136,128]{2,1,0:T(8,128)(2,1)S(1)} %fusion.2), channel_id=1, source_target_pairs={{0,2},{1,3},{2,0},{3,1},{4,6},{5,7},{6,4},{7,5},{8,10},{9,11},{10,... | collective-permute-start | bytes 417800 | tf_op jit(solution)/shard_map/ppermute | solution.py:96
  19.0 10.6 %copy-start.2 = (bf16[512,2048]{1,0:T(8,128)(2,1)}, bf16[512,2048]{1,0:T(8,128)(2,1)S(1)}, u32[]{:S(2)}) copy-start(bf16[512,2048]{1,0:T(8,128)(2,1)S(1)} %collective-permute-done.2.q_recv.q_ref) | copy-start | bytes 6291460
  19.1 6.7 %collective-permute-start.6 = (bf16[4,136,128]{2,1,0:T(8,128)(2,1)S(1)}, bf16[4,136,128]{2,1,0:T(8,128)(2,1)S(1)}, u32[]{:S(2)}, u32[]{:S(2)}) collective-permute-start(bf16[4,136,128]{2,1,0:T(8,128)(2,1)S(1)} %convert_element_type.34), channel_id=1, source_target_pairs={{0,4},{4,8},{8,12},{12,16},{16,20},{20,24},{24,28},{1,5},{5,9},{9,... | collective-permute-start | bytes 417800 | tf_op jit(solution)/shard_map/ppermute | solution.py:25
  25.8 7.0 %collective-permute-start.7 = (bf16[4,136,128]{2,1,0:T(8,128)(2,1)S(1)}, bf16[4,136,128]{2,1,0:T(8,128)(2,1)S(1)}, u32[]{:S(2)}, u32[]{:S(2)}) collective-permute-start(bf16[4,136,128]{2,1,0:T(8,128)(2,1)S(1)} %fusion), channel_id=1, source_target_pairs={{0,8},{4,12},{8,16},{12,20},{16,24},{20,28},{1,9},{5,13},{9,17},{1... | collective-permute-start | bytes 417800 | tf_op jit(solution)/shard_map/ppermute | solution.py:25
  30.2 39.3 %collective-permute-start.5 = (bf16[512,1024]{1,0:T(8,128)(2,1)}, bf16[512,1024]{1,0:T(8,128)(2,1)S(1)}, u32[]{:S(2)}, u32[]{:S(2)}) collective-permute-start(bf16[512,1024]{1,0:T(8,128)(2,1)} %get-tuple-element.19), channel_id=1, source_target_pairs={{0,3},{1,2},{4,7},{5,6},{8,11},{9,10},{12,15},{13,14},{16,19},{17,... | collective-permute-start | bytes 3145736 | tf_op jit(solution)/shard_map/ppermute | solution.py:380
  31.5 49.1 %collective-permute-start.4 = (bf16[512,1024]{1,0:T(8,128)(2,1)}, bf16[512,1024]{1,0:T(8,128)(2,1)S(1)}, u32[]{:S(2)}, u32[]{:S(2)}) collective-permute-start(bf16[512,1024]{1,0:T(8,128)(2,1)} %get-tuple-element.18.k_keep.v_keep), channel_id=1, source_target_pairs={{0,2},{1,3},{4,6},{5,7},{8,10},{9,11},{12,14},{13,15},{16,18},{17,... | collective-permute-start | bytes 3145736 | tf_op jit(solution)/shard_map/ppermute | solution.py:378
  32.9 35.9 %collective-permute-start.8 = (bf16[4,136,128]{2,1,0:T(8,128)(2,1)S(1)}, bf16[4,136,128]{2,1,0:T(8,128)(2,1)S(1)}, u32[]{:S(2)}, u32[]{:S(2)}) collective-permute-start(bf16[4,136,128]{2,1,0:T(8,128)(2,1)S(1)} %fusion.1), channel_id=1, source_target_pairs={{0,16},{4,20},{8,24},{12,28},{1,17},{5,21},{9,25},{13,29},{2,18},{... | collective-permute-start | bytes 417800 | tf_op jit(solution)/shard_map/ppermute | solution.py:25
  69.5 11.1 %copy-start = (bf16[512,1024]{1,0:T(8,128)(2,1)}, bf16[512,1024]{1,0:T(8,128)(2,1)S(1)}, u32[]{:S(2)}) copy-start(bf16[512,1024]{1,0:T(8,128)(2,1)S(1)} %collective-permute-done.5.refs_2_.refs_3_) | copy-start | bytes 3145732
  80.6 1.0 copy-start.1
  111.7 30.7 %collective-permute-start.9 = (bf16[512,2048]{1,0:T(8,128)(2,1)}, bf16[512,2048]{1,0:T(8,128)(2,1)S(1)}, u32[]{:S(2)}, u32[]{:S(2)}) collective-permute-start(bf16[512,2048]{1,0:T(8,128)(2,1)} %shard_map.77), channel_id=1, source_target_pairs={{0,1},{1,0},{2,3},{3,2},{4,5},{5,4},{6,7},{7,6},{8,9},{9,8},{10,11... | collective-permute-start | bytes 6291464 | tf_op jit(solution)/shard_map/ppermute | solution.py:328
  142.4 1.3 copy-start.3

commit v18 on v17

--- a/solution.py
+++ b/solution.py
@@ -25,24 +25,41 @@
     return lax.ppermute(value, axis, [(source, source + steps) for source in range(count - steps)])
 
 
+def head_sums(k_ref, v_ref, o_ref):
+    for head in range(o_ref.shape[0]):
+        lanes = slice(head * HD, (head + 1) * HD)
+        key_feature = feature(k_ref[:, lanes].astype(jnp.float32))
+        value_data = v_ref[:, lanes].astype(jnp.float32)
+        o_ref[head, :HD, :] = jnp.dot(
+            key_feature.T, value_data, precision=lax.Precision.HIGHEST,
+            preferred_element_type=jnp.float32,
+        )
+        o_ref[head, HD:, :] = jnp.zeros((STATE_ROWS - HD, HD), jnp.float32)
+        o_ref[head, HD : HD + 1, :] = jnp.sum(key_feature, axis=0, keepdims=True)
+
+
 def split_kernel(core_ref, k_keep, v_keep, q_send, k_send, v_send, *out_refs):
     k_cols = k_keep.shape[-1]
-    keep_kv, send_q, send_kv = out_refs
+    keep_kv, send_q, send_kv, keep_sums, send_sums = out_refs
     keep_kv[:, :k_cols] = k_keep[...]
     keep_kv[:, k_cols:] = v_keep[...]
     send_q[...] = q_send[...]
     send_kv[:, :k_cols] = k_send[...]
     send_kv[:, k_cols:] = v_send[...]
+    head_sums(k_keep, v_keep, keep_sums)
+    head_sums(k_send, v_send, send_sums)
 
 
 def split_inputs(queries, keys, values, core):
     tokens_here, q_all = queries.shape
     q_cols = q_all // 2
     k_cols = keys.shape[1] // 2
+    kv_group = k_cols // HD
     keep_map = lambda i, c: (0, c[0])
     send_map = lambda i, c: (0, 1 - c[0])
     q_shape = jax.ShapeDtypeStruct((tokens_here, q_cols), queries.dtype)
     kv_shape = jax.ShapeDtypeStruct((tokens_here, 2 * k_cols), keys.dtype)
+    sums_shape = jax.ShapeDtypeStruct((kv_group, STATE_ROWS, HD), jnp.float32)
     grid_spec = pltpu.PrefetchScalarGridSpec(
         num_scalar_prefetch=1,
         grid=(1,),
@@ -57,39 +74,19 @@
             pl.BlockSpec((tokens_here, 2 * k_cols), lambda i, c: (0, 0)),
             pl.BlockSpec((tokens_here, q_cols), lambda i, c: (0, 0)),
             pl.BlockSpec((tokens_here, 2 * k_cols), lambda i, c: (0, 0)),
+            pl.BlockSpec((kv_group, STATE_ROWS, HD), lambda i, c: (0, 0, 0)),
+            pl.BlockSpec((kv_group, STATE_ROWS, HD), lambda i, c: (0, 0, 0)),
         ],
     )
     return pl.pallas_call(
-        split_kernel, grid_spec=grid_spec, out_shape=[kv_shape, q_shape, kv_shape]
+        split_kernel,
+        grid_spec=grid_spec,
+        out_shape=[kv_shape, q_shape, kv_shape, sums_shape, sums_shape],
     )(core.reshape(1), keys, values, queries, keys, values)
 
 
-def delta_kernel(k_ref, v_ref, o_ref):
-    for head in range(o_ref.shape[0]):
-        lanes = slice(head * HD, (head + 1) * HD)
-        key_feature = feature(k_ref[:, lanes].astype(jnp.float32))
-        value_data = v_ref[:, lanes].astype(jnp.float32)
-        o_ref[head, :HD, :] = jnp.dot(
-            key_feature.T, value_data, precision=lax.Precision.HIGHEST,
-            preferred_element_type=jnp.float32,
-        )
-        o_ref[head, HD:, :] = jnp.zeros((STATE_ROWS - HD, HD), jnp.float32)
-        o_ref[head, HD : HD + 1, :] = jnp.sum(key_feature, axis=0, keepdims=True)
-
-
-def local_deltas(keys, values):
-    kv_heads = keys.shape[1] // HD
-    return pl.pallas_call(
-        delta_kernel,
-        out_shape=jax.ShapeDtypeStruct((kv_heads, STATE_ROWS, HD), jnp.float32),
-    )(keys, values)
-
-
-def chip_states(keys, values, core, kv_group):
-    total = local_deltas(keys, values)
+def chip_states(keep, send):
     parts = lax.axis_size("head")
-    keep = lax.dynamic_slice_in_dim(total, core * kv_group, kv_group)
-    send = lax.dynamic_slice_in_dim(total, (1 - core) * kv_group, kv_group)
     total = keep + lax.ppermute(send.astype(jnp.bfloat16), "head", [(p, p ^ 1) for p in range(parts)])
     steps = 2
     while steps < parts:
@@ -365,8 +362,8 @@
     group_size = queries.shape[1] // keys.shape[1]
     sibling = [(p, p ^ 1) for p in range(parts)]
 
-    delta = chip_states(keys, values, core, kv_group)
-    keep_kv, send_q, send_kv = split_inputs(queries, keys, values, core)
+    keep_kv, send_q, send_kv, keep_sums, send_sums = split_inputs(queries, keys, values, core)
+    delta = chip_states(keep_sums, send_sums)
     recv_q = lax.ppermute(send_q, "head", sibling)
     recv_kv = lax.ppermute(send_kv, "head", sibling)
     delta, keep_kv, send_kv, recv_q, recv_kv = lax.optimization_barrier(

time: 147 us -> 148 us (level)
  Pallas kernels: 105 us -> 102 us
  waiting for transfers between devices: 19 us -> 21.5 us
    pallas_call x1 -> x0, Pallas kernels: 4.49 us -> none  [local_deltas(): pl.pallas_call(delta_kernel, out_shape=jax.ShapeDtypeStruct((kv_heads, ST...]
    ppermute x1, waiting for transfers between devices: 1 us -> 3.41 us  [chip_states(): lax.ppermute(send.astype(jnp.bfloat16), 'head', [(p, p ^ 1) for p in rang...]
    pallas_call x1, Pallas kernels: 4.32 us -> 6.45 us  [split_inputs(): pl.pallas_call(split_kernel, grid_spec=grid_spec, out_shape=[kv_shape, q_...]
  transfers between devices with their start and end apart: 10 -> 10, of which waited for: 4 -> 4; matrix products, arithmetic and copies ran while one was open for 5% -> 5% of each run, Pallas kernels for 46% -> 43%
where the time goes in v18:
time: 148 us; the launch traced here: 147 us
  Pallas kernels  102 us (69%)
  waiting for transfers between devices  21.5 us (15%)
  starting transfers between devices  13.7 us (9%)
  local copies, waits for them, and re-layouts  4.83 us (3%)
  other arithmetic  4.47 us (3%)
    pallas_call x2, Pallas kernels, far_call(): pl.pallas_call(functools.partial(far_kernel, group_size=group_size), grid...  60.1 us
    pallas_call x1, Pallas kernels, attend(): pl.pallas_call(functools.partial(near_kernel, group_size=group_size), gri...  32.7 us
    ppermute x1, waiting for transfers between devices, body(): lax.ppermute(keep_kv, 'head', [(p, p + 2 * s) for p in range(parts - 2 *...  11.1 us
    ppermute x3, starting transfers between devices, shifted(): lax.ppermute(value, axis, [(source, source + steps) for source in range(c...  9.48 us
    pallas_call x1, Pallas kernels, split_inputs(): pl.pallas_call(split_kernel, grid_spec=grid_spec, out_shape=[kv_shape, q_...  6.45 us
    ppermute x1, waiting for transfers between devices, chip_states(): lax.ppermute(total.astype(jnp.bfloat16), 'head', [(p, p ^ steps) for p in...  3.96 us
    ppermute x1, waiting for transfers between devices, chip_states(): lax.ppermute(send.astype(jnp.bfloat16), 'head', [(p, p ^ 1) for p in rang...  3.41 us
    pallas_call x1, Pallas kernels, place_back(): pl.pallas_call(place_kernel, grid_spec=grid_spec, out_shape=jax.ShapeDtyp...  3.04 us
  transfers between devices with their start and end apart: 10, of which 4 were waited for; matrix products, arithmetic and copies ran while one was open for 5% of the time, Pallas kernels for 43%

profile of v18, /device:TPU:13, one launch (start us, length us, event | category | flops | bytes accessed | tf_op | source)
XLA Modules:
  0.0 146.8 jit_solution(346964216160616533)
XLA Ops:
  0.0 6.4 %shard_map.73 = (bf16[512,1024]{1,0:T(8,128)(2,1)}, bf16[512,2048]{1,0:T(8,128)(2,1)}, bf16[512,1024]{1,0:T(8,128)(2,1)}, f32[4,136,128]{2,1,0:T(8,128)}, f32[4,136,128]{2,1,0:T(8,128)}) custom-call(s32[1]{0:T(128)} %bitcast.7.core_ref, bf16[512,1024]{1,0:T(8,128)(2,1)} %k_send.1, bf16[512,1024]{1,0:T(8,128)(2,1)} %v_send.1, bf16[512,4096]{1,0:T(8,128)(2,1)} %q_ref.1, ...), custom_call_target="tpu_custom_call" | custom-call | tf_op jit(solution)/shard_map/pallas_call | solution.py:81
  6.4 0.0 copy-start.4
  6.4 0.0 copy-start.5
  6.5 0.7 collective-permute-start.2
  7.2 0.1 collective-permute-start.3
  7.3 1.0 convert_element_type.30
  8.2 0.5 collective-permute-start
  8.7 3.4 %collective-permute-done = bf16[4,136,128]{2,1,0:T(8,128)(2,1)S(1)} collective-permute-done((bf16[4,136,128]{2,1,0:T(8,128)(2,1)S(1)}, bf16[4,136,128]{2,1,0:T(8,128)(2,1)S(1)}, u32[]{:S(2)}, u32[]{:S(2)}) %collective-permute-start) | collective-permute-done | bytes 139296 | tf_op jit(solution)/shard_map/ppermute | solution.py:90
  12.2 1.0 fusion
  13.2 0.3 collective-permute-start.1
  13.4 0.7 constant_dynamic-slice_fusion
  14.1 4.0 %collective-permute-done.1 = bf16[4,136,128]{2,1,0:T(8,128)(2,1)S(1)} collective-permute-done((bf16[4,136,128]{2,1,0:T(8,128)(2,1)S(1)}, bf16[4,136,128]{2,1,0:T(8,128)(2,1)S(1)}, u32[]{:S(2)}, u32[]{:S(2)}) %collective-permute-start.1) | collective-permute-done | bytes 139296 | tf_op jit(solution)/shard_map/ppermute | solution.py:93
  18.1 1.0 convert_add_fusion.2
  19.1 0.0 collective-permute-done.3.k_recv.v_recv
  19.1 0.0 collective-permute-done.2.q_recv.q_ref
  19.1 0.0 copy-start.2
  19.2 3.1 %collective-permute-start.6 = (bf16[4,136,128]{2,1,0:T(8,128)(2,1)S(1)}, bf16[4,136,128]{2,1,0:T(8,128)(2,1)S(1)}, u32[]{:S(2)}, u32[]{:S(2)}) collective-permute-start(bf16[4,136,128]{2,1,0:T(8,128)(2,1)S(1)} %convert_element_type.34), channel_id=1, source_target_pairs={{0,4},{4,8},{8,12},{12,16},{16,20},{20,24},{24,28},{1,5},{5,9},{9,... | collective-permute-start | bytes 417800 | tf_op jit(solution)/shard_map/ppermute | solution.py:25
  22.3 0.6 slice_bitcast_fusion
  22.9 0.0 copy-done.4
  22.9 3.0 %collective-permute-done.6 = bf16[4,136,128]{2,1,0:T(8,128)(2,1)S(1)} collective-permute-done((bf16[4,136,128]{2,1,0:T(8,128)(2,1)S(1)}, bf16[4,136,128]{2,1,0:T(8,128)(2,1)S(1)}, u32[]{:S(2)}, u32[]{:S(2)}) %collective-permute-start.6) | collective-permute-done | bytes 139296 | tf_op jit(solution)/shard_map/ppermute | solution.py:25
  25.9 3.2 %collective-permute-start.7 = (bf16[4,136,128]{2,1,0:T(8,128)(2,1)S(1)}, bf16[4,136,128]{2,1,0:T(8,128)(2,1)S(1)}, u32[]{:S(2)}, u32[]{:S(2)}) collective-permute-start(bf16[4,136,128]{2,1,0:T(8,128)(2,1)S(1)} %fusion.1), channel_id=1, source_target_pairs={{0,8},{4,12},{8,16},{12,20},{16,24},{20,28},{1,9},{5,13},{9,17},{1... | collective-permute-start | bytes 417800 | tf_op jit(solution)/shard_map/ppermute | solution.py:25
  29.1 0.6 slice_bitcast_fusion.5
  29.7 0.0 copy-done.2
  29.7 0.0 copy-done.5
  29.7 0.6 add_divide_fusion.gate_ref
  30.3 1.3 collective-permute-start.5
  31.6 1.3 collective-permute-start.4
  32.9 0.0 collective-permute-done.7
  32.9 0.1 fusion.2
  33.0 3.2 %collective-permute-start.8 = (bf16[4,136,128]{2,1,0:T(8,128)(2,1)S(1)}, bf16[4,136,128]{2,1,0:T(8,128)(2,1)S(1)}, u32[]{:S(2)}, u32[]{:S(2)}) collective-permute-start(bf16[4,136,128]{2,1,0:T(8,128)(2,1)S(1)} %fusion.2), channel_id=1, source_target_pairs={{0,16},{4,20},{8,24},{12,28},{1,17},{5,21},{9,25},{13,29},{2,18},{... | collective-permute-start | bytes 417800 | tf_op jit(solution)/shard_map/ppermute | solution.py:25
  36.2 32.7 %shard_map.74 = (f32[2,512,2048]{2,1,0:T(8,128)}, f32[4,2,512,128]{3,2,1,0:T(8,128)}) custom-call(s32[3]{0:T(128)} %get-tuple-element.42.qs_ref, s32[3]{0:T(128)} %get-tuple-element.41.ks_ref, s32[3]{0:T(128)} %get-tuple-element.40.first_ref, s32[3]{0:T(128)} %get-tuple-element.39.diag_ref, s32[1]{0:T(128)} %bitcast.6.off_ref, bf16[512,4096]{1,0:T(8,128)(2,1)} %q_ref.1, ...), custom_call_target="tpu_custom_call" | custom-call | flops 6442450944 | bytes 14680064 | tf_op jit(solution)/shard_map/pallas_call | solution.py:273
  68.9 0.0 collective-permute-done.8
  68.9 0.8 add_subtract_fusion.refs_4_
  69.6 0.0 collective-permute-done.5.refs_2_.refs_3_
  69.6 0.0 copy-start
  69.6 11.1 %collective-permute-done.4.refs_0_.refs_1_ = bf16[512,1024]{1,0:T(8,128)(2,1)S(1)} collective-permute-done((bf16[512,1024]{1,0:T(8,128)(2,1)}, bf16[512,1024]{1,0:T(8,128)(2,1)S(1)}, u32[]{:S(2)}, u32[]{:S(2)}) %collective-permute-start.4) | collective-permute-done | bytes 1048608 | tf_op jit(solution)/shard_map/ppermute | solution.py:375
  80.8 0.0 copy-start.1
  80.8 0.0 copy-done
  80.8 1.0 copy-done.1
  81.7 30.1 %shard_map.76 = bf16[512,2048]{1,0:T(8,128)(2,1)} custom-call(s32[2]{0:T(128)} %get-tuple-element.33.qp_ref, s32[2]{0:T(128)} %get-tuple-element.32.kp_ref, s32[2]{0:T(128)} %get-tuple-element.31.first_ref, s32[2]{0:T(128)} %get-tuple-element.30.last_ref, s32[2]{0:T(128)} %get-tuple-element.29.valid_ref, s32[1]{0:T(128)} %constant.45.clone.1.off_ref, ...), custom_call_target="tpu_custom_call" | custom-call | flops 2147483648 | bytes 10485760 | tf_op jit(solution)/shard_map/pallas_call | solution.py:312
  111.8 0.0 collective-permute-start.9
  111.8 0.6 slice_bitcast_fusion.9
  112.4 30.1 %shard_map.75.full_ref = bf16[512,4096]{1,0:T(8,128)(2,1)} custom-call(s32[2]{0:T(128)} %get-tuple-element.38.qp_ref, s32[2]{0:T(128)} %get-tuple-element.37.kp_ref, s32[2]{0:T(128)} %get-tuple-element.36.first_ref, s32[2]{0:T(128)} %get-tuple-element.35.last_ref, s32[2]{0:T(128)} %get-tuple-element.34.valid_ref, s32[1]{0:T(128)} %bitcast.6.off_ref, ...), custom_call_target="tpu_custom_call" | custom-call | flops 2147483648 | bytes 10485760 | tf_op jit(solution)/shard_map/pallas_call | solution.py:312
  142.5 0.0 collective-permute-done.9.back_ref
  142.5 0.0 copy-start.3
  142.5 1.3 copy-done.3
  143.8 3.0 %shard_map.77 = bf16[512,4096]{1,0:T(8,128)(2,1)} custom-call(s32[1]{0:T(128)} %bitcast.col_ref, bf16[512,4096]{1,0:T(8,128)(2,1)} %shard_map.75.full_ref, bf16[512,2048]{1,0:T(8,128)(2,1)} %copy-done.3), custom_call_target="tpu_custom_call", output_to_operand_aliasing={{}: (1, {})} | custom-call | tf_op jit(solution)/shard_map/pallas_call | solution.py:346
  (3 shorter events, 0.1 us)
Async XLA Ops:
  6.4 16.4 %copy-start.4 = (s32[2,4,3]{2,1,0:T(4,128)S(1)}, s32[2,4,3]{2,1,0:T(4,128)}, u32[]{:S(2)}) copy-start(s32[2,4,3]{2,1,0:T(4,128)} %constant.46.clone) | copy-start | bytes 292
  6.4 23.3 %copy-start.5 = (f32[32]{0:T(128)S(1)}, f32[32]{0:T(128)}, u32[]{:S(2)}) copy-start(f32[32]{0:T(128)} %param.10) | copy-start | bytes 388
  6.5 12.7 %collective-permute-start.2 = (bf16[512,2048]{1,0:T(8,128)(2,1)}, bf16[512,2048]{1,0:T(8,128)(2,1)S(1)}, u32[]{:S(2)}, u32[]{:S(2)}) collective-permute-start(bf16[512,2048]{1,0:T(8,128)(2,1)} %get-tuple-element.21), channel_id=1, source_target_pairs={{0,1},{1,0},{2,3},{3,2},{4,5},{5,4},{6,7},{7,6},{8,9},{9,8},{10,11... | collective-permute-start | bytes 6291464 | tf_op jit(solution)/shard_map/ppermute | solution.py:367
  7.2 11.9 %collective-permute-start.3 = (bf16[512,1024]{1,0:T(8,128)(2,1)}, bf16[512,1024]{1,0:T(8,128)(2,1)}, u32[]{:S(2)}, u32[]{:S(2)}) collective-permute-start(bf16[512,1024]{1,0:T(8,128)(2,1)} %get-tuple-element.23), channel_id=1, source_target_pairs={{0,1},{1,0},{2,3},{3,2},{4,5},{5,4},{6,7},{7,6},{8,9},{9,8},{10,11... | collective-permute-start | bytes 3145736 | tf_op jit(solution)/shard_map/ppermute | solution.py:368
  8.2 3.9 %collective-permute-start = (bf16[4,136,128]{2,1,0:T(8,128)(2,1)S(1)}, bf16[4,136,128]{2,1,0:T(8,128)(2,1)S(1)}, u32[]{:S(2)}, u32[]{:S(2)}) collective-permute-start(bf16[4,136,128]{2,1,0:T(8,128)(2,1)S(1)} %convert_element_type.30), channel_id=1, source_target_pairs={{0,1},{1,0},{2,3},{3,2},{4,5},{5,4},{6,7},{7,6},{8,9},{9,8},{10,11... | collective-permute-start | bytes 417800 | tf_op jit(solution)/shard_map/ppermute | solution.py:90
  13.2 5.0 %collective-permute-start.1 = (bf16[4,136,128]{2,1,0:T(8,128)(2,1)S(1)}, bf16[4,136,128]{2,1,0:T(8,128)(2,1)S(1)}, u32[]{:S(2)}, u32[]{:S(2)}) collective-permute-start(bf16[4,136,128]{2,1,0:T(8,128)(2,1)S(1)} %fusion), channel_id=1, source_target_pairs={{0,2},{1,3},{2,0},{3,1},{4,6},{5,7},{6,4},{7,5},{8,10},{9,11},{10,... | collective-permute-start | bytes 417800 | tf_op jit(solution)/shard_map/ppermute | solution.py:93
  19.1 10.6 %copy-start.2 = (bf16[512,2048]{1,0:T(8,128)(2,1)}, bf16[512,2048]{1,0:T(8,128)(2,1)S(1)}, u32[]{:S(2)}) copy-start(bf16[512,2048]{1,0:T(8,128)(2,1)S(1)} %collective-permute-done.2.q_recv.q_ref) | copy-start | bytes 6291460
  19.2 6.7 %collective-permute-start.6 = (bf16[4,136,128]{2,1,0:T(8,128)(2,1)S(1)}, bf16[4,136,128]{2,1,0:T(8,128)(2,1)S(1)}, u32[]{:S(2)}, u32[]{:S(2)}) collective-permute-start(bf16[4,136,128]{2,1,0:T(8,128)(2,1)S(1)} %convert_element_type.34), channel_id=1, source_target_pairs={{0,4},{4,8},{8,12},{12,16},{16,20},{20,24},{24,28},{1,5},{5,9},{9,... | collective-permute-start | bytes 417800 | tf_op jit(solution)/shard_map/ppermute | solution.py:25
  25.9 7.0 %collective-permute-start.7 = (bf16[4,136,128]{2,1,0:T(8,128)(2,1)S(1)}, bf16[4,136,128]{2,1,0:T(8,128)(2,1)S(1)}, u32[]{:S(2)}, u32[]{:S(2)}) collective-permute-start(bf16[4,136,128]{2,1,0:T(8,128)(2,1)S(1)} %fusion.1), channel_id=1, source_target_pairs={{0,8},{4,12},{8,16},{12,20},{16,24},{20,28},{1,9},{5,13},{9,17},{1... | collective-permute-start | bytes 417800 | tf_op jit(solution)/shard_map/ppermute | solution.py:25
  30.3 39.3 %collective-permute-start.5 = (bf16[512,1024]{1,0:T(8,128)(2,1)}, bf16[512,1024]{1,0:T(8,128)(2,1)S(1)}, u32[]{:S(2)}, u32[]{:S(2)}) collective-permute-start(bf16[512,1024]{1,0:T(8,128)(2,1)} %get-tuple-element.23), channel_id=1, source_target_pairs={{0,3},{1,2},{4,7},{5,6},{8,11},{9,10},{12,15},{13,14},{16,19},{17,... | collective-permute-start | bytes 3145736 | tf_op jit(solution)/shard_map/ppermute | solution.py:377
  31.6 49.1 %collective-permute-start.4 = (bf16[512,1024]{1,0:T(8,128)(2,1)}, bf16[512,1024]{1,0:T(8,128)(2,1)S(1)}, u32[]{:S(2)}, u32[]{:S(2)}) collective-permute-start(bf16[512,1024]{1,0:T(8,128)(2,1)} %get-tuple-element.22.k_keep.v_keep), channel_id=1, source_target_pairs={{0,2},{1,3},{4,6},{5,7},{8,10},{9,11},{12,14},{13,15},{16,18},{17,... | collective-permute-start | bytes 3145736 | tf_op jit(solution)/shard_map/ppermute | solution.py:375
  33.0 35.9 %collective-permute-start.8 = (bf16[4,136,128]{2,1,0:T(8,128)(2,1)S(1)}, bf16[4,136,128]{2,1,0:T(8,128)(2,1)S(1)}, u32[]{:S(2)}, u32[]{:S(2)}) collective-permute-start(bf16[4,136,128]{2,1,0:T(8,128)(2,1)S(1)} %fusion.2), channel_id=1, source_target_pairs={{0,16},{4,20},{8,24},{12,28},{1,17},{5,21},{9,25},{13,29},{2,18},{... | collective-permute-start | bytes 417800 | tf_op jit(solution)/shard_map/ppermute | solution.py:25
  69.6 11.1 %copy-start = (bf16[512,1024]{1,0:T(8,128)(2,1)}, bf16[512,1024]{1,0:T(8,128)(2,1)S(1)}, u32[]{:S(2)}) copy-start(bf16[512,1024]{1,0:T(8,128)(2,1)S(1)} %collective-permute-done.5.refs_2_.refs_3_) | copy-start | bytes 3145732
  80.8 1.0 copy-start.1
  111.8 30.7 %collective-permute-start.9 = (bf16[512,2048]{1,0:T(8,128)(2,1)}, bf16[512,2048]{1,0:T(8,128)(2,1)S(1)}, u32[]{:S(2)}, u32[]{:S(2)}) collective-permute-start(bf16[512,2048]{1,0:T(8,128)(2,1)} %shard_map.76), channel_id=1, source_target_pairs={{0,1},{1,0},{2,3},{3,2},{4,5},{5,4},{6,7},{7,6},{8,9},{9,8},{10,11... | collective-permute-start | bytes 6291464 | tf_op jit(solution)/shard_map/ppermute | solution.py:325
  142.5 1.3 copy-start.3

commit v19 on v18

--- a/solution.py
+++ b/solution.py
@@ -40,14 +40,13 @@
 
 def split_kernel(core_ref, k_keep, v_keep, q_send, k_send, v_send, *out_refs):
     k_cols = k_keep.shape[-1]
-    keep_kv, send_q, send_kv, keep_sums, send_sums = out_refs
+    keep_kv, send_q, send_kv, keep_sums = out_refs
     keep_kv[:, :k_cols] = k_keep[...]
     keep_kv[:, k_cols:] = v_keep[...]
     send_q[...] = q_send[...]
     send_kv[:, :k_cols] = k_send[...]
     send_kv[:, k_cols:] = v_send[...]
     head_sums(k_keep, v_keep, keep_sums)
-    head_sums(k_send, v_send, send_sums)
 
 
 def split_inputs(queries, keys, values, core):
@@ -75,19 +74,39 @@
             pl.BlockSpec((tokens_here, q_cols), lambda i, c: (0, 0)),
             pl.BlockSpec((tokens_here, 2 * k_cols), lambda i, c: (0, 0)),
             pl.BlockSpec((kv_group, STATE_ROWS, HD), lambda i, c: (0, 0, 0)),
-            pl.BlockSpec((kv_group, STATE_ROWS, HD), lambda i, c: (0, 0, 0)),
         ],
     )
     return pl.pallas_call(
         split_kernel,
         grid_spec=grid_spec,
-        out_shape=[kv_shape, q_shape, kv_shape, sums_shape, sums_shape],
+        out_shape=[kv_shape, q_shape, kv_shape, sums_shape],
     )(core.reshape(1), keys, values, queries, keys, values)
 
 
-def chip_states(keep, send):
+def kv_sums_kernel(kv_ref, o_ref):
+    k_cols = kv_ref.shape[-1] // 2
+    for head in range(o_ref.shape[0]):
+        key_feature = feature(kv_ref[:, head * HD : (head + 1) * HD].astype(jnp.float32))
+        value_data = kv_ref[:, k_cols + head * HD : k_cols + (head + 1) * HD].astype(jnp.float32)
+        o_ref[head, :HD, :] = jnp.dot(
+            key_feature.T, value_data, precision=lax.Precision.HIGHEST,
+            preferred_element_type=jnp.float32,
+        )
+        o_ref[head, HD:, :] = jnp.zeros((STATE_ROWS - HD, HD), jnp.float32)
+        o_ref[head, HD : HD + 1, :] = jnp.sum(key_feature, axis=0, keepdims=True)
+
+
+def kv_sums(kv_rows):
+    kv_group = kv_rows.shape[-1] // (2 * HD)
+    return pl.pallas_call(
+        kv_sums_kernel,
+        out_shape=jax.ShapeDtypeStruct((kv_group, STATE_ROWS, HD), jnp.float32),
+    )(kv_rows)
+
+
+def chip_states(keep, recv_kv):
     parts = lax.axis_size("head")
-    total = keep + lax.ppermute(send.astype(jnp.bfloat16), "head", [(p, p ^ 1) for p in range(parts)])
+    total = keep + kv_sums(recv_kv)
     steps = 2
     while steps < parts:
         across = lax.ppermute(total.astype(jnp.bfloat16), "head", [(p, p ^ steps) for p in range(parts)])
@@ -362,10 +381,10 @@
     group_size = queries.shape[1] // keys.shape[1]
     sibling = [(p, p ^ 1) for p in range(parts)]
 
-    keep_kv, send_q, send_kv, keep_sums, send_sums = split_inputs(queries, keys, values, core)
-    delta = chip_states(keep_sums, send_sums)
+    keep_kv, send_q, send_kv, keep_sums = split_inputs(queries, keys, values, core)
     recv_q = lax.ppermute(send_q, "head", sibling)
     recv_kv = lax.ppermute(send_kv, "head", sibling)
+    delta = chip_states(keep_sums, recv_kv)
     delta, keep_kv, send_kv, recv_q, recv_kv = lax.optimization_barrier(
         (delta, keep_kv, send_kv, recv_q, recv_kv)
     )

time: 148 us -> 150 us (1.014)
  waiting for transfers between devices: 21.5 us -> 23.6 us
  Pallas kernels: 102 us -> 104 us
  other arithmetic: 4.47 us -> 2.64 us
    ppermute x1, waiting for transfers between devices: 0.01 us -> 5.42 us  [body(): recv_kv = lax.ppermute(send_kv, 'head', sibling)]
    ppermute x1 -> x0, waiting for transfers between devices: 3.41 us -> none  [chip_states(): lax.ppermute(send.astype(jnp.bfloat16), 'head', [(p, p ^ 1) for p in rang...]
    pallas_call x0 -> x1, Pallas kernels: none -> 3.08 us  [kv_sums(): pl.pallas_call(kv_sums_kernel, out_shape=jax.ShapeDtypeStruct((kv_group,...]
    unnamed x12 -> x14, local copies, waits for them, and re-layouts: 2.33 us -> 3.35 us
  transfers between devices with their start and end apart: 10 -> 9, of which waited for: 4 -> 4; matrix products, arithmetic and copies ran while one was open for 5% -> 3% of each run, Pallas kernels for 43% -> 44%
where the time goes in v19:
time: 150 us
  Pallas kernels  104 us (69%)
  waiting for transfers between devices  23.6 us (16%)
  starting transfers between devices  13.1 us (9%)
  local copies, waits for them, and re-layouts  5.87 us (4%)
  other arithmetic  2.64 us (2%)
    pallas_call x2, Pallas kernels, far_call(): pl.pallas_call(functools.partial(far_kernel, group_size=group_size), grid...  60.1 us
    pallas_call x1, Pallas kernels, attend(): pl.pallas_call(functools.partial(near_kernel, group_size=group_size), gri...  32.6 us
    ppermute x1, waiting for transfers between devices, body(): lax.ppermute(keep_kv, 'head', [(p, p + 2 * s) for p in range(parts - 2 *...  11.3 us
    ppermute x3, starting transfers between devices, shifted(): lax.ppermute(value, axis, [(source, source + steps) for source in range(c...  9.45 us
    pallas_call x1, Pallas kernels, split_inputs(): pl.pallas_call(split_kernel, grid_spec=grid_spec, out_shape=[kv_shape, q_...  5.47 us
    ppermute x1, waiting for transfers between devices, body(): recv_kv = lax.ppermute(send_kv, 'head', sibling)  5.42 us
    ppermute x1, waiting for transfers between devices, chip_states(): lax.ppermute(total.astype(jnp.bfloat16), 'head', [(p, p ^ steps) for p in...  3.96 us
    unnamed x14, local copies, waits for them, and re-layouts  3.35 us
  transfers between devices with their start and end apart: 9, of which 4 were waited for; matrix products, arithmetic and copies ran while one was open for 3% of the time, Pallas kernels for 44%

profile of v19, /device:TPU:13, one launch (start us, length us, event | category | flops | bytes accessed | tf_op | source)
XLA Modules:
  0.0 149.7 jit_solution(9339512530421593922)
XLA Ops:
  0.0 5.5 %shard_map.73 = (bf16[512,1024]{1,0:T(8,128)(2,1)}, bf16[512,2048]{1,0:T(8,128)(2,1)}, bf16[512,1024]{1,0:T(8,128)(2,1)}, f32[4,136,128]{2,1,0:T(8,128)}) custom-call(s32[1]{0:T(128)} %bitcast.7.core_ref, bf16[512,1024]{1,0:T(8,128)(2,1)} %k_send.1, bf16[512,1024]{1,0:T(8,128)(2,1)} %v_send.1, bf16[512,4096]{1,0:T(8,128)(2,1)} %q_ref.1, ...), custom_call_target="tpu_custom_call" | custom-call | tf_op jit(solution)/shard_map/pallas_call | solution.py:79
  5.5 0.0 copy-start.5
  5.5 0.0 copy-start.6
  5.5 0.7 collective-permute-start.2
  6.2 0.1 collective-permute-start
  6.3 5.4 %collective-permute-done.kv_ref.k_recv.v_recv = bf16[512,1024]{1,0:T(8,128)(2,1)S(1)} collective-permute-done((bf16[512,1024]{1,0:T(8,128)(2,1)}, bf16[512,1024]{1,0:T(8,128)(2,1)S(1)}, u32[]{:S(2)}, u32[]{:S(2)}) %collective-permute-start) | collective-permute-done | bytes 1048608 | tf_op jit(solution)/shard_map/ppermute | solution.py:386
  11.7 0.0 copy-start.4
  11.7 1.0 copy-done.4
  12.7 3.1 %shard_map.74 = f32[4,136,128]{2,1,0:T(8,128)} custom-call(bf16[512,1024]{1,0:T(8,128)(2,1)} %copy-done.4), custom_call_target="tpu_custom_call" | custom-call | tf_op jit(solution)/shard_map/pallas_call | solution.py:101
  15.8 1.1 fusion.2
  16.9 0.3 collective-permute-start.1
  17.2 0.7 constant_dynamic-slice_fusion
  17.9 4.0 %collective-permute-done.1 = bf16[4,136,128]{2,1,0:T(8,128)(2,1)S(1)} collective-permute-done((bf16[4,136,128]{2,1,0:T(8,128)(2,1)S(1)}, bf16[4,136,128]{2,1,0:T(8,128)(2,1)S(1)}, u32[]{:S(2)}, u32[]{:S(2)}) %collective-permute-start.1) | collective-permute-done | bytes 139296 | tf_op jit(solution)/shard_map/ppermute | solution.py:112
  21.9 0.0 collective-permute-done.2.q_recv.q_ref
  21.9 0.0 copy-start.2
  21.9 3.1 %collective-permute-start.5 = (bf16[4,136,128]{2,1,0:T(8,128)(2,1)S(1)}, bf16[4,136,128]{2,1,0:T(8,128)(2,1)S(1)}, u32[]{:S(2)}, u32[]{:S(2)}) collective-permute-start(bf16[4,136,128]{2,1,0:T(8,128)(2,1)S(1)} %convert_element_type.26), channel_id=1, source_target_pairs={{0,4},{4,8},{8,12},{12,16},{16,20},{20,24},{24,28},{1,5},{5,9},{9,... | collective-permute-start | bytes 417800 | tf_op jit(solution)/shard_map/ppermute | solution.py:25
  25.1 0.6 slice_bitcast_fusion
  25.7 0.0 copy-done.5
  25.7 3.0 %collective-permute-done.5 = bf16[4,136,128]{2,1,0:T(8,128)(2,1)S(1)} collective-permute-done((bf16[4,136,128]{2,1,0:T(8,128)(2,1)S(1)}, bf16[4,136,128]{2,1,0:T(8,128)(2,1)S(1)}, u32[]{:S(2)}, u32[]{:S(2)}) %collective-permute-start.5) | collective-permute-done | bytes 139296 | tf_op jit(solution)/shard_map/ppermute | solution.py:25
  28.7 3.2 %collective-permute-start.6 = (bf16[4,136,128]{2,1,0:T(8,128)(2,1)S(1)}, bf16[4,136,128]{2,1,0:T(8,128)(2,1)S(1)}, u32[]{:S(2)}, u32[]{:S(2)}) collective-permute-start(bf16[4,136,128]{2,1,0:T(8,128)(2,1)S(1)} %fusion), channel_id=1, source_target_pairs={{0,8},{4,12},{8,16},{12,20},{16,24},{20,28},{1,9},{5,13},{9,17},{1... | collective-permute-start | bytes 417800 | tf_op jit(solution)/shard_map/ppermute | solution.py:25
  31.9 0.6 slice_bitcast_fusion.5
  32.5 0.0 copy-done.2
  32.5 0.0 copy-done.6
  32.5 0.7 add_divide_fusion.gate_ref
  33.2 1.3 collective-permute-start.4
  34.4 1.3 collective-permute-start.3
  35.7 0.0 collective-permute-done.6
  35.8 0.1 fusion.1
  35.8 3.1 %collective-permute-start.7 = (bf16[4,136,128]{2,1,0:T(8,128)(2,1)S(1)}, bf16[4,136,128]{2,1,0:T(8,128)(2,1)S(1)}, u32[]{:S(2)}, u32[]{:S(2)}) collective-permute-start(bf16[4,136,128]{2,1,0:T(8,128)(2,1)S(1)} %fusion.1), channel_id=1, source_target_pairs={{0,16},{4,20},{8,24},{12,28},{1,17},{5,21},{9,25},{13,29},{2,18},{... | collective-permute-start | bytes 417800 | tf_op jit(solution)/shard_map/ppermute | solution.py:25
  38.9 32.6 %shard_map.75 = (f32[2,512,2048]{2,1,0:T(8,128)}, f32[4,2,512,128]{3,2,1,0:T(8,128)}) custom-call(s32[3]{0:T(128)} %get-tuple-element.42.qs_ref, s32[3]{0:T(128)} %get-tuple-element.41.ks_ref, s32[3]{0:T(128)} %get-tuple-element.40.first_ref, s32[3]{0:T(128)} %get-tuple-element.39.diag_ref, s32[1]{0:T(128)} %bitcast.6.off_ref, bf16[512,4096]{1,0:T(8,128)(2,1)} %q_ref.1, ...), custom_call_target="tpu_custom_call" | custom-call | flops 6442450944 | bytes 14680064 | tf_op jit(solution)/shard_map/pallas_call | solution.py:292
  71.5 0.0 collective-permute-done.7
  71.5 0.8 add_subtract_fusion.refs_4_
  72.3 0.0 collective-permute-done.4.refs_2_.refs_3_
  72.3 0.0 copy-start
  72.3 11.3 %collective-permute-done.3.refs_0_.refs_1_ = bf16[512,1024]{1,0:T(8,128)(2,1)S(1)} collective-permute-done((bf16[512,1024]{1,0:T(8,128)(2,1)}, bf16[512,1024]{1,0:T(8,128)(2,1)S(1)}, u32[]{:S(2)}, u32[]{:S(2)}) %collective-permute-start.3) | collective-permute-done | bytes 1048608 | tf_op jit(solution)/shard_map/ppermute | solution.py:394
  83.6 0.0 copy-start.1
  83.6 0.0 copy-done
  83.6 1.0 copy-done.1
  84.5 30.1 %shard_map.77 = bf16[512,2048]{1,0:T(8,128)(2,1)} custom-call(s32[2]{0:T(128)} %get-tuple-element.33.qp_ref, s32[2]{0:T(128)} %get-tuple-element.32.kp_ref, s32[2]{0:T(128)} %get-tuple-element.31.first_ref, s32[2]{0:T(128)} %get-tuple-element.30.last_ref, s32[2]{0:T(128)} %get-tuple-element.29.valid_ref, s32[1]{0:T(128)} %constant.45.clone.1.off_ref, ...), custom_call_target="tpu_custom_call" | custom-call | flops 2147483648 | bytes 10485760 | tf_op jit(solution)/shard_map/pallas_call | solution.py:331
  114.6 0.0 collective-permute-start.8
  114.6 0.6 slice_bitcast_fusion.9
  115.2 30.1 %shard_map.76.full_ref = bf16[512,4096]{1,0:T(8,128)(2,1)} custom-call(s32[2]{0:T(128)} %get-tuple-element.38.qp_ref, s32[2]{0:T(128)} %get-tuple-element.37.kp_ref, s32[2]{0:T(128)} %get-tuple-element.36.first_ref, s32[2]{0:T(128)} %get-tuple-element.35.last_ref, s32[2]{0:T(128)} %get-tuple-element.34.valid_ref, s32[1]{0:T(128)} %bitcast.6.off_ref, ...), custom_call_target="tpu_custom_call" | custom-call | flops 2147483648 | bytes 10485760 | tf_op jit(solution)/shard_map/pallas_call | solution.py:331
  145.3 0.0 collective-permute-done.8.back_ref
  145.3 0.0 copy-start.3
  145.3 1.3 copy-done.3
  146.6 3.0 %shard_map.78 = bf16[512,4096]{1,0:T(8,128)(2,1)} custom-call(s32[1]{0:T(128)} %bitcast.col_ref, bf16[512,4096]{1,0:T(8,128)(2,1)} %shard_map.76.full_ref, bf16[512,2048]{1,0:T(8,128)(2,1)} %copy-done.3), custom_call_target="tpu_custom_call", output_to_operand_aliasing={{}: (1, {})} | custom-call | tf_op jit(solution)/shard_map/pallas_call | solution.py:365
  (4 shorter events, 0.1 us)
Async XLA Ops:
  5.5 20.2 %copy-start.5 = (s32[2,4,3]{2,1,0:T(4,128)S(1)}, s32[2,4,3]{2,1,0:T(4,128)}, u32[]{:S(2)}) copy-start(s32[2,4,3]{2,1,0:T(4,128)} %constant.46.clone) | copy-start | bytes 292
  5.5 27.0 %copy-start.6 = (f32[32]{0:T(128)S(1)}, f32[32]{0:T(128)}, u32[]{:S(2)}) copy-start(f32[32]{0:T(128)} %param.10) | copy-start | bytes 388
  5.5 16.4 %collective-permute-start.2 = (bf16[512,2048]{1,0:T(8,128)(2,1)}, bf16[512,2048]{1,0:T(8,128)(2,1)S(1)}, u32[]{:S(2)}, u32[]{:S(2)}) collective-permute-start(bf16[512,2048]{1,0:T(8,128)(2,1)} %get-tuple-element.19), channel_id=1, source_target_pairs={{0,1},{1,0},{2,3},{3,2},{4,5},{5,4},{6,7},{7,6},{8,9},{9,8},{10,11... | collective-permute-start | bytes 6291464 | tf_op jit(solution)/shard_map/ppermute | solution.py:385
  6.2 5.5 %collective-permute-start = (bf16[512,1024]{1,0:T(8,128)(2,1)}, bf16[512,1024]{1,0:T(8,128)(2,1)S(1)}, u32[]{:S(2)}, u32[]{:S(2)}) collective-permute-start(bf16[512,1024]{1,0:T(8,128)(2,1)} %get-tuple-element.21), channel_id=1, source_target_pairs={{0,1},{1,0},{2,3},{3,2},{4,5},{5,4},{6,7},{7,6},{8,9},{9,8},{10,11... | collective-permute-start | bytes 3145736 | tf_op jit(solution)/shard_map/ppermute | solution.py:386
  11.7 1.0 copy-start.4
  16.9 5.0 %collective-permute-start.1 = (bf16[4,136,128]{2,1,0:T(8,128)(2,1)S(1)}, bf16[4,136,128]{2,1,0:T(8,128)(2,1)S(1)}, u32[]{:S(2)}, u32[]{:S(2)}) collective-permute-start(bf16[4,136,128]{2,1,0:T(8,128)(2,1)S(1)} %get-tuple-element.27), channel_id=1, source_target_pairs={{0,2},{1,3},{2,0},{3,1},{4,6},{5,7},{6,4},{7,5},{8,10},{9,11},{10,... | collective-permute-start | bytes 417800 | tf_op jit(solution)/shard_map/ppermute | solution.py:112
  21.9 10.6 %copy-start.2 = (bf16[512,2048]{1,0:T(8,128)(2,1)}, bf16[512,2048]{1,0:T(8,128)(2,1)S(1)}, u32[]{:S(2)}) copy-start(bf16[512,2048]{1,0:T(8,128)(2,1)S(1)} %collective-permute-done.2.q_recv.q_ref) | copy-start | bytes 6291460
  21.9 6.7 %collective-permute-start.5 = (bf16[4,136,128]{2,1,0:T(8,128)(2,1)S(1)}, bf16[4,136,128]{2,1,0:T(8,128)(2,1)S(1)}, u32[]{:S(2)}, u32[]{:S(2)}) collective-permute-start(bf16[4,136,128]{2,1,0:T(8,128)(2,1)S(1)} %convert_element_type.26), channel_id=1, source_target_pairs={{0,4},{4,8},{8,12},{12,16},{16,20},{20,24},{24,28},{1,5},{5,9},{9,... | collective-permute-start | bytes 417800 | tf_op jit(solution)/shard_map/ppermute | solution.py:25
  28.7 7.1 %collective-permute-start.6 = (bf16[4,136,128]{2,1,0:T(8,128)(2,1)S(1)}, bf16[4,136,128]{2,1,0:T(8,128)(2,1)S(1)}, u32[]{:S(2)}, u32[]{:S(2)}) collective-permute-start(bf16[4,136,128]{2,1,0:T(8,128)(2,1)S(1)} %fusion), channel_id=1, source_target_pairs={{0,8},{4,12},{8,16},{12,20},{16,24},{20,28},{1,9},{5,13},{9,17},{1... | collective-permute-start | bytes 417800 | tf_op jit(solution)/shard_map/ppermute | solution.py:25
  33.2 39.1 %collective-permute-start.4 = (bf16[512,1024]{1,0:T(8,128)(2,1)}, bf16[512,1024]{1,0:T(8,128)(2,1)S(1)}, u32[]{:S(2)}, u32[]{:S(2)}) collective-permute-start(bf16[512,1024]{1,0:T(8,128)(2,1)} %get-tuple-element.21), channel_id=1, source_target_pairs={{0,3},{1,2},{4,7},{5,6},{8,11},{9,10},{12,15},{13,14},{16,19},{17,... | collective-permute-start | bytes 3145736 | tf_op jit(solution)/shard_map/ppermute | solution.py:396
  34.4 49.1 %collective-permute-start.3 = (bf16[512,1024]{1,0:T(8,128)(2,1)}, bf16[512,1024]{1,0:T(8,128)(2,1)S(1)}, u32[]{:S(2)}, u32[]{:S(2)}) collective-permute-start(bf16[512,1024]{1,0:T(8,128)(2,1)} %get-tuple-element.20.k_keep.v_keep), channel_id=1, source_target_pairs={{0,2},{1,3},{4,6},{5,7},{8,10},{9,11},{12,14},{13,15},{16,18},{17,... | collective-permute-start | bytes 3145736 | tf_op jit(solution)/shard_map/ppermute | solution.py:394
  35.8 35.7 %collective-permute-start.7 = (bf16[4,136,128]{2,1,0:T(8,128)(2,1)S(1)}, bf16[4,136,128]{2,1,0:T(8,128)(2,1)S(1)}, u32[]{:S(2)}, u32[]{:S(2)}) collective-permute-start(bf16[4,136,128]{2,1,0:T(8,128)(2,1)S(1)} %fusion.1), channel_id=1, source_target_pairs={{0,16},{4,20},{8,24},{12,28},{1,17},{5,21},{9,25},{13,29},{2,18},{... | collective-permute-start | bytes 417800 | tf_op jit(solution)/shard_map/ppermute | solution.py:25
  72.3 11.3 %copy-start = (bf16[512,1024]{1,0:T(8,128)(2,1)}, bf16[512,1024]{1,0:T(8,128)(2,1)S(1)}, u32[]{:S(2)}) copy-start(bf16[512,1024]{1,0:T(8,128)(2,1)S(1)} %collective-permute-done.4.refs_2_.refs_3_) | copy-start | bytes 3145732
  83.6 1.0 copy-start.1
  114.6 30.7 %collective-permute-start.8 = (bf16[512,2048]{1,0:T(8,128)(2,1)}, bf16[512,2048]{1,0:T(8,128)(2,1)S(1)}, u32[]{:S(2)}, u32[]{:S(2)}) collective-permute-start(bf16[512,2048]{1,0:T(8,128)(2,1)} %shard_map.77), channel_id=1, source_target_pairs={{0,1},{1,0},{2,3},{3,2},{4,5},{5,4},{6,7},{7,6},{8,9},{9,8},{10,11... | collective-permute-start | bytes 6291464 | tf_op jit(solution)/shard_map/ppermute | solution.py:344
  145.3 1.3 copy-start.3

commit v20 on v18

--- a/solution.py
+++ b/solution.py
@@ -31,7 +31,7 @@
         key_feature = feature(k_ref[:, lanes].astype(jnp.float32))
         value_data = v_ref[:, lanes].astype(jnp.float32)
         o_ref[head, :HD, :] = jnp.dot(
-            key_feature.T, value_data, precision=lax.Precision.HIGHEST,
+            key_feature.T, value_data, precision=lax.Precision.HIGH,
             preferred_element_type=jnp.float32,
         )
         o_ref[head, HD:, :] = jnp.zeros((STATE_ROWS - HD, HD), jnp.float32)
@@ -204,7 +204,7 @@
         local_part = acc_sc[:, lanes] / l_sc[head]
         query_feature = feature(q_ref[:, lanes].astype(jnp.float32))
         numerator = jnp.dot(
-            query_feature, memory, precision=lax.Precision.HIGHEST,
+            query_feature, memory, precision=lax.Precision.HIGH,
             preferred_element_type=jnp.float32,
         )
         denominator = jnp.maximum(

time: 148 us -> 143 us (0.966)
  Pallas kernels: 102 us -> 97.7 us
    pallas_call x2, Pallas kernels: 60.1 us -> 56.2 us  [far_call(): pl.pallas_call(functools.partial(far_kernel, group_size=group_size), grid...]
where the time goes in v20:
time: 143 us; the launch traced here: 142 us
  Pallas kernels  97.7 us (68%)
  waiting for transfers between devices  21.6 us (15%)
  starting transfers between devices  13.5 us (9%)
  local copies, waits for them, and re-layouts  4.83 us (3%)
  other arithmetic  4.47 us (3%)
    pallas_call x2, Pallas kernels, far_call(): pl.pallas_call(functools.partial(far_kernel, group_size=group_size), grid...  56.2 us
    pallas_call x1, Pallas kernels, attend(): pl.pallas_call(functools.partial(near_kernel, group_size=group_size), gri...  32.7 us
    ppermute x1, waiting for transfers between devices, body(): lax.ppermute(keep_kv, 'head', [(p, p + 2 * s) for p in range(parts - 2 *...  11.3 us
    ppermute x3, starting transfers between devices, shifted(): lax.ppermute(value, axis, [(source, source + steps) for source in range(c...  9.3 us
    pallas_call x1, Pallas kernels, split_inputs(): pl.pallas_call(split_kernel, grid_spec=grid_spec, out_shape=[kv_shape, q_...  5.74 us
    ppermute x1, waiting for transfers between devices, chip_states(): lax.ppermute(total.astype(jnp.bfloat16), 'head', [(p, p ^ steps) for p in...  3.96 us
    ppermute x1, waiting for transfers between devices, chip_states(): lax.ppermute(send.astype(jnp.bfloat16), 'head', [(p, p ^ 1) for p in rang...  3.41 us
    pallas_call x1, Pallas kernels, place_back(): pl.pallas_call(place_kernel, grid_spec=grid_spec, out_shape=jax.ShapeDtyp...  3.04 us
  transfers between devices with their start and end apart: 10, of which 4 were waited for; matrix products, arithmetic and copies ran while one was open for 5% of the time, Pallas kernels for 43%

profile of v20, /device:TPU:13, one launch (start us, length us, event | category | flops | bytes accessed | tf_op | source)
XLA Modules:
  0.0 142.2 jit_solution(16564287795267027181)
XLA Ops:
  0.0 5.7 %shard_map.73 = (bf16[512,1024]{1,0:T(8,128)(2,1)}, bf16[512,2048]{1,0:T(8,128)(2,1)}, bf16[512,1024]{1,0:T(8,128)(2,1)}, f32[4,136,128]{2,1,0:T(8,128)}, f32[4,136,128]{2,1,0:T(8,128)}) custom-call(s32[1]{0:T(128)} %bitcast.7.core_ref, bf16[512,1024]{1,0:T(8,128)(2,1)} %k_send.1, bf16[512,1024]{1,0:T(8,128)(2,1)} %v_send.1, bf16[512,4096]{1,0:T(8,128)(2,1)} %q_ref.1, ...), custom_call_target="tpu_custom_call" | custom-call | tf_op jit(solution)/shard_map/pallas_call | solution.py:81
  5.7 0.0 copy-start.4
  5.7 0.0 copy-start.5
  5.7 0.7 collective-permute-start.2
  6.5 0.1 collective-permute-start.3
  6.6 1.0 convert_element_type.30
  7.5 0.5 collective-permute-start
  8.0 3.4 %collective-permute-done = bf16[4,136,128]{2,1,0:T(8,128)(2,1)S(1)} collective-permute-done((bf16[4,136,128]{2,1,0:T(8,128)(2,1)S(1)}, bf16[4,136,128]{2,1,0:T(8,128)(2,1)S(1)}, u32[]{:S(2)}, u32[]{:S(2)}) %collective-permute-start) | collective-permute-done | bytes 139296 | tf_op jit(solution)/shard_map/ppermute | solution.py:90
  11.4 1.0 fusion
  12.4 0.3 collective-permute-start.1
  12.7 0.7 constant_dynamic-slice_fusion
  13.4 4.0 %collective-permute-done.1 = bf16[4,136,128]{2,1,0:T(8,128)(2,1)S(1)} collective-permute-done((bf16[4,136,128]{2,1,0:T(8,128)(2,1)S(1)}, bf16[4,136,128]{2,1,0:T(8,128)(2,1)S(1)}, u32[]{:S(2)}, u32[]{:S(2)}) %collective-permute-start.1) | collective-permute-done | bytes 139296 | tf_op jit(solution)/shard_map/ppermute | solution.py:93
  17.4 1.0 convert_add_fusion.2
  18.4 0.0 collective-permute-done.3.k_recv.v_recv
  18.4 0.0 collective-permute-done.2.q_recv.q_ref
  18.4 0.0 copy-start.2
  18.5 3.1 %collective-permute-start.6 = (bf16[4,136,128]{2,1,0:T(8,128)(2,1)S(1)}, bf16[4,136,128]{2,1,0:T(8,128)(2,1)S(1)}, u32[]{:S(2)}, u32[]{:S(2)}) collective-permute-start(bf16[4,136,128]{2,1,0:T(8,128)(2,1)S(1)} %convert_element_type.34), channel_id=1, source_target_pairs={{0,4},{4,8},{8,12},{12,16},{16,20},{20,24},{24,28},{1,5},{5,9},{9,... | collective-permute-start | bytes 417800 | tf_op jit(solution)/shard_map/ppermute | solution.py:25
  21.6 0.6 slice_bitcast_fusion
  22.2 0.0 copy-done.4
  22.2 3.0 %collective-permute-done.6 = bf16[4,136,128]{2,1,0:T(8,128)(2,1)S(1)} collective-permute-done((bf16[4,136,128]{2,1,0:T(8,128)(2,1)S(1)}, bf16[4,136,128]{2,1,0:T(8,128)(2,1)S(1)}, u32[]{:S(2)}, u32[]{:S(2)}) %collective-permute-start.6) | collective-permute-done | bytes 139296 | tf_op jit(solution)/shard_map/ppermute | solution.py:25
  25.2 3.2 %collective-permute-start.7 = (bf16[4,136,128]{2,1,0:T(8,128)(2,1)S(1)}, bf16[4,136,128]{2,1,0:T(8,128)(2,1)S(1)}, u32[]{:S(2)}, u32[]{:S(2)}) collective-permute-start(bf16[4,136,128]{2,1,0:T(8,128)(2,1)S(1)} %fusion.1), channel_id=1, source_target_pairs={{0,8},{4,12},{8,16},{12,20},{16,24},{20,28},{1,9},{5,13},{9,17},{1... | collective-permute-start | bytes 417800 | tf_op jit(solution)/shard_map/ppermute | solution.py:25
  28.4 0.6 slice_bitcast_fusion.5
  29.0 0.0 copy-done.2
  29.0 0.0 copy-done.5
  29.0 0.6 add_divide_fusion.gate_ref
  29.6 1.3 collective-permute-start.5
  30.9 1.3 collective-permute-start.4
  32.2 0.0 collective-permute-done.7
  32.2 0.1 fusion.2
  32.3 3.0 %collective-permute-start.8 = (bf16[4,136,128]{2,1,0:T(8,128)(2,1)S(1)}, bf16[4,136,128]{2,1,0:T(8,128)(2,1)S(1)}, u32[]{:S(2)}, u32[]{:S(2)}) collective-permute-start(bf16[4,136,128]{2,1,0:T(8,128)(2,1)S(1)} %fusion.2), channel_id=1, source_target_pairs={{0,16},{4,20},{8,24},{12,28},{1,17},{5,21},{9,25},{13,29},{2,18},{... | collective-permute-start | bytes 417800 | tf_op jit(solution)/shard_map/ppermute | solution.py:25
  35.3 32.7 %shard_map.74 = (f32[2,512,2048]{2,1,0:T(8,128)}, f32[4,2,512,128]{3,2,1,0:T(8,128)}) custom-call(s32[3]{0:T(128)} %get-tuple-element.42.qs_ref, s32[3]{0:T(128)} %get-tuple-element.41.ks_ref, s32[3]{0:T(128)} %get-tuple-element.40.first_ref, s32[3]{0:T(128)} %get-tuple-element.39.diag_ref, s32[1]{0:T(128)} %bitcast.6.off_ref, bf16[512,4096]{1,0:T(8,128)(2,1)} %q_ref.1, ...), custom_call_target="tpu_custom_call" | custom-call | flops 6442450944 | bytes 14680064 | tf_op jit(solution)/shard_map/pallas_call | solution.py:273
  68.0 0.0 collective-permute-done.8
  68.0 0.8 add_subtract_fusion.refs_4_
  68.8 0.0 collective-permute-done.5.refs_2_.refs_3_
  68.8 0.0 copy-start
  68.8 11.3 %collective-permute-done.4.refs_0_.refs_1_ = bf16[512,1024]{1,0:T(8,128)(2,1)S(1)} collective-permute-done((bf16[512,1024]{1,0:T(8,128)(2,1)}, bf16[512,1024]{1,0:T(8,128)(2,1)S(1)}, u32[]{:S(2)}, u32[]{:S(2)}) %collective-permute-start.4) | collective-permute-done | bytes 1048608 | tf_op jit(solution)/shard_map/ppermute | solution.py:375
  80.0 0.0 copy-start.1
  80.0 0.0 copy-done
  80.1 1.0 copy-done.1
  81.0 28.2 %shard_map.76 = bf16[512,2048]{1,0:T(8,128)(2,1)} custom-call(s32[2]{0:T(128)} %get-tuple-element.33.qp_ref, s32[2]{0:T(128)} %get-tuple-element.32.kp_ref, s32[2]{0:T(128)} %get-tuple-element.31.first_ref, s32[2]{0:T(128)} %get-tuple-element.30.last_ref, s32[2]{0:T(128)} %get-tuple-element.29.valid_ref, s32[1]{0:T(128)} %constant.45.clone.1.off_ref, ...), custom_call_target="tpu_custom_call" | custom-call | flops 2147483648 | bytes 10485760 | tf_op jit(solution)/shard_map/pallas_call | solution.py:312
  109.2 0.0 collective-permute-start.9
  109.2 0.6 slice_bitcast_fusion.9
  109.8 28.0 %shard_map.75.full_ref = bf16[512,4096]{1,0:T(8,128)(2,1)} custom-call(s32[2]{0:T(128)} %get-tuple-element.38.qp_ref, s32[2]{0:T(128)} %get-tuple-element.37.kp_ref, s32[2]{0:T(128)} %get-tuple-element.36.first_ref, s32[2]{0:T(128)} %get-tuple-element.35.last_ref, s32[2]{0:T(128)} %get-tuple-element.34.valid_ref, s32[1]{0:T(128)} %bitcast.6.off_ref, ...), custom_call_target="tpu_custom_call" | custom-call | flops 2147483648 | bytes 10485760 | tf_op jit(solution)/shard_map/pallas_call | solution.py:312
  137.8 0.0 collective-permute-done.9.back_ref
  137.8 0.0 copy-start.3
  137.8 1.3 copy-done.3
  139.2 3.0 %shard_map.77 = bf16[512,4096]{1,0:T(8,128)(2,1)} custom-call(s32[1]{0:T(128)} %bitcast.col_ref, bf16[512,4096]{1,0:T(8,128)(2,1)} %shard_map.75.full_ref, bf16[512,2048]{1,0:T(8,128)(2,1)} %copy-done.3), custom_call_target="tpu_custom_call", output_to_operand_aliasing={{}: (1, {})} | custom-call | tf_op jit(solution)/shard_map/pallas_call | solution.py:346
  (3 shorter events, 0.1 us)
Async XLA Ops:
  5.7 16.4 %copy-start.4 = (s32[2,4,3]{2,1,0:T(4,128)S(1)}, s32[2,4,3]{2,1,0:T(4,128)}, u32[]{:S(2)}) copy-start(s32[2,4,3]{2,1,0:T(4,128)} %constant.46.clone) | copy-start | bytes 292
  5.7 23.3 %copy-start.5 = (f32[32]{0:T(128)S(1)}, f32[32]{0:T(128)}, u32[]{:S(2)}) copy-start(f32[32]{0:T(128)} %param.10) | copy-start | bytes 388
  5.7 12.7 %collective-permute-start.2 = (bf16[512,2048]{1,0:T(8,128)(2,1)}, bf16[512,2048]{1,0:T(8,128)(2,1)S(1)}, u32[]{:S(2)}, u32[]{:S(2)}) collective-permute-start(bf16[512,2048]{1,0:T(8,128)(2,1)} %get-tuple-element.21), channel_id=1, source_target_pairs={{0,1},{1,0},{2,3},{3,2},{4,5},{5,4},{6,7},{7,6},{8,9},{9,8},{10,11... | collective-permute-start | bytes 6291464 | tf_op jit(solution)/shard_map/ppermute | solution.py:367
  6.5 11.9 %collective-permute-start.3 = (bf16[512,1024]{1,0:T(8,128)(2,1)}, bf16[512,1024]{1,0:T(8,128)(2,1)}, u32[]{:S(2)}, u32[]{:S(2)}) collective-permute-start(bf16[512,1024]{1,0:T(8,128)(2,1)} %get-tuple-element.23), channel_id=1, source_target_pairs={{0,1},{1,0},{2,3},{3,2},{4,5},{5,4},{6,7},{7,6},{8,9},{9,8},{10,11... | collective-permute-start | bytes 3145736 | tf_op jit(solution)/shard_map/ppermute | solution.py:368
  7.5 3.9 %collective-permute-start = (bf16[4,136,128]{2,1,0:T(8,128)(2,1)S(1)}, bf16[4,136,128]{2,1,0:T(8,128)(2,1)S(1)}, u32[]{:S(2)}, u32[]{:S(2)}) collective-permute-start(bf16[4,136,128]{2,1,0:T(8,128)(2,1)S(1)} %convert_element_type.30), channel_id=1, source_target_pairs={{0,1},{1,0},{2,3},{3,2},{4,5},{5,4},{6,7},{7,6},{8,9},{9,8},{10,11... | collective-permute-start | bytes 417800 | tf_op jit(solution)/shard_map/ppermute | solution.py:90
  12.4 5.0 %collective-permute-start.1 = (bf16[4,136,128]{2,1,0:T(8,128)(2,1)S(1)}, bf16[4,136,128]{2,1,0:T(8,128)(2,1)S(1)}, u32[]{:S(2)}, u32[]{:S(2)}) collective-permute-start(bf16[4,136,128]{2,1,0:T(8,128)(2,1)S(1)} %fusion), channel_id=1, source_target_pairs={{0,2},{1,3},{2,0},{3,1},{4,6},{5,7},{6,4},{7,5},{8,10},{9,11},{10,... | collective-permute-start | bytes 417800 | tf_op jit(solution)/shard_map/ppermute | solution.py:93
  18.4 10.6 %copy-start.2 = (bf16[512,2048]{1,0:T(8,128)(2,1)}, bf16[512,2048]{1,0:T(8,128)(2,1)S(1)}, u32[]{:S(2)}) copy-start(bf16[512,2048]{1,0:T(8,128)(2,1)S(1)} %collective-permute-done.2.q_recv.q_ref) | copy-start | bytes 6291460
  18.5 6.7 %collective-permute-start.6 = (bf16[4,136,128]{2,1,0:T(8,128)(2,1)S(1)}, bf16[4,136,128]{2,1,0:T(8,128)(2,1)S(1)}, u32[]{:S(2)}, u32[]{:S(2)}) collective-permute-start(bf16[4,136,128]{2,1,0:T(8,128)(2,1)S(1)} %convert_element_type.34), channel_id=1, source_target_pairs={{0,4},{4,8},{8,12},{12,16},{16,20},{20,24},{24,28},{1,5},{5,9},{9,... | collective-permute-start | bytes 417800 | tf_op jit(solution)/shard_map/ppermute | solution.py:25
  25.2 7.0 %collective-permute-start.7 = (bf16[4,136,128]{2,1,0:T(8,128)(2,1)S(1)}, bf16[4,136,128]{2,1,0:T(8,128)(2,1)S(1)}, u32[]{:S(2)}, u32[]{:S(2)}) collective-permute-start(bf16[4,136,128]{2,1,0:T(8,128)(2,1)S(1)} %fusion.1), channel_id=1, source_target_pairs={{0,8},{4,12},{8,16},{12,20},{16,24},{20,28},{1,9},{5,13},{9,17},{1... | collective-permute-start | bytes 417800 | tf_op jit(solution)/shard_map/ppermute | solution.py:25
  29.6 39.1 %collective-permute-start.5 = (bf16[512,1024]{1,0:T(8,128)(2,1)}, bf16[512,1024]{1,0:T(8,128)(2,1)S(1)}, u32[]{:S(2)}, u32[]{:S(2)}) collective-permute-start(bf16[512,1024]{1,0:T(8,128)(2,1)} %get-tuple-element.23), channel_id=1, source_target_pairs={{0,3},{1,2},{4,7},{5,6},{8,11},{9,10},{12,15},{13,14},{16,19},{17,... | collective-permute-start | bytes 3145736 | tf_op jit(solution)/shard_map/ppermute | solution.py:377
  30.9 49.1 %collective-permute-start.4 = (bf16[512,1024]{1,0:T(8,128)(2,1)}, bf16[512,1024]{1,0:T(8,128)(2,1)S(1)}, u32[]{:S(2)}, u32[]{:S(2)}) collective-permute-start(bf16[512,1024]{1,0:T(8,128)(2,1)} %get-tuple-element.22.k_keep.v_keep), channel_id=1, source_target_pairs={{0,2},{1,3},{4,6},{5,7},{8,10},{9,11},{12,14},{13,15},{16,18},{17,... | collective-permute-start | bytes 3145736 | tf_op jit(solution)/shard_map/ppermute | solution.py:375
  32.3 35.7 %collective-permute-start.8 = (bf16[4,136,128]{2,1,0:T(8,128)(2,1)S(1)}, bf16[4,136,128]{2,1,0:T(8,128)(2,1)S(1)}, u32[]{:S(2)}, u32[]{:S(2)}) collective-permute-start(bf16[4,136,128]{2,1,0:T(8,128)(2,1)S(1)} %fusion.2), channel_id=1, source_target_pairs={{0,16},{4,20},{8,24},{12,28},{1,17},{5,21},{9,25},{13,29},{2,18},{... | collective-permute-start | bytes 417800 | tf_op jit(solution)/shard_map/ppermute | solution.py:25
  68.8 11.3 %copy-start = (bf16[512,1024]{1,0:T(8,128)(2,1)}, bf16[512,1024]{1,0:T(8,128)(2,1)S(1)}, u32[]{:S(2)}) copy-start(bf16[512,1024]{1,0:T(8,128)(2,1)S(1)} %collective-permute-done.5.refs_2_.refs_3_) | copy-start | bytes 3145732
  80.0 1.0 copy-start.1
  109.2 28.6 %collective-permute-start.9 = (bf16[512,2048]{1,0:T(8,128)(2,1)}, bf16[512,2048]{1,0:T(8,128)(2,1)S(1)}, u32[]{:S(2)}, u32[]{:S(2)}) collective-permute-start(bf16[512,2048]{1,0:T(8,128)(2,1)} %shard_map.76), channel_id=1, source_target_pairs={{0,1},{1,0},{2,3},{3,2},{4,5},{5,4},{6,7},{7,6},{8,9},{9,8},{10,11... | collective-permute-start | bytes 6291464 | tf_op jit(solution)/shard_map/ppermute | solution.py:325
  137.8 1.3 copy-start.3
